TPU v7x, 512 devices: a whole 4x8x8 slice. The times are simulated.
512 devices in a mesh: pipe: 16 (over z, core), expert: 32 (over x, y).
Axes of the slice: x: 4, y: 8, z: 8, core: 2. Of those that a mesh axis runs over, the one named last changes fastest.
Arguments:
- acts: bfloat16 [16, 2048, 3584], P('pipe', 'expert'), may hold values from -6 to 6
- norm_gain: bfloat16 [16, 3584], P('pipe'), may hold values from 0.5 to 1.5
- gate_w: bfloat16 [16, 32, 3584, 128], P('pipe', 'expert'), may hold values from -0.09375 to 0.09375
- up_w: bfloat16 [16, 32, 3584, 128], P('pipe', 'expert'), may hold values from -0.09375 to 0.09375
- down_w: bfloat16 [16, 32, 128, 3584], P('pipe', 'expert'), may hold values from -0.1875 to 0.1875
- route_ids: int32 [16, 2, 2048, 1], P('pipe', None, 'expert'), may hold values from 0 to 3; in each aligned block of 64 rows (0 to 63, 64 to 127, ..., all dimensions but the last counted through in order) at most 17 rows name the same one
- route_wts: int32 [16, 2, 2048, 1], P('pipe', None, 'expert'), may hold values from 512 to 2047
Outputs:
- out: bfloat16 [16, 2048, 3584], P('pipe', 'expert')
Inputs may be any that keep to these rules, and one draw needn't show every extreme that they name: `route_ids`: within one row the 1 expert differ. In each aligned block of 64 rows (one device's rows of one section and tick), no expert is named by more than 17 rows; in some blocks an expert is named by exactly 17.
All inputs are finite; a program needn't handle non-finite values.
Results may differ from a plain program's by a relative error of at most 0.0052.
Values may be sent and summed in bfloat16 or wider, within the bound.
No kernel may reach another device: no remote copies, remote signals or barrier semaphores. Data moves between devices by JAX's collectives and lax.ppermute only.
A program may use at most 64 MiB of HBM per device.

v0:
```python
import jax
import jax.numpy as jnp
from jax import lax
from jax.sharding import PartitionSpec as P

EXPERTS = 4
MOST = 17


NORM_EPS = 1e-06
FIXED_UNIT = 1.0 / 4096.0


def shifted(value, axis, steps):
    count = lax.axis_size(axis)
    pairs = [(source, (source + steps) % count) for source in range(count)]
    return lax.ppermute(value, axis, pairs)


def slot_index(expert_ids, capacity, experts):
    flat_ids = expert_ids.reshape(-1)
    onehot = (flat_ids[:, None] == jnp.arange(experts, dtype=jnp.int32)[None, :]).astype(jnp.int32)
    before = jnp.cumsum(onehot, axis=0) - onehot
    slot_rank = jnp.sum(before * onehot, axis=1)
    return (flat_ids * capacity + slot_rank).reshape(expert_ids.shape)


def place_rows(normed, slot_ids, slot_total):
    slot_marks = slot_ids[:, :, None] == jnp.arange(slot_total, dtype=jnp.int32)[None, None, :]
    placing = jnp.sum(slot_marks.astype(jnp.float32), axis=1).T.astype(jnp.bfloat16)
    return jnp.dot(placing, normed, preferred_element_type=jnp.float32).astype(jnp.bfloat16)


def expert_slice(received, w_gate, w_up, w_down):
    model_width = received.shape[2]
    flat_rows = received.reshape(-1, model_width)
    gate_act = jnp.dot(flat_rows, w_gate, preferred_element_type=jnp.float32)
    up_act = jnp.dot(flat_rows, w_up, preferred_element_type=jnp.float32)
    hidden = (jax.nn.silu(gate_act) * up_act).astype(jnp.bfloat16)
    slice_part = jnp.dot(hidden, w_down, preferred_element_type=jnp.float32).astype(jnp.bfloat16)
    return slice_part.reshape(received.shape)


def routed_branch(normed, expert_ids, route_weight, w_gate, w_up, w_down):
    axis_size = lax.axis_size("expert")
    group_size = axis_size // EXPERTS
    model_width = normed.shape[1]
    slot_ids = slot_index(expert_ids, MOST, EXPERTS)
    per_expert = place_rows(normed, slot_ids, EXPERTS * MOST).reshape(EXPERTS, 1, MOST, model_width)
    outgoing = jnp.broadcast_to(per_expert, (EXPERTS, group_size, MOST, model_width)).reshape(
        axis_size, MOST, model_width
    )
    slot_block = lax.all_to_all(outgoing, "expert", split_axis=0, concat_axis=0, tiled=True)
    item_count = slot_block.shape[1]
    slice_part = expert_slice(slot_block, w_gate, w_up, w_down)
    returned_parts = lax.all_to_all(slice_part, "expert", split_axis=0, concat_axis=0, tiled=True)
    grouped = returned_parts.reshape(EXPERTS, group_size, item_count, model_width)
    returned = jnp.sum(grouped.astype(jnp.float32), axis=1)
    picked = returned.reshape(EXPERTS * MOST, model_width)[slot_ids]
    weights = route_weight.astype(jnp.float32) * FIXED_UNIT
    return jnp.sum(weights[:, :, None] * picked, axis=1)


def layer_terms(rows_in, gain_row, w_gate, w_up, w_down, expert_ids, route_weight):
    values = rows_in.astype(jnp.float32)
    inv_rms = lax.rsqrt(jnp.mean(values * values, axis=1, keepdims=True) + NORM_EPS)
    normed = (values * inv_rms * gain_row.astype(jnp.float32)).astype(jnp.bfloat16)
    branch = routed_branch(normed, expert_ids, route_weight, w_gate, w_up, w_down)
    return (values, branch)


def shards(acts, norm_gain, gate_w, up_w, down_w, route_ids, route_wts):
    section_index = lax.axis_index("pipe")
    rows_in = acts[0]
    gain_row = norm_gain[0]
    w_gate = gate_w[0, 0]
    w_up = up_w[0, 0]
    w_down = down_w[0, 0]
    values, branch = layer_terms(
        rows_in, gain_row, w_gate, w_up, w_down, route_ids[0, 0], route_wts[0, 0]
    )
    first_out = (values + branch).astype(jnp.bfloat16)
    arrived = shifted(first_out, "pipe", 1)
    values, branch = layer_terms(
        arrived, gain_row, w_gate, w_up, w_down, route_ids[0, 1], route_wts[0, 1]
    )
    second = (values + branch).astype(jnp.bfloat16)
    result_rows = jnp.where(section_index == 0, arrived, second)
    return result_rows[None]


def solution(mesh):
    return jax.shard_map(
        shards,
        mesh=mesh,
        in_specs=(
            P("pipe", "expert", None),
            P("pipe", None),
            P("pipe", "expert", None, None),
            P("pipe", "expert", None, None),
            P("pipe", "expert", None, None),
            P("pipe", None, "expert", None),
            P("pipe", None, "expert", None),
        ),
        out_specs=P("pipe", "expert", None),
        check_vma=False,
    )
```

profile of v0, /device:TPU:253, one launch (start us, length us, event | category | flops | bytes accessed | tf_op | source)
XLA Modules:
  0.0 596.7 jit_solution(12781625009579676016)
XLA Ops:
  1.1 0.8 convert_reduce_fusion.2
  1.9 1.2 fusion.6
  4.0 1.4 convolution_convert_fusion.3
  5.9 129.5 %all_to_all.20 = bf16[32,17,3584]{2,1,0:T(8,128)(2,1)} all-to-all(bf16[32,17,3584]{2,1,0:T(8,128)(2,1)S(1)} %bitcast.67), channel_id=1, replica_groups=mesh['pipe'=16,'expert'=32] {'expert'}, dimensions={0} | all-to-all | bytes 7798784 | tf_op jit(solution)/shard_map/all_to_all | solution.py:53
  135.4 5.6 reshape.215
  141.0 3.3 fusion.18
  144.4 8.2 %convolution_convert_fusion.1 = bf16[544,3584]{1,0:T(8,128)(2,1)} fusion(bf16[544,3584]{1,0:T(8,128)(2,1)} %reshape.215, bf16[1,1,128,3584]{3,2,1,0:T(8,128)(2,1)S(1)} %copy-done, bf16[1,1,3584,128]{3,2,1,0:T(8,128)(2,1)S(1)} %copy-done.4, f32[544,128]{1,0:T(8,128)S(1)} %fusion.18), kind=kOutput, calls=%fused_computation.5 | convolution fusion | flops 1000611840 | bytes 9912320 | tf_op jit(solution)/shard_map/dot_general | solution.py:40
  152.5 5.5 reshape.216
  158.1 8.5 %all-to-all-start.1 = ((bf16[32,17,3584]{2,1,0:T(8,128)(2,1)}), bf16[32,17,3584]{2,1,0:T(8,128)(2,1)}, u32[]{:S(2)}, u32[]{:S(2)}) async-start(bf16[32,17,3584]{2,1,0:T(8,128)(2,1)} %reshape.216), calls=%async_computation.1 | async-start | bytes 11010048 | tf_op jit(solution)/shard_map/all_to_all | solution.py:56
  166.7 124.0 %all-to-all-done.1 = bf16[32,17,3584]{2,1,0:T(8,128)(2,1)} async-done(((bf16[32,17,3584]{2,1,0:T(8,128)(2,1)}), bf16[32,17,3584]{2,1,0:T(8,128)(2,1)}, u32[]{:S(2)}, u32[]{:S(2)}) %all-to-all-start.1) | async-done | bytes 3899424 | tf_op jit(solution)/shard_map/all_to_all | solution.py:56
  290.7 3.6 convert_reduce_fusion.1
  294.4 0.9 gather_fusion
  295.6 3.7 collective-permute-start
  299.3 5.4 collective-permute-done
  306.4 130.0 %all_to_all.21 = bf16[32,17,3584]{2,1,0:T(8,128)(2,1)} all-to-all(bf16[32,17,3584]{2,1,0:T(8,128)(2,1)S(1)} %bitcast.68), channel_id=1, replica_groups=mesh['pipe'=16,'expert'=32] {'expert'}, dimensions={0} | all-to-all | bytes 7798784 | tf_op jit(solution)/shard_map/all_to_all | solution.py:53
  436.4 5.6 reshape.219
  442.1 3.4 fusion.16
  445.4 8.2 %convolution_convert_fusion = bf16[544,3584]{1,0:T(8,128)(2,1)} fusion(bf16[544,3584]{1,0:T(8,128)(2,1)} %reshape.219, bf16[1,1,128,3584]{3,2,1,0:T(8,128)(2,1)S(1)} %copy-done, bf16[1,1,3584,128]{3,2,1,0:T(8,128)(2,1)S(1)} %copy-done.5, f32[544,128]{1,0:T(8,128)S(1)} %fusion.16), kind=kOutput, calls=%fused_computation.4 | convolution fusion | flops 1000611840 | bytes 9912320 | tf_op jit(solution)/shard_map/dot_general | solution.py:40
  453.6 5.5 reshape.220
  459.1 7.2 %all-to-all-start.3 = ((bf16[32,17,3584]{2,1,0:T(8,128)(2,1)}), bf16[32,17,3584]{2,1,0:T(8,128)(2,1)}, u32[]{:S(2)}, u32[]{:S(2)}) async-start(bf16[32,17,3584]{2,1,0:T(8,128)(2,1)} %reshape.220), calls=%async_computation.3 | async-start | bytes 11010048 | tf_op jit(solution)/shard_map/all_to_all | solution.py:56
  466.4 124.5 %all-to-all-done.3 = bf16[32,17,3584]{2,1,0:T(8,128)(2,1)} async-done(((bf16[32,17,3584]{2,1,0:T(8,128)(2,1)}), bf16[32,17,3584]{2,1,0:T(8,128)(2,1)}, u32[]{:S(2)}, u32[]{:S(2)}) %all-to-all-start.3) | async-done | bytes 3899424 | tf_op jit(solution)/shard_map/all_to_all | solution.py:56
  590.9 3.6 convert_reduce_fusion
  594.7 0.9 gather_fusion.1
  595.7 1.0 fusion.21
  (42 shorter events, 5.0 us)
Async XLA Ops:
  0.0 144.3 %copy-start = (bf16[1,1,128,3584]{3,2,1,0:T(8,128)(2,1)S(1)}, bf16[1,1,128,3584]{3,2,1,0:T(8,128)(2,1)}, u32[]{:S(2)}) copy-start(bf16[1,1,128,3584]{3,2,1,0:T(8,128)(2,1)} %param.11) | copy-start | bytes 2752516
  135.4 5.6 copy-start.8
  141.0 3.4 copy-start.4
  158.1 8.6 %copy-start.6 = (s32[1,2,64,1]{2,3,1,0:T(1,128)S(1)}, s32[1,2,64,1]{2,3,1,0:T(1,128)}, u32[]{:S(2)}) copy-start(s32[1,2,64,1]{2,3,1,0:T(1,128)} %param.12) | copy-start | bytes 1540
  158.1 8.6 %copy-start.7 = (s32[1,2,64,1]{2,3,1,0:T(1,128)S(1)}, s32[1,2,64,1]{2,3,1,0:T(1,128)}, u32[]{:S(2)}) copy-start(s32[1,2,64,1]{2,3,1,0:T(1,128)} %param.13) | copy-start | bytes 1540
  158.1 132.6 %all-to-all-start.1 = ((bf16[32,17,3584]{2,1,0:T(8,128)(2,1)}), bf16[32,17,3584]{2,1,0:T(8,128)(2,1)}, u32[]{:S(2)}, u32[]{:S(2)}) async-start(bf16[32,17,3584]{2,1,0:T(8,128)(2,1)} %reshape.216), calls=%async_computation.1 | async-start | bytes 11010048 | tf_op jit(solution)/shard_map/all_to_all | solution.py:56
  294.4 1.0 copy-start.3
  295.6 9.1 %collective-permute-start = (bf16[64,3584]{1,0:T(8,128)(2,1)S(1)}, bf16[64,3584]{1,0:T(8,128)(2,1)S(1)}, u32[]{:S(2)}, u32[]{:S(2)}) collective-permute-start(bf16[64,3584]{1,0:T(8,128)(2,1)S(1)} %fusion.9), channel_id=1, source_target_pairs={{0,32},{32,64},{64,96},{96,128},{128,160},{160,192},{192,224},{224... | collective-permute-start | bytes 1376264 | tf_op jit(solution)/shard_map/ppermute | solution.py:17
  304.7 0.8 copy-start.1
  436.4 5.6 copy-start.9
  442.1 3.4 copy-start.5
  459.1 131.8 %all-to-all-start.3 = ((bf16[32,17,3584]{2,1,0:T(8,128)(2,1)}), bf16[32,17,3584]{2,1,0:T(8,128)(2,1)}, u32[]{:S(2)}, u32[]{:S(2)}) async-start(bf16[32,17,3584]{2,1,0:T(8,128)(2,1)} %reshape.220), calls=%async_computation.3 | async-start | bytes 11010048 | tf_op jit(solution)/shard_map/all_to_all | solution.py:56
  594.7 1.0 copy-start.2
where the time goes:
time: 598 us; the launch traced here: 597 us
  blocking collectives  260 us (43%)
  waiting for transfers between devices  254 us (42%)
  local copies, waits for them, and re-layouts  27 us (5%)
  matrix products  24.8 us (4%)
  starting transfers between devices  19.4 us (3%)
  other arithmetic  11.7 us (2%)
    all_to_all x2, blocking collectives, routed_branch(): lax.all_to_all(outgoing, 'expert', split_axis=0, concat_axis=0, tiled=True)  260 us
    all_to_all x2, waiting for transfers between devices, routed_branch(): lax.all_to_all(slice_part, 'expert', split_axis=0, concat_axis=0, tiled=T...  249 us
    dot_general x2, matrix products, expert_slice(): jnp.dot(hidden, w_down, preferred_element_type=jnp.float32)  16.4 us
    all_to_all x2, starting transfers between devices, routed_branch(): lax.all_to_all(slice_part, 'expert', split_axis=0, concat_axis=0, tiled=T...  15.8 us
  transfers between devices with their start and end apart: 3, of which 3 were waited for; matrix products, arithmetic and copies ran while one was open for 0% of the time, Pallas kernels for 0%

commit v1 on v0

v1 whole, which is shorter than its diff:
```python
import jax
import jax.numpy as jnp
from jax import lax
from jax.sharding import Mesh
from jax.sharding import PartitionSpec as P

EXPERTS = 4
MOST = 17


NORM_EPS = 1e-06
FIXED_UNIT = 1.0 / 4096.0


def shifted(value, axis, steps):
    count = lax.axis_size(axis)
    pairs = [(source, (source + steps) % count) for source in range(count)]
    return lax.ppermute(value, axis, pairs)


def slot_index(expert_ids, capacity, experts):
    flat_ids = expert_ids.reshape(-1)
    onehot = (flat_ids[:, None] == jnp.arange(experts, dtype=jnp.int32)[None, :]).astype(jnp.int32)
    before = jnp.cumsum(onehot, axis=0) - onehot
    slot_rank = jnp.sum(before * onehot, axis=1)
    return (flat_ids * capacity + slot_rank).reshape(expert_ids.shape)


def place_rows(normed, slot_ids, slot_total):
    slot_marks = slot_ids[:, :, None] == jnp.arange(slot_total, dtype=jnp.int32)[None, None, :]
    placing = jnp.sum(slot_marks.astype(jnp.float32), axis=1).T.astype(jnp.bfloat16)
    return jnp.dot(placing, normed, preferred_element_type=jnp.float32).astype(jnp.bfloat16)


def routed_branch(normed, expert_ids, route_weight, w_gate, w_up, down_all):
    n_x = lax.axis_size("ex")
    model_width = normed.shape[1]
    slot_ids = slot_index(expert_ids, MOST, EXPERTS)
    per_expert = place_rows(normed, slot_ids, EXPERTS * MOST).reshape(EXPERTS, MOST, model_width)
    from_x = lax.all_to_all(per_expert, "ex", split_axis=0, concat_axis=0, tiled=True)
    slot_rows = lax.all_gather(from_x, "ey", axis=0, tiled=False)
    n_y = slot_rows.shape[0]
    flat_rows = slot_rows.reshape(-1, model_width)
    gate_act = jnp.dot(flat_rows, w_gate, preferred_element_type=jnp.float32)
    up_act = jnp.dot(flat_rows, w_up, preferred_element_type=jnp.float32)
    hidden = (jax.nn.silu(gate_act) * up_act).astype(jnp.bfloat16)
    hidden = hidden.reshape(n_y, n_x * MOST, hidden.shape[-1])
    hidden_here = lax.all_to_all(hidden, "ey", split_axis=0, concat_axis=0, tiled=True)
    parts = jnp.einsum("jrh,jhd->jrd", hidden_here, down_all, preferred_element_type=jnp.float32)
    expert_out = jnp.sum(parts.astype(jnp.bfloat16).astype(jnp.float32), axis=0)
    expert_out = expert_out.reshape(n_x, MOST, model_width)
    returned = lax.all_to_all(expert_out, "ex", split_axis=0, concat_axis=0, tiled=True)
    picked = returned.reshape(EXPERTS * MOST, model_width)[slot_ids]
    weights = route_weight.astype(jnp.float32) * FIXED_UNIT
    return jnp.sum(weights[:, :, None] * picked, axis=1)


def layer_terms(rows_in, gain_row, w_gate, w_up, down_all, expert_ids, route_weight):
    values = rows_in.astype(jnp.float32)
    inv_rms = lax.rsqrt(jnp.mean(values * values, axis=1, keepdims=True) + NORM_EPS)
    normed = (values * inv_rms * gain_row.astype(jnp.float32)).astype(jnp.bfloat16)
    branch = routed_branch(normed, expert_ids, route_weight, w_gate, w_up, down_all)
    return (values, branch)


def shards(acts, norm_gain, gate_w, up_w, down_w, route_ids, route_wts):
    section_index = lax.axis_index("pipe")
    rows_in = acts[0]
    gain_row = norm_gain[0]
    w_gate = gate_w[0, 0]
    w_up = up_w[0, 0]
    down_all = lax.all_gather(down_w[0, 0], "ey", axis=0, tiled=False)
    values, branch = layer_terms(
        rows_in, gain_row, w_gate, w_up, down_all, route_ids[0, 0], route_wts[0, 0]
    )
    first_out = (values + branch).astype(jnp.bfloat16)
    arrived = shifted(first_out, "pipe", 1)
    values, branch = layer_terms(
        arrived, gain_row, w_gate, w_up, down_all, route_ids[0, 1], route_wts[0, 1]
    )
    second = (values + branch).astype(jnp.bfloat16)
    result_rows = jnp.where(section_index == 0, arrived, second)
    return result_rows[None]


def solution(mesh):
    n_x = EXPERTS
    n_pipe, n_expert = mesh.devices.shape
    split_mesh = Mesh(
        mesh.devices.reshape(n_pipe, n_x, n_expert // n_x), ("pipe", "ex", "ey")
    )
    rows = ("ex", "ey")
    return jax.shard_map(
        shards,
        mesh=split_mesh,
        in_specs=(
            P("pipe", rows, None),
            P("pipe", None),
            P("pipe", rows, None, None),
            P("pipe", rows, None, None),
            P("pipe", rows, None, None),
            P("pipe", None, rows, None),
            P("pipe", None, rows, None),
        ),
        out_specs=P("pipe", rows, None),
        check_vma=False,
    )
```

time: 598 us -> 370 us (0.62)
  the two profiles are of different devices: /device:TPU:253 before, /device:TPU:1 now
where the time goes in v1:
time: 370 us; the launch traced here: 367 us
  waiting for transfers between devices  250 us (68%)
  blocking collectives  50.9 us (14%)
  matrix products  19.6 us (5%)
  local copies, waits for them, and re-layouts  17.9 us (5%)
  between operations  13.3 us (4%)
  starting transfers between devices  10.9 us (3%)
  other arithmetic  4.58 us (1%)
    all_gather x2, waiting for transfers between devices, routed_branch(): slot_rows = lax.all_gather(from_x, 'ey', axis=0, tiled=False)  144 us
    all_gather x1, waiting for transfers between devices, shards(): down_all = lax.all_gather(down_w[0, 0], 'ey', axis=0, tiled=False)  66.1 us
    all_to_all x2, waiting for transfers between devices, routed_branch(): lax.all_to_all(expert_out, 'ex', split_axis=0, concat_axis=0, tiled=True)  33.8 us
    all_to_all x2, blocking collectives, routed_branch(): lax.all_to_all(hidden, 'ey', split_axis=0, concat_axis=0, tiled=True)  26.4 us
    all_to_all x2, blocking collectives, routed_branch(): lax.all_to_all(per_expert, 'ex', split_axis=0, concat_axis=0, tiled=True)  24.5 us
    reshape x2, local copies, waits for them, and re-layouts, routed_branch(): flat_rows = slot_rows.reshape(-1, model_width)  11.1 us
    dot_general x2, matrix products, routed_branch(): jnp.einsum('jrh,jhd->jrd', hidden_here, down_all, preferred_element_type=...  8.74 us
    all_to_all x2, starting transfers between devices, routed_branch(): lax.all_to_all(expert_out, 'ex', split_axis=0, concat_axis=0, tiled=True)  7.94 us
  transfers between devices with their start and end apart: 6, of which 6 were waited for; matrix products, arithmetic and copies ran while one was open for 3% of the time, Pallas kernels for 0%

profile of v1, /device:TPU:1, one launch (start us, length us, event | category | flops | bytes accessed | tf_op | source)
XLA Modules:
  0.0 367.4 jit_solution(11265322246094201349)
XLA Ops:
  8.4 1.2 fusion.20
  10.5 1.4 convolution_convert_fusion.1
  12.0 12.6 %all_to_all.30 = bf16[4,17,3584]{2,1,0:T(8,128)(2,1)} all-to-all(bf16[4,17,3584]{2,1,0:T(8,128)(2,1)S(1)} %reshape.210), channel_id=1, replica_groups=mesh['pipe'=16,'ex'=4,'ey'=8] {'ex'}, dimensions={0} | all-to-all | bytes 974848 | tf_op jit(solution)/shard_map/all_to_all | solution.py:40
  25.4 75.3 %all-gather.7.cloned.1.call-done = bf16[32,17,3584]{2,1,0:T(8,128)(2,1)} async-done(((bf16[4,17,3584]{2,1,0:T(8,128)(2,1)}), bf16[32,17,3584]{2,1,0:T(8,128)(2,1)}) %all-gather.7.cloned.1.call-update) | async-done | bytes 3899408 | tf_op jit(solution)/shard_map/all_gather | solution.py:41
  100.7 5.6 %reshape.211 = bf16[544,3584]{1,0:T(8,128)(2,1)} reshape(bf16[32,17,3584]{2,1,0:T(8,128)(2,1)} %all-gather.7.cloned.1.call-done) | data formatting | bytes 7798784 | tf_op jit(solution)/shard_map/reshape | solution.py:43
  106.3 3.4 fusion.28
  111.0 14.5 %all_to_all.31 = bf16[8,68,128]{2,1,0:T(8,128)(2,1)S(1)} all-to-all(bf16[8,68,128]{2,1,0:T(8,128)(2,1)S(1)} %reshape.212), channel_id=1, replica_groups=mesh['pipe'=16,'ex'=4,'ey'=8] {'ey'}, dimensions={0} | all-to-all | bytes 278528 | tf_op jit(solution)/shard_map/all_to_all | solution.py:48
  125.5 66.1 %all-gather.9.cloned.1.call-done = bf16[8,1,128,3584]{3,2,1,0:T(8,128)(2,1)} async-done(((bf16[1,1,128,3584]{3,2,1,0:T(8,128)(2,1)}), bf16[8,1,128,3584]{3,2,1,0:T(8,128)(2,1)}) %all-gather.9.cloned.1.call-update) | async-done | bytes 7340048 | tf_op jit(solution)/shard_map/all_gather | solution.py:72
  191.7 4.4 %convert_reduce_fusion.1 = f32[68,3584]{1,0:T(8,128)S(1)} fusion(bf16[8,68,128]{2,1,0:T(8,128)(2,1)S(1)} %all_to_all.31, bf16[8,1,128,3584]{3,2,1,0:T(8,128)(2,1)} %all-gather.9.cloned.1.call-done), kind=kOutput, calls=%fused_computation.3 | convolution fusion | flops 504727552 | bytes 8454144 | tf_op jit(solution)/shard_map/jrh,jhd->jrd/dot_general | solution.py:49
  196.1 1.3 reshape.213
  197.3 4.0 %all-to-all-start.2 = ((f32[4,17,3584]{2,1,0:T(8,128)}), f32[4,17,3584]{2,1,0:T(8,128)S(1)}, u32[]{:S(2)}, u32[]{:S(2)}) async-start(f32[4,17,3584]{2,1,0:T(8,128)} %reshape.213), calls=%async_computation.2 | async-start | bytes 2752512 | tf_op jit(solution)/shard_map/all_to_all | solution.py:52
  201.4 17.9 %all-to-all-done.2 = f32[4,17,3584]{2,1,0:T(8,128)S(1)} async-done(((f32[4,17,3584]{2,1,0:T(8,128)}), f32[4,17,3584]{2,1,0:T(8,128)S(1)}, u32[]{:S(2)}, u32[]{:S(2)}) %all-to-all-start.2) | async-done | bytes 974880 | tf_op jit(solution)/shard_map/all_to_all | solution.py:52
  220.6 2.9 collective-permute-start
  223.5 5.4 %collective-permute-done = bf16[64,3584]{1,0:T(8,128)(2,1)S(1)} collective-permute-done((bf16[64,3584]{1,0:T(8,128)(2,1)S(1)}, bf16[64,3584]{1,0:T(8,128)(2,1)S(1)}, u32[]{:S(2)}, u32[]{:S(2)}) %collective-permute-start) | collective-permute-done | bytes 458784 | tf_op jit(solution)/shard_map/ppermute | solution.py:18
  230.2 11.9 %all_to_all.32 = bf16[4,17,3584]{2,1,0:T(8,128)(2,1)} all-to-all(bf16[4,17,3584]{2,1,0:T(8,128)(2,1)S(1)} %reshape.215), channel_id=1, replica_groups=mesh['pipe'=16,'ex'=4,'ey'=8] {'ex'}, dimensions={0} | all-to-all | bytes 974848 | tf_op jit(solution)/shard_map/all_to_all | solution.py:40
  242.1 68.8 %all-gather.11.cloned.1.call-done = bf16[32,17,3584]{2,1,0:T(8,128)(2,1)} async-done(((bf16[4,17,3584]{2,1,0:T(8,128)(2,1)}), bf16[32,17,3584]{2,1,0:T(8,128)(2,1)}) %all-gather.11.cloned.1.call-update) | async-done | bytes 3899408 | tf_op jit(solution)/shard_map/all_gather | solution.py:41
  311.0 5.6 %reshape.216 = bf16[544,3584]{1,0:T(8,128)(2,1)} reshape(bf16[32,17,3584]{2,1,0:T(8,128)(2,1)} %all-gather.11.cloned.1.call-done) | data formatting | bytes 7798784 | tf_op jit(solution)/shard_map/reshape | solution.py:43
  316.5 3.4 fusion.26
  320.1 1.2 fusion.15
  321.3 11.9 %all_to_all.33 = bf16[8,68,128]{2,1,0:T(8,128)(2,1)S(1)} all-to-all(bf16[8,68,128]{2,1,0:T(8,128)(2,1)S(1)} %reshape.217), channel_id=1, replica_groups=mesh['pipe'=16,'ex'=4,'ey'=8] {'ey'}, dimensions={0} | all-to-all | bytes 278528 | tf_op jit(solution)/shard_map/all_to_all | solution.py:48
  333.2 4.4 %convert_reduce_fusion = f32[68,3584]{1,0:T(8,128)S(1)} fusion(bf16[8,68,128]{2,1,0:T(8,128)(2,1)S(1)} %all_to_all.33, bf16[8,1,128,3584]{3,2,1,0:T(8,128)(2,1)} %all-gather.9.cloned.1.call-done), kind=kOutput, calls=%fused_computation.2 | convolution fusion | flops 504727552 | bytes 8454144 | tf_op jit(solution)/shard_map/jrh,jhd->jrd/dot_general | solution.py:49
  337.6 1.2 reshape.218
  338.8 4.0 %all-to-all-start.5 = ((f32[4,17,3584]{2,1,0:T(8,128)}), f32[4,17,3584]{2,1,0:T(8,128)S(1)}, u32[]{:S(2)}, u32[]{:S(2)}) async-start(f32[4,17,3584]{2,1,0:T(8,128)} %reshape.218), calls=%async_computation.5 | async-start | bytes 2752512 | tf_op jit(solution)/shard_map/all_to_all | solution.py:52
  342.8 15.9 %all-to-all-done.5 = f32[4,17,3584]{2,1,0:T(8,128)S(1)} async-done(((f32[4,17,3584]{2,1,0:T(8,128)}), f32[4,17,3584]{2,1,0:T(8,128)S(1)}, u32[]{:S(2)}, u32[]{:S(2)}) %all-to-all-start.5) | async-done | bytes 974880 | tf_op jit(solution)/shard_map/all_to_all | solution.py:52
  (53 shorter events, 9.9 us)
Async XLA Ops:
  6.5 99.8 %copy-start = (bf16[1,1,3584,128]{3,2,1,0:T(8,128)(2,1)S(1)}, bf16[1,1,3584,128]{3,2,1,0:T(8,128)(2,1)}, u32[]{:S(2)}) copy-start(bf16[1,1,3584,128]{3,2,1,0:T(8,128)(2,1)} %param.9) | copy-start | bytes 2752516
  6.5 94.2 %all-gather.7.cloned.1.call-start = ((), (), s32[]{:S(2)}) async-start(), calls=%async_computation.6 | async-start | bytes 6193152 | tf_op jit(solution)/shard_map/all_gather | solution.py:41
  24.6 167.0 %all-gather.9.cloned.1.call-start = ((), (), s32[]{:S(2)}) async-start(), calls=%async_computation.7 | async-start | bytes 8257536 | tf_op jit(solution)/shard_map/all_gather | solution.py:72
  106.3 3.4 copy-start.4
  106.3 3.5 copy-start.8
  196.0 5.3 %copy-start.6 = (s32[1,2,64,1]{2,3,1,0:T(1,128)S(1)}, s32[1,2,64,1]{2,3,1,0:T(1,128)}, u32[]{:S(2)}) copy-start(s32[1,2,64,1]{2,3,1,0:T(1,128)} %param.12) | copy-start | bytes 1540
  196.0 5.3 %copy-start.7 = (s32[1,2,64,1]{2,3,1,0:T(1,128)S(1)}, s32[1,2,64,1]{2,3,1,0:T(1,128)}, u32[]{:S(2)}) copy-start(s32[1,2,64,1]{2,3,1,0:T(1,128)} %param.13) | copy-start | bytes 1540
  197.3 21.9 %all-to-all-start.2 = ((f32[4,17,3584]{2,1,0:T(8,128)}), f32[4,17,3584]{2,1,0:T(8,128)S(1)}, u32[]{:S(2)}, u32[]{:S(2)}) async-start(f32[4,17,3584]{2,1,0:T(8,128)} %reshape.213), calls=%async_computation.2 | async-start | bytes 2752512 | tf_op jit(solution)/shard_map/all_to_all | solution.py:52
  201.3 109.7 %all-gather.11.cloned.1.call-start = ((), (), s32[]{:S(2)}) async-start(), calls=%async_computation.8 | async-start | bytes 6193152 | tf_op jit(solution)/shard_map/all_gather | solution.py:41
  219.4 1.0 copy-start.3
  220.6 8.3 %collective-permute-start = (bf16[64,3584]{1,0:T(8,128)(2,1)S(1)}, bf16[64,3584]{1,0:T(8,128)(2,1)S(1)}, u32[]{:S(2)}, u32[]{:S(2)}) collective-permute-start(bf16[64,3584]{1,0:T(8,128)(2,1)S(1)} %fusion.23), channel_id=1, source_target_pairs={{0,32},{32,64},{64,96},{96,128},{128,160},{160,192},{192,224},{224... | collective-permute-start | bytes 1376264 | tf_op jit(solution)/shard_map/ppermute | solution.py:18
  228.9 0.8 copy-start.1
  316.5 3.4 copy-start.5
  316.5 3.5 copy-start.9
  338.8 19.9 %all-to-all-start.5 = ((f32[4,17,3584]{2,1,0:T(8,128)}), f32[4,17,3584]{2,1,0:T(8,128)S(1)}, u32[]{:S(2)}, u32[]{:S(2)}) async-start(f32[4,17,3584]{2,1,0:T(8,128)} %reshape.218), calls=%async_computation.5 | async-start | bytes 2752512 | tf_op jit(solution)/shard_map/all_to_all | solution.py:52
  358.8 1.0 copy-start.2
Sparse Core Ops, SparseCore 0:
  24.7 75.9 all-gather.6
  102.8 88.8 all-gather.8
  242.3 68.6 all-gather.10

commit v2 on v1

--- a/solution.py
+++ b/solution.py
@@ -6,6 +6,7 @@
 
 EXPERTS = 4
 MOST = 17
+LANE = 128
 
 
 NORM_EPS = 1e-06
@@ -36,7 +37,8 @@
     n_x = lax.axis_size("ex")
     model_width = normed.shape[1]
     slot_ids = slot_index(expert_ids, MOST, EXPERTS)
-    per_expert = place_rows(normed, slot_ids, EXPERTS * MOST).reshape(EXPERTS, MOST, model_width)
+    block_rows = MOST * model_width // LANE
+    per_expert = place_rows(normed, slot_ids, EXPERTS * MOST).reshape(EXPERTS, block_rows, LANE)
     from_x = lax.all_to_all(per_expert, "ex", split_axis=0, concat_axis=0, tiled=True)
     slot_rows = lax.all_gather(from_x, "ey", axis=0, tiled=False)
     n_y = slot_rows.shape[0]
@@ -48,7 +50,7 @@
     hidden_here = lax.all_to_all(hidden, "ey", split_axis=0, concat_axis=0, tiled=True)
     parts = jnp.einsum("jrh,jhd->jrd", hidden_here, down_all, preferred_element_type=jnp.float32)
     expert_out = jnp.sum(parts.astype(jnp.bfloat16).astype(jnp.float32), axis=0)
-    expert_out = expert_out.reshape(n_x, MOST, model_width)
+    expert_out = expert_out.reshape(n_x, block_rows, LANE)
     returned = lax.all_to_all(expert_out, "ex", split_axis=0, concat_axis=0, tiled=True)
     picked = returned.reshape(EXPERTS * MOST, model_width)[slot_ids]
     weights = route_weight.astype(jnp.float32) * FIXED_UNIT

time: 370 us -> 332 us (0.90)
  waiting for transfers between devices: 250 us -> 210 us
    all_gather x2, waiting for transfers between devices: 144 us -> 115 us  [routed_branch(): slot_rows = lax.all_gather(from_x, 'ey', axis=0, tiled=False)]
    all_to_all x2, waiting for transfers between devices: 33.8 us -> 24.8 us  [routed_branch(): lax.all_to_all(expert_out, 'ex', split_axis=0, concat_axis=0, tiled=True)]
  transfers between devices with their start and end apart: 6 -> 6, of which waited for: 6 -> 6; matrix products, arithmetic and copies ran while one was open for 3% -> 4% of each run, Pallas kernels for 0% -> 0%
where the time goes in v2:
time: 332 us; the launch traced here: 329 us
  waiting for transfers between devices  210 us (63%)
  blocking collectives  47.7 us (14%)
  local copies, waits for them, and re-layouts  21.4 us (6%)
  matrix products  19.7 us (6%)
  between operations  13.3 us (4%)
  starting transfers between devices  11.1 us (3%)
  other arithmetic  5.76 us (2%)
    all_gather x2, waiting for transfers between devices, routed_branch(): slot_rows = lax.all_gather(from_x, 'ey', axis=0, tiled=False)  115 us
    all_gather x1, waiting for transfers between devices, shards(): down_all = lax.all_gather(down_w[0, 0], 'ey', axis=0, tiled=False)  64.8 us
    all_to_all x2, blocking collectives, routed_branch(): lax.all_to_all(hidden, 'ey', split_axis=0, concat_axis=0, tiled=True)  26.3 us
    all_to_all x2, waiting for transfers between devices, routed_branch(): lax.all_to_all(expert_out, 'ex', split_axis=0, concat_axis=0, tiled=True)  24.8 us
    all_to_all x2, blocking collectives, routed_branch(): lax.all_to_all(per_expert, 'ex', split_axis=0, concat_axis=0, tiled=True)  21.3 us
    reshape x2, local copies, waits for them, and re-layouts, routed_branch(): flat_rows = slot_rows.reshape(-1, model_width)  14 us
    dot_general x2, matrix products, routed_branch(): jnp.einsum('jrh,jhd->jrd', hidden_here, down_all, preferred_element_type=...  8.74 us
    all_to_all x2, starting transfers between devices, routed_branch(): lax.all_to_all(expert_out, 'ex', split_axis=0, concat_axis=0, tiled=True)  7.93 us
  transfers between devices with their start and end apart: 6, of which 6 were waited for; matrix products, arithmetic and copies ran while one was open for 4% of the time, Pallas kernels for 0%

profile of v2, /device:TPU:1, one launch (start us, length us, event | category | flops | bytes accessed | tf_op | source)
XLA Modules:
  0.0 329.1 jit_solution(13385658414739562058)
XLA Ops:
  8.4 1.2 fusion.20
  10.5 1.4 convolution_convert_fusion.1
  12.5 11.5 %all_to_all.30 = bf16[4,476,128]{2,1,0:T(8,128)(2,1)} all-to-all(bf16[4,476,128]{2,1,0:T(8,128)(2,1)S(1)} %reshape.210), channel_id=1, replica_groups=mesh['pipe'=16,'ex'=4,'ey'=8] {'ex'}, dimensions={0} | all-to-all | bytes 974848 | tf_op jit(solution)/shard_map/all_to_all | solution.py:42
  24.8 59.5 %all-gather.7.cloned.1.call-done = bf16[32,476,128]{2,1,0:T(8,128)(2,1)} async-done(((bf16[4,476,128]{2,1,0:T(8,128)(2,1)}), bf16[32,476,128]{2,1,0:T(8,128)(2,1)}) %all-gather.7.cloned.1.call-update) | async-done | bytes 3899408 | tf_op jit(solution)/shard_map/all_gather | solution.py:43
  84.3 7.0 %reshape.211 = bf16[544,3584]{1,0:T(8,128)(2,1)} reshape(bf16[32,476,128]{2,1,0:T(8,128)(2,1)} %all-gather.7.cloned.1.call-done) | data formatting | bytes 7798784 | tf_op jit(solution)/shard_map/reshape | solution.py:45
  91.3 3.4 %fusion.28 = f32[544,128]{1,0:T(8,128)S(1)} fusion(bf16[544,3584]{1,0:T(8,128)(2,1)} %reshape.211, bf16[1,1,3584,128]{3,2,1,0:T(8,128)(2,1)S(1)} %copy-done), kind=kOutput, calls=%fused_computation.34 | convolution fusion | flops 499122176 | bytes 5095424 | tf_op jit(solution)/shard_map/dot_general | solution.py:46
  96.1 14.4 %all_to_all.31 = bf16[8,68,128]{2,1,0:T(8,128)(2,1)S(1)} all-to-all(bf16[8,68,128]{2,1,0:T(8,128)(2,1)S(1)} %reshape.212), channel_id=1, replica_groups=mesh['pipe'=16,'ex'=4,'ey'=8] {'ey'}, dimensions={0} | all-to-all | bytes 278528 | tf_op jit(solution)/shard_map/all_to_all | solution.py:50
  110.5 64.8 %all-gather.9.cloned.1.call-done = bf16[8,1,128,3584]{3,2,1,0:T(8,128)(2,1)} async-done(((bf16[1,1,128,3584]{3,2,1,0:T(8,128)(2,1)}), bf16[8,1,128,3584]{3,2,1,0:T(8,128)(2,1)}) %all-gather.9.cloned.1.call-update) | async-done | bytes 7340048 | tf_op jit(solution)/shard_map/all_gather | solution.py:74
  175.3 4.4 %convert_reduce_fusion.1 = f32[68,3584]{1,0:T(8,128)S(1)} fusion(bf16[8,68,128]{2,1,0:T(8,128)(2,1)S(1)} %all_to_all.31, bf16[8,1,128,3584]{3,2,1,0:T(8,128)(2,1)} %all-gather.9.cloned.1.call-done), kind=kOutput, calls=%fused_computation.3 | convolution fusion | flops 504727552 | bytes 8454144 | tf_op jit(solution)/shard_map/jrh,jhd->jrd/dot_general | solution.py:51
  180.7 4.0 %all-to-all-start.2 = ((f32[4,476,128]{2,1,0:T(8,128)}), f32[4,476,128]{2,1,0:T(8,128)S(1)}, u32[]{:S(2)}, u32[]{:S(2)}) async-start(f32[4,476,128]{2,1,0:T(8,128)} %reshape.213), calls=%async_computation.2 | async-start | bytes 1966080 | tf_op jit(solution)/shard_map/all_to_all | solution.py:54
  184.7 13.4 %all-to-all-done.2 = f32[4,476,128]{2,1,0:T(8,128)S(1)} async-done(((f32[4,476,128]{2,1,0:T(8,128)}), f32[4,476,128]{2,1,0:T(8,128)S(1)}, u32[]{:S(2)}, u32[]{:S(2)}) %all-to-all-start.2) | async-done | bytes 974880 | tf_op jit(solution)/shard_map/all_to_all | solution.py:54
  198.3 1.8 gather_fusion
  200.1 1.4 fusion.23
  201.5 3.1 collective-permute-start
  204.6 5.4 %collective-permute-done = bf16[64,3584]{1,0:T(8,128)(2,1)S(1)} collective-permute-done((bf16[64,3584]{1,0:T(8,128)(2,1)S(1)}, bf16[64,3584]{1,0:T(8,128)(2,1)S(1)}, u32[]{:S(2)}, u32[]{:S(2)}) %collective-permute-start) | collective-permute-done | bytes 458784 | tf_op jit(solution)/shard_map/ppermute | solution.py:19
  211.3 9.8 %all_to_all.32 = bf16[4,476,128]{2,1,0:T(8,128)(2,1)} all-to-all(bf16[4,476,128]{2,1,0:T(8,128)(2,1)S(1)} %reshape.215), channel_id=1, replica_groups=mesh['pipe'=16,'ex'=4,'ey'=8] {'ex'}, dimensions={0} | all-to-all | bytes 974848 | tf_op jit(solution)/shard_map/all_to_all | solution.py:42
  221.1 55.0 %all-gather.11.cloned.1.call-done = bf16[32,476,128]{2,1,0:T(8,128)(2,1)} async-done(((bf16[4,476,128]{2,1,0:T(8,128)(2,1)}), bf16[32,476,128]{2,1,0:T(8,128)(2,1)}) %all-gather.11.cloned.1.call-update) | async-done | bytes 3899408 | tf_op jit(solution)/shard_map/all_gather | solution.py:43
  276.1 7.0 %reshape.216 = bf16[544,3584]{1,0:T(8,128)(2,1)} reshape(bf16[32,476,128]{2,1,0:T(8,128)(2,1)} %all-gather.11.cloned.1.call-done) | data formatting | bytes 7798784 | tf_op jit(solution)/shard_map/reshape | solution.py:45
  283.1 3.4 %fusion.26 = f32[544,128]{1,0:T(8,128)S(1)} fusion(bf16[544,3584]{1,0:T(8,128)(2,1)} %reshape.216, bf16[1,1,3584,128]{3,2,1,0:T(8,128)(2,1)S(1)} %copy-done), kind=kOutput, calls=%fused_computation.32 | convolution fusion | flops 499122176 | bytes 5095424 | tf_op jit(solution)/shard_map/dot_general | solution.py:46
  286.6 1.2 fusion.15
  287.8 11.9 %all_to_all.33 = bf16[8,68,128]{2,1,0:T(8,128)(2,1)S(1)} all-to-all(bf16[8,68,128]{2,1,0:T(8,128)(2,1)S(1)} %reshape.217), channel_id=1, replica_groups=mesh['pipe'=16,'ex'=4,'ey'=8] {'ey'}, dimensions={0} | all-to-all | bytes 278528 | tf_op jit(solution)/shard_map/all_to_all | solution.py:50
  299.8 4.4 %convert_reduce_fusion = f32[68,3584]{1,0:T(8,128)S(1)} fusion(bf16[8,68,128]{2,1,0:T(8,128)(2,1)S(1)} %all_to_all.33, bf16[8,1,128,3584]{3,2,1,0:T(8,128)(2,1)} %all-gather.9.cloned.1.call-done), kind=kOutput, calls=%fused_computation.2 | convolution fusion | flops 504727552 | bytes 8454144 | tf_op jit(solution)/shard_map/jrh,jhd->jrd/dot_general | solution.py:51
  305.2 4.0 %all-to-all-start.5 = ((f32[4,476,128]{2,1,0:T(8,128)}), f32[4,476,128]{2,1,0:T(8,128)S(1)}, u32[]{:S(2)}, u32[]{:S(2)}) async-start(f32[4,476,128]{2,1,0:T(8,128)} %reshape.218), calls=%async_computation.5 | async-start | bytes 1966080 | tf_op jit(solution)/shard_map/all_to_all | solution.py:54
  309.2 11.4 %all-to-all-done.5 = f32[4,476,128]{2,1,0:T(8,128)S(1)} async-done(((f32[4,476,128]{2,1,0:T(8,128)}), f32[4,476,128]{2,1,0:T(8,128)S(1)}, u32[]{:S(2)}, u32[]{:S(2)}) %all-to-all-start.5) | async-done | bytes 974880 | tf_op jit(solution)/shard_map/all_to_all | solution.py:54
  (49 shorter events, 11.1 us)
Async XLA Ops:
  6.5 84.8 %copy-start = (bf16[1,1,3584,128]{3,2,1,0:T(8,128)(2,1)S(1)}, bf16[1,1,3584,128]{3,2,1,0:T(8,128)(2,1)}, u32[]{:S(2)}) copy-start(bf16[1,1,3584,128]{3,2,1,0:T(8,128)(2,1)} %param.9) | copy-start | bytes 2752516
  6.5 77.8 %all-gather.7.cloned.1.call-start = ((), (), s32[]{:S(2)}) async-start(), calls=%async_computation.6 | async-start | bytes 4423680 | tf_op jit(solution)/shard_map/all_gather | solution.py:43
  24.0 151.2 %all-gather.9.cloned.1.call-start = ((), (), s32[]{:S(2)}) async-start(), calls=%async_computation.7 | async-start | bytes 8257536 | tf_op jit(solution)/shard_map/all_gather | solution.py:74
  91.3 3.4 %copy-start.2 = (bf16[544,3584]{1,0:T(8,128)(2,1)S(1)}, bf16[544,3584]{1,0:T(8,128)(2,1)}, u32[]{:S(2)}) copy-start(bf16[544,3584]{1,0:T(8,128)(2,1)} %reshape.211) | copy-start | bytes 11698180
  91.3 3.5 %copy-start.6 = (bf16[1,1,3584,128]{3,2,1,0:T(8,128)(2,1)S(1)}, bf16[1,1,3584,128]{3,2,1,0:T(8,128)(2,1)}, u32[]{:S(2)}) copy-start(bf16[1,1,3584,128]{3,2,1,0:T(8,128)(2,1)} %param.10) | copy-start | bytes 2752516
  179.6 5.1 %copy-start.4 = (s32[1,2,64,1]{2,3,1,0:T(1,128)S(1)}, s32[1,2,64,1]{2,3,1,0:T(1,128)}, u32[]{:S(2)}) copy-start(s32[1,2,64,1]{2,3,1,0:T(1,128)} %param.12) | copy-start | bytes 1540
  179.7 5.1 %copy-start.5 = (s32[1,2,64,1]{2,3,1,0:T(1,128)S(1)}, s32[1,2,64,1]{2,3,1,0:T(1,128)}, u32[]{:S(2)}) copy-start(s32[1,2,64,1]{2,3,1,0:T(1,128)} %param.13) | copy-start | bytes 1540
  180.7 17.4 %all-to-all-start.2 = ((f32[4,476,128]{2,1,0:T(8,128)}), f32[4,476,128]{2,1,0:T(8,128)S(1)}, u32[]{:S(2)}, u32[]{:S(2)}) async-start(f32[4,476,128]{2,1,0:T(8,128)} %reshape.213), calls=%async_computation.2 | async-start | bytes 1966080 | tf_op jit(solution)/shard_map/all_to_all | solution.py:54
  184.7 91.4 %all-gather.11.cloned.1.call-start = ((), (), s32[]{:S(2)}) async-start(), calls=%async_computation.8 | async-start | bytes 4423680 | tf_op jit(solution)/shard_map/all_gather | solution.py:43
  198.3 1.8 copy-start.1
  201.5 8.6 %collective-permute-start = (bf16[64,3584]{1,0:T(8,128)(2,1)S(1)}, bf16[64,3584]{1,0:T(8,128)(2,1)S(1)}, u32[]{:S(2)}, u32[]{:S(2)}) collective-permute-start(bf16[64,3584]{1,0:T(8,128)(2,1)S(1)} %fusion.23), channel_id=1, source_target_pairs={{0,32},{32,64},{64,96},{96,128},{128,160},{160,192},{192,224},{224... | collective-permute-start | bytes 1376264 | tf_op jit(solution)/shard_map/ppermute | solution.py:19
  283.1 3.4 %copy-start.3 = (bf16[544,3584]{1,0:T(8,128)(2,1)S(1)}, bf16[544,3584]{1,0:T(8,128)(2,1)}, u32[]{:S(2)}) copy-start(bf16[544,3584]{1,0:T(8,128)(2,1)} %reshape.216) | copy-start | bytes 11698180
  283.1 3.5 %copy-start.7 = (bf16[1,1,3584,128]{3,2,1,0:T(8,128)(2,1)S(1)}, bf16[1,1,3584,128]{3,2,1,0:T(8,128)(2,1)}, u32[]{:S(2)}) copy-start(bf16[1,1,3584,128]{3,2,1,0:T(8,128)(2,1)} %param.10) | copy-start | bytes 2752516
  305.2 15.4 %all-to-all-start.5 = ((f32[4,476,128]{2,1,0:T(8,128)}), f32[4,476,128]{2,1,0:T(8,128)S(1)}, u32[]{:S(2)}, u32[]{:S(2)}) async-start(f32[4,476,128]{2,1,0:T(8,128)} %reshape.218), calls=%async_computation.5 | async-start | bytes 1966080 | tf_op jit(solution)/shard_map/all_to_all | solution.py:54
Sparse Core Ops, SparseCore 0:
  24.2 60.1 all-gather.6
  86.4 88.8 all-gather.8
  221.2 54.8 all-gather.10

commit v3 on v2

v3 whole, which is shorter than its diff:
```python
import jax
import jax.numpy as jnp
from jax import lax
from jax.sharding import Mesh
from jax.sharding import PartitionSpec as P

EXPERTS = 4
MOST = 17
LANE = 128


NORM_EPS = 1e-06
FIXED_UNIT = 1.0 / 4096.0


def shifted(value, axis, steps):
    count = lax.axis_size(axis)
    pairs = [(source, (source + steps) % count) for source in range(count)]
    return lax.ppermute(value, axis, pairs)


def next_section_shift(value, steps):
    n_pipe = lax.axis_size("pipe")
    n_x = lax.axis_size("ex")
    pairs = []
    for p in range(n_pipe):
        for x in range(n_x):
            pairs.append((p * n_x + x, ((p + 1) % n_pipe) * n_x + (x + steps) % n_x))
    return lax.ppermute(value, ("pipe", "ex"), pairs)


def slot_index(expert_ids, me_x):
    flat_ids = expert_ids.reshape(-1)
    relative = (flat_ids - me_x) % EXPERTS
    onehot = (relative[:, None] == jnp.arange(EXPERTS, dtype=jnp.int32)[None, :]).astype(jnp.int32)
    before = jnp.cumsum(onehot, axis=0) - onehot
    slot_rank = jnp.sum(before * onehot, axis=1)
    return (relative * MOST + slot_rank).reshape(expert_ids.shape)


def place_rows(normed, slot_ids, slot_total):
    slot_marks = slot_ids[:, :, None] == jnp.arange(slot_total, dtype=jnp.int32)[None, None, :]
    placing = jnp.sum(slot_marks.astype(jnp.float32), axis=1).T.astype(jnp.bfloat16)
    return jnp.dot(placing, normed, preferred_element_type=jnp.float32).astype(jnp.bfloat16)


def normalize(rows_in, gain_row):
    values = rows_in.astype(jnp.float32)
    inv_rms = lax.rsqrt(jnp.mean(values * values, axis=1, keepdims=True) + NORM_EPS)
    normed = (values * inv_rms * gain_row.astype(jnp.float32)).astype(jnp.bfloat16)
    return values, normed


def slot_blocks(normed, slot_ids):
    model_width = normed.shape[1]
    placed = place_rows(normed, slot_ids, EXPERTS * MOST)
    return placed.reshape(EXPERTS, MOST * model_width // LANE, LANE)


def serve(from_x, w_gate, w_up, down_all):
    n_x = from_x.shape[0]
    model_width = w_gate.shape[0]
    me_y = lax.axis_index("ey")
    slot_rows = lax.all_gather(from_x, "ey", axis=0, tiled=False)
    n_y = slot_rows.shape[0]
    flat_rows = slot_rows.reshape(-1, model_width)
    gate_act = jnp.dot(flat_rows, w_gate, preferred_element_type=jnp.float32)
    up_act = jnp.dot(flat_rows, w_up, preferred_element_type=jnp.float32)
    hidden = (jax.nn.silu(gate_act) * up_act).astype(jnp.bfloat16)
    hidden = hidden.reshape(n_y, n_x * MOST, hidden.shape[-1])
    received = [hidden[me_y][None]]
    for d in range(1, n_y):
        piece = lax.dynamic_index_in_dim(hidden, (me_y + d) % n_y, 0, keepdims=True)
        received.append(shifted(piece, "ey", d))
    received = jnp.concatenate(received, axis=0)
    hidden_here = jnp.take(received, (me_y - jnp.arange(n_y)) % n_y, axis=0)
    parts = jnp.einsum("jrh,jhd->jrd", hidden_here, down_all, preferred_element_type=jnp.float32)
    expert_out = jnp.sum(parts.astype(jnp.bfloat16).astype(jnp.float32), axis=0)
    expert_out = expert_out.reshape(n_x, MOST * model_width // LANE, LANE)
    back = [expert_out[0]]
    for d in range(1, n_x):
        back.append(shifted(expert_out[d], "ex", -d))
    return jnp.stack(back, axis=0)


def finish(values, returned, slot_ids, route_weight):
    model_width = values.shape[1]
    picked = returned.reshape(EXPERTS * MOST, model_width)[slot_ids]
    weights = route_weight.astype(jnp.float32) * FIXED_UNIT
    branch = jnp.sum(weights[:, :, None] * picked, axis=1)
    return (values + branch).astype(jnp.bfloat16)


def shards(acts, norm_gain, gate_w, up_w, down_w, route_ids, route_wts):
    section_index = lax.axis_index("pipe")
    me_x = lax.axis_index("ex")
    rows_in = acts[0]
    gain_row = norm_gain[0]
    w_gate = gate_w[0, 0]
    w_up = up_w[0, 0]
    down_all = lax.all_gather(down_w[0, 0], "ey", axis=0, tiled=False)
    gain_next = shifted(gain_row, "pipe", -1)
    ids_next = shifted(route_ids[0, 1], "pipe", -1)

    values, normed = normalize(rows_in, gain_row)
    slot_ids = slot_index(route_ids[0, 0], me_x)
    blocks = slot_blocks(normed, slot_ids)
    from_x = [blocks[0]]
    for d in range(1, EXPERTS):
        from_x.append(shifted(blocks[d], "ex", d))
    returned = serve(jnp.stack(from_x, axis=0), w_gate, w_up, down_all)
    first_out = finish(values, returned, slot_ids, route_wts[0, 0])

    arrived = shifted(first_out, "pipe", 1)
    _, normed_next = normalize(first_out, gain_next)
    blocks_next = slot_blocks(normed_next, slot_index(ids_next, me_x))
    from_x = [next_section_shift(blocks_next[d], d) for d in range(EXPERTS)]
    returned = serve(jnp.stack(from_x, axis=0), w_gate, w_up, down_all)
    slot_ids = slot_index(route_ids[0, 1], me_x)
    second = finish(arrived.astype(jnp.float32), returned, slot_ids, route_wts[0, 1])

    result_rows = jnp.where(section_index == 0, arrived, second)
    return result_rows[None]


def solution(mesh):
    n_x = EXPERTS
    n_pipe, n_expert = mesh.devices.shape
    split_mesh = Mesh(
        mesh.devices.reshape(n_pipe, n_x, n_expert // n_x), ("pipe", "ex", "ey")
    )
    rows = ("ex", "ey")
    return jax.shard_map(
        shards,
        mesh=split_mesh,
        in_specs=(
            P("pipe", rows, None),
            P("pipe", None),
            P("pipe", rows, None, None),
            P("pipe", rows, None, None),
            P("pipe", rows, None, None),
            P("pipe", None, rows, None),
            P("pipe", None, rows, None),
        ),
        out_specs=P("pipe", rows, None),
        check_vma=False,
    )
```

time: 332 us -> 358 us (1.078)
  starting transfers between devices: 11.1 us -> 105 us
  blocking collectives: 47.7 us -> 0 us
  waiting for transfers between devices: 210 us -> 187 us
  other arithmetic: 5.76 us -> 10 us
    ppermute x1 -> x26, starting transfers between devices: 3.13 us -> 92.7 us  [shifted(): return lax.ppermute(value, axis, pairs)]
    all_to_all x4 -> x0, blocking collectives: 47.7 us -> none  [the longest x2 26.3 us: routed_branch(): lax.all_to_all(hidden, 'ey', split_axis=0, concat_axis=0, tiled=True)]
    ppermute x1 -> x26, waiting for transfers between devices: 5.42 us -> 30.6 us  [shifted(): return lax.ppermute(value, axis, pairs)]
    all_to_all x2 -> x0, waiting for transfers between devices: 24.8 us -> none  [routed_branch(): lax.all_to_all(expert_out, 'ex', split_axis=0, concat_axis=0, tiled=True)]
    all_gather x1, waiting for transfers between devices: 64.8 us -> 49.4 us  [shards(): down_all = lax.all_gather(down_w[0, 0], 'ey', axis=0, tiled=False)]
    all_gather x2, waiting for transfers between devices: 115 us -> 102 us  [serve(): slot_rows = lax.all_gather(from_x, 'ey', axis=0, tiled=False)]
    ppermute x0 -> x4, starting transfers between devices: none -> 11.7 us  [next_section_shift(): return lax.ppermute(value, ('pipe', 'ex'), pairs)]
    all_to_all x2 -> x0, starting transfers between devices: 7.93 us -> none  [routed_branch(): lax.all_to_all(expert_out, 'ex', split_axis=0, concat_axis=0, tiled=True)]
  transfers between devices with their start and end apart: 6 -> 33, of which waited for: 6 -> 14; matrix products, arithmetic and copies ran while one was open for 4% -> 7% of each run, Pallas kernels for 0% -> 0%
where the time goes in v3:
time: 358 us; the launch traced here: 357 us
  waiting for transfers between devices  187 us (52%)
  starting transfers between devices  105 us (29%)
  matrix products  20.8 us (6%)
  local copies, waits for them, and re-layouts  20.5 us (6%)
  between operations  14 us (4%)
  other arithmetic  10 us (3%)
    all_gather x2, waiting for transfers between devices, serve(): slot_rows = lax.all_gather(from_x, 'ey', axis=0, tiled=False)  102 us
    ppermute x26, starting transfers between devices, shifted(): return lax.ppermute(value, axis, pairs)  92.7 us
    all_gather x1, waiting for transfers between devices, shards(): down_all = lax.all_gather(down_w[0, 0], 'ey', axis=0, tiled=False)  49.4 us
    ppermute x26, waiting for transfers between devices, shifted(): return lax.ppermute(value, axis, pairs)  30.6 us
    reshape x2, local copies, waits for them, and re-layouts, serve(): flat_rows = slot_rows.reshape(-1, model_width)  14 us
    ppermute x4, starting transfers between devices, next_section_shift(): return lax.ppermute(value, ('pipe', 'ex'), pairs)  11.7 us
    dot_general x2, matrix products, serve(): jnp.einsum('jrh,jhd->jrd', hidden_here, down_all, preferred_element_type=...  8.85 us
  transfers between devices with their start and end apart: 33, of which 14 were waited for; matrix products, arithmetic and copies ran while one was open for 7% of the time, Pallas kernels for 0%

profile of v3, /device:TPU:1, one launch (start us, length us, event | category | flops | bytes accessed | tf_op | source)
XLA Modules:
  0.0 356.9 jit_solution(17554786735243540540)
XLA Ops:
  11.6 3.9 %collective-permute-start = (bf16[476,128]{1,0:T(8,128)(2,1)S(1)}, bf16[476,128]{1,0:T(8,128)(2,1)S(1)}, u32[]{:S(2)}, u32[]{:S(2)}) collective-permute-start(bf16[476,128]{1,0:T(8,128)(2,1)S(1)} %squeeze.52), channel_id=1, source_target_pairs={{0,8},{8,16},{16,24},{24,0},{1,9},{9,17},{17,25},{25,1},{2,10},{10... | collective-permute-start | bytes 365576 | tf_op jit(solution)/shard_map/ppermute | solution.py:19
  15.7 4.4 %collective-permute-start.1 = (bf16[476,128]{1,0:T(8,128)(2,1)S(1)}, bf16[476,128]{1,0:T(8,128)(2,1)S(1)}, u32[]{:S(2)}, u32[]{:S(2)}) collective-permute-start(bf16[476,128]{1,0:T(8,128)(2,1)S(1)} %squeeze.53), channel_id=1, source_target_pairs={{0,16},{8,24},{16,0},{24,8},{1,17},{9,25},{17,1},{25,9},{2,18},{10... | collective-permute-start | bytes 365576 | tf_op jit(solution)/shard_map/ppermute | solution.py:19
  27.7 5.5 %collective-permute-start.15 = (bf16[3584]{0:T(1024)(128)(2,1)S(1)}, bf16[3584]{0:T(1024)(128)(2,1)S(1)}, u32[]{:S(2)}, u32[]{:S(2)}) collective-permute-start(bf16[3584]{0:T(1024)(128)(2,1)S(1)} %reduce), channel_id=1, source_target_pairs={{0,480},{32,0},{64,32},{96,64},{128,96},{160,128},{192,160},{224,1... | collective-permute-start | bytes 21512 | tf_op jit(solution)/shard_map/ppermute | solution.py:19
  37.5 50.0 %all-gather.7.cloned.1.call-done = bf16[32,476,128]{2,1,0:T(8,128)(2,1)} async-done(((bf16[4,476,128]{2,1,0:T(8,128)(2,1)}), bf16[32,476,128]{2,1,0:T(8,128)(2,1)}) %all-gather.7.cloned.1.call-update) | async-done | bytes 3899408 | tf_op jit(solution)/shard_map/all_gather | solution.py:64
  87.6 7.0 %reshape.361 = bf16[544,3584]{1,0:T(8,128)(2,1)} reshape(bf16[32,476,128]{2,1,0:T(8,128)(2,1)} %all-gather.7.cloned.1.call-done) | data formatting | bytes 7798784 | tf_op jit(solution)/shard_map/reshape | solution.py:66
  101.4 5.1 %collective-permute-start.4 = (bf16[1,68,128]{2,1,0:T(8,128)(2,1)S(1)}, bf16[1,68,128]{2,1,0:T(8,128)(2,1)S(1)}, u32[]{:S(2)}, u32[]{:S(2)}) collective-permute-start(bf16[1,68,128]{2,1,0:T(8,128)(2,1)S(1)} %get-tuple-element.37), channel_id=1, source_target_pairs={{0,2},{1,3},{2,4},{3,5},{4,6},{5,7},{6,0},{7,1},{8,10},{9,11},{10,... | collective-permute-start | bytes 52232 | tf_op jit(solution)/shard_map/ppermute | solution.py:19
  113.2 4.7 %collective-permute-start.7 = (bf16[1,68,128]{2,1,0:T(8,128)(2,1)S(1)}, bf16[1,68,128]{2,1,0:T(8,128)(2,1)S(1)}, u32[]{:S(2)}, u32[]{:S(2)}) collective-permute-start(bf16[1,68,128]{2,1,0:T(8,128)(2,1)S(1)} %get-tuple-element.34), channel_id=1, source_target_pairs={{0,5},{1,6},{2,7},{3,0},{4,1},{5,2},{6,3},{7,4},{8,13},{9,14},{10,... | collective-permute-start | bytes 52232 | tf_op jit(solution)/shard_map/ppermute | solution.py:19
  118.0 5.2 %collective-permute-start.8 = (bf16[1,68,128]{2,1,0:T(8,128)(2,1)S(1)}, bf16[1,68,128]{2,1,0:T(8,128)(2,1)S(1)}, u32[]{:S(2)}, u32[]{:S(2)}) collective-permute-start(bf16[1,68,128]{2,1,0:T(8,128)(2,1)S(1)} %get-tuple-element.33), channel_id=1, source_target_pairs={{0,6},{1,7},{2,0},{3,1},{4,2},{5,3},{6,4},{7,5},{8,14},{9,15},{10,... | collective-permute-start | bytes 52232 | tf_op jit(solution)/shard_map/ppermute | solution.py:19
  129.1 49.4 %all-gather.9.cloned.1.call-done = bf16[8,1,128,3584]{3,2,1,0:T(8,128)(2,1)} async-done(((bf16[1,1,128,3584]{3,2,1,0:T(8,128)(2,1)}), bf16[8,1,128,3584]{3,2,1,0:T(8,128)(2,1)}) %all-gather.9.cloned.1.call-update) | async-done | bytes 7340048 | tf_op jit(solution)/shard_map/all_gather | solution.py:101
  178.5 4.4 %convert_reduce_fusion.1 = f32[68,3584]{1,0:T(8,128)S(1)} fusion(bf16[8,1,128,3584]{3,2,1,0:T(8,128)(2,1)} %all-gather.9.cloned.1.call-done, bf16[8,68,128]{2,1,0:T(8,128)(2,1)S(1)} %gather_fusion.2, pred[8]{0:T(512)(128)(4,1)S(1)} %compare_and_fusion), kind=kOutput, calls=%fused_computation.5 | convolution fusion | flops 504797184 | bytes 8454152 | tf_op jit(solution)/shard_map/jrh,jhd->jrd/dot_general | solution.py:77
  183.1 4.3 %collective-permute-start.10 = (f32[476,128]{1,0:T(8,128)S(1)}, f32[476,128]{1,0:T(8,128)S(1)}, u32[]{:S(2)}, u32[]{:S(2)}) collective-permute-start(f32[476,128]{1,0:T(8,128)S(1)} %squeeze.57), channel_id=1, source_target_pairs={{0,24},{8,0},{16,8},{24,16},{1,25},{9,1},{17,9},{25,17},{2,26},{10... | collective-permute-start | bytes 731144 | tf_op jit(solution)/shard_map/ppermute | solution.py:19
  193.0 4.6 %collective-permute-done.11 = f32[476,128]{1,0:T(8,128)S(1)} collective-permute-done((f32[476,128]{1,0:T(8,128)S(1)}, f32[476,128]{1,0:T(8,128)S(1)}, u32[]{:S(2)}, u32[]{:S(2)}) %collective-permute-start.11) | collective-permute-done | bytes 243744 | tf_op jit(solution)/shard_map/ppermute | solution.py:19
  197.6 6.4 %collective-permute-done.12 = f32[476,128]{1,0:T(8,128)S(1)} collective-permute-done((f32[476,128]{1,0:T(8,128)S(1)}, f32[476,128]{1,0:T(8,128)S(1)}, u32[]{:S(2)}, u32[]{:S(2)}) %collective-permute-start.12) | collective-permute-done | bytes 243744 | tf_op jit(solution)/shard_map/ppermute | solution.py:19
  214.0 4.8 %collective-permute-start.18 = (bf16[476,128]{1,0:T(8,128)(2,1)S(1)}, bf16[476,128]{1,0:T(8,128)(2,1)S(1)}, u32[]{:S(2)}, u32[]{:S(2)}) collective-permute-start(bf16[476,128]{1,0:T(8,128)(2,1)S(1)} %squeeze.63), channel_id=1, source_target_pairs={{0,48},{8,56},{16,32},{24,40},{32,80},{40,88},{48,64},{56,72},{64,... | collective-permute-start | bytes 365576 | tf_op jit(solution)/shard_map/ppermute | solution.py:29
  227.3 52.1 %all-gather.11.cloned.1.call-done = bf16[32,476,128]{2,1,0:T(8,128)(2,1)} async-done(((bf16[4,476,128]{2,1,0:T(8,128)(2,1)}), bf16[32,476,128]{2,1,0:T(8,128)(2,1)}) %all-gather.11.cloned.1.call-update) | async-done | bytes 3899408 | tf_op jit(solution)/shard_map/all_gather | solution.py:64
  279.4 7.0 %reshape.364 = bf16[544,3584]{1,0:T(8,128)(2,1)} reshape(bf16[32,476,128]{2,1,0:T(8,128)(2,1)} %all-gather.11.cloned.1.call-done) | data formatting | bytes 7798784 | tf_op jit(solution)/shard_map/reshape | solution.py:66
  295.1 5.2 %collective-permute-start.21 = (bf16[1,68,128]{2,1,0:T(8,128)(2,1)S(1)}, bf16[1,68,128]{2,1,0:T(8,128)(2,1)S(1)}, u32[]{:S(2)}, u32[]{:S(2)}) collective-permute-start(bf16[1,68,128]{2,1,0:T(8,128)(2,1)S(1)} %get-tuple-element.29), channel_id=1, source_target_pairs={{0,2},{1,3},{2,4},{3,5},{4,6},{5,7},{6,0},{7,1},{8,10},{9,11},{10,... | collective-permute-start | bytes 52232 | tf_op jit(solution)/shard_map/ppermute | solution.py:19
  303.5 4.1 %collective-permute-start.23 = (bf16[1,68,128]{2,1,0:T(8,128)(2,1)S(1)}, bf16[1,68,128]{2,1,0:T(8,128)(2,1)S(1)}, u32[]{:S(2)}, u32[]{:S(2)}) collective-permute-start(bf16[1,68,128]{2,1,0:T(8,128)(2,1)S(1)} %get-tuple-element.27), channel_id=1, source_target_pairs={{0,4},{1,5},{2,6},{3,7},{4,0},{5,1},{6,2},{7,3},{8,12},{9,13},{10,... | collective-permute-start | bytes 52232 | tf_op jit(solution)/shard_map/ppermute | solution.py:19
  307.7 4.2 %collective-permute-start.24 = (bf16[1,68,128]{2,1,0:T(8,128)(2,1)S(1)}, bf16[1,68,128]{2,1,0:T(8,128)(2,1)S(1)}, u32[]{:S(2)}, u32[]{:S(2)}) collective-permute-start(bf16[1,68,128]{2,1,0:T(8,128)(2,1)S(1)} %get-tuple-element.26), channel_id=1, source_target_pairs={{0,5},{1,6},{2,7},{3,0},{4,1},{5,2},{6,3},{7,4},{8,13},{9,14},{10,... | collective-permute-start | bytes 52232 | tf_op jit(solution)/shard_map/ppermute | solution.py:19
  311.9 5.2 %collective-permute-start.25 = (bf16[1,68,128]{2,1,0:T(8,128)(2,1)S(1)}, bf16[1,68,128]{2,1,0:T(8,128)(2,1)S(1)}, u32[]{:S(2)}, u32[]{:S(2)}) collective-permute-start(bf16[1,68,128]{2,1,0:T(8,128)(2,1)S(1)} %get-tuple-element.25), channel_id=1, source_target_pairs={{0,6},{1,7},{2,0},{3,1},{4,2},{5,3},{6,4},{7,5},{8,14},{9,15},{10,... | collective-permute-start | bytes 52232 | tf_op jit(solution)/shard_map/ppermute | solution.py:19
  322.2 4.4 %convert_reduce_fusion = f32[68,3584]{1,0:T(8,128)S(1)} fusion(bf16[8,1,128,3584]{3,2,1,0:T(8,128)(2,1)} %all-gather.9.cloned.1.call-done, bf16[8,68,128]{2,1,0:T(8,128)(2,1)S(1)} %gather_fusion.3, pred[8]{0:T(512)(128)(4,1)S(1)} %compare_and_fusion), kind=kOutput, calls=%fused_computation.4 | convolution fusion | flops 504797184 | bytes 8454152 | tf_op jit(solution)/shard_map/jrh,jhd->jrd/dot_general | solution.py:77
  326.8 4.3 %collective-permute-start.27 = (f32[476,128]{1,0:T(8,128)S(1)}, f32[476,128]{1,0:T(8,128)S(1)}, u32[]{:S(2)}, u32[]{:S(2)}) collective-permute-start(f32[476,128]{1,0:T(8,128)S(1)} %squeeze.65), channel_id=1, source_target_pairs={{0,24},{8,0},{16,8},{24,16},{1,25},{9,1},{17,9},{25,17},{2,26},{10... | collective-permute-start | bytes 731144 | tf_op jit(solution)/shard_map/ppermute | solution.py:19
  336.2 4.3 %collective-permute-done.28 = f32[476,128]{1,0:T(8,128)} collective-permute-done((f32[476,128]{1,0:T(8,128)S(1)}, f32[476,128]{1,0:T(8,128)}, u32[]{:S(2)}, u32[]{:S(2)}) %collective-permute-start.28) | collective-permute-done | bytes 243744 | tf_op jit(solution)/shard_map/ppermute | solution.py:19
  340.5 6.6 %collective-permute-done.29 = f32[476,128]{1,0:T(8,128)} collective-permute-done((f32[476,128]{1,0:T(8,128)S(1)}, f32[476,128]{1,0:T(8,128)}, u32[]{:S(2)}, u32[]{:S(2)}) %collective-permute-start.29) | collective-permute-done | bytes 243744 | tf_op jit(solution)/shard_map/ppermute | solution.py:19
  (155 shorter events, 85.8 us)
Async XLA Ops:
  6.5 81.0 %all-gather.7.cloned.1.call-start = ((), (), s32[]{:S(2)}) async-start(), calls=%async_computation | async-start | bytes 4423680 | tf_op jit(solution)/shard_map/all_gather | solution.py:64
  11.6 11.9 %collective-permute-start = (bf16[476,128]{1,0:T(8,128)(2,1)S(1)}, bf16[476,128]{1,0:T(8,128)(2,1)S(1)}, u32[]{:S(2)}, u32[]{:S(2)}) collective-permute-start(bf16[476,128]{1,0:T(8,128)(2,1)S(1)} %squeeze.52), channel_id=1, source_target_pairs={{0,8},{8,16},{16,24},{24,0},{1,9},{9,17},{17,25},{25,1},{2,10},{10... | collective-permute-start | bytes 365576 | tf_op jit(solution)/shard_map/ppermute | solution.py:19
  26.9 151.6 %all-gather.9.cloned.1.call-start = ((), (), s32[]{:S(2)}) async-start(), calls=%async_computation.1 | async-start | bytes 8257536 | tf_op jit(solution)/shard_map/all_gather | solution.py:101
  27.7 251.8 %all-gather.11.cloned.1.call-start = ((), (), s32[]{:S(2)}) async-start(), calls=%async_computation.2 | async-start | bytes 4423680 | tf_op jit(solution)/shard_map/all_gather | solution.py:64
  27.7 164.9 %collective-permute-start.15 = (bf16[3584]{0:T(1024)(128)(2,1)S(1)}, bf16[3584]{0:T(1024)(128)(2,1)S(1)}, u32[]{:S(2)}, u32[]{:S(2)}) collective-permute-start(bf16[3584]{0:T(1024)(128)(2,1)S(1)} %reduce), channel_id=1, source_target_pairs={{0,480},{32,0},{64,32},{96,64},{128,96},{160,128},{192,160},{224,1... | collective-permute-start | bytes 21512 | tf_op jit(solution)/shard_map/ppermute | solution.py:19
  99.3 13.9 %collective-permute-start.3 = (bf16[1,68,128]{2,1,0:T(8,128)(2,1)S(1)}, bf16[1,68,128]{2,1,0:T(8,128)(2,1)S(1)}, u32[]{:S(2)}, u32[]{:S(2)}) collective-permute-start(bf16[1,68,128]{2,1,0:T(8,128)(2,1)S(1)} %get-tuple-element.38), channel_id=1, source_target_pairs={{0,1},{1,2},{2,3},{3,4},{4,5},{5,6},{6,7},{7,0},{8,9},{9,10},{10,1... | collective-permute-start | bytes 52232 | tf_op jit(solution)/shard_map/ppermute | solution.py:19
  101.4 16.6 %collective-permute-start.4 = (bf16[1,68,128]{2,1,0:T(8,128)(2,1)S(1)}, bf16[1,68,128]{2,1,0:T(8,128)(2,1)S(1)}, u32[]{:S(2)}, u32[]{:S(2)}) collective-permute-start(bf16[1,68,128]{2,1,0:T(8,128)(2,1)S(1)} %get-tuple-element.37), channel_id=1, source_target_pairs={{0,2},{1,3},{2,4},{3,5},{4,6},{5,7},{6,0},{7,1},{8,10},{9,11},{10,... | collective-permute-start | bytes 52232 | tf_op jit(solution)/shard_map/ppermute | solution.py:19
  106.5 16.7 %collective-permute-start.5 = (bf16[1,68,128]{2,1,0:T(8,128)(2,1)S(1)}, bf16[1,68,128]{2,1,0:T(8,128)(2,1)S(1)}, u32[]{:S(2)}, u32[]{:S(2)}) collective-permute-start(bf16[1,68,128]{2,1,0:T(8,128)(2,1)S(1)} %get-tuple-element.36), channel_id=1, source_target_pairs={{0,3},{1,4},{2,5},{3,6},{4,7},{5,0},{6,1},{7,2},{8,11},{9,12},{10,... | collective-permute-start | bytes 52232 | tf_op jit(solution)/shard_map/ppermute | solution.py:19
  109.7 15.8 %collective-permute-start.6 = (bf16[1,68,128]{2,1,0:T(8,128)(2,1)S(1)}, bf16[1,68,128]{2,1,0:T(8,128)(2,1)S(1)}, u32[]{:S(2)}, u32[]{:S(2)}) collective-permute-start(bf16[1,68,128]{2,1,0:T(8,128)(2,1)S(1)} %get-tuple-element.35), channel_id=1, source_target_pairs={{0,4},{1,5},{2,6},{3,7},{4,0},{5,1},{6,2},{7,3},{8,12},{9,13},{10,... | collective-permute-start | bytes 52232 | tf_op jit(solution)/shard_map/ppermute | solution.py:19
  113.2 12.2 %collective-permute-start.7 = (bf16[1,68,128]{2,1,0:T(8,128)(2,1)S(1)}, bf16[1,68,128]{2,1,0:T(8,128)(2,1)S(1)}, u32[]{:S(2)}, u32[]{:S(2)}) collective-permute-start(bf16[1,68,128]{2,1,0:T(8,128)(2,1)S(1)} %get-tuple-element.34), channel_id=1, source_target_pairs={{0,5},{1,6},{2,7},{3,0},{4,1},{5,2},{6,3},{7,4},{8,13},{9,14},{10,... | collective-permute-start | bytes 52232 | tf_op jit(solution)/shard_map/ppermute | solution.py:19
  183.1 9.9 %collective-permute-start.10 = (f32[476,128]{1,0:T(8,128)S(1)}, f32[476,128]{1,0:T(8,128)S(1)}, u32[]{:S(2)}, u32[]{:S(2)}) collective-permute-start(f32[476,128]{1,0:T(8,128)S(1)} %squeeze.57), channel_id=1, source_target_pairs={{0,24},{8,0},{16,8},{24,16},{1,25},{9,1},{17,9},{25,17},{2,26},{10... | collective-permute-start | bytes 731144 | tf_op jit(solution)/shard_map/ppermute | solution.py:19
  187.4 10.2 %collective-permute-start.11 = (f32[476,128]{1,0:T(8,128)S(1)}, f32[476,128]{1,0:T(8,128)S(1)}, u32[]{:S(2)}, u32[]{:S(2)}) collective-permute-start(f32[476,128]{1,0:T(8,128)S(1)} %squeeze.58), channel_id=1, source_target_pairs={{0,16},{8,24},{16,0},{24,8},{1,17},{9,25},{17,1},{25,9},{2,18},{10... | collective-permute-start | bytes 731144 | tf_op jit(solution)/shard_map/ppermute | solution.py:19
  189.9 14.0 %collective-permute-start.12 = (f32[476,128]{1,0:T(8,128)S(1)}, f32[476,128]{1,0:T(8,128)S(1)}, u32[]{:S(2)}, u32[]{:S(2)}) collective-permute-start(f32[476,128]{1,0:T(8,128)S(1)} %squeeze.59), channel_id=1, source_target_pairs={{0,8},{8,16},{16,24},{24,0},{1,9},{9,17},{17,25},{25,1},{2,10},{10... | collective-permute-start | bytes 731144 | tf_op jit(solution)/shard_map/ppermute | solution.py:19
  209.9 12.3 %collective-permute-start.16 = (bf16[476,128]{1,0:T(8,128)(2,1)S(1)}, bf16[476,128]{1,0:T(8,128)(2,1)S(1)}, u32[]{:S(2)}, u32[]{:S(2)}) collective-permute-start(bf16[476,128]{1,0:T(8,128)(2,1)S(1)} %squeeze.61), channel_id=1, source_target_pairs={{0,32},{8,40},{16,48},{24,56},{32,64},{40,72},{48,80},{56,88},{64,... | collective-permute-start | bytes 365576 | tf_op jit(solution)/shard_map/ppermute | solution.py:29
  211.9 11.4 %collective-permute-start.17 = (bf16[476,128]{1,0:T(8,128)(2,1)S(1)}, bf16[476,128]{1,0:T(8,128)(2,1)S(1)}, u32[]{:S(2)}, u32[]{:S(2)}) collective-permute-start(bf16[476,128]{1,0:T(8,128)(2,1)S(1)} %squeeze.62), channel_id=1, source_target_pairs={{0,40},{8,48},{16,56},{24,32},{32,72},{40,80},{48,88},{56,64},{64,... | collective-permute-start | bytes 365576 | tf_op jit(solution)/shard_map/ppermute | solution.py:29
  291.2 16.5 %collective-permute-start.20 = (bf16[1,68,128]{2,1,0:T(8,128)(2,1)S(1)}, bf16[1,68,128]{2,1,0:T(8,128)(2,1)S(1)}, u32[]{:S(2)}, u32[]{:S(2)}) collective-permute-start(bf16[1,68,128]{2,1,0:T(8,128)(2,1)S(1)} %get-tuple-element.30), channel_id=1, source_target_pairs={{0,1},{1,2},{2,3},{3,4},{4,5},{5,6},{6,7},{7,0},{8,9},{9,10},{10,1... | collective-permute-start | bytes 52232 | tf_op jit(solution)/shard_map/ppermute | solution.py:19
  293.1 56.3 %collective-permute-start.13 = (bf16[64,3584]{1,0:T(8,128)(2,1)}, bf16[64,3584]{1,0:T(8,128)(2,1)S(1)}, u32[]{:S(2)}, u32[]{:S(2)}) collective-permute-start(bf16[64,3584]{1,0:T(8,128)(2,1)} %get-tuple-element.7), channel_id=1, source_target_pairs={{0,32},{32,64},{64,96},{96,128},{128,160},{160,192},{192,224},{224... | collective-permute-start | bytes 1376264 | tf_op jit(solution)/shard_map/ppermute | solution.py:19
  295.1 16.8 %collective-permute-start.21 = (bf16[1,68,128]{2,1,0:T(8,128)(2,1)S(1)}, bf16[1,68,128]{2,1,0:T(8,128)(2,1)S(1)}, u32[]{:S(2)}, u32[]{:S(2)}) collective-permute-start(bf16[1,68,128]{2,1,0:T(8,128)(2,1)S(1)} %get-tuple-element.29), channel_id=1, source_target_pairs={{0,2},{1,3},{2,4},{3,5},{4,6},{5,7},{6,0},{7,1},{8,10},{9,11},{10,... | collective-permute-start | bytes 52232 | tf_op jit(solution)/shard_map/ppermute | solution.py:19
  300.4 16.7 %collective-permute-start.22 = (bf16[1,68,128]{2,1,0:T(8,128)(2,1)S(1)}, bf16[1,68,128]{2,1,0:T(8,128)(2,1)S(1)}, u32[]{:S(2)}, u32[]{:S(2)}) collective-permute-start(bf16[1,68,128]{2,1,0:T(8,128)(2,1)S(1)} %get-tuple-element.28), channel_id=1, source_target_pairs={{0,3},{1,4},{2,5},{3,6},{4,7},{5,0},{6,1},{7,2},{8,11},{9,12},{10,... | collective-permute-start | bytes 52232 | tf_op jit(solution)/shard_map/ppermute | solution.py:19
  303.5 15.8 %collective-permute-start.23 = (bf16[1,68,128]{2,1,0:T(8,128)(2,1)S(1)}, bf16[1,68,128]{2,1,0:T(8,128)(2,1)S(1)}, u32[]{:S(2)}, u32[]{:S(2)}) collective-permute-start(bf16[1,68,128]{2,1,0:T(8,128)(2,1)S(1)} %get-tuple-element.27), channel_id=1, source_target_pairs={{0,4},{1,5},{2,6},{3,7},{4,0},{5,1},{6,2},{7,3},{8,12},{9,13},{10,... | collective-permute-start | bytes 52232 | tf_op jit(solution)/shard_map/ppermute | solution.py:19
  307.7 11.7 %collective-permute-start.24 = (bf16[1,68,128]{2,1,0:T(8,128)(2,1)S(1)}, bf16[1,68,128]{2,1,0:T(8,128)(2,1)S(1)}, u32[]{:S(2)}, u32[]{:S(2)}) collective-permute-start(bf16[1,68,128]{2,1,0:T(8,128)(2,1)S(1)} %get-tuple-element.26), channel_id=1, source_target_pairs={{0,5},{1,6},{2,7},{3,0},{4,1},{5,2},{6,3},{7,4},{8,13},{9,14},{10,... | collective-permute-start | bytes 52232 | tf_op jit(solution)/shard_map/ppermute | solution.py:19
  326.8 9.4 %collective-permute-start.27 = (f32[476,128]{1,0:T(8,128)S(1)}, f32[476,128]{1,0:T(8,128)S(1)}, u32[]{:S(2)}, u32[]{:S(2)}) collective-permute-start(f32[476,128]{1,0:T(8,128)S(1)} %squeeze.65), channel_id=1, source_target_pairs={{0,24},{8,0},{16,8},{24,16},{1,25},{9,1},{17,9},{25,17},{2,26},{10... | collective-permute-start | bytes 731144 | tf_op jit(solution)/shard_map/ppermute | solution.py:19
  331.1 9.4 %collective-permute-start.28 = (f32[476,128]{1,0:T(8,128)S(1)}, f32[476,128]{1,0:T(8,128)}, u32[]{:S(2)}, u32[]{:S(2)}) collective-permute-start(f32[476,128]{1,0:T(8,128)S(1)} %squeeze.66), channel_id=1, source_target_pairs={{0,16},{8,24},{16,0},{24,8},{1,17},{9,25},{17,1},{25,9},{2,18},{10... | collective-permute-start | bytes 731144 | tf_op jit(solution)/shard_map/ppermute | solution.py:19
  333.6 13.5 %collective-permute-start.29 = (f32[476,128]{1,0:T(8,128)S(1)}, f32[476,128]{1,0:T(8,128)}, u32[]{:S(2)}, u32[]{:S(2)}) collective-permute-start(f32[476,128]{1,0:T(8,128)S(1)} %squeeze.67), channel_id=1, source_target_pairs={{0,8},{8,16},{16,24},{24,0},{1,9},{9,17},{17,25},{25,1},{2,10},{10... | collective-permute-start | bytes 731144 | tf_op jit(solution)/shard_map/ppermute | solution.py:19
  (21 other events, 248.3 us)
Sparse Core Ops, SparseCore 0:
  27.0 60.4 all-gather.6
  89.6 88.8 all-gather.8
  227.4 51.9 all-gather.10

commit v4 on v2

--- a/solution.py
+++ b/solution.py
@@ -33,14 +33,18 @@
     return jnp.dot(placing, normed, preferred_element_type=jnp.float32).astype(jnp.bfloat16)
 
 
-def routed_branch(normed, expert_ids, route_weight, w_gate, w_up, down_all):
+def routed_branch(normed, expert_ids, route_weight, w_gate, w_up, down_all, down_first=None):
     n_x = lax.axis_size("ex")
     model_width = normed.shape[1]
     slot_ids = slot_index(expert_ids, MOST, EXPERTS)
     block_rows = MOST * model_width // LANE
     per_expert = place_rows(normed, slot_ids, EXPERTS * MOST).reshape(EXPERTS, block_rows, LANE)
     from_x = lax.all_to_all(per_expert, "ex", split_axis=0, concat_axis=0, tiled=True)
+    if down_first is not None:
+        from_x, down_first = lax.optimization_barrier((from_x, down_first))
     slot_rows = lax.all_gather(from_x, "ey", axis=0, tiled=False)
+    if callable(down_all):
+        slot_rows, down_all = down_all(slot_rows, down_first)
     n_y = slot_rows.shape[0]
     flat_rows = slot_rows.reshape(-1, model_width)
     gate_act = jnp.dot(flat_rows, w_gate, preferred_element_type=jnp.float32)
@@ -48,7 +52,12 @@
     hidden = (jax.nn.silu(gate_act) * up_act).astype(jnp.bfloat16)
     hidden = hidden.reshape(n_y, n_x * MOST, hidden.shape[-1])
     hidden_here = lax.all_to_all(hidden, "ey", split_axis=0, concat_axis=0, tiled=True)
-    parts = jnp.einsum("jrh,jhd->jrd", hidden_here, down_all, preferred_element_type=jnp.float32)
+    if isinstance(down_all, tuple):
+        split = down_all[0].shape[1]
+        parts = jnp.einsum("jrh,jhd->jrd", hidden_here[:, :, :split], down_all[0], preferred_element_type=jnp.float32)
+        parts = parts + jnp.einsum("jrh,jhd->jrd", hidden_here[:, :, split:], down_all[1], preferred_element_type=jnp.float32)
+    else:
+        parts = jnp.einsum("jrh,jhd->jrd", hidden_here, down_all, preferred_element_type=jnp.float32)
     expert_out = jnp.sum(parts.astype(jnp.bfloat16).astype(jnp.float32), axis=0)
     expert_out = expert_out.reshape(n_x, block_rows, LANE)
     returned = lax.all_to_all(expert_out, "ex", split_axis=0, concat_axis=0, tiled=True)
@@ -57,11 +66,11 @@
     return jnp.sum(weights[:, :, None] * picked, axis=1)
 
 
-def layer_terms(rows_in, gain_row, w_gate, w_up, down_all, expert_ids, route_weight):
+def layer_terms(rows_in, gain_row, w_gate, w_up, down_all, expert_ids, route_weight, down_first=None):
     values = rows_in.astype(jnp.float32)
     inv_rms = lax.rsqrt(jnp.mean(values * values, axis=1, keepdims=True) + NORM_EPS)
     normed = (values * inv_rms * gain_row.astype(jnp.float32)).astype(jnp.bfloat16)
-    branch = routed_branch(normed, expert_ids, route_weight, w_gate, w_up, down_all)
+    branch = routed_branch(normed, expert_ids, route_weight, w_gate, w_up, down_all, down_first)
     return (values, branch)
 
 
@@ -71,10 +80,19 @@
     gain_row = norm_gain[0]
     w_gate = gate_w[0, 0]
     w_up = up_w[0, 0]
-    down_all = lax.all_gather(down_w[0, 0], "ey", axis=0, tiled=False)
+    split = down_w.shape[2] // 4
+    down_first = lax.all_gather(down_w[0, 0, :split], "ey", axis=0, tiled=False)
+    gathered = []
+
+    def down_rest(slot_rows, first_part):
+        slot_rows, rest = lax.optimization_barrier((slot_rows, down_w[0, 0, split:]))
+        gathered.append((first_part, lax.all_gather(rest, "ey", axis=0, tiled=False)))
+        return slot_rows, gathered[0]
+
     values, branch = layer_terms(
-        rows_in, gain_row, w_gate, w_up, down_all, route_ids[0, 0], route_wts[0, 0]
+        rows_in, gain_row, w_gate, w_up, down_rest, route_ids[0, 0], route_wts[0, 0], down_first
     )
+    down_all = gathered[0]
     first_out = (values + branch).astype(jnp.bfloat16)
     arrived = shifted(first_out, "pipe", 1)
     values, branch = layer_terms(

time: 332 us -> 346 us (1.042)
  waiting for transfers between devices: 210 us -> 220 us
    all_gather x1 -> x2, waiting for transfers between devices: 64.8 us -> 75.5 us  [the longest x1 47.5 us: down_rest(): lax.all_gather(rest, 'ey', axis=0, tiled=False)]
    dot_general x2 -> x4, matrix products: 8.74 us -> 10.8 us  [the longest x2 7.94 us: routed_branch(): jnp.einsum('jrh,jhd->jrd', hidden_here[:, :, split:], down_all[1], prefer...]
  transfers between devices with their start and end apart: 6 -> 7, of which waited for: 6 -> 7; matrix products, arithmetic and copies ran while one was open for 4% -> 5% of each run, Pallas kernels for 0% -> 0%
where the time goes in v4:
time: 346 us; the launch traced here: 343 us
  waiting for transfers between devices  220 us (64%)
  blocking collectives  47.7 us (14%)
  local copies, waits for them, and re-layouts  24.1 us (7%)
  matrix products  21.7 us (6%)
  between operations  13.3 us (4%)
  starting transfers between devices  11.2 us (3%)
  other arithmetic  5.77 us (2%)
    all_gather x2, waiting for transfers between devices, routed_branch(): slot_rows = lax.all_gather(from_x, 'ey', axis=0, tiled=False)  114 us
    all_gather x1, waiting for transfers between devices, down_rest(): lax.all_gather(rest, 'ey', axis=0, tiled=False)  47.5 us
    all_gather x1, waiting for transfers between devices, shards(): down_first = lax.all_gather(down_w[0, 0, :split], 'ey', axis=0, tiled=False)  28.1 us
    all_to_all x2, blocking collectives, routed_branch(): lax.all_to_all(hidden, 'ey', split_axis=0, concat_axis=0, tiled=True)  26.4 us
    all_to_all x2, waiting for transfers between devices, routed_branch(): lax.all_to_all(expert_out, 'ex', split_axis=0, concat_axis=0, tiled=True)  24.8 us
    all_to_all x2, blocking collectives, routed_branch(): lax.all_to_all(per_expert, 'ex', split_axis=0, concat_axis=0, tiled=True)  21.4 us
    reshape x2, local copies, waits for them, and re-layouts, routed_branch(): flat_rows = slot_rows.reshape(-1, model_width)  14.1 us
    dot_general x2, matrix products, routed_branch(): jnp.einsum('jrh,jhd->jrd', hidden_here[:, :, split:], down_all[1], prefer...  7.94 us
  transfers between devices with their start and end apart: 7, of which 7 were waited for; matrix products, arithmetic and copies ran while one was open for 5% of the time, Pallas kernels for 0%

profile of v4, /device:TPU:1, one launch (start us, length us, event | category | flops | bytes accessed | tf_op | source)
XLA Modules:
  0.0 343.4 jit_solution(884899249274071095)
XLA Ops:
  6.5 1.8 slice.32
  14.3 11.5 %all_to_all.30 = bf16[4,476,128]{2,1,0:T(8,128)(2,1)} all-to-all(bf16[4,476,128]{2,1,0:T(8,128)(2,1)S(1)} %reshape.210), channel_id=1, replica_groups=mesh['pipe'=16,'ex'=4,'ey'=8] {'ex'}, dimensions={0} | all-to-all | bytes 974848 | tf_op jit(solution)/shard_map/all_to_all | solution.py:42
  25.8 28.1 %all-gather.9.cloned.1.call-done = bf16[8,1,32,3584]{3,2,1,0:T(8,128)(2,1)} async-done(((bf16[1,1,32,3584]{3,2,1,0:T(8,128)(2,1)}), bf16[8,1,32,3584]{3,2,1,0:T(8,128)(2,1)}) %all-gather.9.cloned.1.call-update) | async-done | bytes 1835024 | tf_op jit(solution)/shard_map/all_gather | solution.py:84
  54.9 58.8 %all-gather.11.cloned.1.call-done = bf16[32,476,128]{2,1,0:T(8,128)(2,1)} async-done(((bf16[4,476,128]{2,1,0:T(8,128)(2,1)}), bf16[32,476,128]{2,1,0:T(8,128)(2,1)}) %all-gather.11.cloned.1.call-update) | async-done | bytes 3899408 | tf_op jit(solution)/shard_map/all_gather | solution.py:45
  113.7 7.1 %reshape.211 = bf16[544,3584]{1,0:T(8,128)(2,1)} reshape(bf16[8,4,476,128]{3,2,1,0:T(8,128)(2,1)} %bitcast.65) | data formatting | bytes 7798784 | tf_op jit(solution)/shard_map/reshape | solution.py:49
  120.8 3.4 fusion.14
  125.5 14.5 %all_to_all.31 = bf16[8,68,128]{2,1,0:T(8,128)(2,1)S(1)} all-to-all(bf16[8,68,128]{2,1,0:T(8,128)(2,1)S(1)} %reshape.212), channel_id=1, replica_groups=mesh['pipe'=16,'ex'=4,'ey'=8] {'ey'}, dimensions={0} | all-to-all | bytes 278528 | tf_op jit(solution)/shard_map/all_to_all | solution.py:54
  139.9 47.5 %all-gather.13.cloned.1.call-done = bf16[768,3584]{1,0:T(8,128)(2,1)} async-done(((bf16[96,3584]{1,0:T(8,128)(2,1)}), bf16[768,3584]{1,0:T(8,128)(2,1)}) %all-gather.13.cloned.1.call-update) | async-done | bytes 5505040 | tf_op jit(solution)/shard_map/all_gather | solution.py:89
  187.4 4.0 %fusion.28 = f32[8,68,3584]{2,1,0:T(8,128)S(1)} fusion(bf16[8,96,3584]{2,1,0:T(8,128)(2,1)} %bitcast.61, bf16[8,68,128]{2,1,0:T(8,128)(2,1)S(1)} %all_to_all.31), kind=kOutput, calls=%fused_computation.43 | convolution fusion | flops 374341632 | bytes 13443072 | tf_op jit(solution)/shard_map/jrh,jhd->jrd/dot_general | solution.py:58
  191.4 1.4 convert_reduce_fusion.1
  193.9 4.0 %all-to-all-start.2 = ((f32[4,476,128]{2,1,0:T(8,128)}), f32[4,476,128]{2,1,0:T(8,128)S(1)}, u32[]{:S(2)}, u32[]{:S(2)}) async-start(f32[4,476,128]{2,1,0:T(8,128)} %reshape.213), calls=%async_computation.2 | async-start | bytes 1966080 | tf_op jit(solution)/shard_map/all_to_all | solution.py:63
  197.9 13.4 %all-to-all-done.2 = f32[4,476,128]{2,1,0:T(8,128)S(1)} async-done(((f32[4,476,128]{2,1,0:T(8,128)}), f32[4,476,128]{2,1,0:T(8,128)S(1)}, u32[]{:S(2)}, u32[]{:S(2)}) %all-to-all-start.2) | async-done | bytes 974880 | tf_op jit(solution)/shard_map/all_to_all | solution.py:63
  211.5 1.8 gather_fusion
  214.7 3.1 collective-permute-start
  217.8 5.4 %collective-permute-done = bf16[64,3584]{1,0:T(8,128)(2,1)S(1)} collective-permute-done((bf16[64,3584]{1,0:T(8,128)(2,1)S(1)}, bf16[64,3584]{1,0:T(8,128)(2,1)S(1)}, u32[]{:S(2)}, u32[]{:S(2)}) %collective-permute-start) | collective-permute-done | bytes 458784 | tf_op jit(solution)/shard_map/ppermute | solution.py:19
  224.5 9.9 %all_to_all.32 = bf16[4,476,128]{2,1,0:T(8,128)(2,1)} all-to-all(bf16[4,476,128]{2,1,0:T(8,128)(2,1)S(1)} %reshape.215), channel_id=1, replica_groups=mesh['pipe'=16,'ex'=4,'ey'=8] {'ex'}, dimensions={0} | all-to-all | bytes 974848 | tf_op jit(solution)/shard_map/all_to_all | solution.py:42
  234.4 55.0 %all-gather.15.cloned.1.call-done = bf16[32,476,128]{2,1,0:T(8,128)(2,1)} async-done(((bf16[4,476,128]{2,1,0:T(8,128)(2,1)}), bf16[32,476,128]{2,1,0:T(8,128)(2,1)}) %all-gather.15.cloned.1.call-update) | async-done | bytes 3899408 | tf_op jit(solution)/shard_map/all_gather | solution.py:45
  289.3 7.1 %reshape.216 = bf16[544,3584]{1,0:T(8,128)(2,1)} reshape(bf16[32,476,128]{2,1,0:T(8,128)(2,1)} %all-gather.15.cloned.1.call-done) | data formatting | bytes 7798784 | tf_op jit(solution)/shard_map/reshape | solution.py:49
  296.4 3.4 fusion.12
  301.1 11.9 %all_to_all.33 = bf16[8,68,128]{2,1,0:T(8,128)(2,1)S(1)} all-to-all(bf16[8,68,128]{2,1,0:T(8,128)(2,1)S(1)} %reshape.217), channel_id=1, replica_groups=mesh['pipe'=16,'ex'=4,'ey'=8] {'ey'}, dimensions={0} | all-to-all | bytes 278528 | tf_op jit(solution)/shard_map/all_to_all | solution.py:54
  313.0 4.0 %fusion.25 = f32[8,68,3584]{2,1,0:T(8,128)S(1)} fusion(bf16[8,96,3584]{2,1,0:T(8,128)(2,1)} %bitcast.62, bf16[8,68,128]{2,1,0:T(8,128)(2,1)S(1)} %all_to_all.33), kind=kOutput, calls=%fused_computation.40 | convolution fusion | flops 374341632 | bytes 13443072 | tf_op jit(solution)/shard_map/jrh,jhd->jrd/dot_general | solution.py:58
  317.0 1.4 convert_reduce_fusion
  319.5 4.0 %all-to-all-start.5 = ((f32[4,476,128]{2,1,0:T(8,128)}), f32[4,476,128]{2,1,0:T(8,128)S(1)}, u32[]{:S(2)}, u32[]{:S(2)}) async-start(f32[4,476,128]{2,1,0:T(8,128)} %reshape.218), calls=%async_computation.5 | async-start | bytes 1966080 | tf_op jit(solution)/shard_map/all_to_all | solution.py:63
  323.5 11.4 %all-to-all-done.5 = f32[4,476,128]{2,1,0:T(8,128)S(1)} async-done(((f32[4,476,128]{2,1,0:T(8,128)}), f32[4,476,128]{2,1,0:T(8,128)S(1)}, u32[]{:S(2)}, u32[]{:S(2)}) %all-to-all-start.5) | async-done | bytes 974880 | tf_op jit(solution)/shard_map/all_to_all | solution.py:63
  (62 shorter events, 16.5 us)
Async XLA Ops:
  6.5 114.2 %copy-start = (bf16[1,1,3584,128]{3,2,1,0:T(8,128)(2,1)S(1)}, bf16[1,1,3584,128]{3,2,1,0:T(8,128)(2,1)}, u32[]{:S(2)}) copy-start(bf16[1,1,3584,128]{3,2,1,0:T(8,128)(2,1)} %param.9) | copy-start | bytes 2752516
  6.5 47.4 %copy-start.6 = (bf16[1,1,128,3584]{3,2,1,0:T(8,128)(2,1)S(1)}, bf16[1,1,128,3584]{3,2,1,0:T(8,128)(2,1)}, u32[]{:S(2)}) copy-start(bf16[1,1,128,3584]{3,2,1,0:T(8,128)(2,1)} %param.11) | copy-start | bytes 2752516
  6.5 47.3 %all-gather.9.cloned.1.call-start = ((), (), s32[]{:S(2)}) async-start(), calls=%async_computation.6 | async-start | bytes 2064384 | tf_op jit(solution)/shard_map/all_gather | solution.py:84
  8.3 105.3 %all-gather.11.cloned.1.call-start = ((), (), s32[]{:S(2)}) async-start(), calls=%async_computation.7 | async-start | bytes 4423680 | tf_op jit(solution)/shard_map/all_gather | solution.py:45
  53.9 133.5 %all-gather.13.cloned.1.call-start = ((), (), s32[]{:S(2)}) async-start(), calls=%async_computation.8 | async-start | bytes 6193152 | tf_op jit(solution)/shard_map/all_gather | solution.py:89
  120.8 3.4 copy-start.4
  120.8 3.5 %copy-start.9 = (bf16[1,1,3584,128]{3,2,1,0:T(8,128)(2,1)S(1)}, bf16[1,1,3584,128]{3,2,1,0:T(8,128)(2,1)}, u32[]{:S(2)}) copy-start(bf16[1,1,3584,128]{3,2,1,0:T(8,128)(2,1)} %param.10) | copy-start | bytes 2752516
  187.4 4.0 %copy-start.1 = (bf16[8,1,32,3584]{3,2,1,0:T(8,128)(2,1)S(1)}, bf16[8,1,32,3584]{3,2,1,0:T(8,128)(2,1)}, u32[]{:S(2)}) copy-start(bf16[8,1,32,3584]{3,2,1,0:T(8,128)(2,1)} %all-gather.9.cloned.1.call-done) | copy-start | bytes 5505028
  192.8 5.1 %copy-start.7 = (s32[1,2,64,1]{2,3,1,0:T(1,128)S(1)}, s32[1,2,64,1]{2,3,1,0:T(1,128)}, u32[]{:S(2)}) copy-start(s32[1,2,64,1]{2,3,1,0:T(1,128)} %param.12) | copy-start | bytes 1540
  192.8 5.1 %copy-start.8 = (s32[1,2,64,1]{2,3,1,0:T(1,128)S(1)}, s32[1,2,64,1]{2,3,1,0:T(1,128)}, u32[]{:S(2)}) copy-start(s32[1,2,64,1]{2,3,1,0:T(1,128)} %param.13) | copy-start | bytes 1540
  193.9 17.4 %all-to-all-start.2 = ((f32[4,476,128]{2,1,0:T(8,128)}), f32[4,476,128]{2,1,0:T(8,128)S(1)}, u32[]{:S(2)}, u32[]{:S(2)}) async-start(f32[4,476,128]{2,1,0:T(8,128)} %reshape.213), calls=%async_computation.2 | async-start | bytes 1966080 | tf_op jit(solution)/shard_map/all_to_all | solution.py:63
  197.9 91.4 %all-gather.15.cloned.1.call-start = ((), (), s32[]{:S(2)}) async-start(), calls=%async_computation.9 | async-start | bytes 4423680 | tf_op jit(solution)/shard_map/all_gather | solution.py:45
  211.5 1.8 copy-start.3
  214.7 8.6 %collective-permute-start = (bf16[64,3584]{1,0:T(8,128)(2,1)S(1)}, bf16[64,3584]{1,0:T(8,128)(2,1)S(1)}, u32[]{:S(2)}, u32[]{:S(2)}) collective-permute-start(bf16[64,3584]{1,0:T(8,128)(2,1)S(1)} %fusion.9), channel_id=1, source_target_pairs={{0,32},{32,64},{64,96},{96,128},{128,160},{160,192},{192,224},{224... | collective-permute-start | bytes 1376264 | tf_op jit(solution)/shard_map/ppermute | solution.py:19
  296.4 3.4 copy-start.5
  296.4 3.5 %copy-start.10 = (bf16[1,1,3584,128]{3,2,1,0:T(8,128)(2,1)S(1)}, bf16[1,1,3584,128]{3,2,1,0:T(8,128)(2,1)}, u32[]{:S(2)}) copy-start(bf16[1,1,3584,128]{3,2,1,0:T(8,128)(2,1)} %param.10) | copy-start | bytes 2752516
  313.0 4.0 %copy-start.2 = (bf16[8,1,32,3584]{3,2,1,0:T(8,128)(2,1)S(1)}, bf16[8,1,32,3584]{3,2,1,0:T(8,128)(2,1)}, u32[]{:S(2)}) copy-start(bf16[8,1,32,3584]{3,2,1,0:T(8,128)(2,1)} %all-gather.9.cloned.1.call-done) | copy-start | bytes 5505028
  319.5 15.4 %all-to-all-start.5 = ((f32[4,476,128]{2,1,0:T(8,128)}), f32[4,476,128]{2,1,0:T(8,128)S(1)}, u32[]{:S(2)}, u32[]{:S(2)}) async-start(f32[4,476,128]{2,1,0:T(8,128)} %reshape.218), calls=%async_computation.5 | async-start | bytes 1966080 | tf_op jit(solution)/shard_map/all_to_all | solution.py:63
Sparse Core Ops, SparseCore 0:
  9.4 44.3 all-gather.8
  56.0 57.6 all-gather.10
  115.8 71.6 all-gather.12
  234.5 54.8 all-gather.14

commit v5 on v2

--- a/solution.py
+++ b/solution.py
@@ -17,6 +17,19 @@
     count = lax.axis_size(axis)
     pairs = [(source, (source + steps) % count) for source in range(count)]
     return lax.ppermute(value, axis, pairs)
+
+
+def ring_gather(value, axis):
+    count = lax.axis_size(axis)
+    ahead, behind = {0: value}, {}
+    forward, backward = value, value
+    for step in range(1, count // 2 + 1):
+        forward = shifted(forward, axis, 1)
+        behind[step] = forward
+        if step < count - step:
+            backward = shifted(backward, axis, -1)
+            ahead[step] = backward
+    return [ahead[d] if d in ahead else behind[count - d] for d in range(count)]
 
 
 def slot_index(expert_ids, capacity, experts):
@@ -48,8 +61,13 @@
     hidden = (jax.nn.silu(gate_act) * up_act).astype(jnp.bfloat16)
     hidden = hidden.reshape(n_y, n_x * MOST, hidden.shape[-1])
     hidden_here = lax.all_to_all(hidden, "ey", split_axis=0, concat_axis=0, tiled=True)
-    parts = jnp.einsum("jrh,jhd->jrd", hidden_here, down_all, preferred_element_type=jnp.float32)
-    expert_out = jnp.sum(parts.astype(jnp.bfloat16).astype(jnp.float32), axis=0)
+    me_y = lax.axis_index("ey")
+    hidden_rel = jnp.take(hidden_here, (me_y + jnp.arange(n_y)) % n_y, axis=0)
+    expert_out = None
+    for d in range(n_y):
+        part = jnp.dot(hidden_rel[d], down_all[d], preferred_element_type=jnp.float32)
+        part = part.astype(jnp.bfloat16).astype(jnp.float32)
+        expert_out = part if expert_out is None else expert_out + part
     expert_out = expert_out.reshape(n_x, block_rows, LANE)
     returned = lax.all_to_all(expert_out, "ex", split_axis=0, concat_axis=0, tiled=True)
     picked = returned.reshape(EXPERTS * MOST, model_width)[slot_ids]
@@ -71,7 +89,7 @@
     gain_row = norm_gain[0]
     w_gate = gate_w[0, 0]
     w_up = up_w[0, 0]
-    down_all = lax.all_gather(down_w[0, 0], "ey", axis=0, tiled=False)
+    down_all = ring_gather(down_w[0, 0], "ey")
     values, branch = layer_terms(
         rows_in, gain_row, w_gate, w_up, down_all, route_ids[0, 0], route_wts[0, 0]
     )

time: 332 us -> 320 us (0.964)
  waiting for transfers between devices: 210 us -> 166 us
  starting transfers between devices: 11.1 us -> 45.1 us
  blocking collectives: 47.7 us -> 33.4 us
  matrix products: 19.7 us -> 29.7 us
    all_gather x1 -> x0, waiting for transfers between devices: 64.8 us -> none  [shards(): down_all = lax.all_gather(down_w[0, 0], 'ey', axis=0, tiled=False)]
    ppermute x1 -> x8, waiting for transfers between devices: 5.42 us -> 67.8 us  [shifted(): return lax.ppermute(value, axis, pairs)]
    all_gather x2, waiting for transfers between devices: 115 us -> 73.4 us  [routed_branch(): slot_rows = lax.all_gather(from_x, 'ey', axis=0, tiled=False)]
    ppermute x1 -> x8, starting transfers between devices: 3.13 us -> 32.1 us  [shifted(): return lax.ppermute(value, axis, pairs)]
    all_to_all x2 -> x1, blocking collectives: 26.3 us -> 12 us  [routed_branch(): lax.all_to_all(hidden, 'ey', split_axis=0, concat_axis=0, tiled=True)]
    dot_general x2 -> x16, matrix products: 8.74 us -> 18.7 us  [routed_branch(): jnp.dot(hidden_rel[d], down_all[d], preferred_element_type=jnp.float32)]
    all_to_all x0 -> x1, starting transfers between devices: none -> 5.26 us  [routed_branch(): lax.all_to_all(hidden, 'ey', split_axis=0, concat_axis=0, tiled=True)]
  transfers between devices with their start and end apart: 6 -> 13, of which waited for: 6 -> 10; matrix products, arithmetic and copies ran while one was open for 4% -> 7% of each run, Pallas kernels for 0% -> 0%
where the time goes in v5:
time: 320 us; the launch traced here: 317 us
  waiting for transfers between devices  166 us (52%)
  starting transfers between devices  45.1 us (14%)
  blocking collectives  33.4 us (10%)
  matrix products  29.7 us (9%)
  local copies, waits for them, and re-layouts  23.2 us (7%)
  between operations  13.8 us (4%)
  other arithmetic  5.96 us (2%)
    all_gather x2, waiting for transfers between devices, routed_branch(): slot_rows = lax.all_gather(from_x, 'ey', axis=0, tiled=False)  73.4 us
    ppermute x8, waiting for transfers between devices, shifted(): return lax.ppermute(value, axis, pairs)  67.8 us
    ppermute x8, starting transfers between devices, shifted(): return lax.ppermute(value, axis, pairs)  32.1 us
    all_to_all x2, waiting for transfers between devices, routed_branch(): lax.all_to_all(expert_out, 'ex', split_axis=0, concat_axis=0, tiled=True)  23 us
    all_to_all x2, blocking collectives, routed_branch(): lax.all_to_all(per_expert, 'ex', split_axis=0, concat_axis=0, tiled=True)  21.4 us
    dot_general x16, matrix products, routed_branch(): jnp.dot(hidden_rel[d], down_all[d], preferred_element_type=jnp.float32)  18.7 us
    reshape x2, local copies, waits for them, and re-layouts, routed_branch(): flat_rows = slot_rows.reshape(-1, model_width)  14 us
    all_to_all x1, blocking collectives, routed_branch(): lax.all_to_all(hidden, 'ey', split_axis=0, concat_axis=0, tiled=True)  12 us
  transfers between devices with their start and end apart: 13, of which 10 were waited for; matrix products, arithmetic and copies ran while one was open for 7% of the time, Pallas kernels for 0%

profile of v5, /device:TPU:1, one launch (start us, length us, event | category | flops | bytes accessed | tf_op | source)
XLA Modules:
  0.0 316.9 jit_solution(11909350486533672586)
XLA Ops:
  12.6 11.5 %all_to_all.30 = bf16[4,476,128]{2,1,0:T(8,128)(2,1)} all-to-all(bf16[4,476,128]{2,1,0:T(8,128)(2,1)S(1)} %reshape.215), channel_id=1, replica_groups=mesh['pipe'=16,'ex'=4,'ey'=8] {'ex'}, dimensions={0} | all-to-all | bytes 974848 | tf_op jit(solution)/shard_map/all_to_all | solution.py:55
  24.1 4.7 %collective-permute-start.3 = (bf16[128,3584]{1,0:T(8,128)(2,1)S(1)}, bf16[128,3584]{1,0:T(8,128)(2,1)S(1)}, u32[]{:S(2)}, u32[]{:S(2)}) collective-permute-start(bf16[128,3584]{1,0:T(8,128)(2,1)S(1)} %bitcast.119), channel_id=1, source_target_pairs={{0,1},{1,2},{2,3},{3,4},{4,5},{5,6},{6,7},{7,0},{8,9},{9,10},{10,1... | collective-permute-start | bytes 2752520 | tf_op jit(solution)/shard_map/ppermute | solution.py:19
  28.8 3.8 %collective-permute-start = (bf16[128,3584]{1,0:T(8,128)(2,1)S(1)}, bf16[128,3584]{1,0:T(8,128)(2,1)}, u32[]{:S(2)}, u32[]{:S(2)}) collective-permute-start(bf16[128,3584]{1,0:T(8,128)(2,1)S(1)} %bitcast.120), channel_id=1, source_target_pairs={{0,7},{1,0},{2,1},{3,2},{4,3},{5,4},{6,5},{7,6},{8,15},{9,8},{10,9... | collective-permute-start | bytes 2752520 | tf_op jit(solution)/shard_map/ppermute | solution.py:19
  32.6 14.1 %collective-permute-done.3 = bf16[128,3584]{1,0:T(8,128)(2,1)S(1)} collective-permute-done((bf16[128,3584]{1,0:T(8,128)(2,1)S(1)}, bf16[128,3584]{1,0:T(8,128)(2,1)S(1)}, u32[]{:S(2)}, u32[]{:S(2)}) %collective-permute-start.3) | collective-permute-done | bytes 917536 | tf_op jit(solution)/shard_map/ppermute | solution.py:19
  46.7 5.7 %collective-permute-start.4 = (bf16[128,3584]{1,0:T(8,128)(2,1)S(1)}, bf16[128,3584]{1,0:T(8,128)(2,1)}, u32[]{:S(2)}, u32[]{:S(2)}) collective-permute-start(bf16[128,3584]{1,0:T(8,128)(2,1)S(1)} %collective-permute-done.3), channel_id=1, source_target_pairs={{0,1},{1,2},{2,3},{3,4},{4,5},{5,6},{6,7},{7,0},{8,9},{9,10},{10,1... | collective-permute-start | bytes 2752520 | tf_op jit(solution)/shard_map/ppermute | solution.py:19
  52.4 4.4 %collective-permute-start.1 = (bf16[128,3584]{1,0:T(8,128)(2,1)}, bf16[128,3584]{1,0:T(8,128)(2,1)}, u32[]{:S(2)}, u32[]{:S(2)}) collective-permute-start(bf16[128,3584]{1,0:T(8,128)(2,1)} %collective-permute-done), channel_id=1, source_target_pairs={{0,7},{1,0},{2,1},{3,2},{4,3},{5,4},{6,5},{7,6},{8,15},{9,8},{10,9... | collective-permute-start | bytes 2752520 | tf_op jit(solution)/shard_map/ppermute | solution.py:19
  56.8 36.4 %collective-permute-done.4 = bf16[128,3584]{1,0:T(8,128)(2,1)} collective-permute-done((bf16[128,3584]{1,0:T(8,128)(2,1)S(1)}, bf16[128,3584]{1,0:T(8,128)(2,1)}, u32[]{:S(2)}, u32[]{:S(2)}) %collective-permute-start.4) | collective-permute-done | bytes 917536 | tf_op jit(solution)/shard_map/ppermute | solution.py:19
  95.1 17.2 %all-gather.5.cloned.1.call-done = bf16[32,476,128]{2,1,0:T(8,128)(2,1)} async-done(((bf16[4,476,128]{2,1,0:T(8,128)(2,1)}), bf16[32,476,128]{2,1,0:T(8,128)(2,1)}) %all-gather.5.cloned.1.call-update) | async-done | bytes 3899408 | tf_op jit(solution)/shard_map/all_gather | solution.py:56
  112.3 7.0 %reshape.216 = bf16[544,3584]{1,0:T(8,128)(2,1)} reshape(bf16[32,476,128]{2,1,0:T(8,128)(2,1)} %all-gather.5.cloned.1.call-done) | data formatting | bytes 7798784 | tf_op jit(solution)/shard_map/reshape | solution.py:58
  119.3 3.4 %fusion.44 = f32[544,128]{1,0:T(8,128)S(1)} fusion(bf16[544,3584]{1,0:T(8,128)(2,1)} %reshape.216, bf16[1,1,3584,128]{3,2,1,0:T(8,128)(2,1)S(1)} %copy-done), kind=kOutput, calls=%fused_computation.74 | convolution fusion | flops 499122176 | bytes 5095424 | tf_op jit(solution)/shard_map/dot_general | solution.py:59
  124.7 5.3 %all-to-all-start.1 = ((bf16[8,68,128]{2,1,0:T(8,128)(2,1)}), bf16[8,68,128]{2,1,0:T(8,128)(2,1)S(1)}, u32[]{:S(2)}, u32[]{:S(2)}) async-start(bf16[8,68,128]{2,1,0:T(8,128)(2,1)} %reshape.217), calls=%async_computation.1 | async-start | bytes 294912 | tf_op jit(solution)/shard_map/all_to_all | solution.py:63
  130.0 4.6 %collective-permute-start.2 = (bf16[128,3584]{1,0:T(8,128)(2,1)}, bf16[128,3584]{1,0:T(8,128)(2,1)}, u32[]{:S(2)}, u32[]{:S(2)}) collective-permute-start(bf16[128,3584]{1,0:T(8,128)(2,1)} %collective-permute-done.1), channel_id=1, source_target_pairs={{0,7},{1,0},{2,1},{3,2},{4,3},{5,4},{6,5},{7,6},{8,15},{9,8},{10,9... | collective-permute-start | bytes 2752520 | tf_op jit(solution)/shard_map/ppermute | solution.py:19
  145.2 10.6 %collective-permute-done.2 = bf16[128,3584]{1,0:T(8,128)(2,1)} collective-permute-done((bf16[128,3584]{1,0:T(8,128)(2,1)}, bf16[128,3584]{1,0:T(8,128)(2,1)}, u32[]{:S(2)}, u32[]{:S(2)}) %collective-permute-start.2) | collective-permute-done | bytes 917536 | tf_op jit(solution)/shard_map/ppermute | solution.py:19
  161.2 3.7 %all-to-all-start.2 = ((f32[4,476,128]{2,1,0:T(8,128)}), f32[4,476,128]{2,1,0:T(8,128)S(1)}, u32[]{:S(2)}, u32[]{:S(2)}) async-start(f32[4,476,128]{2,1,0:T(8,128)} %reshape.218), calls=%async_computation.2 | async-start | bytes 1966080 | tf_op jit(solution)/shard_map/all_to_all | solution.py:72
  165.0 11.6 %all-to-all-done.2 = f32[4,476,128]{2,1,0:T(8,128)S(1)} async-done(((f32[4,476,128]{2,1,0:T(8,128)}), f32[4,476,128]{2,1,0:T(8,128)S(1)}, u32[]{:S(2)}, u32[]{:S(2)}) %all-to-all-start.2) | async-done | bytes 974880 | tf_op jit(solution)/shard_map/all_to_all | solution.py:72
  179.8 5.1 %collective-permute-start.7 = (bf16[64,3584]{1,0:T(8,128)(2,1)S(1)}, bf16[64,3584]{1,0:T(8,128)(2,1)S(1)}, u32[]{:S(2)}, u32[]{:S(2)}) collective-permute-start(bf16[64,3584]{1,0:T(8,128)(2,1)S(1)} %fusion.39), channel_id=1, source_target_pairs={{0,32},{32,64},{64,96},{96,128},{128,160},{160,192},{192,224},{224... | collective-permute-start | bytes 1376264 | tf_op jit(solution)/shard_map/ppermute | solution.py:19
  184.9 5.4 %collective-permute-done.7 = bf16[64,3584]{1,0:T(8,128)(2,1)S(1)} collective-permute-done((bf16[64,3584]{1,0:T(8,128)(2,1)S(1)}, bf16[64,3584]{1,0:T(8,128)(2,1)S(1)}, u32[]{:S(2)}, u32[]{:S(2)}) %collective-permute-start.7) | collective-permute-done | bytes 458784 | tf_op jit(solution)/shard_map/ppermute | solution.py:19
  191.6 9.9 %all_to_all.31 = bf16[4,476,128]{2,1,0:T(8,128)(2,1)} all-to-all(bf16[4,476,128]{2,1,0:T(8,128)(2,1)S(1)} %reshape.220), channel_id=1, replica_groups=mesh['pipe'=16,'ex'=4,'ey'=8] {'ex'}, dimensions={0} | all-to-all | bytes 974848 | tf_op jit(solution)/shard_map/all_to_all | solution.py:55
  201.5 56.2 %all-gather.7.cloned.1.call-done = bf16[32,476,128]{2,1,0:T(8,128)(2,1)} async-done(((bf16[4,476,128]{2,1,0:T(8,128)(2,1)}), bf16[32,476,128]{2,1,0:T(8,128)(2,1)}) %all-gather.7.cloned.1.call-update) | async-done | bytes 3899408 | tf_op jit(solution)/shard_map/all_gather | solution.py:56
  257.7 7.0 %reshape.221 = bf16[544,3584]{1,0:T(8,128)(2,1)} reshape(bf16[32,476,128]{2,1,0:T(8,128)(2,1)} %all-gather.7.cloned.1.call-done) | data formatting | bytes 7798784 | tf_op jit(solution)/shard_map/reshape | solution.py:58
  264.7 3.4 %fusion.42 = f32[544,128]{1,0:T(8,128)S(1)} fusion(bf16[544,3584]{1,0:T(8,128)(2,1)} %reshape.221, bf16[1,1,3584,128]{3,2,1,0:T(8,128)(2,1)S(1)} %copy-done), kind=kOutput, calls=%fused_computation.72 | convolution fusion | flops 499122176 | bytes 5095424 | tf_op jit(solution)/shard_map/dot_general | solution.py:59
  269.4 12.0 %all_to_all.32 = bf16[8,68,128]{2,1,0:T(8,128)(2,1)S(1)} all-to-all(bf16[8,68,128]{2,1,0:T(8,128)(2,1)S(1)} %reshape.222), channel_id=1, replica_groups=mesh['pipe'=16,'ex'=4,'ey'=8] {'ey'}, dimensions={0} | all-to-all | bytes 278528 | tf_op jit(solution)/shard_map/all_to_all | solution.py:63
  292.6 4.0 %all-to-all-start.5 = ((f32[4,476,128]{2,1,0:T(8,128)}), f32[4,476,128]{2,1,0:T(8,128)S(1)}, u32[]{:S(2)}, u32[]{:S(2)}) async-start(f32[4,476,128]{2,1,0:T(8,128)} %reshape.223), calls=%async_computation.5 | async-start | bytes 1966080 | tf_op jit(solution)/shard_map/all_to_all | solution.py:72
  296.6 11.4 %all-to-all-done.5 = f32[4,476,128]{2,1,0:T(8,128)S(1)} async-done(((f32[4,476,128]{2,1,0:T(8,128)}), f32[4,476,128]{2,1,0:T(8,128)S(1)}, u32[]{:S(2)}, u32[]{:S(2)}) %all-to-all-start.5) | async-done | bytes 974880 | tf_op jit(solution)/shard_map/all_to_all | solution.py:72
  (90 shorter events, 44.8 us)
Async XLA Ops:
  6.5 112.8 %copy-start = (bf16[1,1,3584,128]{3,2,1,0:T(8,128)(2,1)S(1)}, bf16[1,1,3584,128]{3,2,1,0:T(8,128)(2,1)}, u32[]{:S(2)}) copy-start(bf16[1,1,3584,128]{3,2,1,0:T(8,128)(2,1)} %param.11) | copy-start | bytes 2752516
  6.5 17.6 %copy-start.4 = (bf16[1,1,128,3584]{3,2,1,0:T(8,128)(2,1)S(1)}, bf16[1,1,128,3584]{3,2,1,0:T(8,128)(2,1)}, u32[]{:S(2)}) copy-start(bf16[1,1,128,3584]{3,2,1,0:T(8,128)(2,1)} %param.13) | copy-start | bytes 2752516
  6.5 105.8 %all-gather.5.cloned.1.call-start = ((), (), s32[]{:S(2)}) async-start(), calls=%async_computation.6 | async-start | bytes 4423680 | tf_op jit(solution)/shard_map/all_gather | solution.py:56
  24.1 22.6 %collective-permute-start.3 = (bf16[128,3584]{1,0:T(8,128)(2,1)S(1)}, bf16[128,3584]{1,0:T(8,128)(2,1)S(1)}, u32[]{:S(2)}, u32[]{:S(2)}) collective-permute-start(bf16[128,3584]{1,0:T(8,128)(2,1)S(1)} %bitcast.119), channel_id=1, source_target_pairs={{0,1},{1,2},{2,3},{3,4},{4,5},{5,6},{6,7},{7,0},{8,9},{9,10},{10,1... | collective-permute-start | bytes 2752520 | tf_op jit(solution)/shard_map/ppermute | solution.py:19
  28.8 23.6 %collective-permute-start = (bf16[128,3584]{1,0:T(8,128)(2,1)S(1)}, bf16[128,3584]{1,0:T(8,128)(2,1)}, u32[]{:S(2)}, u32[]{:S(2)}) collective-permute-start(bf16[128,3584]{1,0:T(8,128)(2,1)S(1)} %bitcast.120), channel_id=1, source_target_pairs={{0,7},{1,0},{2,1},{3,2},{4,3},{5,4},{6,5},{7,6},{8,15},{9,8},{10,9... | collective-permute-start | bytes 2752520 | tf_op jit(solution)/shard_map/ppermute | solution.py:19
  46.7 95.3 %copy-start.6 = (bf16[128,3584]{1,0:T(8,128)(2,1)}, bf16[128,3584]{1,0:T(8,128)(2,1)S(1)}, u32[]{:S(2)}) copy-start(bf16[128,3584]{1,0:T(8,128)(2,1)S(1)} %collective-permute-done.3) | copy-start | bytes 2752516
  46.7 46.6 %collective-permute-start.4 = (bf16[128,3584]{1,0:T(8,128)(2,1)S(1)}, bf16[128,3584]{1,0:T(8,128)(2,1)}, u32[]{:S(2)}, u32[]{:S(2)}) collective-permute-start(bf16[128,3584]{1,0:T(8,128)(2,1)S(1)} %collective-permute-done.3), channel_id=1, source_target_pairs={{0,1},{1,2},{2,3},{3,4},{4,5},{5,6},{6,7},{7,0},{8,9},{9,10},{10,1... | collective-permute-start | bytes 2752520 | tf_op jit(solution)/shard_map/ppermute | solution.py:19
  52.4 77.6 %collective-permute-start.1 = (bf16[128,3584]{1,0:T(8,128)(2,1)}, bf16[128,3584]{1,0:T(8,128)(2,1)}, u32[]{:S(2)}, u32[]{:S(2)}) collective-permute-start(bf16[128,3584]{1,0:T(8,128)(2,1)} %collective-permute-done), channel_id=1, source_target_pairs={{0,7},{1,0},{2,1},{3,2},{4,3},{5,4},{6,5},{7,6},{8,15},{9,8},{10,9... | collective-permute-start | bytes 2752520 | tf_op jit(solution)/shard_map/ppermute | solution.py:19
  93.2 41.4 %collective-permute-start.5 = (bf16[128,3584]{1,0:T(8,128)(2,1)}, bf16[128,3584]{1,0:T(8,128)(2,1)}, u32[]{:S(2)}, u32[]{:S(2)}) collective-permute-start(bf16[128,3584]{1,0:T(8,128)(2,1)} %collective-permute-done.4), channel_id=1, source_target_pairs={{0,1},{1,2},{2,3},{3,4},{4,5},{5,6},{6,7},{7,0},{8,9},{9,10},{10,1... | collective-permute-start | bytes 2752520 | tf_op jit(solution)/shard_map/ppermute | solution.py:19
  119.3 3.4 %copy-start.2 = (bf16[544,3584]{1,0:T(8,128)(2,1)S(1)}, bf16[544,3584]{1,0:T(8,128)(2,1)}, u32[]{:S(2)}) copy-start(bf16[544,3584]{1,0:T(8,128)(2,1)} %reshape.216) | copy-start | bytes 11698180
  119.3 3.5 %copy-start.10 = (bf16[1,1,3584,128]{3,2,1,0:T(8,128)(2,1)S(1)}, bf16[1,1,3584,128]{3,2,1,0:T(8,128)(2,1)}, u32[]{:S(2)}) copy-start(bf16[1,1,3584,128]{3,2,1,0:T(8,128)(2,1)} %param.12) | copy-start | bytes 2752516
  124.7 13.4 %all-to-all-start.1 = ((bf16[8,68,128]{2,1,0:T(8,128)(2,1)}), bf16[8,68,128]{2,1,0:T(8,128)(2,1)S(1)}, u32[]{:S(2)}, u32[]{:S(2)}) async-start(bf16[8,68,128]{2,1,0:T(8,128)(2,1)} %reshape.217), calls=%async_computation.1 | async-start | bytes 294912 | tf_op jit(solution)/shard_map/all_to_all | solution.py:63
  130.0 25.7 %collective-permute-start.2 = (bf16[128,3584]{1,0:T(8,128)(2,1)}, bf16[128,3584]{1,0:T(8,128)(2,1)}, u32[]{:S(2)}, u32[]{:S(2)}) collective-permute-start(bf16[128,3584]{1,0:T(8,128)(2,1)} %collective-permute-done.1), channel_id=1, source_target_pairs={{0,7},{1,0},{2,1},{3,2},{4,3},{5,4},{6,5},{7,6},{8,15},{9,8},{10,9... | collective-permute-start | bytes 2752520 | tf_op jit(solution)/shard_map/ppermute | solution.py:19
  134.6 24.0 %collective-permute-start.6 = (bf16[128,3584]{1,0:T(8,128)(2,1)}, bf16[128,3584]{1,0:T(8,128)(2,1)}, u32[]{:S(2)}, u32[]{:S(2)}) collective-permute-start(bf16[128,3584]{1,0:T(8,128)(2,1)} %collective-permute-done.5), channel_id=1, source_target_pairs={{0,1},{1,2},{2,3},{3,4},{4,5},{5,6},{6,7},{7,0},{8,9},{9,10},{10,1... | collective-permute-start | bytes 2752520 | tf_op jit(solution)/shard_map/ppermute | solution.py:19
  157.2 7.7 %copy-start.8 = (s32[1,2,64,1]{2,3,1,0:T(1,128)S(1)}, s32[1,2,64,1]{2,3,1,0:T(1,128)}, u32[]{:S(2)}) copy-start(s32[1,2,64,1]{2,3,1,0:T(1,128)} %param.14) | copy-start | bytes 1540
  157.2 7.7 %copy-start.9 = (s32[1,2,64,1]{2,3,1,0:T(1,128)S(1)}, s32[1,2,64,1]{2,3,1,0:T(1,128)}, u32[]{:S(2)}) copy-start(s32[1,2,64,1]{2,3,1,0:T(1,128)} %param.15) | copy-start | bytes 1540
  161.2 15.4 %all-to-all-start.2 = ((f32[4,476,128]{2,1,0:T(8,128)}), f32[4,476,128]{2,1,0:T(8,128)S(1)}, u32[]{:S(2)}, u32[]{:S(2)}) async-start(f32[4,476,128]{2,1,0:T(8,128)} %reshape.218), calls=%async_computation.2 | async-start | bytes 1966080 | tf_op jit(solution)/shard_map/all_to_all | solution.py:72
  164.9 92.8 %all-gather.7.cloned.1.call-start = ((), (), s32[]{:S(2)}) async-start(), calls=%async_computation.7 | async-start | bytes 4423680 | tf_op jit(solution)/shard_map/all_gather | solution.py:56
  179.8 10.5 %collective-permute-start.7 = (bf16[64,3584]{1,0:T(8,128)(2,1)S(1)}, bf16[64,3584]{1,0:T(8,128)(2,1)S(1)}, u32[]{:S(2)}, u32[]{:S(2)}) collective-permute-start(bf16[64,3584]{1,0:T(8,128)(2,1)S(1)} %fusion.39), channel_id=1, source_target_pairs={{0,32},{32,64},{64,96},{96,128},{128,160},{160,192},{192,224},{224... | collective-permute-start | bytes 1376264 | tf_op jit(solution)/shard_map/ppermute | solution.py:19
  264.7 3.4 %copy-start.3 = (bf16[544,3584]{1,0:T(8,128)(2,1)S(1)}, bf16[544,3584]{1,0:T(8,128)(2,1)}, u32[]{:S(2)}) copy-start(bf16[544,3584]{1,0:T(8,128)(2,1)} %reshape.221) | copy-start | bytes 11698180
  264.7 3.5 %copy-start.11 = (bf16[1,1,3584,128]{3,2,1,0:T(8,128)(2,1)S(1)}, bf16[1,1,3584,128]{3,2,1,0:T(8,128)(2,1)}, u32[]{:S(2)}) copy-start(bf16[1,1,3584,128]{3,2,1,0:T(8,128)(2,1)} %param.12) | copy-start | bytes 2752516
  268.2 13.9 %copy-start.5 = (bf16[1,1,128,3584]{3,2,1,0:T(8,128)(2,1)S(1)}, bf16[1,1,128,3584]{3,2,1,0:T(8,128)(2,1)}, u32[]{:S(2)}) copy-start(bf16[1,1,128,3584]{3,2,1,0:T(8,128)(2,1)} %param.13) | copy-start | bytes 2752516
  269.4 16.0 %copy-start.7 = (bf16[128,3584]{1,0:T(8,128)(2,1)S(1)}, bf16[128,3584]{1,0:T(8,128)(2,1)}, u32[]{:S(2)}) copy-start(bf16[128,3584]{1,0:T(8,128)(2,1)} %copy-done.6) | copy-start | bytes 2752516
  292.6 15.4 %all-to-all-start.5 = ((f32[4,476,128]{2,1,0:T(8,128)}), f32[4,476,128]{2,1,0:T(8,128)S(1)}, u32[]{:S(2)}, u32[]{:S(2)}) async-start(f32[4,476,128]{2,1,0:T(8,128)} %reshape.223), calls=%async_computation.5 | async-start | bytes 1966080 | tf_op jit(solution)/shard_map/all_to_all | solution.py:72
  (1 other events, 1.8 us)
Sparse Core Ops, SparseCore 0:
  24.2 88.0 all-gather.4
  201.6 56.0 all-gather.6

commit v6 on v5

--- a/solution.py
+++ b/solution.py
@@ -23,12 +23,16 @@
     count = lax.axis_size(axis)
     ahead, behind = {0: value}, {}
     forward, backward = value, value
-    for step in range(1, count // 2 + 1):
+    for step in range(1, (count + 1) // 2):
         forward = shifted(forward, axis, 1)
         behind[step] = forward
-        if step < count - step:
-            backward = shifted(backward, axis, -1)
-            ahead[step] = backward
+        backward = shifted(backward, axis, -1)
+        ahead[step] = backward
+    if count % 2 == 0:
+        half = value.shape[0] // 2
+        ahead[count // 2] = jnp.concatenate(
+            [shifted(forward[:half], axis, 1), shifted(backward[half:], axis, -1)], axis=0
+        )
     return [ahead[d] if d in ahead else behind[count - d] for d in range(count)]
 
 
@@ -63,11 +67,15 @@
     hidden_here = lax.all_to_all(hidden, "ey", split_axis=0, concat_axis=0, tiled=True)
     me_y = lax.axis_index("ey")
     hidden_rel = jnp.take(hidden_here, (me_y + jnp.arange(n_y)) % n_y, axis=0)
-    expert_out = None
-    for d in range(n_y):
-        part = jnp.dot(hidden_rel[d], down_all[d], preferred_element_type=jnp.float32)
-        part = part.astype(jnp.bfloat16).astype(jnp.float32)
-        expert_out = part if expert_out is None else expert_out + part
+    if isinstance(down_all, list):
+        expert_out = None
+        for d in range(n_y):
+            part = jnp.dot(hidden_rel[d], down_all[d], preferred_element_type=jnp.float32)
+            part = part.astype(jnp.bfloat16).astype(jnp.float32)
+            expert_out = part if expert_out is None else expert_out + part
+    else:
+        parts = jnp.einsum("jrh,jhd->jrd", hidden_rel, down_all, preferred_element_type=jnp.float32)
+        expert_out = jnp.sum(parts.astype(jnp.bfloat16).astype(jnp.float32), axis=0)
     expert_out = expert_out.reshape(n_x, block_rows, LANE)
     returned = lax.all_to_all(expert_out, "ex", split_axis=0, concat_axis=0, tiled=True)
     picked = returned.reshape(EXPERTS * MOST, model_width)[slot_ids]
@@ -96,7 +104,7 @@
     first_out = (values + branch).astype(jnp.bfloat16)
     arrived = shifted(first_out, "pipe", 1)
     values, branch = layer_terms(
-        arrived, gain_row, w_gate, w_up, down_all, route_ids[0, 1], route_wts[0, 1]
+        arrived, gain_row, w_gate, w_up, jnp.stack(down_all, axis=0), route_ids[0, 1], route_wts[0, 1]
     )
     second = (values + branch).astype(jnp.bfloat16)
     result_rows = jnp.where(section_index == 0, arrived, second)

time: 320 us -> 342 us (1.069)
  local copies, waits for them, and re-layouts: 23.2 us -> 44.8 us
  starting transfers between devices: 45.1 us -> 61.2 us
  blocking collectives: 33.4 us -> 22.5 us
  waiting for transfers between devices: 166 us -> 162 us
    all_gather x2, waiting for transfers between devices: 73.4 us -> 42.8 us  [routed_branch(): slot_rows = lax.all_gather(from_x, 'ey', axis=0, tiled=False)]
    ppermute x8 -> x9, waiting for transfers between devices: 67.8 us -> 82.9 us  [shifted(): return lax.ppermute(value, axis, pairs)]
    all_to_all x1 -> x2, waiting for transfers between devices: 1.54 us -> 15 us  [routed_branch(): lax.all_to_all(hidden, 'ey', split_axis=0, concat_axis=0, tiled=True)]
    unnamed x24 -> x36, local copies, waits for them, and re-layouts: 0.22 us -> 13 us
    all_to_all x1 -> x0, blocking collectives: 12 us -> none  [routed_branch(): lax.all_to_all(hidden, 'ey', split_axis=0, concat_axis=0, tiled=True)]
    dot_general x16 -> x8, matrix products: 18.7 us -> 8.15 us  [routed_branch(): jnp.dot(hidden_rel[d], down_all[d], preferred_element_type=jnp.float32)]
    ppermute x8 -> x9, starting transfers between devices: 32.1 us -> 40.6 us  [shifted(): return lax.ppermute(value, axis, pairs)]
    all_to_all x1 -> x2, starting transfers between devices: 5.26 us -> 12.1 us  [routed_branch(): lax.all_to_all(hidden, 'ey', split_axis=0, concat_axis=0, tiled=True)]
  transfers between devices with their start and end apart: 13 -> 15, of which waited for: 10 -> 11; matrix products, arithmetic and copies ran while one was open for 7% -> 9% of each run, Pallas kernels for 0% -> 0%
where the time goes in v6:
time: 342 us; the launch traced here: 339 us
  waiting for transfers between devices  162 us (47%)
  starting transfers between devices  61.2 us (18%)
  local copies, waits for them, and re-layouts  44.8 us (13%)
  matrix products  28.8 us (8%)
  blocking collectives  22.5 us (7%)
  between operations  13.9 us (4%)
  other arithmetic  6.03 us (2%)
    ppermute x9, waiting for transfers between devices, shifted(): return lax.ppermute(value, axis, pairs)  82.9 us
    all_gather x2, waiting for transfers between devices, routed_branch(): slot_rows = lax.all_gather(from_x, 'ey', axis=0, tiled=False)  42.8 us
    ppermute x9, starting transfers between devices, shifted(): return lax.ppermute(value, axis, pairs)  40.6 us
    all_to_all x2, blocking collectives, routed_branch(): lax.all_to_all(per_expert, 'ex', split_axis=0, concat_axis=0, tiled=True)  22.5 us
    all_to_all x2, waiting for transfers between devices, routed_branch(): lax.all_to_all(expert_out, 'ex', split_axis=0, concat_axis=0, tiled=True)  21 us
    all_to_all x2, waiting for transfers between devices, routed_branch(): lax.all_to_all(hidden, 'ey', split_axis=0, concat_axis=0, tiled=True)  15 us
    reshape x2, local copies, waits for them, and re-layouts, routed_branch(): flat_rows = slot_rows.reshape(-1, model_width)  14 us
    unnamed x36, local copies, waits for them, and re-layouts  13 us
  transfers between devices with their start and end apart: 15, of which 11 were waited for; matrix products, arithmetic and copies ran while one was open for 9% of the time, Pallas kernels for 0%

profile of v6, /device:TPU:1, one launch (start us, length us, event | category | flops | bytes accessed | tf_op | source)
XLA Modules:
  0.0 338.8 jit_solution(8867417654129103869)
XLA Ops:
  12.5 11.5 %all_to_all.30 = bf16[4,476,128]{2,1,0:T(8,128)(2,1)} all-to-all(bf16[4,476,128]{2,1,0:T(8,128)(2,1)S(1)} %reshape.215), channel_id=1, replica_groups=mesh['pipe'=16,'ex'=4,'ey'=8] {'ex'}, dimensions={0} | all-to-all | bytes 974848 | tf_op jit(solution)/shard_map/all_to_all | solution.py:59
  24.0 4.7 %collective-permute-start.3 = (bf16[128,3584]{1,0:T(8,128)(2,1)}, bf16[128,3584]{1,0:T(8,128)(2,1)S(1)}, u32[]{:S(2)}, u32[]{:S(2)}) collective-permute-start(bf16[128,3584]{1,0:T(8,128)(2,1)} %bitcast.103), channel_id=1, source_target_pairs={{0,1},{1,2},{2,3},{3,4},{4,5},{5,6},{6,7},{7,0},{8,9},{9,10},{10,1... | collective-permute-start | bytes 2752520 | tf_op jit(solution)/shard_map/ppermute | solution.py:19
  32.5 14.3 %collective-permute-done.3 = bf16[128,3584]{1,0:T(8,128)(2,1)S(1)} collective-permute-done((bf16[128,3584]{1,0:T(8,128)(2,1)}, bf16[128,3584]{1,0:T(8,128)(2,1)S(1)}, u32[]{:S(2)}, u32[]{:S(2)}) %collective-permute-start.3) | collective-permute-done | bytes 917536 | tf_op jit(solution)/shard_map/ppermute | solution.py:19
  46.8 6.0 %collective-permute-start.4 = (bf16[128,3584]{1,0:T(8,128)(2,1)S(1)}, bf16[128,3584]{1,0:T(8,128)(2,1)S(1)}, u32[]{:S(2)}, u32[]{:S(2)}) collective-permute-start(bf16[128,3584]{1,0:T(8,128)(2,1)S(1)} %collective-permute-done.3), channel_id=1, source_target_pairs={{0,1},{1,2},{2,3},{3,4},{4,5},{5,6},{6,7},{7,0},{8,9},{9,10},{10,1... | collective-permute-start | bytes 2752520 | tf_op jit(solution)/shard_map/ppermute | solution.py:19
  52.8 4.4 %collective-permute-start.1 = (bf16[128,3584]{1,0:T(8,128)(2,1)S(1)}, bf16[128,3584]{1,0:T(8,128)(2,1)}, u32[]{:S(2)}, u32[]{:S(2)}) collective-permute-start(bf16[128,3584]{1,0:T(8,128)(2,1)S(1)} %collective-permute-done), channel_id=1, source_target_pairs={{0,7},{1,0},{2,1},{3,2},{4,3},{5,4},{6,5},{7,6},{8,15},{9,8},{10,9... | collective-permute-start | bytes 2752520 | tf_op jit(solution)/shard_map/ppermute | solution.py:19
  57.2 36.3 %collective-permute-done.4 = bf16[128,3584]{1,0:T(8,128)(2,1)S(1)} collective-permute-done((bf16[128,3584]{1,0:T(8,128)(2,1)S(1)}, bf16[128,3584]{1,0:T(8,128)(2,1)S(1)}, u32[]{:S(2)}, u32[]{:S(2)}) %collective-permute-start.4) | collective-permute-done | bytes 917536 | tf_op jit(solution)/shard_map/ppermute | solution.py:19
  96.1 4.1 %collective-permute-start.2 = (bf16[128,3584]{1,0:T(8,128)(2,1)}, bf16[128,3584]{1,0:T(8,128)(2,1)S(1)}, u32[]{:S(2)}, u32[]{:S(2)}) collective-permute-start(bf16[128,3584]{1,0:T(8,128)(2,1)} %collective-permute-done.1), channel_id=1, source_target_pairs={{0,7},{1,0},{2,1},{3,2},{4,3},{5,4},{6,5},{7,6},{8,15},{9,8},{10,9... | collective-permute-start | bytes 2752520 | tf_op jit(solution)/shard_map/ppermute | solution.py:19
  100.2 22.9 %collective-permute-done.5 = bf16[128,3584]{1,0:T(8,128)(2,1)S(1)} collective-permute-done((bf16[128,3584]{1,0:T(8,128)(2,1)S(1)}, bf16[128,3584]{1,0:T(8,128)(2,1)S(1)}, u32[]{:S(2)}, u32[]{:S(2)}) %collective-permute-start.5) | collective-permute-done | bytes 917536 | tf_op jit(solution)/shard_map/ppermute | solution.py:19
  127.2 4.4 %collective-permute-start.7 = (bf16[64,3584]{1,0:T(8,128)(2,1)}, bf16[64,3584]{1,0:T(8,128)(2,1)S(1)}, u32[]{:S(2)}, u32[]{:S(2)}) collective-permute-start(bf16[64,3584]{1,0:T(8,128)(2,1)} %slice.70), channel_id=1, source_target_pairs={{0,7},{1,0},{2,1},{3,2},{4,3},{5,4},{6,5},{7,6},{8,15},{9,8},{10,9... | collective-permute-start | bytes 1376264 | tf_op jit(solution)/shard_map/ppermute | solution.py:19
  136.0 7.0 %reshape.216 = bf16[544,3584]{1,0:T(8,128)(2,1)} reshape(bf16[32,476,128]{2,1,0:T(8,128)(2,1)} %all-gather.5.cloned.1.call-done) | data formatting | bytes 7798784 | tf_op jit(solution)/shard_map/reshape | solution.py:62
  150.5 7.9 %all-to-all-start.1 = ((bf16[8,68,128]{2,1,0:T(8,128)(2,1)}), bf16[8,68,128]{2,1,0:T(8,128)(2,1)S(1)}, u32[]{:S(2)}, u32[]{:S(2)}) async-start(bf16[8,68,128]{2,1,0:T(8,128)(2,1)} %reshape.217), calls=%async_computation.1 | async-start | bytes 294912 | tf_op jit(solution)/shard_map/all_to_all | solution.py:67
  158.5 8.0 %all-to-all-done.1 = bf16[8,68,128]{2,1,0:T(8,128)(2,1)S(1)} async-done(((bf16[8,68,128]{2,1,0:T(8,128)(2,1)}), bf16[8,68,128]{2,1,0:T(8,128)(2,1)S(1)}, u32[]{:S(2)}, u32[]{:S(2)}) %all-to-all-start.1) | async-done | bytes 139296 | tf_op jit(solution)/shard_map/all_to_all | solution.py:67
  177.8 4.2 %all-to-all-start.2 = ((f32[4,476,128]{2,1,0:T(8,128)}), f32[4,476,128]{2,1,0:T(8,128)}, u32[]{:S(2)}, u32[]{:S(2)}) async-start(f32[4,476,128]{2,1,0:T(8,128)} %reshape.218), calls=%async_computation.2 | async-start | bytes 1966080 | tf_op jit(solution)/shard_map/all_to_all | solution.py:80
  182.1 9.3 %all-to-all-done.2 = f32[4,476,128]{2,1,0:T(8,128)} async-done(((f32[4,476,128]{2,1,0:T(8,128)}), f32[4,476,128]{2,1,0:T(8,128)}, u32[]{:S(2)}, u32[]{:S(2)}) %all-to-all-start.2) | async-done | bytes 974880 | tf_op jit(solution)/shard_map/all_to_all | solution.py:80
  196.1 9.0 %collective-permute-start.8 = (bf16[64,3584]{1,0:T(8,128)(2,1)S(1)}, bf16[64,3584]{1,0:T(8,128)(2,1)S(1)}, u32[]{:S(2)}, u32[]{:S(2)}) collective-permute-start(bf16[64,3584]{1,0:T(8,128)(2,1)S(1)} %fusion.24), channel_id=1, source_target_pairs={{0,32},{32,64},{64,96},{96,128},{128,160},{160,192},{192,224},{224... | collective-permute-start | bytes 1376264 | tf_op jit(solution)/shard_map/ppermute | solution.py:19
  205.1 5.4 %collective-permute-done.8 = bf16[64,3584]{1,0:T(8,128)(2,1)S(1)} collective-permute-done((bf16[64,3584]{1,0:T(8,128)(2,1)S(1)}, bf16[64,3584]{1,0:T(8,128)(2,1)S(1)}, u32[]{:S(2)}, u32[]{:S(2)}) %collective-permute-start.8) | collective-permute-done | bytes 458784 | tf_op jit(solution)/shard_map/ppermute | solution.py:19
  214.4 11.0 %all_to_all.31 = bf16[4,476,128]{2,1,0:T(8,128)(2,1)} all-to-all(bf16[4,476,128]{2,1,0:T(8,128)(2,1)} %reshape.220), channel_id=1, replica_groups=mesh['pipe'=16,'ex'=4,'ey'=8] {'ex'}, dimensions={0} | all-to-all | bytes 974848 | tf_op jit(solution)/shard_map/all_to_all | solution.py:59
  237.3 42.7 %all-gather.7.cloned.1.call-done = bf16[32,476,128]{2,1,0:T(8,128)(2,1)} async-done(((bf16[4,476,128]{2,1,0:T(8,128)(2,1)}), bf16[32,476,128]{2,1,0:T(8,128)(2,1)}) %all-gather.7.cloned.1.call-update) | async-done | bytes 3899408 | tf_op jit(solution)/shard_map/all_gather | solution.py:60
  280.0 7.0 %reshape.221 = bf16[544,3584]{1,0:T(8,128)(2,1)} reshape(bf16[32,476,128]{2,1,0:T(8,128)(2,1)} %all-gather.7.cloned.1.call-done) | data formatting | bytes 7798784 | tf_op jit(solution)/shard_map/reshape | solution.py:62
  294.6 4.2 %all-to-all-start.4 = ((bf16[8,68,128]{2,1,0:T(8,128)(2,1)}), bf16[8,68,128]{2,1,0:T(8,128)(2,1)S(1)}, u32[]{:S(2)}, u32[]{:S(2)}) async-start(bf16[8,68,128]{2,1,0:T(8,128)(2,1)} %reshape.222), calls=%async_computation.4 | async-start | bytes 294912 | tf_op jit(solution)/shard_map/all_to_all | solution.py:67
  299.8 6.9 %all-to-all-done.4 = bf16[8,68,128]{2,1,0:T(8,128)(2,1)S(1)} async-done(((bf16[8,68,128]{2,1,0:T(8,128)(2,1)}), bf16[8,68,128]{2,1,0:T(8,128)(2,1)S(1)}, u32[]{:S(2)}, u32[]{:S(2)}) %all-to-all-start.4) | async-done | bytes 139296 | tf_op jit(solution)/shard_map/all_to_all | solution.py:67
  307.3 4.4 %convert_reduce_fusion = f32[68,3584]{1,0:T(8,128)S(1)} fusion(bf16[8,128,3584]{2,1,0:T(8,128)(2,1)} %bitcast_dynamic-update-slice_fusion, bf16[8,68,128]{2,1,0:T(8,128)(2,1)S(1)} %gather_fusion.3, pred[8]{0:T(512)(128)(4,1)S(1)} %compare_and_fusion), kind=kOutput, calls=%fused_computation.4 | convolution fusion | flops 504797184 | bytes 8454152 | tf_op jit(solution)/shard_map/jrh,jhd->jrd/dot_general | solution.py:77
  312.8 4.2 %all-to-all-start.5 = ((f32[4,476,128]{2,1,0:T(8,128)}), f32[4,476,128]{2,1,0:T(8,128)}, u32[]{:S(2)}, u32[]{:S(2)}) async-start(f32[4,476,128]{2,1,0:T(8,128)} %reshape.223), calls=%async_computation.5 | async-start | bytes 1966080 | tf_op jit(solution)/shard_map/all_to_all | solution.py:80
  317.0 11.7 %all-to-all-done.5 = f32[4,476,128]{2,1,0:T(8,128)} async-done(((f32[4,476,128]{2,1,0:T(8,128)}), f32[4,476,128]{2,1,0:T(8,128)}, u32[]{:S(2)}, u32[]{:S(2)}) %all-to-all-start.5) | async-done | bytes 974880 | tf_op jit(solution)/shard_map/all_to_all | solution.py:80
  (101 shorter events, 73.2 us)
Async XLA Ops:
  6.5 136.5 %copy-start = (bf16[1,1,3584,128]{3,2,1,0:T(8,128)(2,1)S(1)}, bf16[1,1,3584,128]{3,2,1,0:T(8,128)(2,1)}, u32[]{:S(2)}) copy-start(bf16[1,1,3584,128]{3,2,1,0:T(8,128)(2,1)} %param.11) | copy-start | bytes 2752516
  6.5 129.5 %all-gather.5.cloned.1.call-start = ((), (), s32[]{:S(2)}) async-start(), calls=%async_computation.6 | async-start | bytes 4423680 | tf_op jit(solution)/shard_map/all_gather | solution.py:60
  24.0 22.7 %collective-permute-start.3 = (bf16[128,3584]{1,0:T(8,128)(2,1)}, bf16[128,3584]{1,0:T(8,128)(2,1)S(1)}, u32[]{:S(2)}, u32[]{:S(2)}) collective-permute-start(bf16[128,3584]{1,0:T(8,128)(2,1)} %bitcast.103), channel_id=1, source_target_pairs={{0,1},{1,2},{2,3},{3,4},{4,5},{5,6},{6,7},{7,0},{8,9},{9,10},{10,1... | collective-permute-start | bytes 2752520 | tf_op jit(solution)/shard_map/ppermute | solution.py:19
  28.7 24.1 %collective-permute-start = (bf16[128,3584]{1,0:T(8,128)(2,1)}, bf16[128,3584]{1,0:T(8,128)(2,1)S(1)}, u32[]{:S(2)}, u32[]{:S(2)}) collective-permute-start(bf16[128,3584]{1,0:T(8,128)(2,1)} %bitcast.104), channel_id=1, source_target_pairs={{0,7},{1,0},{2,1},{3,2},{4,3},{5,4},{6,5},{7,6},{8,15},{9,8},{10,9... | collective-permute-start | bytes 2752520 | tf_op jit(solution)/shard_map/ppermute | solution.py:19
  46.8 49.3 %copy-start.6 = (bf16[128,3584]{1,0:T(8,128)(2,1)}, bf16[128,3584]{1,0:T(8,128)(2,1)S(1)}, u32[]{:S(2)}) copy-start(bf16[128,3584]{1,0:T(8,128)(2,1)S(1)} %collective-permute-done.3) | copy-start | bytes 2752516
  46.8 46.8 %collective-permute-start.4 = (bf16[128,3584]{1,0:T(8,128)(2,1)S(1)}, bf16[128,3584]{1,0:T(8,128)(2,1)S(1)}, u32[]{:S(2)}, u32[]{:S(2)}) collective-permute-start(bf16[128,3584]{1,0:T(8,128)(2,1)S(1)} %collective-permute-done.3), channel_id=1, source_target_pairs={{0,1},{1,2},{2,3},{3,4},{4,5},{5,6},{6,7},{7,0},{8,9},{9,10},{10,1... | collective-permute-start | bytes 2752520 | tf_op jit(solution)/shard_map/ppermute | solution.py:19
  52.8 47.4 %copy-start.10 = (bf16[128,3584]{1,0:T(8,128)(2,1)}, bf16[128,3584]{1,0:T(8,128)(2,1)S(1)}, u32[]{:S(2)}) copy-start(bf16[128,3584]{1,0:T(8,128)(2,1)S(1)} %collective-permute-done) | copy-start | bytes 2752516
  52.8 43.3 %collective-permute-start.1 = (bf16[128,3584]{1,0:T(8,128)(2,1)S(1)}, bf16[128,3584]{1,0:T(8,128)(2,1)}, u32[]{:S(2)}, u32[]{:S(2)}) collective-permute-start(bf16[128,3584]{1,0:T(8,128)(2,1)S(1)} %collective-permute-done), channel_id=1, source_target_pairs={{0,7},{1,0},{2,1},{3,2},{4,3},{5,4},{6,5},{7,6},{8,15},{9,8},{10,9... | collective-permute-start | bytes 2752520 | tf_op jit(solution)/shard_map/ppermute | solution.py:19
  93.6 29.6 %collective-permute-start.5 = (bf16[128,3584]{1,0:T(8,128)(2,1)S(1)}, bf16[128,3584]{1,0:T(8,128)(2,1)S(1)}, u32[]{:S(2)}, u32[]{:S(2)}) collective-permute-start(bf16[128,3584]{1,0:T(8,128)(2,1)S(1)} %collective-permute-done.4), channel_id=1, source_target_pairs={{0,1},{1,2},{2,3},{3,4},{4,5},{5,6},{6,7},{7,0},{8,9},{9,10},{10,1... | collective-permute-start | bytes 2752520 | tf_op jit(solution)/shard_map/ppermute | solution.py:19
  96.1 30.2 %collective-permute-start.2 = (bf16[128,3584]{1,0:T(8,128)(2,1)}, bf16[128,3584]{1,0:T(8,128)(2,1)S(1)}, u32[]{:S(2)}, u32[]{:S(2)}) collective-permute-start(bf16[128,3584]{1,0:T(8,128)(2,1)} %collective-permute-done.1), channel_id=1, source_target_pairs={{0,7},{1,0},{2,1},{3,2},{4,3},{5,4},{6,5},{7,6},{8,15},{9,8},{10,9... | collective-permute-start | bytes 2752520 | tf_op jit(solution)/shard_map/ppermute | solution.py:19
  124.0 10.9 %collective-permute-start.6 = (bf16[64,3584]{1,0:T(8,128)(2,1)}, bf16[64,3584]{1,0:T(8,128)(2,1)}, u32[]{:S(2)}, u32[]{:S(2)}) collective-permute-start(bf16[64,3584]{1,0:T(8,128)(2,1)} %slice.69), channel_id=1, source_target_pairs={{0,1},{1,2},{2,3},{3,4},{4,5},{5,6},{6,7},{7,0},{8,9},{9,10},{10,1... | collective-permute-start | bytes 1376264 | tf_op jit(solution)/shard_map/ppermute | solution.py:19
  127.2 31.2 %collective-permute-start.7 = (bf16[64,3584]{1,0:T(8,128)(2,1)}, bf16[64,3584]{1,0:T(8,128)(2,1)S(1)}, u32[]{:S(2)}, u32[]{:S(2)}) collective-permute-start(bf16[64,3584]{1,0:T(8,128)(2,1)} %slice.70), channel_id=1, source_target_pairs={{0,7},{1,0},{2,1},{3,2},{4,3},{5,4},{6,5},{7,6},{8,15},{9,8},{10,9... | collective-permute-start | bytes 1376264 | tf_op jit(solution)/shard_map/ppermute | solution.py:19
  150.5 16.0 %all-to-all-start.1 = ((bf16[8,68,128]{2,1,0:T(8,128)(2,1)}), bf16[8,68,128]{2,1,0:T(8,128)(2,1)S(1)}, u32[]{:S(2)}, u32[]{:S(2)}) async-start(bf16[8,68,128]{2,1,0:T(8,128)(2,1)} %reshape.217), calls=%async_computation.1 | async-start | bytes 294912 | tf_op jit(solution)/shard_map/all_to_all | solution.py:67
  158.5 15.6 %copy-start.1 = (bf16[128,3584]{1,0:T(8,128)(2,1)}, bf16[128,3584]{1,0:T(8,128)(2,1)S(1)}, u32[]{:S(2)}) copy-start(bf16[128,3584]{1,0:T(8,128)(2,1)S(1)} %constant_dynamic-update-slice_fusion) | copy-start | bytes 2752516
  172.5 9.6 %copy-start.13 = (s32[1,2,64,1]{2,3,1,0:T(1,128)S(1)}, s32[1,2,64,1]{2,3,1,0:T(1,128)}, u32[]{:S(2)}) copy-start(s32[1,2,64,1]{2,3,1,0:T(1,128)} %param.15) | copy-start | bytes 1540
  175.4 19.2 %copy-start.5 = (bf16[1,64,3584]{2,1,0:T(8,128)(2,1)S(1)}, bf16[1,64,3584]{2,1,0:T(8,128)(2,1)}, u32[]{:S(2)}) copy-start(bf16[1,64,3584]{2,1,0:T(8,128)(2,1)} %param.9) | copy-start | bytes 1376260
  177.8 13.7 %all-to-all-start.2 = ((f32[4,476,128]{2,1,0:T(8,128)}), f32[4,476,128]{2,1,0:T(8,128)}, u32[]{:S(2)}, u32[]{:S(2)}) async-start(f32[4,476,128]{2,1,0:T(8,128)} %reshape.218), calls=%async_computation.2 | async-start | bytes 1966080 | tf_op jit(solution)/shard_map/all_to_all | solution.py:80
  182.0 98.0 %all-gather.7.cloned.1.call-start = ((), (), s32[]{:S(2)}) async-start(), calls=%async_computation.7 | async-start | bytes 4423680 | tf_op jit(solution)/shard_map/all_gather | solution.py:60
  194.6 39.6 %copy-start.2 = (bf16[128,3584]{1,0:T(8,128)(2,1)S(1)}, bf16[128,3584]{1,0:T(8,128)(2,1)}, u32[]{:S(2)}) copy-start(bf16[128,3584]{1,0:T(8,128)(2,1)} %copy-done.1) | copy-start | bytes 2752516
  196.1 14.4 %collective-permute-start.8 = (bf16[64,3584]{1,0:T(8,128)(2,1)S(1)}, bf16[64,3584]{1,0:T(8,128)(2,1)S(1)}, u32[]{:S(2)}, u32[]{:S(2)}) collective-permute-start(bf16[64,3584]{1,0:T(8,128)(2,1)S(1)} %fusion.24), channel_id=1, source_target_pairs={{0,32},{32,64},{64,96},{96,128},{128,160},{160,192},{192,224},{224... | collective-permute-start | bytes 1376264 | tf_op jit(solution)/shard_map/ppermute | solution.py:19
  225.4 10.9 %copy-start.9 = (bf16[128,3584]{1,0:T(8,128)(2,1)S(1)}, bf16[128,3584]{1,0:T(8,128)(2,1)}, u32[]{:S(2)}) copy-start(bf16[128,3584]{1,0:T(8,128)(2,1)} %copy-done.8) | copy-start | bytes 2752516
  287.0 11.8 %copy-start.7 = (bf16[128,3584]{1,0:T(8,128)(2,1)S(1)}, bf16[128,3584]{1,0:T(8,128)(2,1)}, u32[]{:S(2)}) copy-start(bf16[128,3584]{1,0:T(8,128)(2,1)} %copy-done.6) | copy-start | bytes 2752516
  294.6 12.1 %all-to-all-start.4 = ((bf16[8,68,128]{2,1,0:T(8,128)(2,1)}), bf16[8,68,128]{2,1,0:T(8,128)(2,1)S(1)}, u32[]{:S(2)}, u32[]{:S(2)}) async-start(bf16[8,68,128]{2,1,0:T(8,128)(2,1)} %reshape.222), calls=%async_computation.4 | async-start | bytes 294912 | tf_op jit(solution)/shard_map/all_to_all | solution.py:67
  312.8 15.9 %all-to-all-start.5 = ((f32[4,476,128]{2,1,0:T(8,128)}), f32[4,476,128]{2,1,0:T(8,128)}, u32[]{:S(2)}, u32[]{:S(2)}) async-start(f32[4,476,128]{2,1,0:T(8,128)} %reshape.223), calls=%async_computation.5 | async-start | bytes 1966080 | tf_op jit(solution)/shard_map/all_to_all | solution.py:80
  (5 other events, 32.0 us)
Sparse Core Ops, SparseCore 0:
  24.2 88.1 all-gather.4
  225.5 54.4 all-gather.6

commit v7 on v5

--- a/solution.py
+++ b/solution.py
@@ -19,11 +19,16 @@
     return lax.ppermute(value, axis, pairs)
 
 
-def ring_gather(value, axis):
+def ring_gather(value, axis, first_hop=None):
     count = lax.axis_size(axis)
     ahead, behind = {0: value}, {}
     forward, backward = value, value
-    for step in range(1, count // 2 + 1):
+    start = 1
+    if first_hop is not None:
+        forward, backward = first_hop
+        behind[1], ahead[1] = forward, backward
+        start = 2
+    for step in range(start, count // 2 + 1):
         forward = shifted(forward, axis, 1)
         behind[step] = forward
         if step < count - step:
@@ -46,12 +51,14 @@
     return jnp.dot(placing, normed, preferred_element_type=jnp.float32).astype(jnp.bfloat16)
 
 
-def routed_branch(normed, expert_ids, route_weight, w_gate, w_up, down_all):
+def routed_branch(normed, expert_ids, route_weight, w_gate, w_up, down_all, before_x=None):
     n_x = lax.axis_size("ex")
     model_width = normed.shape[1]
     slot_ids = slot_index(expert_ids, MOST, EXPERTS)
     block_rows = MOST * model_width // LANE
     per_expert = place_rows(normed, slot_ids, EXPERTS * MOST).reshape(EXPERTS, block_rows, LANE)
+    if before_x is not None:
+        per_expert, down_all = before_x(per_expert)
     from_x = lax.all_to_all(per_expert, "ex", split_axis=0, concat_axis=0, tiled=True)
     slot_rows = lax.all_gather(from_x, "ey", axis=0, tiled=False)
     n_y = slot_rows.shape[0]
@@ -75,11 +82,11 @@
     return jnp.sum(weights[:, :, None] * picked, axis=1)
 
 
-def layer_terms(rows_in, gain_row, w_gate, w_up, down_all, expert_ids, route_weight):
+def layer_terms(rows_in, gain_row, w_gate, w_up, down_all, expert_ids, route_weight, before_x=None):
     values = rows_in.astype(jnp.float32)
     inv_rms = lax.rsqrt(jnp.mean(values * values, axis=1, keepdims=True) + NORM_EPS)
     normed = (values * inv_rms * gain_row.astype(jnp.float32)).astype(jnp.bfloat16)
-    branch = routed_branch(normed, expert_ids, route_weight, w_gate, w_up, down_all)
+    branch = routed_branch(normed, expert_ids, route_weight, w_gate, w_up, down_all, before_x)
     return (values, branch)
 
 
@@ -89,10 +96,19 @@
     gain_row = norm_gain[0]
     w_gate = gate_w[0, 0]
     w_up = up_w[0, 0]
-    down_all = ring_gather(down_w[0, 0], "ey")
+    own_down = down_w[0, 0]
+    first_hop = (shifted(own_down, "ey", 1), shifted(own_down, "ey", -1))
+    gathered = []
+
+    def before_x(per_expert):
+        per_expert, hop = lax.optimization_barrier((per_expert, first_hop))
+        gathered.append(ring_gather(own_down, "ey", hop))
+        return per_expert, gathered[0]
+
     values, branch = layer_terms(
-        rows_in, gain_row, w_gate, w_up, down_all, route_ids[0, 0], route_wts[0, 0]
+        rows_in, gain_row, w_gate, w_up, None, route_ids[0, 0], route_wts[0, 0], before_x
     )
+    down_all = gathered[0]
     first_out = (values + branch).astype(jnp.bfloat16)
     arrived = shifted(first_out, "pipe", 1)
     values, branch = layer_terms(

time: 320 us -> 338 us (1.056)
  waiting for transfers between devices: 166 us -> 181 us
  blocking collectives: 33.4 us -> 36.8 us
    all_gather x2, waiting for transfers between devices: 73.4 us -> 114 us  [routed_branch(): slot_rows = lax.all_gather(from_x, 'ey', axis=0, tiled=False)]
    ppermute x8, waiting for transfers between devices: 67.8 us -> 41.8 us  [shifted(): return lax.ppermute(value, axis, pairs)]
    all_to_all x2, blocking collectives: 21.4 us -> 24.8 us  [routed_branch(): lax.all_to_all(per_expert, 'ex', split_axis=0, concat_axis=0, tiled=True)]
  transfers between devices with their start and end apart: 13 -> 13, of which waited for: 10 -> 11; matrix products, arithmetic and copies ran while one was open for 7% -> 8% of each run, Pallas kernels for 0% -> 0%
where the time goes in v7:
time: 338 us; the launch traced here: 335 us
  waiting for transfers between devices  181 us (54%)
  starting transfers between devices  43.6 us (13%)
  blocking collectives  36.8 us (11%)
  matrix products  29.7 us (9%)
  local copies, waits for them, and re-layouts  23.9 us (7%)
  between operations  13.8 us (4%)
  other arithmetic  5.96 us (2%)
    all_gather x2, waiting for transfers between devices, routed_branch(): slot_rows = lax.all_gather(from_x, 'ey', axis=0, tiled=False)  114 us
    ppermute x8, waiting for transfers between devices, shifted(): return lax.ppermute(value, axis, pairs)  41.8 us
    ppermute x8, starting transfers between devices, shifted(): return lax.ppermute(value, axis, pairs)  30.3 us
    all_to_all x2, blocking collectives, routed_branch(): lax.all_to_all(per_expert, 'ex', split_axis=0, concat_axis=0, tiled=True)  24.8 us
    all_to_all x2, waiting for transfers between devices, routed_branch(): lax.all_to_all(expert_out, 'ex', split_axis=0, concat_axis=0, tiled=True)  23.2 us
    dot_general x16, matrix products, routed_branch(): jnp.dot(hidden_rel[d], down_all[d], preferred_element_type=jnp.float32)  18.7 us
    reshape x2, local copies, waits for them, and re-layouts, routed_branch(): flat_rows = slot_rows.reshape(-1, model_width)  14 us
    all_to_all x1, blocking collectives, routed_branch(): lax.all_to_all(hidden, 'ey', split_axis=0, concat_axis=0, tiled=True)  12 us
  transfers between devices with their start and end apart: 13, of which 11 were waited for; matrix products, arithmetic and copies ran while one was open for 8% of the time, Pallas kernels for 0%

profile of v7, /device:TPU:1, one launch (start us, length us, event | category | flops | bytes accessed | tf_op | source)
XLA Modules:
  0.0 334.7 jit_solution(17799710969892143118)
XLA Ops:
  6.5 4.2 %collective-permute-start = (bf16[128,3584]{1,0:T(8,128)(2,1)}, bf16[128,3584]{1,0:T(8,128)(2,1)S(1)}, u32[]{:S(2)}, u32[]{:S(2)}) collective-permute-start(bf16[128,3584]{1,0:T(8,128)(2,1)} %bitcast.119), channel_id=1, source_target_pairs={{0,1},{1,2},{2,3},{3,4},{4,5},{5,6},{6,7},{7,0},{8,9},{9,10},{10,1... | collective-permute-start | bytes 2752520 | tf_op jit(solution)/shard_map/ppermute | solution.py:19
  10.7 3.8 %collective-permute-start.1 = (bf16[128,3584]{1,0:T(8,128)(2,1)}, bf16[128,3584]{1,0:T(8,128)(2,1)S(1)}, u32[]{:S(2)}, u32[]{:S(2)}) collective-permute-start(bf16[128,3584]{1,0:T(8,128)(2,1)} %bitcast.120), channel_id=1, source_target_pairs={{0,7},{1,0},{2,1},{3,2},{4,3},{5,4},{6,5},{7,6},{8,15},{9,8},{10,9... | collective-permute-start | bytes 2752520 | tf_op jit(solution)/shard_map/ppermute | solution.py:19
  21.2 6.4 %collective-permute-done = bf16[128,3584]{1,0:T(8,128)(2,1)S(1)} collective-permute-done((bf16[128,3584]{1,0:T(8,128)(2,1)}, bf16[128,3584]{1,0:T(8,128)(2,1)S(1)}, u32[]{:S(2)}, u32[]{:S(2)}) %collective-permute-start) | collective-permute-done | bytes 917536 | tf_op jit(solution)/shard_map/ppermute | solution.py:19
  29.9 14.9 %all_to_all.30 = bf16[4,476,128]{2,1,0:T(8,128)(2,1)} all-to-all(bf16[4,476,128]{2,1,0:T(8,128)(2,1)} %reshape.215), channel_id=1, replica_groups=mesh['pipe'=16,'ex'=4,'ey'=8] {'ex'}, dimensions={0} | all-to-all | bytes 974848 | tf_op jit(solution)/shard_map/all_to_all | solution.py:62
  44.8 3.1 collective-permute-start.4
  47.9 4.2 %collective-permute-start.2 = (bf16[128,3584]{1,0:T(8,128)(2,1)S(1)}, bf16[128,3584]{1,0:T(8,128)(2,1)}, u32[]{:S(2)}, u32[]{:S(2)}) collective-permute-start(bf16[128,3584]{1,0:T(8,128)(2,1)S(1)} %collective-permute-done.1), channel_id=1, source_target_pairs={{0,7},{1,0},{2,1},{3,2},{4,3},{5,4},{6,5},{7,6},{8,15},{9,8},{10,9... | collective-permute-start | bytes 2752520 | tf_op jit(solution)/shard_map/ppermute | solution.py:19
  52.2 15.8 %collective-permute-done.4 = bf16[128,3584]{1,0:T(8,128)(2,1)} collective-permute-done((bf16[128,3584]{1,0:T(8,128)(2,1)S(1)}, bf16[128,3584]{1,0:T(8,128)(2,1)}, u32[]{:S(2)}, u32[]{:S(2)}) %collective-permute-start.4) | collective-permute-done | bytes 917536 | tf_op jit(solution)/shard_map/ppermute | solution.py:19
  71.0 57.2 %all-gather.5.cloned.1.call-done = bf16[32,476,128]{2,1,0:T(8,128)(2,1)} async-done(((bf16[4,476,128]{2,1,0:T(8,128)(2,1)}), bf16[32,476,128]{2,1,0:T(8,128)(2,1)}) %all-gather.5.cloned.1.call-update) | async-done | bytes 3899408 | tf_op jit(solution)/shard_map/all_gather | solution.py:63
  128.2 7.0 %reshape.216 = bf16[544,3584]{1,0:T(8,128)(2,1)} reshape(bf16[32,476,128]{2,1,0:T(8,128)(2,1)} %all-gather.5.cloned.1.call-done) | data formatting | bytes 7798784 | tf_op jit(solution)/shard_map/reshape | solution.py:65
  135.3 3.4 %fusion.44 = f32[544,128]{1,0:T(8,128)S(1)} fusion(bf16[544,3584]{1,0:T(8,128)(2,1)} %reshape.216, bf16[1,1,3584,128]{3,2,1,0:T(8,128)(2,1)S(1)} %copy-done), kind=kOutput, calls=%fused_computation.74 | convolution fusion | flops 499122176 | bytes 5095424 | tf_op jit(solution)/shard_map/dot_general | solution.py:66
  140.6 5.8 %all-to-all-start.1 = ((bf16[8,68,128]{2,1,0:T(8,128)(2,1)}), bf16[8,68,128]{2,1,0:T(8,128)(2,1)S(1)}, u32[]{:S(2)}, u32[]{:S(2)}) async-start(bf16[8,68,128]{2,1,0:T(8,128)(2,1)} %reshape.217), calls=%async_computation.1 | async-start | bytes 294912 | tf_op jit(solution)/shard_map/all_to_all | solution.py:70
  146.5 4.6 %collective-permute-start.3 = (bf16[128,3584]{1,0:T(8,128)(2,1)}, bf16[128,3584]{1,0:T(8,128)(2,1)}, u32[]{:S(2)}, u32[]{:S(2)}) collective-permute-start(bf16[128,3584]{1,0:T(8,128)(2,1)} %collective-permute-done.2), channel_id=1, source_target_pairs={{0,7},{1,0},{2,1},{3,2},{4,3},{5,4},{6,5},{7,6},{8,15},{9,8},{10,9... | collective-permute-start | bytes 2752520 | tf_op jit(solution)/shard_map/ppermute | solution.py:19
  161.7 10.6 %collective-permute-done.3 = bf16[128,3584]{1,0:T(8,128)(2,1)} collective-permute-done((bf16[128,3584]{1,0:T(8,128)(2,1)}, bf16[128,3584]{1,0:T(8,128)(2,1)}, u32[]{:S(2)}, u32[]{:S(2)}) %collective-permute-start.3) | collective-permute-done | bytes 917536 | tf_op jit(solution)/shard_map/ppermute | solution.py:19
  177.6 3.5 %all-to-all-start.2 = ((f32[4,476,128]{2,1,0:T(8,128)}), f32[4,476,128]{2,1,0:T(8,128)S(1)}, u32[]{:S(2)}, u32[]{:S(2)}) async-start(f32[4,476,128]{2,1,0:T(8,128)} %reshape.218), calls=%async_computation.2 | async-start | bytes 1966080 | tf_op jit(solution)/shard_map/all_to_all | solution.py:79
  181.3 11.8 %all-to-all-done.2 = f32[4,476,128]{2,1,0:T(8,128)S(1)} async-done(((f32[4,476,128]{2,1,0:T(8,128)}), f32[4,476,128]{2,1,0:T(8,128)S(1)}, u32[]{:S(2)}, u32[]{:S(2)}) %all-to-all-start.2) | async-done | bytes 974880 | tf_op jit(solution)/shard_map/all_to_all | solution.py:79
  196.3 5.4 %collective-permute-start.7 = (bf16[64,3584]{1,0:T(8,128)(2,1)S(1)}, bf16[64,3584]{1,0:T(8,128)(2,1)S(1)}, u32[]{:S(2)}, u32[]{:S(2)}) collective-permute-start(bf16[64,3584]{1,0:T(8,128)(2,1)S(1)} %fusion.39), channel_id=1, source_target_pairs={{0,32},{32,64},{64,96},{96,128},{128,160},{160,192},{192,224},{224... | collective-permute-start | bytes 1376264 | tf_op jit(solution)/shard_map/ppermute | solution.py:19
  201.8 5.4 %collective-permute-done.7 = bf16[64,3584]{1,0:T(8,128)(2,1)S(1)} collective-permute-done((bf16[64,3584]{1,0:T(8,128)(2,1)S(1)}, bf16[64,3584]{1,0:T(8,128)(2,1)S(1)}, u32[]{:S(2)}, u32[]{:S(2)}) %collective-permute-start.7) | collective-permute-done | bytes 458784 | tf_op jit(solution)/shard_map/ppermute | solution.py:19
  208.4 9.8 %all_to_all.31 = bf16[4,476,128]{2,1,0:T(8,128)(2,1)} all-to-all(bf16[4,476,128]{2,1,0:T(8,128)(2,1)S(1)} %reshape.220), channel_id=1, replica_groups=mesh['pipe'=16,'ex'=4,'ey'=8] {'ex'}, dimensions={0} | all-to-all | bytes 974848 | tf_op jit(solution)/shard_map/all_to_all | solution.py:62
  218.3 57.2 %all-gather.7.cloned.1.call-done = bf16[32,476,128]{2,1,0:T(8,128)(2,1)} async-done(((bf16[4,476,128]{2,1,0:T(8,128)(2,1)}), bf16[32,476,128]{2,1,0:T(8,128)(2,1)}) %all-gather.7.cloned.1.call-update) | async-done | bytes 3899408 | tf_op jit(solution)/shard_map/all_gather | solution.py:63
  275.5 7.0 %reshape.221 = bf16[544,3584]{1,0:T(8,128)(2,1)} reshape(bf16[32,476,128]{2,1,0:T(8,128)(2,1)} %all-gather.7.cloned.1.call-done) | data formatting | bytes 7798784 | tf_op jit(solution)/shard_map/reshape | solution.py:65
  282.5 3.4 %fusion.42 = f32[544,128]{1,0:T(8,128)S(1)} fusion(bf16[544,3584]{1,0:T(8,128)(2,1)} %reshape.221, bf16[1,1,3584,128]{3,2,1,0:T(8,128)(2,1)S(1)} %copy-done), kind=kOutput, calls=%fused_computation.72 | convolution fusion | flops 499122176 | bytes 5095424 | tf_op jit(solution)/shard_map/dot_general | solution.py:66
  287.2 12.0 %all_to_all.32 = bf16[8,68,128]{2,1,0:T(8,128)(2,1)S(1)} all-to-all(bf16[8,68,128]{2,1,0:T(8,128)(2,1)S(1)} %reshape.222), channel_id=1, replica_groups=mesh['pipe'=16,'ex'=4,'ey'=8] {'ey'}, dimensions={0} | all-to-all | bytes 278528 | tf_op jit(solution)/shard_map/all_to_all | solution.py:70
  310.4 4.0 %all-to-all-start.5 = ((f32[4,476,128]{2,1,0:T(8,128)}), f32[4,476,128]{2,1,0:T(8,128)S(1)}, u32[]{:S(2)}, u32[]{:S(2)}) async-start(f32[4,476,128]{2,1,0:T(8,128)} %reshape.223), calls=%async_computation.5 | async-start | bytes 1966080 | tf_op jit(solution)/shard_map/all_to_all | solution.py:79
  314.4 11.4 %all-to-all-done.5 = f32[4,476,128]{2,1,0:T(8,128)S(1)} async-done(((f32[4,476,128]{2,1,0:T(8,128)}), f32[4,476,128]{2,1,0:T(8,128)S(1)}, u32[]{:S(2)}, u32[]{:S(2)}) %all-to-all-start.5) | async-done | bytes 974880 | tf_op jit(solution)/shard_map/all_to_all | solution.py:79
  (92 shorter events, 48.9 us)
Async XLA Ops:
  6.5 128.7 %copy-start = (bf16[1,1,3584,128]{3,2,1,0:T(8,128)(2,1)S(1)}, bf16[1,1,3584,128]{3,2,1,0:T(8,128)(2,1)}, u32[]{:S(2)}) copy-start(bf16[1,1,3584,128]{3,2,1,0:T(8,128)(2,1)} %param.11) | copy-start | bytes 2752516
  6.5 121.7 %all-gather.5.cloned.1.call-start = ((), (), s32[]{:S(2)}) async-start(), calls=%async_computation.6 | async-start | bytes 4423680 | tf_op jit(solution)/shard_map/all_gather | solution.py:63
  6.5 21.1 %collective-permute-start = (bf16[128,3584]{1,0:T(8,128)(2,1)}, bf16[128,3584]{1,0:T(8,128)(2,1)S(1)}, u32[]{:S(2)}, u32[]{:S(2)}) collective-permute-start(bf16[128,3584]{1,0:T(8,128)(2,1)} %bitcast.119), channel_id=1, source_target_pairs={{0,1},{1,2},{2,3},{3,4},{4,5},{5,6},{6,7},{7,0},{8,9},{9,10},{10,1... | collective-permute-start | bytes 2752520 | tf_op jit(solution)/shard_map/ppermute | solution.py:19
  10.7 19.2 %collective-permute-start.1 = (bf16[128,3584]{1,0:T(8,128)(2,1)}, bf16[128,3584]{1,0:T(8,128)(2,1)S(1)}, u32[]{:S(2)}, u32[]{:S(2)}) collective-permute-start(bf16[128,3584]{1,0:T(8,128)(2,1)} %bitcast.120), channel_id=1, source_target_pairs={{0,7},{1,0},{2,1},{3,2},{4,3},{5,4},{6,5},{7,6},{8,15},{9,8},{10,9... | collective-permute-start | bytes 2752520 | tf_op jit(solution)/shard_map/ppermute | solution.py:19
  27.7 107.6 %copy-start.8 = (bf16[128,3584]{1,0:T(8,128)(2,1)}, bf16[128,3584]{1,0:T(8,128)(2,1)S(1)}, u32[]{:S(2)}) copy-start(bf16[128,3584]{1,0:T(8,128)(2,1)S(1)} %collective-permute-done) | copy-start | bytes 2752516
  29.9 131.5 %copy-start.4 = (bf16[128,3584]{1,0:T(8,128)(2,1)}, bf16[128,3584]{1,0:T(8,128)(2,1)S(1)}, u32[]{:S(2)}) copy-start(bf16[128,3584]{1,0:T(8,128)(2,1)S(1)} %collective-permute-done.1) | copy-start | bytes 2752516
  44.8 23.1 %collective-permute-start.4 = (bf16[128,3584]{1,0:T(8,128)(2,1)S(1)}, bf16[128,3584]{1,0:T(8,128)(2,1)}, u32[]{:S(2)}, u32[]{:S(2)}) collective-permute-start(bf16[128,3584]{1,0:T(8,128)(2,1)S(1)} %collective-permute-done), channel_id=1, source_target_pairs={{0,1},{1,2},{2,3},{3,4},{4,5},{5,6},{6,7},{7,0},{8,9},{9,10},{10,1... | collective-permute-start | bytes 2752520 | tf_op jit(solution)/shard_map/ppermute | solution.py:19
  47.9 98.5 %collective-permute-start.2 = (bf16[128,3584]{1,0:T(8,128)(2,1)S(1)}, bf16[128,3584]{1,0:T(8,128)(2,1)}, u32[]{:S(2)}, u32[]{:S(2)}) collective-permute-start(bf16[128,3584]{1,0:T(8,128)(2,1)S(1)} %collective-permute-done.1), channel_id=1, source_target_pairs={{0,7},{1,0},{2,1},{3,2},{4,3},{5,4},{6,5},{7,6},{8,15},{9,8},{10,9... | collective-permute-start | bytes 2752520 | tf_op jit(solution)/shard_map/ppermute | solution.py:19
  68.0 83.1 %collective-permute-start.5 = (bf16[128,3584]{1,0:T(8,128)(2,1)}, bf16[128,3584]{1,0:T(8,128)(2,1)}, u32[]{:S(2)}, u32[]{:S(2)}) collective-permute-start(bf16[128,3584]{1,0:T(8,128)(2,1)} %collective-permute-done.4), channel_id=1, source_target_pairs={{0,1},{1,2},{2,3},{3,4},{4,5},{5,6},{6,7},{7,0},{8,9},{9,10},{10,1... | collective-permute-start | bytes 2752520 | tf_op jit(solution)/shard_map/ppermute | solution.py:19
  135.2 3.4 %copy-start.2 = (bf16[544,3584]{1,0:T(8,128)(2,1)S(1)}, bf16[544,3584]{1,0:T(8,128)(2,1)}, u32[]{:S(2)}) copy-start(bf16[544,3584]{1,0:T(8,128)(2,1)} %reshape.216) | copy-start | bytes 11698180
  135.2 3.5 %copy-start.11 = (bf16[1,1,3584,128]{3,2,1,0:T(8,128)(2,1)S(1)}, bf16[1,1,3584,128]{3,2,1,0:T(8,128)(2,1)}, u32[]{:S(2)}) copy-start(bf16[1,1,3584,128]{3,2,1,0:T(8,128)(2,1)} %param.12) | copy-start | bytes 2752516
  138.8 16.5 %copy-start.6 = (bf16[1,1,128,3584]{3,2,1,0:T(8,128)(2,1)S(1)}, bf16[1,1,128,3584]{3,2,1,0:T(8,128)(2,1)}, u32[]{:S(2)}) copy-start(bf16[1,1,128,3584]{3,2,1,0:T(8,128)(2,1)} %param.13) | copy-start | bytes 2752516
  140.6 13.9 %all-to-all-start.1 = ((bf16[8,68,128]{2,1,0:T(8,128)(2,1)}), bf16[8,68,128]{2,1,0:T(8,128)(2,1)S(1)}, u32[]{:S(2)}, u32[]{:S(2)}) async-start(bf16[8,68,128]{2,1,0:T(8,128)(2,1)} %reshape.217), calls=%async_computation.1 | async-start | bytes 294912 | tf_op jit(solution)/shard_map/all_to_all | solution.py:70
  146.5 25.7 %collective-permute-start.3 = (bf16[128,3584]{1,0:T(8,128)(2,1)}, bf16[128,3584]{1,0:T(8,128)(2,1)}, u32[]{:S(2)}, u32[]{:S(2)}) collective-permute-start(bf16[128,3584]{1,0:T(8,128)(2,1)} %collective-permute-done.2), channel_id=1, source_target_pairs={{0,7},{1,0},{2,1},{3,2},{4,3},{5,4},{6,5},{7,6},{8,15},{9,8},{10,9... | collective-permute-start | bytes 2752520 | tf_op jit(solution)/shard_map/ppermute | solution.py:19
  151.1 24.0 %collective-permute-start.6 = (bf16[128,3584]{1,0:T(8,128)(2,1)}, bf16[128,3584]{1,0:T(8,128)(2,1)}, u32[]{:S(2)}, u32[]{:S(2)}) collective-permute-start(bf16[128,3584]{1,0:T(8,128)(2,1)} %collective-permute-done.5), channel_id=1, source_target_pairs={{0,1},{1,2},{2,3},{3,4},{4,5},{5,6},{6,7},{7,0},{8,9},{9,10},{10,1... | collective-permute-start | bytes 2752520 | tf_op jit(solution)/shard_map/ppermute | solution.py:19
  173.7 7.5 %copy-start.9 = (s32[1,2,64,1]{2,3,1,0:T(1,128)S(1)}, s32[1,2,64,1]{2,3,1,0:T(1,128)}, u32[]{:S(2)}) copy-start(s32[1,2,64,1]{2,3,1,0:T(1,128)} %param.14) | copy-start | bytes 1540
  173.7 7.5 %copy-start.10 = (s32[1,2,64,1]{2,3,1,0:T(1,128)S(1)}, s32[1,2,64,1]{2,3,1,0:T(1,128)}, u32[]{:S(2)}) copy-start(s32[1,2,64,1]{2,3,1,0:T(1,128)} %param.15) | copy-start | bytes 1540
  177.6 15.4 %all-to-all-start.2 = ((f32[4,476,128]{2,1,0:T(8,128)}), f32[4,476,128]{2,1,0:T(8,128)S(1)}, u32[]{:S(2)}, u32[]{:S(2)}) async-start(f32[4,476,128]{2,1,0:T(8,128)} %reshape.218), calls=%async_computation.2 | async-start | bytes 1966080 | tf_op jit(solution)/shard_map/all_to_all | solution.py:79
  181.1 94.3 %all-gather.7.cloned.1.call-start = ((), (), s32[]{:S(2)}) async-start(), calls=%async_computation.7 | async-start | bytes 4423680 | tf_op jit(solution)/shard_map/all_gather | solution.py:63
  196.3 10.8 %collective-permute-start.7 = (bf16[64,3584]{1,0:T(8,128)(2,1)S(1)}, bf16[64,3584]{1,0:T(8,128)(2,1)S(1)}, u32[]{:S(2)}, u32[]{:S(2)}) collective-permute-start(bf16[64,3584]{1,0:T(8,128)(2,1)S(1)} %fusion.39), channel_id=1, source_target_pairs={{0,32},{32,64},{64,96},{96,128},{128,160},{160,192},{192,224},{224... | collective-permute-start | bytes 1376264 | tf_op jit(solution)/shard_map/ppermute | solution.py:19
  282.5 3.5 %copy-start.12 = (bf16[1,1,3584,128]{3,2,1,0:T(8,128)(2,1)S(1)}, bf16[1,1,3584,128]{3,2,1,0:T(8,128)(2,1)}, u32[]{:S(2)}) copy-start(bf16[1,1,3584,128]{3,2,1,0:T(8,128)(2,1)} %param.12) | copy-start | bytes 2752516
  286.0 13.9 %copy-start.7 = (bf16[1,1,128,3584]{3,2,1,0:T(8,128)(2,1)S(1)}, bf16[1,1,128,3584]{3,2,1,0:T(8,128)(2,1)}, u32[]{:S(2)}) copy-start(bf16[1,1,128,3584]{3,2,1,0:T(8,128)(2,1)} %param.13) | copy-start | bytes 2752516
  287.2 16.0 %copy-start.5 = (bf16[128,3584]{1,0:T(8,128)(2,1)S(1)}, bf16[128,3584]{1,0:T(8,128)(2,1)}, u32[]{:S(2)}) copy-start(bf16[128,3584]{1,0:T(8,128)(2,1)} %copy-done.4) | copy-start | bytes 2752516
  310.4 15.4 %all-to-all-start.5 = ((f32[4,476,128]{2,1,0:T(8,128)}), f32[4,476,128]{2,1,0:T(8,128)S(1)}, u32[]{:S(2)}, u32[]{:S(2)}) async-start(f32[4,476,128]{2,1,0:T(8,128)} %reshape.223), calls=%async_computation.5 | async-start | bytes 1966080 | tf_op jit(solution)/shard_map/all_to_all | solution.py:79
  (2 other events, 5.2 us)
Sparse Core Ops, SparseCore 0:
  45.0 83.2 all-gather.4
  218.4 57.0 all-gather.6

commit v8 on v5

--- a/solution.py
+++ b/solution.py
@@ -66,7 +66,7 @@
     expert_out = None
     for d in range(n_y):
         part = jnp.dot(hidden_rel[d], down_all[d], preferred_element_type=jnp.float32)
-        part = part.astype(jnp.bfloat16).astype(jnp.float32)
+        part = lax.reduce_precision(part, exponent_bits=8, mantissa_bits=7)
         expert_out = part if expert_out is None else expert_out + part
     expert_out = expert_out.reshape(n_x, block_rows, LANE)
     returned = lax.all_to_all(expert_out, "ex", split_axis=0, concat_axis=0, tiled=True)

time: 320 us -> 320 us (level)
  no operation moved by 1% of the time
where the time goes in v8:
time: 320 us; the launch traced here: 317 us
  waiting for transfers between devices  166 us (52%)
  starting transfers between devices  45.1 us (14%)
  blocking collectives  33.4 us (10%)
  matrix products  29.7 us (9%)
  local copies, waits for them, and re-layouts  23.2 us (7%)
  between operations  13.9 us (4%)
  other arithmetic  5.96 us (2%)
    all_gather x2, waiting for transfers between devices, routed_branch(): slot_rows = lax.all_gather(from_x, 'ey', axis=0, tiled=False)  73.4 us
    ppermute x8, waiting for transfers between devices, shifted(): return lax.ppermute(value, axis, pairs)  67.8 us
    ppermute x8, starting transfers between devices, shifted(): return lax.ppermute(value, axis, pairs)  32.1 us
    all_to_all x2, waiting for transfers between devices, routed_branch(): lax.all_to_all(expert_out, 'ex', split_axis=0, concat_axis=0, tiled=True)  23 us
    all_to_all x2, blocking collectives, routed_branch(): lax.all_to_all(per_expert, 'ex', split_axis=0, concat_axis=0, tiled=True)  21.4 us
    dot_general x16, matrix products, routed_branch(): jnp.dot(hidden_rel[d], down_all[d], preferred_element_type=jnp.float32)  18.8 us
    reshape x2, local copies, waits for them, and re-layouts, routed_branch(): flat_rows = slot_rows.reshape(-1, model_width)  14 us
    all_to_all x1, blocking collectives, routed_branch(): lax.all_to_all(hidden, 'ey', split_axis=0, concat_axis=0, tiled=True)  12 us
  transfers between devices with their start and end apart: 13, of which 10 were waited for; matrix products, arithmetic and copies ran while one was open for 7% of the time, Pallas kernels for 0%

profile of v8, /device:TPU:1, one launch (start us, length us, event | category | flops | bytes accessed | tf_op | source)
XLA Modules:
  0.0 316.9 jit_solution(832300018340763411)
XLA Ops:
  12.6 11.5 %all_to_all.30 = bf16[4,476,128]{2,1,0:T(8,128)(2,1)} all-to-all(bf16[4,476,128]{2,1,0:T(8,128)(2,1)S(1)} %reshape.215), channel_id=1, replica_groups=mesh['pipe'=16,'ex'=4,'ey'=8] {'ex'}, dimensions={0} | all-to-all | bytes 974848 | tf_op jit(solution)/shard_map/all_to_all | solution.py:55
  24.1 4.7 %collective-permute-start.3 = (bf16[128,3584]{1,0:T(8,128)(2,1)S(1)}, bf16[128,3584]{1,0:T(8,128)(2,1)S(1)}, u32[]{:S(2)}, u32[]{:S(2)}) collective-permute-start(bf16[128,3584]{1,0:T(8,128)(2,1)S(1)} %bitcast.119), channel_id=1, source_target_pairs={{0,1},{1,2},{2,3},{3,4},{4,5},{5,6},{6,7},{7,0},{8,9},{9,10},{10,1... | collective-permute-start | bytes 2752520 | tf_op jit(solution)/shard_map/ppermute | solution.py:19
  28.8 3.8 %collective-permute-start = (bf16[128,3584]{1,0:T(8,128)(2,1)S(1)}, bf16[128,3584]{1,0:T(8,128)(2,1)}, u32[]{:S(2)}, u32[]{:S(2)}) collective-permute-start(bf16[128,3584]{1,0:T(8,128)(2,1)S(1)} %bitcast.120), channel_id=1, source_target_pairs={{0,7},{1,0},{2,1},{3,2},{4,3},{5,4},{6,5},{7,6},{8,15},{9,8},{10,9... | collective-permute-start | bytes 2752520 | tf_op jit(solution)/shard_map/ppermute | solution.py:19
  32.6 14.1 %collective-permute-done.3 = bf16[128,3584]{1,0:T(8,128)(2,1)S(1)} collective-permute-done((bf16[128,3584]{1,0:T(8,128)(2,1)S(1)}, bf16[128,3584]{1,0:T(8,128)(2,1)S(1)}, u32[]{:S(2)}, u32[]{:S(2)}) %collective-permute-start.3) | collective-permute-done | bytes 917536 | tf_op jit(solution)/shard_map/ppermute | solution.py:19
  46.7 5.7 %collective-permute-start.4 = (bf16[128,3584]{1,0:T(8,128)(2,1)S(1)}, bf16[128,3584]{1,0:T(8,128)(2,1)}, u32[]{:S(2)}, u32[]{:S(2)}) collective-permute-start(bf16[128,3584]{1,0:T(8,128)(2,1)S(1)} %collective-permute-done.3), channel_id=1, source_target_pairs={{0,1},{1,2},{2,3},{3,4},{4,5},{5,6},{6,7},{7,0},{8,9},{9,10},{10,1... | collective-permute-start | bytes 2752520 | tf_op jit(solution)/shard_map/ppermute | solution.py:19
  52.4 4.4 %collective-permute-start.1 = (bf16[128,3584]{1,0:T(8,128)(2,1)}, bf16[128,3584]{1,0:T(8,128)(2,1)}, u32[]{:S(2)}, u32[]{:S(2)}) collective-permute-start(bf16[128,3584]{1,0:T(8,128)(2,1)} %collective-permute-done), channel_id=1, source_target_pairs={{0,7},{1,0},{2,1},{3,2},{4,3},{5,4},{6,5},{7,6},{8,15},{9,8},{10,9... | collective-permute-start | bytes 2752520 | tf_op jit(solution)/shard_map/ppermute | solution.py:19
  56.8 36.4 %collective-permute-done.4 = bf16[128,3584]{1,0:T(8,128)(2,1)} collective-permute-done((bf16[128,3584]{1,0:T(8,128)(2,1)S(1)}, bf16[128,3584]{1,0:T(8,128)(2,1)}, u32[]{:S(2)}, u32[]{:S(2)}) %collective-permute-start.4) | collective-permute-done | bytes 917536 | tf_op jit(solution)/shard_map/ppermute | solution.py:19
  95.1 17.2 %all-gather.5.cloned.1.call-done = bf16[32,476,128]{2,1,0:T(8,128)(2,1)} async-done(((bf16[4,476,128]{2,1,0:T(8,128)(2,1)}), bf16[32,476,128]{2,1,0:T(8,128)(2,1)}) %all-gather.5.cloned.1.call-update) | async-done | bytes 3899408 | tf_op jit(solution)/shard_map/all_gather | solution.py:56
  112.3 7.0 %reshape.216 = bf16[544,3584]{1,0:T(8,128)(2,1)} reshape(bf16[32,476,128]{2,1,0:T(8,128)(2,1)} %all-gather.5.cloned.1.call-done) | data formatting | bytes 7798784 | tf_op jit(solution)/shard_map/reshape | solution.py:58
  119.3 3.4 %fusion.28 = f32[544,128]{1,0:T(8,128)S(1)} fusion(bf16[544,3584]{1,0:T(8,128)(2,1)} %reshape.216, bf16[1,1,3584,128]{3,2,1,0:T(8,128)(2,1)S(1)} %copy-done), kind=kOutput, calls=%fused_computation.58 | convolution fusion | flops 499122176 | bytes 5095424 | tf_op jit(solution)/shard_map/dot_general | solution.py:59
  124.7 5.3 %all-to-all-start.1 = ((bf16[8,68,128]{2,1,0:T(8,128)(2,1)}), bf16[8,68,128]{2,1,0:T(8,128)(2,1)S(1)}, u32[]{:S(2)}, u32[]{:S(2)}) async-start(bf16[8,68,128]{2,1,0:T(8,128)(2,1)} %reshape.217), calls=%async_computation.1 | async-start | bytes 294912 | tf_op jit(solution)/shard_map/all_to_all | solution.py:63
  130.0 4.6 %collective-permute-start.2 = (bf16[128,3584]{1,0:T(8,128)(2,1)}, bf16[128,3584]{1,0:T(8,128)(2,1)}, u32[]{:S(2)}, u32[]{:S(2)}) collective-permute-start(bf16[128,3584]{1,0:T(8,128)(2,1)} %collective-permute-done.1), channel_id=1, source_target_pairs={{0,7},{1,0},{2,1},{3,2},{4,3},{5,4},{6,5},{7,6},{8,15},{9,8},{10,9... | collective-permute-start | bytes 2752520 | tf_op jit(solution)/shard_map/ppermute | solution.py:19
  145.2 10.5 %collective-permute-done.2 = bf16[128,3584]{1,0:T(8,128)(2,1)} collective-permute-done((bf16[128,3584]{1,0:T(8,128)(2,1)}, bf16[128,3584]{1,0:T(8,128)(2,1)}, u32[]{:S(2)}, u32[]{:S(2)}) %collective-permute-start.2) | collective-permute-done | bytes 917536 | tf_op jit(solution)/shard_map/ppermute | solution.py:19
  161.2 3.7 %all-to-all-start.2 = ((f32[4,476,128]{2,1,0:T(8,128)}), f32[4,476,128]{2,1,0:T(8,128)S(1)}, u32[]{:S(2)}, u32[]{:S(2)}) async-start(f32[4,476,128]{2,1,0:T(8,128)} %reshape.218), calls=%async_computation.2 | async-start | bytes 1966080 | tf_op jit(solution)/shard_map/all_to_all | solution.py:72
  165.0 11.6 %all-to-all-done.2 = f32[4,476,128]{2,1,0:T(8,128)S(1)} async-done(((f32[4,476,128]{2,1,0:T(8,128)}), f32[4,476,128]{2,1,0:T(8,128)S(1)}, u32[]{:S(2)}, u32[]{:S(2)}) %all-to-all-start.2) | async-done | bytes 974880 | tf_op jit(solution)/shard_map/all_to_all | solution.py:72
  179.8 5.1 %collective-permute-start.7 = (bf16[64,3584]{1,0:T(8,128)(2,1)S(1)}, bf16[64,3584]{1,0:T(8,128)(2,1)S(1)}, u32[]{:S(2)}, u32[]{:S(2)}) collective-permute-start(bf16[64,3584]{1,0:T(8,128)(2,1)S(1)} %fusion.23), channel_id=1, source_target_pairs={{0,32},{32,64},{64,96},{96,128},{128,160},{160,192},{192,224},{224... | collective-permute-start | bytes 1376264 | tf_op jit(solution)/shard_map/ppermute | solution.py:19
  184.9 5.4 %collective-permute-done.7 = bf16[64,3584]{1,0:T(8,128)(2,1)S(1)} collective-permute-done((bf16[64,3584]{1,0:T(8,128)(2,1)S(1)}, bf16[64,3584]{1,0:T(8,128)(2,1)S(1)}, u32[]{:S(2)}, u32[]{:S(2)}) %collective-permute-start.7) | collective-permute-done | bytes 458784 | tf_op jit(solution)/shard_map/ppermute | solution.py:19
  191.6 9.9 %all_to_all.31 = bf16[4,476,128]{2,1,0:T(8,128)(2,1)} all-to-all(bf16[4,476,128]{2,1,0:T(8,128)(2,1)S(1)} %reshape.220), channel_id=1, replica_groups=mesh['pipe'=16,'ex'=4,'ey'=8] {'ex'}, dimensions={0} | all-to-all | bytes 974848 | tf_op jit(solution)/shard_map/all_to_all | solution.py:55
  201.5 56.2 %all-gather.7.cloned.1.call-done = bf16[32,476,128]{2,1,0:T(8,128)(2,1)} async-done(((bf16[4,476,128]{2,1,0:T(8,128)(2,1)}), bf16[32,476,128]{2,1,0:T(8,128)(2,1)}) %all-gather.7.cloned.1.call-update) | async-done | bytes 3899408 | tf_op jit(solution)/shard_map/all_gather | solution.py:56
  257.7 7.0 %reshape.221 = bf16[544,3584]{1,0:T(8,128)(2,1)} reshape(bf16[32,476,128]{2,1,0:T(8,128)(2,1)} %all-gather.7.cloned.1.call-done) | data formatting | bytes 7798784 | tf_op jit(solution)/shard_map/reshape | solution.py:58
  264.7 3.4 %fusion.26 = f32[544,128]{1,0:T(8,128)S(1)} fusion(bf16[544,3584]{1,0:T(8,128)(2,1)} %reshape.221, bf16[1,1,3584,128]{3,2,1,0:T(8,128)(2,1)S(1)} %copy-done), kind=kOutput, calls=%fused_computation.56 | convolution fusion | flops 499122176 | bytes 5095424 | tf_op jit(solution)/shard_map/dot_general | solution.py:59
  269.4 12.0 %all_to_all.32 = bf16[8,68,128]{2,1,0:T(8,128)(2,1)S(1)} all-to-all(bf16[8,68,128]{2,1,0:T(8,128)(2,1)S(1)} %reshape.222), channel_id=1, replica_groups=mesh['pipe'=16,'ex'=4,'ey'=8] {'ey'}, dimensions={0} | all-to-all | bytes 278528 | tf_op jit(solution)/shard_map/all_to_all | solution.py:63
  292.7 4.0 %all-to-all-start.5 = ((f32[4,476,128]{2,1,0:T(8,128)}), f32[4,476,128]{2,1,0:T(8,128)S(1)}, u32[]{:S(2)}, u32[]{:S(2)}) async-start(f32[4,476,128]{2,1,0:T(8,128)} %reshape.223), calls=%async_computation.5 | async-start | bytes 1966080 | tf_op jit(solution)/shard_map/all_to_all | solution.py:72
  296.6 11.4 %all-to-all-done.5 = f32[4,476,128]{2,1,0:T(8,128)S(1)} async-done(((f32[4,476,128]{2,1,0:T(8,128)}), f32[4,476,128]{2,1,0:T(8,128)S(1)}, u32[]{:S(2)}, u32[]{:S(2)}) %all-to-all-start.5) | async-done | bytes 974880 | tf_op jit(solution)/shard_map/all_to_all | solution.py:72
  (90 shorter events, 44.8 us)
Async XLA Ops:
  6.5 112.8 %copy-start = (bf16[1,1,3584,128]{3,2,1,0:T(8,128)(2,1)S(1)}, bf16[1,1,3584,128]{3,2,1,0:T(8,128)(2,1)}, u32[]{:S(2)}) copy-start(bf16[1,1,3584,128]{3,2,1,0:T(8,128)(2,1)} %param.11) | copy-start | bytes 2752516
  6.5 17.6 %copy-start.4 = (bf16[1,1,128,3584]{3,2,1,0:T(8,128)(2,1)S(1)}, bf16[1,1,128,3584]{3,2,1,0:T(8,128)(2,1)}, u32[]{:S(2)}) copy-start(bf16[1,1,128,3584]{3,2,1,0:T(8,128)(2,1)} %param.13) | copy-start | bytes 2752516
  6.5 105.8 %all-gather.5.cloned.1.call-start = ((), (), s32[]{:S(2)}) async-start(), calls=%async_computation.6 | async-start | bytes 4423680 | tf_op jit(solution)/shard_map/all_gather | solution.py:56
  24.1 22.6 %collective-permute-start.3 = (bf16[128,3584]{1,0:T(8,128)(2,1)S(1)}, bf16[128,3584]{1,0:T(8,128)(2,1)S(1)}, u32[]{:S(2)}, u32[]{:S(2)}) collective-permute-start(bf16[128,3584]{1,0:T(8,128)(2,1)S(1)} %bitcast.119), channel_id=1, source_target_pairs={{0,1},{1,2},{2,3},{3,4},{4,5},{5,6},{6,7},{7,0},{8,9},{9,10},{10,1... | collective-permute-start | bytes 2752520 | tf_op jit(solution)/shard_map/ppermute | solution.py:19
  28.8 23.6 %collective-permute-start = (bf16[128,3584]{1,0:T(8,128)(2,1)S(1)}, bf16[128,3584]{1,0:T(8,128)(2,1)}, u32[]{:S(2)}, u32[]{:S(2)}) collective-permute-start(bf16[128,3584]{1,0:T(8,128)(2,1)S(1)} %bitcast.120), channel_id=1, source_target_pairs={{0,7},{1,0},{2,1},{3,2},{4,3},{5,4},{6,5},{7,6},{8,15},{9,8},{10,9... | collective-permute-start | bytes 2752520 | tf_op jit(solution)/shard_map/ppermute | solution.py:19
  46.7 95.3 %copy-start.6 = (bf16[128,3584]{1,0:T(8,128)(2,1)}, bf16[128,3584]{1,0:T(8,128)(2,1)S(1)}, u32[]{:S(2)}) copy-start(bf16[128,3584]{1,0:T(8,128)(2,1)S(1)} %collective-permute-done.3) | copy-start | bytes 2752516
  46.7 46.6 %collective-permute-start.4 = (bf16[128,3584]{1,0:T(8,128)(2,1)S(1)}, bf16[128,3584]{1,0:T(8,128)(2,1)}, u32[]{:S(2)}, u32[]{:S(2)}) collective-permute-start(bf16[128,3584]{1,0:T(8,128)(2,1)S(1)} %collective-permute-done.3), channel_id=1, source_target_pairs={{0,1},{1,2},{2,3},{3,4},{4,5},{5,6},{6,7},{7,0},{8,9},{9,10},{10,1... | collective-permute-start | bytes 2752520 | tf_op jit(solution)/shard_map/ppermute | solution.py:19
  52.4 77.6 %collective-permute-start.1 = (bf16[128,3584]{1,0:T(8,128)(2,1)}, bf16[128,3584]{1,0:T(8,128)(2,1)}, u32[]{:S(2)}, u32[]{:S(2)}) collective-permute-start(bf16[128,3584]{1,0:T(8,128)(2,1)} %collective-permute-done), channel_id=1, source_target_pairs={{0,7},{1,0},{2,1},{3,2},{4,3},{5,4},{6,5},{7,6},{8,15},{9,8},{10,9... | collective-permute-start | bytes 2752520 | tf_op jit(solution)/shard_map/ppermute | solution.py:19
  93.2 41.4 %collective-permute-start.5 = (bf16[128,3584]{1,0:T(8,128)(2,1)}, bf16[128,3584]{1,0:T(8,128)(2,1)}, u32[]{:S(2)}, u32[]{:S(2)}) collective-permute-start(bf16[128,3584]{1,0:T(8,128)(2,1)} %collective-permute-done.4), channel_id=1, source_target_pairs={{0,1},{1,2},{2,3},{3,4},{4,5},{5,6},{6,7},{7,0},{8,9},{9,10},{10,1... | collective-permute-start | bytes 2752520 | tf_op jit(solution)/shard_map/ppermute | solution.py:19
  119.3 3.4 %copy-start.2 = (bf16[544,3584]{1,0:T(8,128)(2,1)S(1)}, bf16[544,3584]{1,0:T(8,128)(2,1)}, u32[]{:S(2)}) copy-start(bf16[544,3584]{1,0:T(8,128)(2,1)} %reshape.216) | copy-start | bytes 11698180
  119.3 3.5 %copy-start.10 = (bf16[1,1,3584,128]{3,2,1,0:T(8,128)(2,1)S(1)}, bf16[1,1,3584,128]{3,2,1,0:T(8,128)(2,1)}, u32[]{:S(2)}) copy-start(bf16[1,1,3584,128]{3,2,1,0:T(8,128)(2,1)} %param.12) | copy-start | bytes 2752516
  124.7 13.4 %all-to-all-start.1 = ((bf16[8,68,128]{2,1,0:T(8,128)(2,1)}), bf16[8,68,128]{2,1,0:T(8,128)(2,1)S(1)}, u32[]{:S(2)}, u32[]{:S(2)}) async-start(bf16[8,68,128]{2,1,0:T(8,128)(2,1)} %reshape.217), calls=%async_computation.1 | async-start | bytes 294912 | tf_op jit(solution)/shard_map/all_to_all | solution.py:63
  130.0 25.7 %collective-permute-start.2 = (bf16[128,3584]{1,0:T(8,128)(2,1)}, bf16[128,3584]{1,0:T(8,128)(2,1)}, u32[]{:S(2)}, u32[]{:S(2)}) collective-permute-start(bf16[128,3584]{1,0:T(8,128)(2,1)} %collective-permute-done.1), channel_id=1, source_target_pairs={{0,7},{1,0},{2,1},{3,2},{4,3},{5,4},{6,5},{7,6},{8,15},{9,8},{10,9... | collective-permute-start | bytes 2752520 | tf_op jit(solution)/shard_map/ppermute | solution.py:19
  134.6 24.0 %collective-permute-start.6 = (bf16[128,3584]{1,0:T(8,128)(2,1)}, bf16[128,3584]{1,0:T(8,128)(2,1)}, u32[]{:S(2)}, u32[]{:S(2)}) collective-permute-start(bf16[128,3584]{1,0:T(8,128)(2,1)} %collective-permute-done.5), channel_id=1, source_target_pairs={{0,1},{1,2},{2,3},{3,4},{4,5},{5,6},{6,7},{7,0},{8,9},{9,10},{10,1... | collective-permute-start | bytes 2752520 | tf_op jit(solution)/shard_map/ppermute | solution.py:19
  157.2 7.7 %copy-start.8 = (s32[1,2,64,1]{2,3,1,0:T(1,128)S(1)}, s32[1,2,64,1]{2,3,1,0:T(1,128)}, u32[]{:S(2)}) copy-start(s32[1,2,64,1]{2,3,1,0:T(1,128)} %param.14) | copy-start | bytes 1540
  157.2 7.7 %copy-start.9 = (s32[1,2,64,1]{2,3,1,0:T(1,128)S(1)}, s32[1,2,64,1]{2,3,1,0:T(1,128)}, u32[]{:S(2)}) copy-start(s32[1,2,64,1]{2,3,1,0:T(1,128)} %param.15) | copy-start | bytes 1540
  161.2 15.4 %all-to-all-start.2 = ((f32[4,476,128]{2,1,0:T(8,128)}), f32[4,476,128]{2,1,0:T(8,128)S(1)}, u32[]{:S(2)}, u32[]{:S(2)}) async-start(f32[4,476,128]{2,1,0:T(8,128)} %reshape.218), calls=%async_computation.2 | async-start | bytes 1966080 | tf_op jit(solution)/shard_map/all_to_all | solution.py:72
  164.9 92.8 %all-gather.7.cloned.1.call-start = ((), (), s32[]{:S(2)}) async-start(), calls=%async_computation.7 | async-start | bytes 4423680 | tf_op jit(solution)/shard_map/all_gather | solution.py:56
  179.8 10.5 %collective-permute-start.7 = (bf16[64,3584]{1,0:T(8,128)(2,1)S(1)}, bf16[64,3584]{1,0:T(8,128)(2,1)S(1)}, u32[]{:S(2)}, u32[]{:S(2)}) collective-permute-start(bf16[64,3584]{1,0:T(8,128)(2,1)S(1)} %fusion.23), channel_id=1, source_target_pairs={{0,32},{32,64},{64,96},{96,128},{128,160},{160,192},{192,224},{224... | collective-permute-start | bytes 1376264 | tf_op jit(solution)/shard_map/ppermute | solution.py:19
  264.7 3.4 %copy-start.3 = (bf16[544,3584]{1,0:T(8,128)(2,1)S(1)}, bf16[544,3584]{1,0:T(8,128)(2,1)}, u32[]{:S(2)}) copy-start(bf16[544,3584]{1,0:T(8,128)(2,1)} %reshape.221) | copy-start | bytes 11698180
  264.7 3.5 %copy-start.11 = (bf16[1,1,3584,128]{3,2,1,0:T(8,128)(2,1)S(1)}, bf16[1,1,3584,128]{3,2,1,0:T(8,128)(2,1)}, u32[]{:S(2)}) copy-start(bf16[1,1,3584,128]{3,2,1,0:T(8,128)(2,1)} %param.12) | copy-start | bytes 2752516
  268.2 13.9 %copy-start.5 = (bf16[1,1,128,3584]{3,2,1,0:T(8,128)(2,1)S(1)}, bf16[1,1,128,3584]{3,2,1,0:T(8,128)(2,1)}, u32[]{:S(2)}) copy-start(bf16[1,1,128,3584]{3,2,1,0:T(8,128)(2,1)} %param.13) | copy-start | bytes 2752516
  269.4 16.0 %copy-start.7 = (bf16[128,3584]{1,0:T(8,128)(2,1)S(1)}, bf16[128,3584]{1,0:T(8,128)(2,1)}, u32[]{:S(2)}) copy-start(bf16[128,3584]{1,0:T(8,128)(2,1)} %copy-done.6) | copy-start | bytes 2752516
  292.7 15.4 %all-to-all-start.5 = ((f32[4,476,128]{2,1,0:T(8,128)}), f32[4,476,128]{2,1,0:T(8,128)S(1)}, u32[]{:S(2)}, u32[]{:S(2)}) async-start(f32[4,476,128]{2,1,0:T(8,128)} %reshape.223), calls=%async_computation.5 | async-start | bytes 1966080 | tf_op jit(solution)/shard_map/all_to_all | solution.py:72
  (1 other events, 1.8 us)
Sparse Core Ops, SparseCore 0:
  24.2 88.0 all-gather.4
  201.6 56.0 all-gather.6

commit v9 on v8

--- a/solution.py
+++ b/solution.py
@@ -46,13 +46,30 @@
     return jnp.dot(placing, normed, preferred_element_type=jnp.float32).astype(jnp.bfloat16)
 
 
-def routed_branch(normed, expert_ids, route_weight, w_gate, w_up, down_all):
+def slot_blocks(normed, slot_ids):
+    model_width = normed.shape[1]
+    placed = place_rows(normed, slot_ids, EXPERTS * MOST)
+    return placed.reshape(EXPERTS, MOST * model_width // LANE, LANE)
+
+
+def next_section_shift(value, steps):
+    n_pipe = lax.axis_size("pipe")
+    n_x = lax.axis_size("ex")
+    pairs = []
+    for p in range(n_pipe):
+        for x in range(n_x):
+            pairs.append((p * n_x + x, ((p + 1) % n_pipe) * n_x + (x + steps) % n_x))
+    return lax.ppermute(value, ("pipe", "ex"), pairs)
+
+
+def routed_branch(normed, expert_ids, route_weight, w_gate, w_up, down_all, from_x=None):
     n_x = lax.axis_size("ex")
     model_width = normed.shape[1]
     slot_ids = slot_index(expert_ids, MOST, EXPERTS)
     block_rows = MOST * model_width // LANE
-    per_expert = place_rows(normed, slot_ids, EXPERTS * MOST).reshape(EXPERTS, block_rows, LANE)
-    from_x = lax.all_to_all(per_expert, "ex", split_axis=0, concat_axis=0, tiled=True)
+    if from_x is None:
+        per_expert = slot_blocks(normed, slot_ids)
+        from_x = lax.all_to_all(per_expert, "ex", split_axis=0, concat_axis=0, tiled=True)
     slot_rows = lax.all_gather(from_x, "ey", axis=0, tiled=False)
     n_y = slot_rows.shape[0]
     flat_rows = slot_rows.reshape(-1, model_width)
@@ -75,11 +92,16 @@
     return jnp.sum(weights[:, :, None] * picked, axis=1)
 
 
-def layer_terms(rows_in, gain_row, w_gate, w_up, down_all, expert_ids, route_weight):
+def normalize(rows_in, gain_row):
     values = rows_in.astype(jnp.float32)
     inv_rms = lax.rsqrt(jnp.mean(values * values, axis=1, keepdims=True) + NORM_EPS)
     normed = (values * inv_rms * gain_row.astype(jnp.float32)).astype(jnp.bfloat16)
-    branch = routed_branch(normed, expert_ids, route_weight, w_gate, w_up, down_all)
+    return values, normed
+
+
+def layer_terms(rows_in, gain_row, w_gate, w_up, down_all, expert_ids, route_weight, from_x=None):
+    values, normed = normalize(rows_in, gain_row)
+    branch = routed_branch(normed, expert_ids, route_weight, w_gate, w_up, down_all, from_x)
     return (values, branch)
 
 
@@ -90,13 +112,24 @@
     w_gate = gate_w[0, 0]
     w_up = up_w[0, 0]
     down_all = ring_gather(down_w[0, 0], "ey")
+    gain_next = shifted(gain_row, "pipe", -1)
+    ids_next = shifted(route_ids[0, 1], "pipe", -1)
     values, branch = layer_terms(
         rows_in, gain_row, w_gate, w_up, down_all, route_ids[0, 0], route_wts[0, 0]
     )
     first_out = (values + branch).astype(jnp.bfloat16)
     arrived = shifted(first_out, "pipe", 1)
+    me_x = lax.axis_index("ex")
+    _, normed_next = normalize(first_out, gain_next)
+    blocks_next = slot_blocks(normed_next, slot_index(ids_next, MOST, EXPERTS))
+    received = []
+    for d in range(EXPERTS):
+        block = lax.dynamic_index_in_dim(blocks_next, (me_x + d) % EXPERTS, 0, keepdims=False)
+        received.append(next_section_shift(block, d))
+    received = jnp.stack(received, axis=0)
+    from_x = jnp.take(received, (me_x - jnp.arange(EXPERTS)) % EXPERTS, axis=0)
     values, branch = layer_terms(
-        arrived, gain_row, w_gate, w_up, down_all, route_ids[0, 1], route_wts[0, 1]
+        arrived, gain_row, w_gate, w_up, down_all, route_ids[0, 1], route_wts[0, 1], from_x
     )
     second = (values + branch).astype(jnp.bfloat16)
     result_rows = jnp.where(section_index == 0, arrived, second)

time: 320 us -> 324 us (1.012)
  starting transfers between devices: 45.1 us -> 75.1 us
  waiting for transfers between devices: 166 us -> 141 us
  blocking collectives: 33.4 us -> 23.6 us
  local copies, waits for them, and re-layouts: 23.2 us -> 29.6 us
    ppermute x8 -> x10, waiting for transfers between devices: 67.8 us -> 46.7 us  [shifted(): return lax.ppermute(value, axis, pairs)]
    ppermute x0 -> x4, starting transfers between devices: none -> 15.4 us  [next_section_shift(): return lax.ppermute(value, ('pipe', 'ex'), pairs)]
    ppermute x8 -> x10, starting transfers between devices: 32.1 us -> 46.7 us  [shifted(): return lax.ppermute(value, axis, pairs)]
    all_to_all x2 -> x1, blocking collectives: 21.4 us -> 11.5 us  [routed_branch(): lax.all_to_all(per_expert, 'ex', split_axis=0, concat_axis=0, tiled=True)]
    all_gather x0 -> x1, local copies, waits for them, and re-layouts: none -> 4.62 us  [routed_branch(): slot_rows = lax.all_gather(from_x, 'ey', axis=0, tiled=False)]
    ppermute x0 -> x4, waiting for transfers between devices: none -> 4.58 us  [next_section_shift(): return lax.ppermute(value, ('pipe', 'ex'), pairs)]
    all_to_all x2, waiting for transfers between devices: 23 us -> 18.6 us  [routed_branch(): lax.all_to_all(expert_out, 'ex', split_axis=0, concat_axis=0, tiled=True)]
    all_gather x2, waiting for transfers between devices: 73.4 us -> 69.3 us  [routed_branch(): slot_rows = lax.all_gather(from_x, 'ey', axis=0, tiled=False)]
  transfers between devices with their start and end apart: 13 -> 19, of which waited for: 10 -> 10; matrix products, arithmetic and copies ran while one was open for 7% -> 8% of each run, Pallas kernels for 0% -> 0%
where the time goes in v9:
time: 324 us; the launch traced here: 320 us
  waiting for transfers between devices  141 us (44%)
  starting transfers between devices  75.1 us (23%)
  matrix products  29.7 us (9%)
  local copies, waits for them, and re-layouts  29.6 us (9%)
  blocking collectives  23.6 us (7%)
  between operations  14 us (4%)
  other arithmetic  7.64 us (2%)
    all_gather x2, waiting for transfers between devices, routed_branch(): slot_rows = lax.all_gather(from_x, 'ey', axis=0, tiled=False)  69.3 us
    ppermute x10, waiting for transfers between devices, shifted(): return lax.ppermute(value, axis, pairs)  46.7 us
    ppermute x10, starting transfers between devices, shifted(): return lax.ppermute(value, axis, pairs)  46.7 us
    dot_general x16, matrix products, routed_branch(): jnp.dot(hidden_rel[d], down_all[d], preferred_element_type=jnp.float32)  18.8 us
    all_to_all x2, waiting for transfers between devices, routed_branch(): lax.all_to_all(expert_out, 'ex', split_axis=0, concat_axis=0, tiled=True)  18.6 us
    ppermute x4, starting transfers between devices, next_section_shift(): return lax.ppermute(value, ('pipe', 'ex'), pairs)  15.4 us
    reshape x2, local copies, waits for them, and re-layouts, routed_branch(): flat_rows = slot_rows.reshape(-1, model_width)  14 us
    all_to_all x1, blocking collectives, routed_branch(): lax.all_to_all(hidden, 'ey', split_axis=0, concat_axis=0, tiled=True)  12 us
  transfers between devices with their start and end apart: 19, of which 10 were waited for; matrix products, arithmetic and copies ran while one was open for 8% of the time, Pallas kernels for 0%

profile of v9, /device:TPU:1, one launch (start us, length us, event | category | flops | bytes accessed | tf_op | source)
XLA Modules:
  0.0 320.2 jit_solution(3950060930247219898)
XLA Ops:
  12.6 11.5 %all_to_all.25 = bf16[4,476,128]{2,1,0:T(8,128)(2,1)} all-to-all(bf16[4,476,128]{2,1,0:T(8,128)(2,1)S(1)} %reshape.283), channel_id=1, replica_groups=mesh['pipe'=16,'ex'=4,'ey'=8] {'ex'}, dimensions={0} | all-to-all | bytes 974848 | tf_op jit(solution)/shard_map/all_to_all | solution.py:72
  24.1 4.7 %collective-permute-start.3 = (bf16[128,3584]{1,0:T(8,128)(2,1)S(1)}, bf16[128,3584]{1,0:T(8,128)(2,1)S(1)}, u32[]{:S(2)}, u32[]{:S(2)}) collective-permute-start(bf16[128,3584]{1,0:T(8,128)(2,1)S(1)} %bitcast.138), channel_id=1, source_target_pairs={{0,1},{1,2},{2,3},{3,4},{4,5},{5,6},{6,7},{7,0},{8,9},{9,10},{10,1... | collective-permute-start | bytes 2752520 | tf_op jit(solution)/shard_map/ppermute | solution.py:19
  32.6 14.1 %collective-permute-done.3 = bf16[128,3584]{1,0:T(8,128)(2,1)S(1)} collective-permute-done((bf16[128,3584]{1,0:T(8,128)(2,1)S(1)}, bf16[128,3584]{1,0:T(8,128)(2,1)S(1)}, u32[]{:S(2)}, u32[]{:S(2)}) %collective-permute-start.3) | collective-permute-done | bytes 917536 | tf_op jit(solution)/shard_map/ppermute | solution.py:19
  46.7 5.7 %collective-permute-start.4 = (bf16[128,3584]{1,0:T(8,128)(2,1)S(1)}, bf16[128,3584]{1,0:T(8,128)(2,1)}, u32[]{:S(2)}, u32[]{:S(2)}) collective-permute-start(bf16[128,3584]{1,0:T(8,128)(2,1)S(1)} %collective-permute-done.3), channel_id=1, source_target_pairs={{0,1},{1,2},{2,3},{3,4},{4,5},{5,6},{6,7},{7,0},{8,9},{9,10},{10,1... | collective-permute-start | bytes 2752520 | tf_op jit(solution)/shard_map/ppermute | solution.py:19
  52.4 11.6 %collective-permute-start.9 = (bf16[3584]{0:T(1024)(128)(2,1)S(1)}, bf16[3584]{0:T(1024)(128)(2,1)S(1)}, u32[]{:S(2)}, u32[]{:S(2)}) collective-permute-start(bf16[3584]{0:T(1024)(128)(2,1)S(1)} %reduce), channel_id=1, source_target_pairs={{0,480},{32,0},{64,32},{96,64},{128,96},{160,128},{192,160},{224,1... | collective-permute-start | bytes 21512 | tf_op jit(solution)/shard_map/ppermute | solution.py:19
  64.0 3.9 %collective-permute-start.8 = (s32[64,1]{0,1:T(1,128)S(1)}, s32[64,1]{0,1:T(1,128)S(1)}, u32[]{:S(2)}, u32[]{:S(2)}) collective-permute-start(s32[64,1]{0,1:T(1,128)S(1)} %get-tuple-element.17), channel_id=1, source_target_pairs={{0,480},{32,0},{64,32},{96,64},{128,96},{160,128},{192,160},{224,1... | collective-permute-start | bytes 776 | tf_op jit(solution)/shard_map/ppermute | solution.py:19
  68.0 4.6 %collective-permute-start.1 = (bf16[128,3584]{1,0:T(8,128)(2,1)}, bf16[128,3584]{1,0:T(8,128)(2,1)}, u32[]{:S(2)}, u32[]{:S(2)}) collective-permute-start(bf16[128,3584]{1,0:T(8,128)(2,1)} %collective-permute-done), channel_id=1, source_target_pairs={{0,7},{1,0},{2,1},{3,2},{4,3},{5,4},{6,5},{7,6},{8,15},{9,8},{10,9... | collective-permute-start | bytes 2752520 | tf_op jit(solution)/shard_map/ppermute | solution.py:19
  72.5 20.7 %collective-permute-done.4 = bf16[128,3584]{1,0:T(8,128)(2,1)} collective-permute-done((bf16[128,3584]{1,0:T(8,128)(2,1)S(1)}, bf16[128,3584]{1,0:T(8,128)(2,1)}, u32[]{:S(2)}, u32[]{:S(2)}) %collective-permute-start.4) | collective-permute-done | bytes 917536 | tf_op jit(solution)/shard_map/ppermute | solution.py:19
  95.2 17.2 %all-gather.6.cloned.1.call-done = bf16[32,476,128]{2,1,0:T(8,128)(2,1)} async-done(((bf16[4,476,128]{2,1,0:T(8,128)(2,1)}), bf16[32,476,128]{2,1,0:T(8,128)(2,1)}) %all-gather.6.cloned.1.call-update) | async-done | bytes 3899408 | tf_op jit(solution)/shard_map/all_gather | solution.py:73
  112.3 7.0 %reshape.284 = bf16[544,3584]{1,0:T(8,128)(2,1)} reshape(bf16[32,476,128]{2,1,0:T(8,128)(2,1)} %all-gather.6.cloned.1.call-done) | data formatting | bytes 7798784 | tf_op jit(solution)/shard_map/reshape | solution.py:75
  124.7 5.2 %all-to-all-start.1 = ((bf16[8,68,128]{2,1,0:T(8,128)(2,1)}), bf16[8,68,128]{2,1,0:T(8,128)(2,1)S(1)}, u32[]{:S(2)}, u32[]{:S(2)}) async-start(bf16[8,68,128]{2,1,0:T(8,128)(2,1)} %reshape.285), calls=%async_computation.1 | async-start | bytes 294912 | tf_op jit(solution)/shard_map/all_to_all | solution.py:80
  130.0 4.6 %collective-permute-start.2 = (bf16[128,3584]{1,0:T(8,128)(2,1)}, bf16[128,3584]{1,0:T(8,128)(2,1)}, u32[]{:S(2)}, u32[]{:S(2)}) collective-permute-start(bf16[128,3584]{1,0:T(8,128)(2,1)} %collective-permute-done.1), channel_id=1, source_target_pairs={{0,7},{1,0},{2,1},{3,2},{4,3},{5,4},{6,5},{7,6},{8,15},{9,8},{10,9... | collective-permute-start | bytes 2752520 | tf_op jit(solution)/shard_map/ppermute | solution.py:19
  145.1 10.6 %collective-permute-done.2 = bf16[128,3584]{1,0:T(8,128)(2,1)} collective-permute-done((bf16[128,3584]{1,0:T(8,128)(2,1)}, bf16[128,3584]{1,0:T(8,128)(2,1)}, u32[]{:S(2)}, u32[]{:S(2)}) %collective-permute-start.2) | collective-permute-done | bytes 917536 | tf_op jit(solution)/shard_map/ppermute | solution.py:19
  165.4 11.1 %all-to-all-done.2 = f32[4,476,128]{2,1,0:T(8,128)S(1)} async-done(((f32[4,476,128]{2,1,0:T(8,128)}), f32[4,476,128]{2,1,0:T(8,128)S(1)}, u32[]{:S(2)}, u32[]{:S(2)}) %all-to-all-start.2) | async-done | bytes 974880 | tf_op jit(solution)/shard_map/all_to_all | solution.py:89
  181.1 5.1 %collective-permute-start.10 = (bf16[476,128]{1,0:T(8,128)(2,1)S(1)}, bf16[476,128]{1,0:T(8,128)(2,1)S(1)}, u32[]{:S(2)}, u32[]{:S(2)}) collective-permute-start(bf16[476,128]{1,0:T(8,128)(2,1)S(1)} %get-tuple-element.8), channel_id=1, source_target_pairs={{0,32},{8,40},{16,48},{24,56},{32,64},{40,72},{48,80},{56,88},{64,... | collective-permute-start | bytes 365576 | tf_op jit(solution)/shard_map/ppermute | solution.py:62
  188.1 5.7 %collective-permute-start.12 = (bf16[476,128]{1,0:T(8,128)(2,1)S(1)}, bf16[476,128]{1,0:T(8,128)(2,1)S(1)}, u32[]{:S(2)}, u32[]{:S(2)}) collective-permute-start(bf16[476,128]{1,0:T(8,128)(2,1)S(1)} %get-tuple-element.10), channel_id=1, source_target_pairs={{0,48},{8,56},{16,32},{24,40},{32,80},{40,88},{48,64},{56,72},{64,... | collective-permute-start | bytes 365576 | tf_op jit(solution)/shard_map/ppermute | solution.py:62
  196.6 4.6 %collective-permute-done.13 = bf16[476,128]{1,0:T(8,128)(2,1)S(1)} collective-permute-done((bf16[476,128]{1,0:T(8,128)(2,1)S(1)}, bf16[476,128]{1,0:T(8,128)(2,1)S(1)}, u32[]{:S(2)}, u32[]{:S(2)}) %collective-permute-start.13) | collective-permute-done | bytes 121888 | tf_op jit(solution)/shard_map/ppermute | solution.py:62
  203.0 52.2 %all-gather.4.cloned.1.call-done = bf16[8,4,476,128]{3,1,2,0:T(4,128)(2,1)} async-done(((bf16[1,4,476,128]{3,1,2,0:T(4,128)(2,1)}), bf16[8,4,476,128]{3,1,2,0:T(4,128)(2,1)}) %all-gather.4.cloned.1.call-update) | async-done | bytes 3899408 | tf_op jit(solution)/shard_map/all_gather | solution.py:73
  255.2 4.6 %copy.10 = bf16[8,4,476,128]{3,2,1,0:T(8,128)(2,1)} copy(bf16[8,4,476,128]{3,1,2,0:T(4,128)(2,1)} %all-gather.4.cloned.1.call-done) | data formatting | bytes 7798784 | tf_op jit(solution)/shard_map/all_gather | solution.py:73
  259.8 7.0 %reshape.290 = bf16[544,3584]{1,0:T(8,128)(2,1)} reshape(bf16[8,4,476,128]{3,2,1,0:T(8,128)(2,1)} %copy.10) | data formatting | bytes 7798784 | tf_op jit(solution)/shard_map/reshape | solution.py:75
  271.6 12.0 %all_to_all.26 = bf16[8,68,128]{2,1,0:T(8,128)(2,1)S(1)} all-to-all(bf16[8,68,128]{2,1,0:T(8,128)(2,1)S(1)} %reshape.291), channel_id=1, replica_groups=mesh['pipe'=16,'ex'=4,'ey'=8] {'ey'}, dimensions={0} | all-to-all | bytes 278528 | tf_op jit(solution)/shard_map/all_to_all | solution.py:80
  294.8 4.0 %all-to-all-start.4 = ((f32[4,476,128]{2,1,0:T(8,128)}), f32[4,476,128]{2,1,0:T(8,128)S(1)}, u32[]{:S(2)}, u32[]{:S(2)}) async-start(f32[4,476,128]{2,1,0:T(8,128)} %reshape.292), calls=%async_computation.4 | async-start | bytes 1966080 | tf_op jit(solution)/shard_map/all_to_all | solution.py:89
  298.8 4.0 %collective-permute-start.7 = (bf16[64,3584]{1,0:T(8,128)(2,1)S(1)}, bf16[64,3584]{1,0:T(8,128)(2,1)}, u32[]{:S(2)}, u32[]{:S(2)}) collective-permute-start(bf16[64,3584]{1,0:T(8,128)(2,1)S(1)} %get-tuple-element.7), channel_id=1, source_target_pairs={{0,32},{32,64},{64,96},{96,128},{128,160},{160,192},{192,224},{224... | collective-permute-start | bytes 1376264 | tf_op jit(solution)/shard_map/ppermute | solution.py:19
  302.8 7.4 %all-to-all-done.4 = f32[4,476,128]{2,1,0:T(8,128)S(1)} async-done(((f32[4,476,128]{2,1,0:T(8,128)}), f32[4,476,128]{2,1,0:T(8,128)S(1)}, u32[]{:S(2)}, u32[]{:S(2)}) %all-to-all-start.4) | async-done | bytes 974880 | tf_op jit(solution)/shard_map/all_to_all | solution.py:89
  (115 shorter events, 67.2 us)
Async XLA Ops:
  6.5 112.8 %copy-start = (bf16[1,1,3584,128]{3,2,1,0:T(8,128)(2,1)S(1)}, bf16[1,1,3584,128]{3,2,1,0:T(8,128)(2,1)}, u32[]{:S(2)}) copy-start(bf16[1,1,3584,128]{3,2,1,0:T(8,128)(2,1)} %param.11) | copy-start | bytes 2752516
  6.5 17.6 %copy-start.4 = (bf16[1,1,128,3584]{3,2,1,0:T(8,128)(2,1)S(1)}, bf16[1,1,128,3584]{3,2,1,0:T(8,128)(2,1)}, u32[]{:S(2)}) copy-start(bf16[1,1,128,3584]{3,2,1,0:T(8,128)(2,1)} %param.13) | copy-start | bytes 2752516
  6.5 61.4 %copy-start.9 = (s32[1,2,64,1]{2,3,1,0:T(1,128)S(1)}, s32[1,2,64,1]{2,3,1,0:T(1,128)}, u32[]{:S(2)}) copy-start(s32[1,2,64,1]{2,3,1,0:T(1,128)} %param.15) | copy-start | bytes 1540
  6.5 105.8 %all-gather.6.cloned.1.call-start = ((), (), s32[]{:S(2)}) async-start(), calls=%async_computation.6 | async-start | bytes 4423680 | tf_op jit(solution)/shard_map/all_gather | solution.py:73
  24.1 22.6 %collective-permute-start.3 = (bf16[128,3584]{1,0:T(8,128)(2,1)S(1)}, bf16[128,3584]{1,0:T(8,128)(2,1)S(1)}, u32[]{:S(2)}, u32[]{:S(2)}) collective-permute-start(bf16[128,3584]{1,0:T(8,128)(2,1)S(1)} %bitcast.138), channel_id=1, source_target_pairs={{0,1},{1,2},{2,3},{3,4},{4,5},{5,6},{6,7},{7,0},{8,9},{9,10},{10,1... | collective-permute-start | bytes 2752520 | tf_op jit(solution)/shard_map/ppermute | solution.py:19
  28.8 39.2 %collective-permute-start = (bf16[128,3584]{1,0:T(8,128)(2,1)S(1)}, bf16[128,3584]{1,0:T(8,128)(2,1)}, u32[]{:S(2)}, u32[]{:S(2)}) collective-permute-start(bf16[128,3584]{1,0:T(8,128)(2,1)S(1)} %bitcast.139), channel_id=1, source_target_pairs={{0,7},{1,0},{2,1},{3,2},{4,3},{5,4},{6,5},{7,6},{8,15},{9,8},{10,9... | collective-permute-start | bytes 2752520 | tf_op jit(solution)/shard_map/ppermute | solution.py:19
  46.7 95.2 %copy-start.6 = (bf16[128,3584]{1,0:T(8,128)(2,1)}, bf16[128,3584]{1,0:T(8,128)(2,1)S(1)}, u32[]{:S(2)}) copy-start(bf16[128,3584]{1,0:T(8,128)(2,1)S(1)} %collective-permute-done.3) | copy-start | bytes 2752516
  46.7 46.6 %collective-permute-start.4 = (bf16[128,3584]{1,0:T(8,128)(2,1)S(1)}, bf16[128,3584]{1,0:T(8,128)(2,1)}, u32[]{:S(2)}, u32[]{:S(2)}) collective-permute-start(bf16[128,3584]{1,0:T(8,128)(2,1)S(1)} %collective-permute-done.3), channel_id=1, source_target_pairs={{0,1},{1,2},{2,3},{3,4},{4,5},{5,6},{6,7},{7,0},{8,9},{9,10},{10,1... | collective-permute-start | bytes 2752520 | tf_op jit(solution)/shard_map/ppermute | solution.py:19
  52.4 113.0 %collective-permute-start.9 = (bf16[3584]{0:T(1024)(128)(2,1)S(1)}, bf16[3584]{0:T(1024)(128)(2,1)S(1)}, u32[]{:S(2)}, u32[]{:S(2)}) collective-permute-start(bf16[3584]{0:T(1024)(128)(2,1)S(1)} %reduce), channel_id=1, source_target_pairs={{0,480},{32,0},{64,32},{96,64},{128,96},{160,128},{192,160},{224,1... | collective-permute-start | bytes 21512 | tf_op jit(solution)/shard_map/ppermute | solution.py:19
  64.0 101.0 %collective-permute-start.8 = (s32[64,1]{0,1:T(1,128)S(1)}, s32[64,1]{0,1:T(1,128)S(1)}, u32[]{:S(2)}, u32[]{:S(2)}) collective-permute-start(s32[64,1]{0,1:T(1,128)S(1)} %get-tuple-element.17), channel_id=1, source_target_pairs={{0,480},{32,0},{64,32},{96,64},{128,96},{160,128},{192,160},{224,1... | collective-permute-start | bytes 776 | tf_op jit(solution)/shard_map/ppermute | solution.py:19
  68.0 62.0 %collective-permute-start.1 = (bf16[128,3584]{1,0:T(8,128)(2,1)}, bf16[128,3584]{1,0:T(8,128)(2,1)}, u32[]{:S(2)}, u32[]{:S(2)}) collective-permute-start(bf16[128,3584]{1,0:T(8,128)(2,1)} %collective-permute-done), channel_id=1, source_target_pairs={{0,7},{1,0},{2,1},{3,2},{4,3},{5,4},{6,5},{7,6},{8,15},{9,8},{10,9... | collective-permute-start | bytes 2752520 | tf_op jit(solution)/shard_map/ppermute | solution.py:19
  93.2 41.3 %collective-permute-start.5 = (bf16[128,3584]{1,0:T(8,128)(2,1)}, bf16[128,3584]{1,0:T(8,128)(2,1)}, u32[]{:S(2)}, u32[]{:S(2)}) collective-permute-start(bf16[128,3584]{1,0:T(8,128)(2,1)} %collective-permute-done.4), channel_id=1, source_target_pairs={{0,1},{1,2},{2,3},{3,4},{4,5},{5,6},{6,7},{7,0},{8,9},{9,10},{10,1... | collective-permute-start | bytes 2752520 | tf_op jit(solution)/shard_map/ppermute | solution.py:19
  124.7 13.3 %all-to-all-start.1 = ((bf16[8,68,128]{2,1,0:T(8,128)(2,1)}), bf16[8,68,128]{2,1,0:T(8,128)(2,1)S(1)}, u32[]{:S(2)}, u32[]{:S(2)}) async-start(bf16[8,68,128]{2,1,0:T(8,128)(2,1)} %reshape.285), calls=%async_computation.1 | async-start | bytes 294912 | tf_op jit(solution)/shard_map/all_to_all | solution.py:80
  130.0 25.7 %collective-permute-start.2 = (bf16[128,3584]{1,0:T(8,128)(2,1)}, bf16[128,3584]{1,0:T(8,128)(2,1)}, u32[]{:S(2)}, u32[]{:S(2)}) collective-permute-start(bf16[128,3584]{1,0:T(8,128)(2,1)} %collective-permute-done.1), channel_id=1, source_target_pairs={{0,7},{1,0},{2,1},{3,2},{4,3},{5,4},{6,5},{7,6},{8,15},{9,8},{10,9... | collective-permute-start | bytes 2752520 | tf_op jit(solution)/shard_map/ppermute | solution.py:19
  134.6 23.9 %collective-permute-start.6 = (bf16[128,3584]{1,0:T(8,128)(2,1)}, bf16[128,3584]{1,0:T(8,128)(2,1)}, u32[]{:S(2)}, u32[]{:S(2)}) collective-permute-start(bf16[128,3584]{1,0:T(8,128)(2,1)} %collective-permute-done.5), channel_id=1, source_target_pairs={{0,1},{1,2},{2,3},{3,4},{4,5},{5,6},{6,7},{7,0},{8,9},{9,10},{10,1... | collective-permute-start | bytes 2752520 | tf_op jit(solution)/shard_map/ppermute | solution.py:19
  161.1 15.5 %all-to-all-start.2 = ((f32[4,476,128]{2,1,0:T(8,128)}), f32[4,476,128]{2,1,0:T(8,128)S(1)}, u32[]{:S(2)}, u32[]{:S(2)}) async-start(f32[4,476,128]{2,1,0:T(8,128)} %reshape.286), calls=%async_computation.2 | async-start | bytes 1966080 | tf_op jit(solution)/shard_map/all_to_all | solution.py:89
  164.9 90.3 %all-gather.4.cloned.1.call-start = ((), (), s32[]{:S(2)}) async-start(), calls=%async_computation.5 | async-start | bytes 4386816 | tf_op jit(solution)/shard_map/all_gather | solution.py:73
  181.1 15.4 %collective-permute-start.10 = (bf16[476,128]{1,0:T(8,128)(2,1)S(1)}, bf16[476,128]{1,0:T(8,128)(2,1)S(1)}, u32[]{:S(2)}, u32[]{:S(2)}) collective-permute-start(bf16[476,128]{1,0:T(8,128)(2,1)S(1)} %get-tuple-element.8), channel_id=1, source_target_pairs={{0,32},{8,40},{16,48},{24,56},{32,64},{40,72},{48,80},{56,88},{64,... | collective-permute-start | bytes 365576 | tf_op jit(solution)/shard_map/ppermute | solution.py:62
  186.2 10.4 %collective-permute-start.11 = (bf16[476,128]{1,0:T(8,128)(2,1)S(1)}, bf16[476,128]{1,0:T(8,128)(2,1)S(1)}, u32[]{:S(2)}, u32[]{:S(2)}) collective-permute-start(bf16[476,128]{1,0:T(8,128)(2,1)S(1)} %get-tuple-element.11), channel_id=1, source_target_pairs={{0,40},{8,48},{16,56},{24,32},{32,72},{40,80},{48,88},{56,64},{64,... | collective-permute-start | bytes 365576 | tf_op jit(solution)/shard_map/ppermute | solution.py:62
  188.1 8.5 %collective-permute-start.12 = (bf16[476,128]{1,0:T(8,128)(2,1)S(1)}, bf16[476,128]{1,0:T(8,128)(2,1)S(1)}, u32[]{:S(2)}, u32[]{:S(2)}) collective-permute-start(bf16[476,128]{1,0:T(8,128)(2,1)S(1)} %get-tuple-element.10), channel_id=1, source_target_pairs={{0,48},{8,56},{16,32},{24,40},{32,80},{40,88},{48,64},{56,72},{64,... | collective-permute-start | bytes 365576 | tf_op jit(solution)/shard_map/ppermute | solution.py:62
  193.8 7.3 %collective-permute-start.13 = (bf16[476,128]{1,0:T(8,128)(2,1)S(1)}, bf16[476,128]{1,0:T(8,128)(2,1)S(1)}, u32[]{:S(2)}, u32[]{:S(2)}) collective-permute-start(bf16[476,128]{1,0:T(8,128)(2,1)S(1)} %get-tuple-element.9), channel_id=1, source_target_pairs={{0,56},{8,32},{16,40},{24,48},{32,88},{40,64},{48,72},{56,80},{64,... | collective-permute-start | bytes 365576 | tf_op jit(solution)/shard_map/ppermute | solution.py:62
  271.5 16.0 %copy-start.7 = (bf16[128,3584]{1,0:T(8,128)(2,1)S(1)}, bf16[128,3584]{1,0:T(8,128)(2,1)}, u32[]{:S(2)}) copy-start(bf16[128,3584]{1,0:T(8,128)(2,1)} %copy-done.6) | copy-start | bytes 2752516
  294.8 15.4 %all-to-all-start.4 = ((f32[4,476,128]{2,1,0:T(8,128)}), f32[4,476,128]{2,1,0:T(8,128)S(1)}, u32[]{:S(2)}, u32[]{:S(2)}) async-start(f32[4,476,128]{2,1,0:T(8,128)} %reshape.292), calls=%async_computation.4 | async-start | bytes 1966080 | tf_op jit(solution)/shard_map/all_to_all | solution.py:89
  298.8 12.5 %collective-permute-start.7 = (bf16[64,3584]{1,0:T(8,128)(2,1)S(1)}, bf16[64,3584]{1,0:T(8,128)(2,1)}, u32[]{:S(2)}, u32[]{:S(2)}) collective-permute-start(bf16[64,3584]{1,0:T(8,128)(2,1)S(1)} %get-tuple-element.7), channel_id=1, source_target_pairs={{0,32},{32,64},{64,96},{96,128},{128,160},{160,192},{192,224},{224... | collective-permute-start | bytes 1376264 | tf_op jit(solution)/shard_map/ppermute | solution.py:19
  (7 other events, 36.7 us)
Sparse Core Ops, SparseCore 0:
  24.2 88.0 all-gather.5
  203.1 52.0 all-gather.3

commit v10 on v8

--- a/solution.py
+++ b/solution.py
@@ -63,11 +63,16 @@
     hidden_here = lax.all_to_all(hidden, "ey", split_axis=0, concat_axis=0, tiled=True)
     me_y = lax.axis_index("ey")
     hidden_rel = jnp.take(hidden_here, (me_y + jnp.arange(n_y)) % n_y, axis=0)
-    expert_out = None
-    for d in range(n_y):
-        part = jnp.dot(hidden_rel[d], down_all[d], preferred_element_type=jnp.float32)
-        part = lax.reduce_precision(part, exponent_bits=8, mantissa_bits=7)
-        expert_out = part if expert_out is None else expert_out + part
+    if isinstance(down_all, list):
+        expert_out = None
+        for d in range(n_y):
+            part = jnp.dot(hidden_rel[d], down_all[d], preferred_element_type=jnp.float32)
+            part = lax.reduce_precision(part, exponent_bits=8, mantissa_bits=7)
+            expert_out = part if expert_out is None else expert_out + part
+    else:
+        parts = jnp.einsum("jrh,jhd->jrd", hidden_rel, down_all, preferred_element_type=jnp.float32)
+        parts = lax.reduce_precision(parts, exponent_bits=8, mantissa_bits=7)
+        expert_out = jnp.sum(parts, axis=0)
     expert_out = expert_out.reshape(n_x, block_rows, LANE)
     returned = lax.all_to_all(expert_out, "ex", split_axis=0, concat_axis=0, tiled=True)
     picked = returned.reshape(EXPERTS * MOST, model_width)[slot_ids]
@@ -95,8 +100,10 @@
     )
     first_out = (values + branch).astype(jnp.bfloat16)
     arrived = shifted(first_out, "pipe", 1)
+    first_out, down_all = lax.optimization_barrier((first_out, down_all))
+    down_stack = jnp.stack(down_all, axis=0)
     values, branch = layer_terms(
-        arrived, gain_row, w_gate, w_up, down_all, route_ids[0, 1], route_wts[0, 1]
+        arrived, gain_row, w_gate, w_up, down_stack, route_ids[0, 1], route_wts[0, 1]
     )
     second = (values + branch).astype(jnp.bfloat16)
     result_rows = jnp.where(section_index == 0, arrived, second)

time: 320 us -> 318 us (level)
  local copies, waits for them, and re-layouts: 23.2 us -> 39.1 us
  blocking collectives: 33.4 us -> 21.4 us
  waiting for transfers between devices: 166 us -> 157 us
  starting transfers between devices: 45.1 us -> 49.6 us
    all_gather x2, waiting for transfers between devices: 73.4 us -> 57.4 us  [routed_branch(): slot_rows = lax.all_gather(from_x, 'ey', axis=0, tiled=False)]
    unnamed x24 -> x23, local copies, waits for them, and re-layouts: 0.22 us -> 15.3 us
    all_to_all x1 -> x0, blocking collectives: 12 us -> none  [routed_branch(): lax.all_to_all(hidden, 'ey', split_axis=0, concat_axis=0, tiled=True)]
    dot_general x16 -> x8, matrix products: 18.8 us -> 9.38 us  [routed_branch(): jnp.dot(hidden_rel[d], down_all[d], preferred_element_type=jnp.float32)]
    all_to_all x1 -> x2, waiting for transfers between devices: 1.54 us -> 8.4 us  [routed_branch(): lax.all_to_all(hidden, 'ey', split_axis=0, concat_axis=0, tiled=True)]
    dot_general x0 -> x1, matrix products: none -> 4.46 us  [routed_branch(): jnp.einsum('jrh,jhd->jrd', hidden_rel, down_all, preferred_element_type=j...]
    dot_general x2, matrix products: 2.34 us -> 6.8 us  [routed_branch(): up_act = jnp.dot(flat_rows, w_up, preferred_element_type=jnp.float32)]
    all_to_all x1 -> x2, starting transfers between devices: 5.26 us -> 9.48 us  [routed_branch(): lax.all_to_all(hidden, 'ey', split_axis=0, concat_axis=0, tiled=True)]
  transfers between devices with their start and end apart: 13 -> 14, of which waited for: 10 -> 11; matrix products, arithmetic and copies ran while one was open for 7% -> 13% of each run, Pallas kernels for 0% -> 0%
where the time goes in v10:
time: 318 us; the launch traced here: 314 us
  waiting for transfers between devices  157 us (49%)
  starting transfers between devices  49.6 us (16%)
  local copies, waits for them, and re-layouts  39.1 us (12%)
  matrix products  29.1 us (9%)
  blocking collectives  21.4 us (7%)
  between operations  13.8 us (4%)
  other arithmetic  4.77 us (1%)
    ppermute x8, waiting for transfers between devices, shifted(): return lax.ppermute(value, axis, pairs)  67.9 us
    all_gather x2, waiting for transfers between devices, routed_branch(): slot_rows = lax.all_gather(from_x, 'ey', axis=0, tiled=False)  57.4 us
    ppermute x8, starting transfers between devices, shifted(): return lax.ppermute(value, axis, pairs)  32.6 us
    all_to_all x2, waiting for transfers between devices, routed_branch(): lax.all_to_all(expert_out, 'ex', split_axis=0, concat_axis=0, tiled=True)  23 us
    all_to_all x2, blocking collectives, routed_branch(): lax.all_to_all(per_expert, 'ex', split_axis=0, concat_axis=0, tiled=True)  21.4 us
    unnamed x23, local copies, waits for them, and re-layouts  15.3 us
    reshape x2, local copies, waits for them, and re-layouts, routed_branch(): flat_rows = slot_rows.reshape(-1, model_width)  14 us
    all_to_all x2, starting transfers between devices, routed_branch(): lax.all_to_all(hidden, 'ey', split_axis=0, concat_axis=0, tiled=True)  9.48 us
  transfers between devices with their start and end apart: 14, of which 11 were waited for; matrix products, arithmetic and copies ran while one was open for 13% of the time, Pallas kernels for 0%

profile of v10, /device:TPU:1, one launch (start us, length us, event | category | flops | bytes accessed | tf_op | source)
XLA Modules:
  0.0 314.4 jit_solution(12161633762439090799)
XLA Ops:
  12.5 11.5 %all_to_all.30 = bf16[4,476,128]{2,1,0:T(8,128)(2,1)} all-to-all(bf16[4,476,128]{2,1,0:T(8,128)(2,1)S(1)} %reshape.215), channel_id=1, replica_groups=mesh['pipe'=16,'ex'=4,'ey'=8] {'ex'}, dimensions={0} | all-to-all | bytes 974848 | tf_op jit(solution)/shard_map/all_to_all | solution.py:55
  24.0 4.7 %collective-permute-start.3 = (bf16[128,3584]{1,0:T(8,128)(2,1)}, bf16[128,3584]{1,0:T(8,128)(2,1)S(1)}, u32[]{:S(2)}, u32[]{:S(2)}) collective-permute-start(bf16[128,3584]{1,0:T(8,128)(2,1)} %bitcast.103), channel_id=1, source_target_pairs={{0,1},{1,2},{2,3},{3,4},{4,5},{5,6},{6,7},{7,0},{8,9},{9,10},{10,1... | collective-permute-start | bytes 2752520 | tf_op jit(solution)/shard_map/ppermute | solution.py:19
  28.7 3.8 %collective-permute-start = (bf16[128,3584]{1,0:T(8,128)(2,1)}, bf16[128,3584]{1,0:T(8,128)(2,1)}, u32[]{:S(2)}, u32[]{:S(2)}) collective-permute-start(bf16[128,3584]{1,0:T(8,128)(2,1)} %bitcast.104), channel_id=1, source_target_pairs={{0,7},{1,0},{2,1},{3,2},{4,3},{5,4},{6,5},{7,6},{8,15},{9,8},{10,9... | collective-permute-start | bytes 2752520 | tf_op jit(solution)/shard_map/ppermute | solution.py:19
  32.5 14.3 %collective-permute-done.3 = bf16[128,3584]{1,0:T(8,128)(2,1)S(1)} collective-permute-done((bf16[128,3584]{1,0:T(8,128)(2,1)}, bf16[128,3584]{1,0:T(8,128)(2,1)S(1)}, u32[]{:S(2)}, u32[]{:S(2)}) %collective-permute-start.3) | collective-permute-done | bytes 917536 | tf_op jit(solution)/shard_map/ppermute | solution.py:19
  46.8 6.0 %collective-permute-start.4 = (bf16[128,3584]{1,0:T(8,128)(2,1)S(1)}, bf16[128,3584]{1,0:T(8,128)(2,1)}, u32[]{:S(2)}, u32[]{:S(2)}) collective-permute-start(bf16[128,3584]{1,0:T(8,128)(2,1)S(1)} %collective-permute-done.3), channel_id=1, source_target_pairs={{0,1},{1,2},{2,3},{3,4},{4,5},{5,6},{6,7},{7,0},{8,9},{9,10},{10,1... | collective-permute-start | bytes 2752520 | tf_op jit(solution)/shard_map/ppermute | solution.py:19
  52.8 4.4 %collective-permute-start.1 = (bf16[128,3584]{1,0:T(8,128)(2,1)}, bf16[128,3584]{1,0:T(8,128)(2,1)}, u32[]{:S(2)}, u32[]{:S(2)}) collective-permute-start(bf16[128,3584]{1,0:T(8,128)(2,1)} %collective-permute-done), channel_id=1, source_target_pairs={{0,7},{1,0},{2,1},{3,2},{4,3},{5,4},{6,5},{7,6},{8,15},{9,8},{10,9... | collective-permute-start | bytes 2752520 | tf_op jit(solution)/shard_map/ppermute | solution.py:19
  57.2 36.3 %collective-permute-done.4 = bf16[128,3584]{1,0:T(8,128)(2,1)} collective-permute-done((bf16[128,3584]{1,0:T(8,128)(2,1)S(1)}, bf16[128,3584]{1,0:T(8,128)(2,1)}, u32[]{:S(2)}, u32[]{:S(2)}) %collective-permute-start.4) | collective-permute-done | bytes 917536 | tf_op jit(solution)/shard_map/ppermute | solution.py:19
  95.5 16.9 %all-gather.5.cloned.1.call-done = bf16[32,476,128]{2,1,0:T(8,128)(2,1)} async-done(((bf16[4,476,128]{2,1,0:T(8,128)(2,1)}), bf16[32,476,128]{2,1,0:T(8,128)(2,1)}) %all-gather.5.cloned.1.call-update) | async-done | bytes 3899408 | tf_op jit(solution)/shard_map/all_gather | solution.py:56
  112.3 7.0 %reshape.216 = bf16[544,3584]{1,0:T(8,128)(2,1)} reshape(bf16[32,476,128]{2,1,0:T(8,128)(2,1)} %all-gather.5.cloned.1.call-done) | data formatting | bytes 7798784 | tf_op jit(solution)/shard_map/reshape | solution.py:58
  126.9 5.3 %all-to-all-start.1 = ((bf16[8,68,128]{2,1,0:T(8,128)(2,1)}), bf16[8,68,128]{2,1,0:T(8,128)(2,1)S(1)}, u32[]{:S(2)}, u32[]{:S(2)}) async-start(bf16[8,68,128]{2,1,0:T(8,128)(2,1)} %reshape.217), calls=%async_computation.1 | async-start | bytes 294912 | tf_op jit(solution)/shard_map/all_to_all | solution.py:63
  132.3 4.6 %collective-permute-start.2 = (bf16[128,3584]{1,0:T(8,128)(2,1)}, bf16[128,3584]{1,0:T(8,128)(2,1)}, u32[]{:S(2)}, u32[]{:S(2)}) collective-permute-start(bf16[128,3584]{1,0:T(8,128)(2,1)} %collective-permute-done.1), channel_id=1, source_target_pairs={{0,7},{1,0},{2,1},{3,2},{4,3},{5,4},{6,5},{7,6},{8,15},{9,8},{10,9... | collective-permute-start | bytes 2752520 | tf_op jit(solution)/shard_map/ppermute | solution.py:19
  147.5 10.5 %collective-permute-done.2 = bf16[128,3584]{1,0:T(8,128)(2,1)} collective-permute-done((bf16[128,3584]{1,0:T(8,128)(2,1)}, bf16[128,3584]{1,0:T(8,128)(2,1)}, u32[]{:S(2)}, u32[]{:S(2)}) %collective-permute-start.2) | collective-permute-done | bytes 917536 | tf_op jit(solution)/shard_map/ppermute | solution.py:19
  163.4 3.6 %all-to-all-start.2 = ((f32[4,476,128]{2,1,0:T(8,128)}), f32[4,476,128]{2,1,0:T(8,128)S(1)}, u32[]{:S(2)}, u32[]{:S(2)}) async-start(f32[4,476,128]{2,1,0:T(8,128)} %reshape.218), calls=%async_computation.2 | async-start | bytes 1966080 | tf_op jit(solution)/shard_map/all_to_all | solution.py:77
  167.1 11.6 %all-to-all-done.2 = f32[4,476,128]{2,1,0:T(8,128)S(1)} async-done(((f32[4,476,128]{2,1,0:T(8,128)}), f32[4,476,128]{2,1,0:T(8,128)S(1)}, u32[]{:S(2)}, u32[]{:S(2)}) %all-to-all-start.2) | async-done | bytes 974880 | tf_op jit(solution)/shard_map/all_to_all | solution.py:77
  179.9 5.3 %collective-permute-start.7 = (bf16[64,3584]{1,0:T(8,128)(2,1)S(1)}, bf16[64,3584]{1,0:T(8,128)(2,1)S(1)}, u32[]{:S(2)}, u32[]{:S(2)}) collective-permute-start(bf16[64,3584]{1,0:T(8,128)(2,1)S(1)} %fusion.16), channel_id=1, source_target_pairs={{0,32},{32,64},{64,96},{96,128},{128,160},{160,192},{192,224},{224... | collective-permute-start | bytes 1376264 | tf_op jit(solution)/shard_map/ppermute | solution.py:19
  185.1 5.4 %collective-permute-done.7 = bf16[64,3584]{1,0:T(8,128)(2,1)S(1)} collective-permute-done((bf16[64,3584]{1,0:T(8,128)(2,1)S(1)}, bf16[64,3584]{1,0:T(8,128)(2,1)S(1)}, u32[]{:S(2)}, u32[]{:S(2)}) %collective-permute-start.7) | collective-permute-done | bytes 458784 | tf_op jit(solution)/shard_map/ppermute | solution.py:19
  191.8 9.9 %all_to_all.31 = bf16[4,476,128]{2,1,0:T(8,128)(2,1)} all-to-all(bf16[4,476,128]{2,1,0:T(8,128)(2,1)S(1)} %reshape.220), channel_id=1, replica_groups=mesh['pipe'=16,'ex'=4,'ey'=8] {'ex'}, dimensions={0} | all-to-all | bytes 974848 | tf_op jit(solution)/shard_map/all_to_all | solution.py:55
  217.0 40.6 %all-gather.7.cloned.1.call-done = bf16[32,476,128]{2,1,0:T(8,128)(2,1)} async-done(((bf16[4,476,128]{2,1,0:T(8,128)(2,1)}), bf16[32,476,128]{2,1,0:T(8,128)(2,1)}) %all-gather.7.cloned.1.call-update) | async-done | bytes 3899408 | tf_op jit(solution)/shard_map/all_gather | solution.py:56
  257.6 7.0 %reshape.221 = bf16[544,3584]{1,0:T(8,128)(2,1)} reshape(bf16[32,476,128]{2,1,0:T(8,128)(2,1)} %all-gather.7.cloned.1.call-done) | data formatting | bytes 7798784 | tf_op jit(solution)/shard_map/reshape | solution.py:58
  271.9 4.2 %all-to-all-start.4 = ((bf16[8,68,128]{2,1,0:T(8,128)(2,1)}), bf16[8,68,128]{2,1,0:T(8,128)(2,1)S(1)}, u32[]{:S(2)}, u32[]{:S(2)}) async-start(bf16[8,68,128]{2,1,0:T(8,128)(2,1)} %reshape.222), calls=%async_computation.4 | async-start | bytes 294912 | tf_op jit(solution)/shard_map/all_to_all | solution.py:63
  277.2 6.9 %all-to-all-done.4 = bf16[8,68,128]{2,1,0:T(8,128)(2,1)S(1)} async-done(((bf16[8,68,128]{2,1,0:T(8,128)(2,1)}), bf16[8,68,128]{2,1,0:T(8,128)(2,1)S(1)}, u32[]{:S(2)}, u32[]{:S(2)}) %all-to-all-start.4) | async-done | bytes 139296 | tf_op jit(solution)/shard_map/all_to_all | solution.py:63
  284.6 4.5 %reduce-precision_reduce_fusion = f32[68,3584]{1,0:T(8,128)S(1)} fusion(bf16[8,128,3584]{2,1,0:T(8,128)(2,1)} %bitcast_dynamic-update-slice_fusion, bf16[8,68,128]{2,1,0:T(8,128)(2,1)S(1)} %gather_fusion.3, pred[8]{0:T(512)(128)(4,1)S(1)} %compare_and_fusion), kind=kOutput, calls=%fused_computation.4 | convolution fusion | flops 502847488 | bytes 8454152 | tf_op jit(solution)/shard_map/jrh,jhd->jrd/dot_general | solution.py:73
  290.1 4.0 %all-to-all-start.5 = ((f32[4,476,128]{2,1,0:T(8,128)}), f32[4,476,128]{2,1,0:T(8,128)S(1)}, u32[]{:S(2)}, u32[]{:S(2)}) async-start(f32[4,476,128]{2,1,0:T(8,128)} %reshape.223), calls=%async_computation.5 | async-start | bytes 1966080 | tf_op jit(solution)/shard_map/all_to_all | solution.py:77
  294.1 11.4 %all-to-all-done.5 = f32[4,476,128]{2,1,0:T(8,128)S(1)} async-done(((f32[4,476,128]{2,1,0:T(8,128)}), f32[4,476,128]{2,1,0:T(8,128)S(1)}, u32[]{:S(2)}, u32[]{:S(2)}) %all-to-all-start.5) | async-done | bytes 974880 | tf_op jit(solution)/shard_map/all_to_all | solution.py:77
  (83 shorter events, 61.2 us)
Async XLA Ops:
  6.5 112.8 %copy-start = (bf16[1,1,3584,128]{3,2,1,0:T(8,128)(2,1)S(1)}, bf16[1,1,3584,128]{3,2,1,0:T(8,128)(2,1)}, u32[]{:S(2)}) copy-start(bf16[1,1,3584,128]{3,2,1,0:T(8,128)(2,1)} %param.11) | copy-start | bytes 2752516
  6.5 105.8 %all-gather.5.cloned.1.call-start = ((), (), s32[]{:S(2)}) async-start(), calls=%async_computation.6 | async-start | bytes 4423680 | tf_op jit(solution)/shard_map/all_gather | solution.py:56
  24.0 22.7 %collective-permute-start.3 = (bf16[128,3584]{1,0:T(8,128)(2,1)}, bf16[128,3584]{1,0:T(8,128)(2,1)S(1)}, u32[]{:S(2)}, u32[]{:S(2)}) collective-permute-start(bf16[128,3584]{1,0:T(8,128)(2,1)} %bitcast.103), channel_id=1, source_target_pairs={{0,1},{1,2},{2,3},{3,4},{4,5},{5,6},{6,7},{7,0},{8,9},{9,10},{10,1... | collective-permute-start | bytes 2752520 | tf_op jit(solution)/shard_map/ppermute | solution.py:19
  28.7 24.1 %collective-permute-start = (bf16[128,3584]{1,0:T(8,128)(2,1)}, bf16[128,3584]{1,0:T(8,128)(2,1)}, u32[]{:S(2)}, u32[]{:S(2)}) collective-permute-start(bf16[128,3584]{1,0:T(8,128)(2,1)} %bitcast.104), channel_id=1, source_target_pairs={{0,7},{1,0},{2,1},{3,2},{4,3},{5,4},{6,5},{7,6},{8,15},{9,8},{10,9... | collective-permute-start | bytes 2752520 | tf_op jit(solution)/shard_map/ppermute | solution.py:19
  46.8 94.5 %copy-start.3 = (bf16[128,3584]{1,0:T(8,128)(2,1)}, bf16[128,3584]{1,0:T(8,128)(2,1)S(1)}, u32[]{:S(2)}) copy-start(bf16[128,3584]{1,0:T(8,128)(2,1)S(1)} %collective-permute-done.3) | copy-start | bytes 2752516
  46.8 46.8 %collective-permute-start.4 = (bf16[128,3584]{1,0:T(8,128)(2,1)S(1)}, bf16[128,3584]{1,0:T(8,128)(2,1)}, u32[]{:S(2)}, u32[]{:S(2)}) collective-permute-start(bf16[128,3584]{1,0:T(8,128)(2,1)S(1)} %collective-permute-done.3), channel_id=1, source_target_pairs={{0,1},{1,2},{2,3},{3,4},{4,5},{5,6},{6,7},{7,0},{8,9},{9,10},{10,1... | collective-permute-start | bytes 2752520 | tf_op jit(solution)/shard_map/ppermute | solution.py:19
  52.8 79.5 %collective-permute-start.1 = (bf16[128,3584]{1,0:T(8,128)(2,1)}, bf16[128,3584]{1,0:T(8,128)(2,1)}, u32[]{:S(2)}, u32[]{:S(2)}) collective-permute-start(bf16[128,3584]{1,0:T(8,128)(2,1)} %collective-permute-done), channel_id=1, source_target_pairs={{0,7},{1,0},{2,1},{3,2},{4,3},{5,4},{6,5},{7,6},{8,15},{9,8},{10,9... | collective-permute-start | bytes 2752520 | tf_op jit(solution)/shard_map/ppermute | solution.py:19
  93.5 43.3 %collective-permute-start.5 = (bf16[128,3584]{1,0:T(8,128)(2,1)}, bf16[128,3584]{1,0:T(8,128)(2,1)}, u32[]{:S(2)}, u32[]{:S(2)}) collective-permute-start(bf16[128,3584]{1,0:T(8,128)(2,1)} %collective-permute-done.4), channel_id=1, source_target_pairs={{0,1},{1,2},{2,3},{3,4},{4,5},{5,6},{6,7},{7,0},{8,9},{9,10},{10,1... | collective-permute-start | bytes 2752520 | tf_op jit(solution)/shard_map/ppermute | solution.py:19
  119.4 21.7 %copy-start.2 = (bf16[1,1,128,3584]{3,2,1,0:T(8,128)(2,1)S(1)}, bf16[1,1,128,3584]{3,2,1,0:T(8,128)(2,1)}, u32[]{:S(2)}) copy-start(bf16[1,1,128,3584]{3,2,1,0:T(8,128)(2,1)} %param.13) | copy-start | bytes 2752516
  126.9 13.4 %all-to-all-start.1 = ((bf16[8,68,128]{2,1,0:T(8,128)(2,1)}), bf16[8,68,128]{2,1,0:T(8,128)(2,1)S(1)}, u32[]{:S(2)}, u32[]{:S(2)}) async-start(bf16[8,68,128]{2,1,0:T(8,128)(2,1)} %reshape.217), calls=%async_computation.1 | async-start | bytes 294912 | tf_op jit(solution)/shard_map/all_to_all | solution.py:63
  132.3 25.7 %collective-permute-start.2 = (bf16[128,3584]{1,0:T(8,128)(2,1)}, bf16[128,3584]{1,0:T(8,128)(2,1)}, u32[]{:S(2)}, u32[]{:S(2)}) collective-permute-start(bf16[128,3584]{1,0:T(8,128)(2,1)} %collective-permute-done.1), channel_id=1, source_target_pairs={{0,7},{1,0},{2,1},{3,2},{4,3},{5,4},{6,5},{7,6},{8,15},{9,8},{10,9... | collective-permute-start | bytes 2752520 | tf_op jit(solution)/shard_map/ppermute | solution.py:19
  136.9 24.0 %collective-permute-start.6 = (bf16[128,3584]{1,0:T(8,128)(2,1)}, bf16[128,3584]{1,0:T(8,128)(2,1)}, u32[]{:S(2)}, u32[]{:S(2)}) collective-permute-start(bf16[128,3584]{1,0:T(8,128)(2,1)} %collective-permute-done.5), channel_id=1, source_target_pairs={{0,1},{1,2},{2,3},{3,4},{4,5},{5,6},{6,7},{7,0},{8,9},{9,10},{10,1... | collective-permute-start | bytes 2752520 | tf_op jit(solution)/shard_map/ppermute | solution.py:19
  146.0 21.0 %copy-start.5 = (s32[1,2,64,1]{2,3,1,0:T(1,128)S(1)}, s32[1,2,64,1]{2,3,1,0:T(1,128)}, u32[]{:S(2)}) copy-start(s32[1,2,64,1]{2,3,1,0:T(1,128)} %param.14) | copy-start | bytes 1540
  146.0 21.0 %copy-start.6 = (s32[1,2,64,1]{2,3,1,0:T(1,128)S(1)}, s32[1,2,64,1]{2,3,1,0:T(1,128)}, u32[]{:S(2)}) copy-start(s32[1,2,64,1]{2,3,1,0:T(1,128)} %param.15) | copy-start | bytes 1540
  162.4 17.3 %copy-start.1 = (bf16[1,64,3584]{2,1,0:T(8,128)(2,1)S(1)}, bf16[1,64,3584]{2,1,0:T(8,128)(2,1)}, u32[]{:S(2)}) copy-start(bf16[1,64,3584]{2,1,0:T(8,128)(2,1)} %param.9) | copy-start | bytes 1376260
  163.4 15.2 %all-to-all-start.2 = ((f32[4,476,128]{2,1,0:T(8,128)}), f32[4,476,128]{2,1,0:T(8,128)S(1)}, u32[]{:S(2)}, u32[]{:S(2)}) async-start(f32[4,476,128]{2,1,0:T(8,128)} %reshape.218), calls=%async_computation.2 | async-start | bytes 1966080 | tf_op jit(solution)/shard_map/all_to_all | solution.py:77
  167.0 90.6 %all-gather.7.cloned.1.call-start = ((), (), s32[]{:S(2)}) async-start(), calls=%async_computation.7 | async-start | bytes 4423680 | tf_op jit(solution)/shard_map/all_gather | solution.py:56
  179.9 10.7 %collective-permute-start.7 = (bf16[64,3584]{1,0:T(8,128)(2,1)S(1)}, bf16[64,3584]{1,0:T(8,128)(2,1)S(1)}, u32[]{:S(2)}, u32[]{:S(2)}) collective-permute-start(bf16[64,3584]{1,0:T(8,128)(2,1)S(1)} %fusion.16), channel_id=1, source_target_pairs={{0,32},{32,64},{64,96},{96,128},{128,160},{160,192},{192,224},{224... | collective-permute-start | bytes 1376264 | tf_op jit(solution)/shard_map/ppermute | solution.py:19
  217.0 51.0 %copy-start.7 = (bf16[1,1,3584,128]{3,2,1,0:T(8,128)(2,1)S(1)}, bf16[1,1,3584,128]{3,2,1,0:T(8,128)(2,1)}, u32[]{:S(2)}) copy-start(bf16[1,1,3584,128]{3,2,1,0:T(8,128)(2,1)} %param.12) | copy-start | bytes 2752516
  264.6 11.5 %copy-start.4 = (bf16[128,3584]{1,0:T(8,128)(2,1)S(1)}, bf16[128,3584]{1,0:T(8,128)(2,1)}, u32[]{:S(2)}) copy-start(bf16[128,3584]{1,0:T(8,128)(2,1)} %copy-done.3) | copy-start | bytes 2752516
  271.9 12.1 %all-to-all-start.4 = ((bf16[8,68,128]{2,1,0:T(8,128)(2,1)}), bf16[8,68,128]{2,1,0:T(8,128)(2,1)S(1)}, u32[]{:S(2)}, u32[]{:S(2)}) async-start(bf16[8,68,128]{2,1,0:T(8,128)(2,1)} %reshape.222), calls=%async_computation.4 | async-start | bytes 294912 | tf_op jit(solution)/shard_map/all_to_all | solution.py:63
  290.1 15.4 %all-to-all-start.5 = ((f32[4,476,128]{2,1,0:T(8,128)}), f32[4,476,128]{2,1,0:T(8,128)S(1)}, u32[]{:S(2)}, u32[]{:S(2)}) async-start(f32[4,476,128]{2,1,0:T(8,128)} %reshape.223), calls=%async_computation.5 | async-start | bytes 1966080 | tf_op jit(solution)/shard_map/all_to_all | solution.py:77
Sparse Core Ops, SparseCore 0:
  24.2 88.1 all-gather.4
  201.8 55.7 all-gather.6

commit v11 on v10

--- a/solution.py
+++ b/solution.py
@@ -53,15 +53,26 @@
     block_rows = MOST * model_width // LANE
     per_expert = place_rows(normed, slot_ids, EXPERTS * MOST).reshape(EXPERTS, block_rows, LANE)
     from_x = lax.all_to_all(per_expert, "ex", split_axis=0, concat_axis=0, tiled=True)
-    slot_rows = lax.all_gather(from_x, "ey", axis=0, tiled=False)
-    n_y = slot_rows.shape[0]
-    flat_rows = slot_rows.reshape(-1, model_width)
-    gate_act = jnp.dot(flat_rows, w_gate, preferred_element_type=jnp.float32)
-    up_act = jnp.dot(flat_rows, w_up, preferred_element_type=jnp.float32)
-    hidden = (jax.nn.silu(gate_act) * up_act).astype(jnp.bfloat16)
-    hidden = hidden.reshape(n_y, n_x * MOST, hidden.shape[-1])
+    me_y = lax.axis_index("ey")
+    if isinstance(down_all, list):
+        slot_rows = lax.all_gather(from_x, "ey", axis=0, tiled=False)
+        n_y = slot_rows.shape[0]
+        flat_rows = slot_rows.reshape(-1, model_width)
+        gate_act = jnp.dot(flat_rows, w_gate, preferred_element_type=jnp.float32)
+        up_act = jnp.dot(flat_rows, w_up, preferred_element_type=jnp.float32)
+        hidden = (jax.nn.silu(gate_act) * up_act).astype(jnp.bfloat16)
+        hidden = hidden.reshape(n_y, n_x * MOST, hidden.shape[-1])
+    else:
+        blocks = ring_gather(from_x, "ey")
+        n_y = len(blocks)
+        served = []
+        for block in blocks:
+            rows = block.reshape(-1, model_width)
+            gate_act = jnp.dot(rows, w_gate, preferred_element_type=jnp.float32)
+            up_act = jnp.dot(rows, w_up, preferred_element_type=jnp.float32)
+            served.append((jax.nn.silu(gate_act) * up_act).astype(jnp.bfloat16))
+        hidden = jnp.take(jnp.stack(served, axis=0), (jnp.arange(n_y) - me_y) % n_y, axis=0)
     hidden_here = lax.all_to_all(hidden, "ey", split_axis=0, concat_axis=0, tiled=True)
-    me_y = lax.axis_index("ey")
     hidden_rel = jnp.take(hidden_here, (me_y + jnp.arange(n_y)) % n_y, axis=0)
     if isinstance(down_all, list):
         expert_out = None

time: 318 us -> 346 us (1.088)
  starting transfers between devices: 49.6 us -> 74.4 us
  waiting for transfers between devices: 157 us -> 142 us
  local copies, waits for them, and re-layouts: 39.1 us -> 50 us
  matrix products: 29.1 us -> 39.5 us
  blocking collectives: 21.4 us -> 11.5 us
    all_gather x2 -> x1, waiting for transfers between devices: 57.4 us -> 16.8 us  [routed_branch(): slot_rows = lax.all_gather(from_x, 'ey', axis=0, tiled=False)]
    ppermute x8 -> x15, waiting for transfers between devices: 67.9 us -> 89.5 us  [shifted(): return lax.ppermute(value, axis, pairs)]
    ppermute x8 -> x15, starting transfers between devices: 32.6 us -> 51.5 us  [shifted(): return lax.ppermute(value, axis, pairs)]
    dot_general x0 -> x16, matrix products: none -> 16.1 us  [the longest x8 8.71 us: routed_branch(): up_act = jnp.dot(rows, w_up, preferred_element_type=jnp.float32)]
    reshape x0 -> x8, local copies, waits for them, and re-layouts: none -> 12.5 us  [routed_branch(): rows = block.reshape(-1, model_width)]
    all_to_all x2 -> x1, blocking collectives: 21.4 us -> 11.5 us  [routed_branch(): lax.all_to_all(per_expert, 'ex', split_axis=0, concat_axis=0, tiled=True)]
    reshape x2 -> x1, local copies, waits for them, and re-layouts: 14 us -> 7.02 us  [routed_branch(): flat_rows = slot_rows.reshape(-1, model_width)]
    all_to_all x0 -> x1, waiting for transfers between devices: none -> 6.02 us  [routed_branch(): lax.all_to_all(per_expert, 'ex', split_axis=0, concat_axis=0, tiled=True)]
  transfers between devices with their start and end apart: 14 -> 21, of which waited for: 11 -> 15; matrix products, arithmetic and copies ran while one was open for 13% -> 18% of each run, Pallas kernels for 0% -> 0%
where the time goes in v11:
time: 346 us; the launch traced here: 340 us
  waiting for transfers between devices  142 us (41%)
  starting transfers between devices  74.4 us (22%)
  local copies, waits for them, and re-layouts  50 us (14%)
  matrix products  39.5 us (11%)
  between operations  13.9 us (4%)
  blocking collectives  11.5 us (3%)
  other arithmetic  7.94 us (2%)
    ppermute x15, waiting for transfers between devices, shifted(): return lax.ppermute(value, axis, pairs)  89.5 us
    ppermute x15, starting transfers between devices, shifted(): return lax.ppermute(value, axis, pairs)  51.5 us
    all_to_all x2, waiting for transfers between devices, routed_branch(): lax.all_to_all(expert_out, 'ex', split_axis=0, concat_axis=0, tiled=True)  21.4 us
    all_gather x1, waiting for transfers between devices, routed_branch(): slot_rows = lax.all_gather(from_x, 'ey', axis=0, tiled=False)  16.8 us
    unnamed x29, local copies, waits for them, and re-layouts  15.9 us
    reshape x8, local copies, waits for them, and re-layouts, routed_branch(): rows = block.reshape(-1, model_width)  12.5 us
    all_to_all x1, blocking collectives, routed_branch(): lax.all_to_all(per_expert, 'ex', split_axis=0, concat_axis=0, tiled=True)  11.5 us
    all_to_all x2, starting transfers between devices, routed_branch(): lax.all_to_all(hidden, 'ey', split_axis=0, concat_axis=0, tiled=True)  11 us
  transfers between devices with their start and end apart: 21, of which 15 were waited for; matrix products, arithmetic and copies ran while one was open for 18% of the time, Pallas kernels for 0%

profile of v11, /device:TPU:1, one launch (start us, length us, event | category | flops | bytes accessed | tf_op | source)
XLA Modules:
  0.0 339.6 jit_solution(12528188529398248451)
XLA Ops:
  12.6 11.5 %all_to_all.30 = bf16[4,476,128]{2,1,0:T(8,128)(2,1)} all-to-all(bf16[4,476,128]{2,1,0:T(8,128)(2,1)S(1)} %reshape.233), channel_id=1, replica_groups=mesh['pipe'=16,'ex'=4,'ey'=8] {'ex'}, dimensions={0} | all-to-all | bytes 974848 | tf_op jit(solution)/shard_map/all_to_all | solution.py:55
  24.1 4.7 %collective-permute-start.3 = (bf16[128,3584]{1,0:T(8,128)(2,1)}, bf16[128,3584]{1,0:T(8,128)(2,1)S(1)}, u32[]{:S(2)}, u32[]{:S(2)}) collective-permute-start(bf16[128,3584]{1,0:T(8,128)(2,1)} %bitcast.177), channel_id=1, source_target_pairs={{0,1},{1,2},{2,3},{3,4},{4,5},{5,6},{6,7},{7,0},{8,9},{9,10},{10,1... | collective-permute-start | bytes 2752520 | tf_op jit(solution)/shard_map/ppermute | solution.py:19
  32.6 14.3 %collective-permute-done.3 = bf16[128,3584]{1,0:T(8,128)(2,1)S(1)} collective-permute-done((bf16[128,3584]{1,0:T(8,128)(2,1)}, bf16[128,3584]{1,0:T(8,128)(2,1)S(1)}, u32[]{:S(2)}, u32[]{:S(2)}) %collective-permute-start.3) | collective-permute-done | bytes 917536 | tf_op jit(solution)/shard_map/ppermute | solution.py:19
  46.9 6.0 %collective-permute-start.4 = (bf16[128,3584]{1,0:T(8,128)(2,1)S(1)}, bf16[128,3584]{1,0:T(8,128)(2,1)}, u32[]{:S(2)}, u32[]{:S(2)}) collective-permute-start(bf16[128,3584]{1,0:T(8,128)(2,1)S(1)} %collective-permute-done.3), channel_id=1, source_target_pairs={{0,1},{1,2},{2,3},{3,4},{4,5},{5,6},{6,7},{7,0},{8,9},{9,10},{10,1... | collective-permute-start | bytes 2752520 | tf_op jit(solution)/shard_map/ppermute | solution.py:19
  52.9 4.4 %collective-permute-start.1 = (bf16[128,3584]{1,0:T(8,128)(2,1)}, bf16[128,3584]{1,0:T(8,128)(2,1)}, u32[]{:S(2)}, u32[]{:S(2)}) collective-permute-start(bf16[128,3584]{1,0:T(8,128)(2,1)} %collective-permute-done), channel_id=1, source_target_pairs={{0,7},{1,0},{2,1},{3,2},{4,3},{5,4},{6,5},{7,6},{8,15},{9,8},{10,9... | collective-permute-start | bytes 2752520 | tf_op jit(solution)/shard_map/ppermute | solution.py:19
  57.3 36.3 %collective-permute-done.4 = bf16[128,3584]{1,0:T(8,128)(2,1)} collective-permute-done((bf16[128,3584]{1,0:T(8,128)(2,1)S(1)}, bf16[128,3584]{1,0:T(8,128)(2,1)}, u32[]{:S(2)}, u32[]{:S(2)}) %collective-permute-start.4) | collective-permute-done | bytes 917536 | tf_op jit(solution)/shard_map/ppermute | solution.py:19
  95.6 16.8 %all-gather.3.cloned.1.call-done = bf16[32,476,128]{2,1,0:T(8,128)(2,1)} async-done(((bf16[4,476,128]{2,1,0:T(8,128)(2,1)}), bf16[32,476,128]{2,1,0:T(8,128)(2,1)}) %all-gather.3.cloned.1.call-update) | async-done | bytes 3899408 | tf_op jit(solution)/shard_map/all_gather | solution.py:58
  112.4 7.0 %reshape.234 = bf16[544,3584]{1,0:T(8,128)(2,1)} reshape(bf16[32,476,128]{2,1,0:T(8,128)(2,1)} %all-gather.3.cloned.1.call-done) | data formatting | bytes 7798784 | tf_op jit(solution)/shard_map/reshape | solution.py:60
  126.7 5.3 %all-to-all-start.1 = ((bf16[8,68,128]{2,1,0:T(8,128)(2,1)}), bf16[8,68,128]{2,1,0:T(8,128)(2,1)S(1)}, u32[]{:S(2)}, u32[]{:S(2)}) async-start(bf16[8,68,128]{2,1,0:T(8,128)(2,1)} %reshape.235), calls=%async_computation.1 | async-start | bytes 294912 | tf_op jit(solution)/shard_map/all_to_all | solution.py:75
  132.1 4.6 %collective-permute-start.2 = (bf16[128,3584]{1,0:T(8,128)(2,1)}, bf16[128,3584]{1,0:T(8,128)(2,1)}, u32[]{:S(2)}, u32[]{:S(2)}) collective-permute-start(bf16[128,3584]{1,0:T(8,128)(2,1)} %collective-permute-done.1), channel_id=1, source_target_pairs={{0,7},{1,0},{2,1},{3,2},{4,3},{5,4},{6,5},{7,6},{8,15},{9,8},{10,9... | collective-permute-start | bytes 2752520 | tf_op jit(solution)/shard_map/ppermute | solution.py:19
  148.5 9.3 %collective-permute-done.2 = bf16[128,3584]{1,0:T(8,128)(2,1)} collective-permute-done((bf16[128,3584]{1,0:T(8,128)(2,1)}, bf16[128,3584]{1,0:T(8,128)(2,1)}, u32[]{:S(2)}, u32[]{:S(2)}) %collective-permute-start.2) | collective-permute-done | bytes 917536 | tf_op jit(solution)/shard_map/ppermute | solution.py:19
  163.3 4.2 %all-to-all-start.2 = ((f32[4,476,128]{2,1,0:T(8,128)}), f32[4,476,128]{2,1,0:T(8,128)}, u32[]{:S(2)}, u32[]{:S(2)}) async-start(f32[4,476,128]{2,1,0:T(8,128)} %reshape.236), calls=%async_computation.2 | async-start | bytes 1966080 | tf_op jit(solution)/shard_map/all_to_all | solution.py:88
  167.6 11.9 %all-to-all-done.2 = f32[4,476,128]{2,1,0:T(8,128)} async-done(((f32[4,476,128]{2,1,0:T(8,128)}), f32[4,476,128]{2,1,0:T(8,128)}, u32[]{:S(2)}, u32[]{:S(2)}) %all-to-all-start.2) | async-done | bytes 974880 | tf_op jit(solution)/shard_map/all_to_all | solution.py:88
  184.0 5.1 %collective-permute-start.7 = (bf16[64,3584]{1,0:T(8,128)(2,1)S(1)}, bf16[64,3584]{1,0:T(8,128)(2,1)S(1)}, u32[]{:S(2)}, u32[]{:S(2)}) collective-permute-start(bf16[64,3584]{1,0:T(8,128)(2,1)S(1)} %fusion.18), channel_id=1, source_target_pairs={{0,32},{32,64},{64,96},{96,128},{128,160},{160,192},{192,224},{224... | collective-permute-start | bytes 1376264 | tf_op jit(solution)/shard_map/ppermute | solution.py:19
  210.4 6.0 %all-to-all-done.3 = bf16[4,476,128]{2,1,0:T(8,128)(2,1)S(1)} async-done(((bf16[4,476,128]{2,1,0:T(8,128)(2,1)}), bf16[4,476,128]{2,1,0:T(8,128)(2,1)S(1)}, u32[]{:S(2)}, u32[]{:S(2)}) %all-to-all-start.3) | async-done | bytes 487456 | tf_op jit(solution)/shard_map/all_to_all | solution.py:55
  222.9 9.2 %collective-permute-done.8 = bf16[4,476,128]{2,1,0:T(8,128)(2,1)} collective-permute-done((bf16[4,476,128]{2,1,0:T(8,128)(2,1)S(1)}, bf16[4,476,128]{2,1,0:T(8,128)(2,1)}, u32[]{:S(2)}, u32[]{:S(2)}) %collective-permute-start.8) | collective-permute-done | bytes 487456 | tf_op jit(solution)/shard_map/ppermute | solution.py:19
  243.8 4.6 %collective-permute-done.9 = bf16[4,476,128]{2,1,0:T(8,128)(2,1)} collective-permute-done((bf16[4,476,128]{2,1,0:T(8,128)(2,1)}, bf16[4,476,128]{2,1,0:T(8,128)(2,1)}, u32[]{:S(2)}, u32[]{:S(2)}) %collective-permute-start.9) | collective-permute-done | bytes 487456 | tf_op jit(solution)/shard_map/ppermute | solution.py:19
  250.0 4.5 %collective-permute-start.10 = (bf16[4,476,128]{2,1,0:T(8,128)(2,1)}, bf16[4,476,128]{2,1,0:T(8,128)(2,1)}, u32[]{:S(2)}, u32[]{:S(2)}) collective-permute-start(bf16[4,476,128]{2,1,0:T(8,128)(2,1)} %collective-permute-done.9), channel_id=1, source_target_pairs={{0,7},{1,0},{2,1},{3,2},{4,3},{5,4},{6,5},{7,6},{8,15},{9,8},{10,9... | collective-permute-start | bytes 1462280 | tf_op jit(solution)/shard_map/ppermute | solution.py:19
  275.8 7.9 %collective-permute-done.14 = bf16[4,476,128]{2,1,0:T(8,128)(2,1)} collective-permute-done((bf16[4,476,128]{2,1,0:T(8,128)(2,1)}, bf16[4,476,128]{2,1,0:T(8,128)(2,1)}, u32[]{:S(2)}, u32[]{:S(2)}) %collective-permute-start.14) | collective-permute-done | bytes 487456 | tf_op jit(solution)/shard_map/ppermute | solution.py:19
  293.6 5.7 %all-to-all-start.4 = ((bf16[8,68,128]{2,1,0:T(8,128)(2,1)}), bf16[8,68,128]{2,1,0:T(8,128)(2,1)S(1)}, u32[]{:S(2)}, u32[]{:S(2)}) async-start(bf16[8,68,128]{2,1,0:T(8,128)(2,1)} %broadcast_select_fusion), calls=%async_computation.4 | async-start | bytes 294912 | tf_op jit(solution)/shard_map/all_to_all | solution.py:75
  300.3 7.2 %all-to-all-done.4 = bf16[8,68,128]{2,1,0:T(8,128)(2,1)S(1)} async-done(((bf16[8,68,128]{2,1,0:T(8,128)(2,1)}), bf16[8,68,128]{2,1,0:T(8,128)(2,1)S(1)}, u32[]{:S(2)}, u32[]{:S(2)}) %all-to-all-start.4) | async-done | bytes 139296 | tf_op jit(solution)/shard_map/all_to_all | solution.py:75
  308.1 4.5 %reduce-precision_reduce_fusion = f32[68,3584]{1,0:T(8,128)S(1)} fusion(bf16[8,128,3584]{2,1,0:T(8,128)(2,1)} %bitcast_dynamic-update-slice_fusion, bf16[8,68,128]{2,1,0:T(8,128)(2,1)S(1)} %gather_fusion.4, pred[8]{0:T(512)(128)(4,1)S(1)} %compare_and_fusion.1), kind=kOutput, calls=%fused_computation.5 | convolution fusion | flops 502847488 | bytes 8454152 | tf_op jit(solution)/shard_map/jrh,jhd->jrd/dot_general | solution.py:84
  313.7 4.2 %all-to-all-start.5 = ((f32[4,476,128]{2,1,0:T(8,128)}), f32[4,476,128]{2,1,0:T(8,128)}, u32[]{:S(2)}, u32[]{:S(2)}) async-start(f32[4,476,128]{2,1,0:T(8,128)} %reshape.247), calls=%async_computation.5 | async-start | bytes 1966080 | tf_op jit(solution)/shard_map/all_to_all | solution.py:88
  317.9 9.5 %all-to-all-done.5 = f32[4,476,128]{2,1,0:T(8,128)} async-done(((f32[4,476,128]{2,1,0:T(8,128)}), f32[4,476,128]{2,1,0:T(8,128)}, u32[]{:S(2)}, u32[]{:S(2)}) %all-to-all-start.5) | async-done | bytes 974880 | tf_op jit(solution)/shard_map/all_to_all | solution.py:88
  (126 shorter events, 121.0 us)
Async XLA Ops:
  6.5 116.2 %copy-start = (bf16[1,1,3584,128]{3,2,1,0:T(8,128)(2,1)S(1)}, bf16[1,1,3584,128]{3,2,1,0:T(8,128)(2,1)}, u32[]{:S(2)}) copy-start(bf16[1,1,3584,128]{3,2,1,0:T(8,128)(2,1)} %param.12) | copy-start | bytes 2752516
  6.5 112.9 %copy-start.1 = (bf16[1,1,3584,128]{3,2,1,0:T(8,128)(2,1)S(1)}, bf16[1,1,3584,128]{3,2,1,0:T(8,128)(2,1)}, u32[]{:S(2)}) copy-start(bf16[1,1,3584,128]{3,2,1,0:T(8,128)(2,1)} %param.11) | copy-start | bytes 2752516
  6.5 105.8 %all-gather.3.cloned.1.call-start = ((), (), s32[]{:S(2)}) async-start(), calls=%async_computation.6 | async-start | bytes 4423680 | tf_op jit(solution)/shard_map/all_gather | solution.py:58
  24.1 22.8 %collective-permute-start.3 = (bf16[128,3584]{1,0:T(8,128)(2,1)}, bf16[128,3584]{1,0:T(8,128)(2,1)S(1)}, u32[]{:S(2)}, u32[]{:S(2)}) collective-permute-start(bf16[128,3584]{1,0:T(8,128)(2,1)} %bitcast.177), channel_id=1, source_target_pairs={{0,1},{1,2},{2,3},{3,4},{4,5},{5,6},{6,7},{7,0},{8,9},{9,10},{10,1... | collective-permute-start | bytes 2752520 | tf_op jit(solution)/shard_map/ppermute | solution.py:19
  28.8 24.1 %collective-permute-start = (bf16[128,3584]{1,0:T(8,128)(2,1)}, bf16[128,3584]{1,0:T(8,128)(2,1)}, u32[]{:S(2)}, u32[]{:S(2)}) collective-permute-start(bf16[128,3584]{1,0:T(8,128)(2,1)} %bitcast.178), channel_id=1, source_target_pairs={{0,7},{1,0},{2,1},{3,2},{4,3},{5,4},{6,5},{7,6},{8,15},{9,8},{10,9... | collective-permute-start | bytes 2752520 | tf_op jit(solution)/shard_map/ppermute | solution.py:19
  46.9 65.5 %copy-start.7 = (bf16[128,3584]{1,0:T(8,128)(2,1)}, bf16[128,3584]{1,0:T(8,128)(2,1)S(1)}, u32[]{:S(2)}) copy-start(bf16[128,3584]{1,0:T(8,128)(2,1)S(1)} %collective-permute-done.3) | copy-start | bytes 2752516
  46.9 46.8 %collective-permute-start.4 = (bf16[128,3584]{1,0:T(8,128)(2,1)S(1)}, bf16[128,3584]{1,0:T(8,128)(2,1)}, u32[]{:S(2)}, u32[]{:S(2)}) collective-permute-start(bf16[128,3584]{1,0:T(8,128)(2,1)S(1)} %collective-permute-done.3), channel_id=1, source_target_pairs={{0,1},{1,2},{2,3},{3,4},{4,5},{5,6},{6,7},{7,0},{8,9},{9,10},{10,1... | collective-permute-start | bytes 2752520 | tf_op jit(solution)/shard_map/ppermute | solution.py:19
  52.9 79.2 %collective-permute-start.1 = (bf16[128,3584]{1,0:T(8,128)(2,1)}, bf16[128,3584]{1,0:T(8,128)(2,1)}, u32[]{:S(2)}, u32[]{:S(2)}) collective-permute-start(bf16[128,3584]{1,0:T(8,128)(2,1)} %collective-permute-done), channel_id=1, source_target_pairs={{0,7},{1,0},{2,1},{3,2},{4,3},{5,4},{6,5},{7,6},{8,15},{9,8},{10,9... | collective-permute-start | bytes 2752520 | tf_op jit(solution)/shard_map/ppermute | solution.py:19
  93.6 43.0 %collective-permute-start.5 = (bf16[128,3584]{1,0:T(8,128)(2,1)}, bf16[128,3584]{1,0:T(8,128)(2,1)}, u32[]{:S(2)}, u32[]{:S(2)}) collective-permute-start(bf16[128,3584]{1,0:T(8,128)(2,1)} %collective-permute-done.4), channel_id=1, source_target_pairs={{0,1},{1,2},{2,3},{3,4},{4,5},{5,6},{6,7},{7,0},{8,9},{9,10},{10,1... | collective-permute-start | bytes 2752520 | tf_op jit(solution)/shard_map/ppermute | solution.py:19
  126.7 13.4 %all-to-all-start.1 = ((bf16[8,68,128]{2,1,0:T(8,128)(2,1)}), bf16[8,68,128]{2,1,0:T(8,128)(2,1)S(1)}, u32[]{:S(2)}, u32[]{:S(2)}) async-start(bf16[8,68,128]{2,1,0:T(8,128)(2,1)} %reshape.235), calls=%async_computation.1 | async-start | bytes 294912 | tf_op jit(solution)/shard_map/all_to_all | solution.py:75
  132.1 25.7 %collective-permute-start.2 = (bf16[128,3584]{1,0:T(8,128)(2,1)}, bf16[128,3584]{1,0:T(8,128)(2,1)}, u32[]{:S(2)}, u32[]{:S(2)}) collective-permute-start(bf16[128,3584]{1,0:T(8,128)(2,1)} %collective-permute-done.1), channel_id=1, source_target_pairs={{0,7},{1,0},{2,1},{3,2},{4,3},{5,4},{6,5},{7,6},{8,15},{9,8},{10,9... | collective-permute-start | bytes 2752520 | tf_op jit(solution)/shard_map/ppermute | solution.py:19
  136.7 24.0 %collective-permute-start.6 = (bf16[128,3584]{1,0:T(8,128)(2,1)}, bf16[128,3584]{1,0:T(8,128)(2,1)}, u32[]{:S(2)}, u32[]{:S(2)}) collective-permute-start(bf16[128,3584]{1,0:T(8,128)(2,1)} %collective-permute-done.5), channel_id=1, source_target_pairs={{0,1},{1,2},{2,3},{3,4},{4,5},{5,6},{6,7},{7,0},{8,9},{9,10},{10,1... | collective-permute-start | bytes 2752520 | tf_op jit(solution)/shard_map/ppermute | solution.py:19
  163.3 16.2 %all-to-all-start.2 = ((f32[4,476,128]{2,1,0:T(8,128)}), f32[4,476,128]{2,1,0:T(8,128)}, u32[]{:S(2)}, u32[]{:S(2)}) async-start(f32[4,476,128]{2,1,0:T(8,128)} %reshape.236), calls=%async_computation.2 | async-start | bytes 1966080 | tf_op jit(solution)/shard_map/all_to_all | solution.py:88
  184.0 18.2 %collective-permute-start.7 = (bf16[64,3584]{1,0:T(8,128)(2,1)S(1)}, bf16[64,3584]{1,0:T(8,128)(2,1)S(1)}, u32[]{:S(2)}, u32[]{:S(2)}) collective-permute-start(bf16[64,3584]{1,0:T(8,128)(2,1)S(1)} %fusion.18), channel_id=1, source_target_pairs={{0,32},{32,64},{64,96},{96,128},{128,160},{160,192},{192,224},{224... | collective-permute-start | bytes 1376264 | tf_op jit(solution)/shard_map/ppermute | solution.py:19
  204.7 11.7 %all-to-all-start.3 = ((bf16[4,476,128]{2,1,0:T(8,128)(2,1)}), bf16[4,476,128]{2,1,0:T(8,128)(2,1)S(1)}, u32[]{:S(2)}, u32[]{:S(2)}) async-start(bf16[4,476,128]{2,1,0:T(8,128)(2,1)} %reshape.238), calls=%async_computation.3 | async-start | bytes 983040 | tf_op jit(solution)/shard_map/all_to_all | solution.py:55
  216.9 15.2 %collective-permute-start.8 = (bf16[4,476,128]{2,1,0:T(8,128)(2,1)S(1)}, bf16[4,476,128]{2,1,0:T(8,128)(2,1)}, u32[]{:S(2)}, u32[]{:S(2)}) collective-permute-start(bf16[4,476,128]{2,1,0:T(8,128)(2,1)S(1)} %all-to-all-done.3), channel_id=1, source_target_pairs={{0,7},{1,0},{2,1},{3,2},{4,3},{5,4},{6,5},{7,6},{8,15},{9,8},{10,9... | collective-permute-start | bytes 1462280 | tf_op jit(solution)/shard_map/ppermute | solution.py:19
  219.1 18.9 %collective-permute-start.11 = (bf16[4,476,128]{2,1,0:T(8,128)(2,1)S(1)}, bf16[4,476,128]{2,1,0:T(8,128)(2,1)}, u32[]{:S(2)}, u32[]{:S(2)}) collective-permute-start(bf16[4,476,128]{2,1,0:T(8,128)(2,1)S(1)} %all-to-all-done.3), channel_id=1, source_target_pairs={{0,1},{1,2},{2,3},{3,4},{4,5},{5,6},{6,7},{7,0},{8,9},{9,10},{10,1... | collective-permute-start | bytes 1462280 | tf_op jit(solution)/shard_map/ppermute | solution.py:19
  233.7 14.7 %collective-permute-start.9 = (bf16[4,476,128]{2,1,0:T(8,128)(2,1)}, bf16[4,476,128]{2,1,0:T(8,128)(2,1)}, u32[]{:S(2)}, u32[]{:S(2)}) collective-permute-start(bf16[4,476,128]{2,1,0:T(8,128)(2,1)} %collective-permute-done.8), channel_id=1, source_target_pairs={{0,7},{1,0},{2,1},{3,2},{4,3},{5,4},{6,5},{7,6},{8,15},{9,8},{10,9... | collective-permute-start | bytes 1462280 | tf_op jit(solution)/shard_map/ppermute | solution.py:19
  238.0 17.4 %collective-permute-start.12 = (bf16[4,476,128]{2,1,0:T(8,128)(2,1)}, bf16[4,476,128]{2,1,0:T(8,128)(2,1)}, u32[]{:S(2)}, u32[]{:S(2)}) collective-permute-start(bf16[4,476,128]{2,1,0:T(8,128)(2,1)} %collective-permute-done.11), channel_id=1, source_target_pairs={{0,1},{1,2},{2,3},{3,4},{4,5},{5,6},{6,7},{7,0},{8,9},{9,10},{10,1... | collective-permute-start | bytes 1462280 | tf_op jit(solution)/shard_map/ppermute | solution.py:19
  250.0 14.1 %collective-permute-start.10 = (bf16[4,476,128]{2,1,0:T(8,128)(2,1)}, bf16[4,476,128]{2,1,0:T(8,128)(2,1)}, u32[]{:S(2)}, u32[]{:S(2)}) collective-permute-start(bf16[4,476,128]{2,1,0:T(8,128)(2,1)} %collective-permute-done.9), channel_id=1, source_target_pairs={{0,7},{1,0},{2,1},{3,2},{4,3},{5,4},{6,5},{7,6},{8,15},{9,8},{10,9... | collective-permute-start | bytes 1462280 | tf_op jit(solution)/shard_map/ppermute | solution.py:19
  255.4 14.6 %collective-permute-start.13 = (bf16[4,476,128]{2,1,0:T(8,128)(2,1)}, bf16[4,476,128]{2,1,0:T(8,128)(2,1)}, u32[]{:S(2)}, u32[]{:S(2)}) collective-permute-start(bf16[4,476,128]{2,1,0:T(8,128)(2,1)} %collective-permute-done.12), channel_id=1, source_target_pairs={{0,1},{1,2},{2,3},{3,4},{4,5},{5,6},{6,7},{7,0},{8,9},{9,10},{10,1... | collective-permute-start | bytes 1462280 | tf_op jit(solution)/shard_map/ppermute | solution.py:19
  270.0 13.7 %collective-permute-start.14 = (bf16[4,476,128]{2,1,0:T(8,128)(2,1)}, bf16[4,476,128]{2,1,0:T(8,128)(2,1)}, u32[]{:S(2)}, u32[]{:S(2)}) collective-permute-start(bf16[4,476,128]{2,1,0:T(8,128)(2,1)} %collective-permute-done.13), channel_id=1, source_target_pairs={{0,1},{1,2},{2,3},{3,4},{4,5},{5,6},{6,7},{7,0},{8,9},{9,10},{10,1... | collective-permute-start | bytes 1462280 | tf_op jit(solution)/shard_map/ppermute | solution.py:19
  293.6 13.9 %all-to-all-start.4 = ((bf16[8,68,128]{2,1,0:T(8,128)(2,1)}), bf16[8,68,128]{2,1,0:T(8,128)(2,1)S(1)}, u32[]{:S(2)}, u32[]{:S(2)}) async-start(bf16[8,68,128]{2,1,0:T(8,128)(2,1)} %broadcast_select_fusion), calls=%async_computation.4 | async-start | bytes 294912 | tf_op jit(solution)/shard_map/all_to_all | solution.py:75
  313.7 13.7 %all-to-all-start.5 = ((f32[4,476,128]{2,1,0:T(8,128)}), f32[4,476,128]{2,1,0:T(8,128)}, u32[]{:S(2)}, u32[]{:S(2)}) async-start(f32[4,476,128]{2,1,0:T(8,128)} %reshape.247), calls=%async_computation.5 | async-start | bytes 1966080 | tf_op jit(solution)/shard_map/all_to_all | solution.py:88
  (8 other events, 117.9 us)
Sparse Core Ops, SparseCore 0:
  24.2 88.1 all-gather.2

commit v12 on v10

--- a/solution.py
+++ b/solution.py
@@ -7,6 +7,7 @@
 EXPERTS = 4
 MOST = 17
 LANE = 128
+SUBLANE = 8
 
 
 NORM_EPS = 1e-06
@@ -53,13 +54,21 @@
     block_rows = MOST * model_width // LANE
     per_expert = place_rows(normed, slot_ids, EXPERTS * MOST).reshape(EXPERTS, block_rows, LANE)
     from_x = lax.all_to_all(per_expert, "ex", split_axis=0, concat_axis=0, tiled=True)
-    slot_rows = lax.all_gather(from_x, "ey", axis=0, tiled=False)
-    n_y = slot_rows.shape[0]
-    flat_rows = slot_rows.reshape(-1, model_width)
+    if isinstance(down_all, list):
+        slot_rows = lax.all_gather(from_x, "ey", axis=0, tiled=False)
+        n_y = slot_rows.shape[0]
+        flat_rows = slot_rows.reshape(-1, model_width)
+    else:
+        held = n_x * MOST
+        padded = -(-held // SUBLANE) * SUBLANE
+        own_rows = jnp.pad(from_x.reshape(held, model_width), ((0, padded - held), (0, 0)))
+        slot_rows = lax.all_gather(own_rows, "ey", axis=0, tiled=False)
+        n_y = slot_rows.shape[0]
+        flat_rows = slot_rows.reshape(-1, model_width)
     gate_act = jnp.dot(flat_rows, w_gate, preferred_element_type=jnp.float32)
     up_act = jnp.dot(flat_rows, w_up, preferred_element_type=jnp.float32)
     hidden = (jax.nn.silu(gate_act) * up_act).astype(jnp.bfloat16)
-    hidden = hidden.reshape(n_y, n_x * MOST, hidden.shape[-1])
+    hidden = hidden.reshape(n_y, -1, hidden.shape[-1])[:, : n_x * MOST]
     hidden_here = lax.all_to_all(hidden, "ey", split_axis=0, concat_axis=0, tiled=True)
     me_y = lax.axis_index("ey")
     hidden_rel = jnp.take(hidden_here, (me_y + jnp.arange(n_y)) % n_y, axis=0)

time: 318 us -> 317 us (level)
  local copies, waits for them, and re-layouts: 39.1 us -> 33.4 us
    all_gather x0 -> x1, waiting for transfers between devices: none -> 43.5 us  [routed_branch(): slot_rows = lax.all_gather(own_rows, 'ey', axis=0, tiled=False)]
    all_gather x2 -> x1, waiting for transfers between devices: 57.4 us -> 16.9 us  [routed_branch(): slot_rows = lax.all_gather(from_x, 'ey', axis=0, tiled=False)]
    reshape x2 -> x1, local copies, waits for them, and re-layouts: 14 us -> 7.01 us  [routed_branch(): flat_rows = slot_rows.reshape(-1, model_width)]
    unnamed x23 -> x25, local copies, waits for them, and re-layouts: 15.3 us -> 14.2 us
  transfers between devices with their start and end apart: 14 -> 14, of which waited for: 11 -> 11; matrix products, arithmetic and copies ran while one was open for 13% -> 12% of each run, Pallas kernels for 0% -> 0%
where the time goes in v12:
time: 317 us; the launch traced here: 314 us
  waiting for transfers between devices  160 us (50%)
  starting transfers between devices  49.6 us (16%)
  local copies, waits for them, and re-layouts  33.4 us (11%)
  matrix products  29.9 us (9%)
  blocking collectives  22.5 us (7%)
  between operations  13.8 us (4%)
  other arithmetic  4.77 us (2%)
    ppermute x8, waiting for transfers between devices, shifted(): return lax.ppermute(value, axis, pairs)  67.9 us
    all_gather x1, waiting for transfers between devices, routed_branch(): slot_rows = lax.all_gather(own_rows, 'ey', axis=0, tiled=False)  43.5 us
    ppermute x8, starting transfers between devices, shifted(): return lax.ppermute(value, axis, pairs)  32.6 us
    all_to_all x2, waiting for transfers between devices, routed_branch(): lax.all_to_all(expert_out, 'ex', split_axis=0, concat_axis=0, tiled=True)  23 us
    all_to_all x2, blocking collectives, routed_branch(): lax.all_to_all(per_expert, 'ex', split_axis=0, concat_axis=0, tiled=True)  22.5 us
    all_gather x1, waiting for transfers between devices, routed_branch(): slot_rows = lax.all_gather(from_x, 'ey', axis=0, tiled=False)  16.9 us
    unnamed x25, local copies, waits for them, and re-layouts  14.2 us
    all_to_all x2, starting transfers between devices, routed_branch(): lax.all_to_all(hidden, 'ey', split_axis=0, concat_axis=0, tiled=True)  9.48 us
  transfers between devices with their start and end apart: 14, of which 11 were waited for; matrix products, arithmetic and copies ran while one was open for 12% of the time, Pallas kernels for 0%

profile of v12, /device:TPU:1, one launch (start us, length us, event | category | flops | bytes accessed | tf_op | source)
XLA Modules:
  0.0 313.7 jit_solution(3644914241703645569)
XLA Ops:
  12.5 11.5 %all_to_all.30 = bf16[4,476,128]{2,1,0:T(8,128)(2,1)} all-to-all(bf16[4,476,128]{2,1,0:T(8,128)(2,1)S(1)} %reshape.218), channel_id=1, replica_groups=mesh['pipe'=16,'ex'=4,'ey'=8] {'ex'}, dimensions={0} | all-to-all | bytes 974848 | tf_op jit(solution)/shard_map/all_to_all | solution.py:56
  24.0 4.7 %collective-permute-start.3 = (bf16[128,3584]{1,0:T(8,128)(2,1)}, bf16[128,3584]{1,0:T(8,128)(2,1)S(1)}, u32[]{:S(2)}, u32[]{:S(2)}) collective-permute-start(bf16[128,3584]{1,0:T(8,128)(2,1)} %bitcast.105), channel_id=1, source_target_pairs={{0,1},{1,2},{2,3},{3,4},{4,5},{5,6},{6,7},{7,0},{8,9},{9,10},{10,1... | collective-permute-start | bytes 2752520 | tf_op jit(solution)/shard_map/ppermute | solution.py:20
  28.7 3.8 %collective-permute-start = (bf16[128,3584]{1,0:T(8,128)(2,1)}, bf16[128,3584]{1,0:T(8,128)(2,1)}, u32[]{:S(2)}, u32[]{:S(2)}) collective-permute-start(bf16[128,3584]{1,0:T(8,128)(2,1)} %bitcast.106), channel_id=1, source_target_pairs={{0,7},{1,0},{2,1},{3,2},{4,3},{5,4},{6,5},{7,6},{8,15},{9,8},{10,9... | collective-permute-start | bytes 2752520 | tf_op jit(solution)/shard_map/ppermute | solution.py:20
  32.5 14.3 %collective-permute-done.3 = bf16[128,3584]{1,0:T(8,128)(2,1)S(1)} collective-permute-done((bf16[128,3584]{1,0:T(8,128)(2,1)}, bf16[128,3584]{1,0:T(8,128)(2,1)S(1)}, u32[]{:S(2)}, u32[]{:S(2)}) %collective-permute-start.3) | collective-permute-done | bytes 917536 | tf_op jit(solution)/shard_map/ppermute | solution.py:20
  46.8 6.0 %collective-permute-start.4 = (bf16[128,3584]{1,0:T(8,128)(2,1)S(1)}, bf16[128,3584]{1,0:T(8,128)(2,1)}, u32[]{:S(2)}, u32[]{:S(2)}) collective-permute-start(bf16[128,3584]{1,0:T(8,128)(2,1)S(1)} %collective-permute-done.3), channel_id=1, source_target_pairs={{0,1},{1,2},{2,3},{3,4},{4,5},{5,6},{6,7},{7,0},{8,9},{9,10},{10,1... | collective-permute-start | bytes 2752520 | tf_op jit(solution)/shard_map/ppermute | solution.py:20
  52.8 4.4 %collective-permute-start.1 = (bf16[128,3584]{1,0:T(8,128)(2,1)}, bf16[128,3584]{1,0:T(8,128)(2,1)}, u32[]{:S(2)}, u32[]{:S(2)}) collective-permute-start(bf16[128,3584]{1,0:T(8,128)(2,1)} %collective-permute-done), channel_id=1, source_target_pairs={{0,7},{1,0},{2,1},{3,2},{4,3},{5,4},{6,5},{7,6},{8,15},{9,8},{10,9... | collective-permute-start | bytes 2752520 | tf_op jit(solution)/shard_map/ppermute | solution.py:20
  57.2 36.3 %collective-permute-done.4 = bf16[128,3584]{1,0:T(8,128)(2,1)} collective-permute-done((bf16[128,3584]{1,0:T(8,128)(2,1)S(1)}, bf16[128,3584]{1,0:T(8,128)(2,1)}, u32[]{:S(2)}, u32[]{:S(2)}) %collective-permute-start.4) | collective-permute-done | bytes 917536 | tf_op jit(solution)/shard_map/ppermute | solution.py:20
  95.5 16.9 %all-gather.5.cloned.1.call-done = bf16[32,476,128]{2,1,0:T(8,128)(2,1)} async-done(((bf16[4,476,128]{2,1,0:T(8,128)(2,1)}), bf16[32,476,128]{2,1,0:T(8,128)(2,1)}) %all-gather.5.cloned.1.call-update) | async-done | bytes 3899408 | tf_op jit(solution)/shard_map/all_gather | solution.py:58
  112.3 7.0 %reshape.219 = bf16[544,3584]{1,0:T(8,128)(2,1)} reshape(bf16[32,476,128]{2,1,0:T(8,128)(2,1)} %all-gather.5.cloned.1.call-done) | data formatting | bytes 7798784 | tf_op jit(solution)/shard_map/reshape | solution.py:60
  126.9 5.3 %all-to-all-start.1 = ((bf16[8,68,128]{2,1,0:T(8,128)(2,1)}), bf16[8,68,128]{2,1,0:T(8,128)(2,1)S(1)}, u32[]{:S(2)}, u32[]{:S(2)}) async-start(bf16[8,68,128]{2,1,0:T(8,128)(2,1)} %reshape.220), calls=%async_computation.1 | async-start | bytes 294912 | tf_op jit(solution)/shard_map/all_to_all | solution.py:72
  132.3 4.6 %collective-permute-start.2 = (bf16[128,3584]{1,0:T(8,128)(2,1)}, bf16[128,3584]{1,0:T(8,128)(2,1)}, u32[]{:S(2)}, u32[]{:S(2)}) collective-permute-start(bf16[128,3584]{1,0:T(8,128)(2,1)} %collective-permute-done.1), channel_id=1, source_target_pairs={{0,7},{1,0},{2,1},{3,2},{4,3},{5,4},{6,5},{7,6},{8,15},{9,8},{10,9... | collective-permute-start | bytes 2752520 | tf_op jit(solution)/shard_map/ppermute | solution.py:20
  147.5 10.5 %collective-permute-done.2 = bf16[128,3584]{1,0:T(8,128)(2,1)} collective-permute-done((bf16[128,3584]{1,0:T(8,128)(2,1)}, bf16[128,3584]{1,0:T(8,128)(2,1)}, u32[]{:S(2)}, u32[]{:S(2)}) %collective-permute-start.2) | collective-permute-done | bytes 917536 | tf_op jit(solution)/shard_map/ppermute | solution.py:20
  163.4 3.6 %all-to-all-start.2 = ((f32[4,476,128]{2,1,0:T(8,128)}), f32[4,476,128]{2,1,0:T(8,128)S(1)}, u32[]{:S(2)}, u32[]{:S(2)}) async-start(f32[4,476,128]{2,1,0:T(8,128)} %reshape.221), calls=%async_computation.2 | async-start | bytes 1966080 | tf_op jit(solution)/shard_map/all_to_all | solution.py:86
  167.0 11.6 %all-to-all-done.2 = f32[4,476,128]{2,1,0:T(8,128)S(1)} async-done(((f32[4,476,128]{2,1,0:T(8,128)}), f32[4,476,128]{2,1,0:T(8,128)S(1)}, u32[]{:S(2)}, u32[]{:S(2)}) %all-to-all-start.2) | async-done | bytes 974880 | tf_op jit(solution)/shard_map/all_to_all | solution.py:86
  179.9 5.3 %collective-permute-start.7 = (bf16[64,3584]{1,0:T(8,128)(2,1)S(1)}, bf16[64,3584]{1,0:T(8,128)(2,1)S(1)}, u32[]{:S(2)}, u32[]{:S(2)}) collective-permute-start(bf16[64,3584]{1,0:T(8,128)(2,1)S(1)} %fusion.16), channel_id=1, source_target_pairs={{0,32},{32,64},{64,96},{96,128},{128,160},{160,192},{192,224},{224... | collective-permute-start | bytes 1376264 | tf_op jit(solution)/shard_map/ppermute | solution.py:20
  185.1 5.4 %collective-permute-done.7 = bf16[64,3584]{1,0:T(8,128)(2,1)S(1)} collective-permute-done((bf16[64,3584]{1,0:T(8,128)(2,1)S(1)}, bf16[64,3584]{1,0:T(8,128)(2,1)S(1)}, u32[]{:S(2)}, u32[]{:S(2)}) %collective-permute-start.7) | collective-permute-done | bytes 458784 | tf_op jit(solution)/shard_map/ppermute | solution.py:20
  192.6 11.0 %all_to_all.31 = bf16[4,476,128]{2,1,0:T(8,128)(2,1)} all-to-all(bf16[4,476,128]{2,1,0:T(8,128)(2,1)} %reshape.223), channel_id=1, replica_groups=mesh['pipe'=16,'ex'=4,'ey'=8] {'ex'}, dimensions={0} | all-to-all | bytes 974848 | tf_op jit(solution)/shard_map/all_to_all | solution.py:56
  220.2 43.5 %all-gather.7.cloned.1.call-done = bf16[576,3584]{1,0:T(8,128)(2,1)} async-done(((bf16[72,3584]{1,0:T(8,128)(2,1)}), bf16[576,3584]{1,0:T(8,128)(2,1)}) %all-gather.7.cloned.1.call-update) | async-done | bytes 4128784 | tf_op jit(solution)/shard_map/all_gather | solution.py:65
  267.1 4.1 %fusion.7 = bf16[576,128]{1,0:T(8,128)(2,1)} fusion(bf16[576,3584]{1,0:T(8,128)(2,1)} %all-gather.7.cloned.1.call-done, bf16[1,1,3584,128]{3,2,1,0:T(8,128)(2,1)S(1)} %copy-done.8, f32[576,128]{1,0:T(8,128)S(1)} %fusion.19), kind=kOutput, calls=%fused_computation.30 | convolution fusion | flops 528924672 | bytes 5488640 | tf_op jit(solution)/shard_map/dot_general | solution.py:69
  271.2 4.2 %all-to-all-start.4 = ((bf16[8,68,128]{2,1,0:T(8,128)(2,1)}), bf16[8,68,128]{2,1,0:T(8,128)(2,1)S(1)}, u32[]{:S(2)}, u32[]{:S(2)}) async-start(bf16[8,68,128]{2,1,0:T(8,128)(2,1)} %bitcast.104), calls=%async_computation.4 | async-start | bytes 294912 | tf_op jit(solution)/shard_map/all_to_all | solution.py:72
  276.4 6.9 %all-to-all-done.4 = bf16[8,68,128]{2,1,0:T(8,128)(2,1)S(1)} async-done(((bf16[8,68,128]{2,1,0:T(8,128)(2,1)}), bf16[8,68,128]{2,1,0:T(8,128)(2,1)S(1)}, u32[]{:S(2)}, u32[]{:S(2)}) %all-to-all-start.4) | async-done | bytes 139296 | tf_op jit(solution)/shard_map/all_to_all | solution.py:72
  283.9 4.5 %reduce-precision_reduce_fusion = f32[68,3584]{1,0:T(8,128)S(1)} fusion(bf16[8,128,3584]{2,1,0:T(8,128)(2,1)} %bitcast_dynamic-update-slice_fusion, bf16[8,68,128]{2,1,0:T(8,128)(2,1)S(1)} %gather_fusion.3, pred[8]{0:T(512)(128)(4,1)S(1)} %compare_and_fusion), kind=kOutput, calls=%fused_computation.4 | convolution fusion | flops 502847488 | bytes 8454152 | tf_op jit(solution)/shard_map/jrh,jhd->jrd/dot_general | solution.py:82
  289.4 4.0 %all-to-all-start.5 = ((f32[4,476,128]{2,1,0:T(8,128)}), f32[4,476,128]{2,1,0:T(8,128)S(1)}, u32[]{:S(2)}, u32[]{:S(2)}) async-start(f32[4,476,128]{2,1,0:T(8,128)} %reshape.227), calls=%async_computation.5 | async-start | bytes 1966080 | tf_op jit(solution)/shard_map/all_to_all | solution.py:86
  293.4 11.4 %all-to-all-done.5 = f32[4,476,128]{2,1,0:T(8,128)S(1)} async-done(((f32[4,476,128]{2,1,0:T(8,128)}), f32[4,476,128]{2,1,0:T(8,128)S(1)}, u32[]{:S(2)}, u32[]{:S(2)}) %all-to-all-start.5) | async-done | bytes 974880 | tf_op jit(solution)/shard_map/all_to_all | solution.py:86
  (85 shorter events, 59.3 us)
Async XLA Ops:
  6.5 112.8 %copy-start = (bf16[1,1,3584,128]{3,2,1,0:T(8,128)(2,1)S(1)}, bf16[1,1,3584,128]{3,2,1,0:T(8,128)(2,1)}, u32[]{:S(2)}) copy-start(bf16[1,1,3584,128]{3,2,1,0:T(8,128)(2,1)} %param.11) | copy-start | bytes 2752516
  6.5 105.8 %all-gather.5.cloned.1.call-start = ((), (), s32[]{:S(2)}) async-start(), calls=%async_computation.6 | async-start | bytes 4423680 | tf_op jit(solution)/shard_map/all_gather | solution.py:58
  24.0 22.7 %collective-permute-start.3 = (bf16[128,3584]{1,0:T(8,128)(2,1)}, bf16[128,3584]{1,0:T(8,128)(2,1)S(1)}, u32[]{:S(2)}, u32[]{:S(2)}) collective-permute-start(bf16[128,3584]{1,0:T(8,128)(2,1)} %bitcast.105), channel_id=1, source_target_pairs={{0,1},{1,2},{2,3},{3,4},{4,5},{5,6},{6,7},{7,0},{8,9},{9,10},{10,1... | collective-permute-start | bytes 2752520 | tf_op jit(solution)/shard_map/ppermute | solution.py:20
  28.7 24.1 %collective-permute-start = (bf16[128,3584]{1,0:T(8,128)(2,1)}, bf16[128,3584]{1,0:T(8,128)(2,1)}, u32[]{:S(2)}, u32[]{:S(2)}) collective-permute-start(bf16[128,3584]{1,0:T(8,128)(2,1)} %bitcast.106), channel_id=1, source_target_pairs={{0,7},{1,0},{2,1},{3,2},{4,3},{5,4},{6,5},{7,6},{8,15},{9,8},{10,9... | collective-permute-start | bytes 2752520 | tf_op jit(solution)/shard_map/ppermute | solution.py:20
  46.8 94.5 %copy-start.4 = (bf16[128,3584]{1,0:T(8,128)(2,1)}, bf16[128,3584]{1,0:T(8,128)(2,1)S(1)}, u32[]{:S(2)}) copy-start(bf16[128,3584]{1,0:T(8,128)(2,1)S(1)} %collective-permute-done.3) | copy-start | bytes 2752516
  46.8 46.8 %collective-permute-start.4 = (bf16[128,3584]{1,0:T(8,128)(2,1)S(1)}, bf16[128,3584]{1,0:T(8,128)(2,1)}, u32[]{:S(2)}, u32[]{:S(2)}) collective-permute-start(bf16[128,3584]{1,0:T(8,128)(2,1)S(1)} %collective-permute-done.3), channel_id=1, source_target_pairs={{0,1},{1,2},{2,3},{3,4},{4,5},{5,6},{6,7},{7,0},{8,9},{9,10},{10,1... | collective-permute-start | bytes 2752520 | tf_op jit(solution)/shard_map/ppermute | solution.py:20
  52.8 79.5 %collective-permute-start.1 = (bf16[128,3584]{1,0:T(8,128)(2,1)}, bf16[128,3584]{1,0:T(8,128)(2,1)}, u32[]{:S(2)}, u32[]{:S(2)}) collective-permute-start(bf16[128,3584]{1,0:T(8,128)(2,1)} %collective-permute-done), channel_id=1, source_target_pairs={{0,7},{1,0},{2,1},{3,2},{4,3},{5,4},{6,5},{7,6},{8,15},{9,8},{10,9... | collective-permute-start | bytes 2752520 | tf_op jit(solution)/shard_map/ppermute | solution.py:20
  93.5 43.3 %collective-permute-start.5 = (bf16[128,3584]{1,0:T(8,128)(2,1)}, bf16[128,3584]{1,0:T(8,128)(2,1)}, u32[]{:S(2)}, u32[]{:S(2)}) collective-permute-start(bf16[128,3584]{1,0:T(8,128)(2,1)} %collective-permute-done.4), channel_id=1, source_target_pairs={{0,1},{1,2},{2,3},{3,4},{4,5},{5,6},{6,7},{7,0},{8,9},{9,10},{10,1... | collective-permute-start | bytes 2752520 | tf_op jit(solution)/shard_map/ppermute | solution.py:20
  119.3 21.7 %copy-start.2 = (bf16[1,1,128,3584]{3,2,1,0:T(8,128)(2,1)S(1)}, bf16[1,1,128,3584]{3,2,1,0:T(8,128)(2,1)}, u32[]{:S(2)}) copy-start(bf16[1,1,128,3584]{3,2,1,0:T(8,128)(2,1)} %param.13) | copy-start | bytes 2752516
  126.9 13.4 %all-to-all-start.1 = ((bf16[8,68,128]{2,1,0:T(8,128)(2,1)}), bf16[8,68,128]{2,1,0:T(8,128)(2,1)S(1)}, u32[]{:S(2)}, u32[]{:S(2)}) async-start(bf16[8,68,128]{2,1,0:T(8,128)(2,1)} %reshape.220), calls=%async_computation.1 | async-start | bytes 294912 | tf_op jit(solution)/shard_map/all_to_all | solution.py:72
  132.3 25.7 %collective-permute-start.2 = (bf16[128,3584]{1,0:T(8,128)(2,1)}, bf16[128,3584]{1,0:T(8,128)(2,1)}, u32[]{:S(2)}, u32[]{:S(2)}) collective-permute-start(bf16[128,3584]{1,0:T(8,128)(2,1)} %collective-permute-done.1), channel_id=1, source_target_pairs={{0,7},{1,0},{2,1},{3,2},{4,3},{5,4},{6,5},{7,6},{8,15},{9,8},{10,9... | collective-permute-start | bytes 2752520 | tf_op jit(solution)/shard_map/ppermute | solution.py:20
  136.9 24.0 %collective-permute-start.6 = (bf16[128,3584]{1,0:T(8,128)(2,1)}, bf16[128,3584]{1,0:T(8,128)(2,1)}, u32[]{:S(2)}, u32[]{:S(2)}) collective-permute-start(bf16[128,3584]{1,0:T(8,128)(2,1)} %collective-permute-done.5), channel_id=1, source_target_pairs={{0,1},{1,2},{2,3},{3,4},{4,5},{5,6},{6,7},{7,0},{8,9},{9,10},{10,1... | collective-permute-start | bytes 2752520 | tf_op jit(solution)/shard_map/ppermute | solution.py:20
  146.0 21.0 %copy-start.6 = (s32[1,2,64,1]{2,3,1,0:T(1,128)S(1)}, s32[1,2,64,1]{2,3,1,0:T(1,128)}, u32[]{:S(2)}) copy-start(s32[1,2,64,1]{2,3,1,0:T(1,128)} %param.14) | copy-start | bytes 1540
  146.0 21.0 %copy-start.7 = (s32[1,2,64,1]{2,3,1,0:T(1,128)S(1)}, s32[1,2,64,1]{2,3,1,0:T(1,128)}, u32[]{:S(2)}) copy-start(s32[1,2,64,1]{2,3,1,0:T(1,128)} %param.15) | copy-start | bytes 1540
  162.4 17.3 %copy-start.1 = (bf16[1,64,3584]{2,1,0:T(8,128)(2,1)S(1)}, bf16[1,64,3584]{2,1,0:T(8,128)(2,1)}, u32[]{:S(2)}) copy-start(bf16[1,64,3584]{2,1,0:T(8,128)(2,1)} %param.9) | copy-start | bytes 1376260
  163.4 15.2 %all-to-all-start.2 = ((f32[4,476,128]{2,1,0:T(8,128)}), f32[4,476,128]{2,1,0:T(8,128)S(1)}, u32[]{:S(2)}, u32[]{:S(2)}) async-start(f32[4,476,128]{2,1,0:T(8,128)} %reshape.221), calls=%async_computation.2 | async-start | bytes 1966080 | tf_op jit(solution)/shard_map/all_to_all | solution.py:86
  167.0 96.7 %all-gather.7.cloned.1.call-start = ((), (), s32[]{:S(2)}) async-start(), calls=%async_computation.7 | async-start | bytes 4644864 | tf_op jit(solution)/shard_map/all_gather | solution.py:65
  179.7 26.3 %copy-start.3 = (bf16[1,1,128,3584]{3,2,1,0:T(8,128)(2,1)S(1)}, bf16[1,1,128,3584]{3,2,1,0:T(8,128)(2,1)}, u32[]{:S(2)}) copy-start(bf16[1,1,128,3584]{3,2,1,0:T(8,128)(2,1)} %param.13) | copy-start | bytes 2752516
  179.9 10.7 %collective-permute-start.7 = (bf16[64,3584]{1,0:T(8,128)(2,1)S(1)}, bf16[64,3584]{1,0:T(8,128)(2,1)S(1)}, u32[]{:S(2)}, u32[]{:S(2)}) collective-permute-start(bf16[64,3584]{1,0:T(8,128)(2,1)S(1)} %fusion.16), channel_id=1, source_target_pairs={{0,32},{32,64},{64,96},{96,128},{128,160},{160,192},{192,224},{224... | collective-permute-start | bytes 1376264 | tf_op jit(solution)/shard_map/ppermute | solution.py:20
  211.4 55.7 %copy-start.8 = (bf16[1,1,3584,128]{3,2,1,0:T(8,128)(2,1)S(1)}, bf16[1,1,3584,128]{3,2,1,0:T(8,128)(2,1)}, u32[]{:S(2)}) copy-start(bf16[1,1,3584,128]{3,2,1,0:T(8,128)(2,1)} %param.12) | copy-start | bytes 2752516
  220.2 55.2 %copy-start.5 = (bf16[128,3584]{1,0:T(8,128)(2,1)S(1)}, bf16[128,3584]{1,0:T(8,128)(2,1)}, u32[]{:S(2)}) copy-start(bf16[128,3584]{1,0:T(8,128)(2,1)} %copy-done.4) | copy-start | bytes 2752516
  271.2 12.1 %all-to-all-start.4 = ((bf16[8,68,128]{2,1,0:T(8,128)(2,1)}), bf16[8,68,128]{2,1,0:T(8,128)(2,1)S(1)}, u32[]{:S(2)}, u32[]{:S(2)}) async-start(bf16[8,68,128]{2,1,0:T(8,128)(2,1)} %bitcast.104), calls=%async_computation.4 | async-start | bytes 294912 | tf_op jit(solution)/shard_map/all_to_all | solution.py:72
  289.4 15.4 %all-to-all-start.5 = ((f32[4,476,128]{2,1,0:T(8,128)}), f32[4,476,128]{2,1,0:T(8,128)S(1)}, u32[]{:S(2)}, u32[]{:S(2)}) async-start(f32[4,476,128]{2,1,0:T(8,128)} %reshape.227), calls=%async_computation.5 | async-start | bytes 1966080 | tf_op jit(solution)/shard_map/all_to_all | solution.py:86
Sparse Core Ops, SparseCore 0:
  24.2 88.1 all-gather.4
  206.1 57.5 all-gather.6

commit v13 on v10

--- a/solution.py
+++ b/solution.py
@@ -7,6 +7,7 @@
 EXPERTS = 4
 MOST = 17
 LANE = 128
+SUBLANE = 8
 
 
 NORM_EPS = 1e-06
@@ -53,13 +54,16 @@
     block_rows = MOST * model_width // LANE
     per_expert = place_rows(normed, slot_ids, EXPERTS * MOST).reshape(EXPERTS, block_rows, LANE)
     from_x = lax.all_to_all(per_expert, "ex", split_axis=0, concat_axis=0, tiled=True)
-    slot_rows = lax.all_gather(from_x, "ey", axis=0, tiled=False)
+    held = n_x * MOST
+    padded = -(-held // SUBLANE) * SUBLANE
+    own_rows = jnp.pad(from_x.reshape(held, model_width), ((0, padded - held), (0, 0)))
+    slot_rows = lax.all_gather(own_rows, "ey", axis=0, tiled=False)
     n_y = slot_rows.shape[0]
     flat_rows = slot_rows.reshape(-1, model_width)
     gate_act = jnp.dot(flat_rows, w_gate, preferred_element_type=jnp.float32)
     up_act = jnp.dot(flat_rows, w_up, preferred_element_type=jnp.float32)
     hidden = (jax.nn.silu(gate_act) * up_act).astype(jnp.bfloat16)
-    hidden = hidden.reshape(n_y, n_x * MOST, hidden.shape[-1])
+    hidden = hidden.reshape(n_y, -1, hidden.shape[-1])[:, : n_x * MOST]
     hidden_here = lax.all_to_all(hidden, "ey", split_axis=0, concat_axis=0, tiled=True)
     me_y = lax.axis_index("ey")
     hidden_rel = jnp.take(hidden_here, (me_y + jnp.arange(n_y)) % n_y, axis=0)

time: 318 us -> 314 us (0.987)
  local copies, waits for them, and re-layouts: 39.1 us -> 27.1 us
  waiting for transfers between devices: 157 us -> 163 us
    reshape x4 -> x2, local copies, waits for them, and re-layouts: 15.4 us -> 2.13 us  [routed_branch(): from_x.reshape(held, model_width)]
    all_gather x2, waiting for transfers between devices: 57.4 us -> 63 us  [routed_branch(): slot_rows = lax.all_gather(own_rows, 'ey', axis=0, tiled=False)]
    unnamed x23 -> x25, local copies, waits for them, and re-layouts: 15.3 us -> 14.2 us
  transfers between devices with their start and end apart: 14 -> 14, of which waited for: 11 -> 12; matrix products, arithmetic and copies ran while one was open for 13% -> 10% of each run, Pallas kernels for 0% -> 0%
where the time goes in v13:
time: 314 us; the launch traced here: 311 us
  waiting for transfers between devices  163 us (52%)
  starting transfers between devices  49.3 us (16%)
  matrix products  30.7 us (10%)
  local copies, waits for them, and re-layouts  27.1 us (9%)
  blocking collectives  22.3 us (7%)
  between operations  13.8 us (4%)
  other arithmetic  4.77 us (2%)
    ppermute x8, waiting for transfers between devices, shifted(): return lax.ppermute(value, axis, pairs)  68.1 us
    all_gather x2, waiting for transfers between devices, routed_branch(): slot_rows = lax.all_gather(own_rows, 'ey', axis=0, tiled=False)  63 us
    ppermute x8, starting transfers between devices, shifted(): return lax.ppermute(value, axis, pairs)  32 us
    all_to_all x2, waiting for transfers between devices, routed_branch(): lax.all_to_all(expert_out, 'ex', split_axis=0, concat_axis=0, tiled=True)  23 us
    all_to_all x2, blocking collectives, routed_branch(): lax.all_to_all(per_expert, 'ex', split_axis=0, concat_axis=0, tiled=True)  22.3 us
    unnamed x25, local copies, waits for them, and re-layouts  14.2 us
    dot_general x8, matrix products, routed_branch(): jnp.dot(hidden_rel[d], down_all[d], preferred_element_type=jnp.float32)  9.38 us
    all_to_all x2, starting transfers between devices, routed_branch(): lax.all_to_all(hidden, 'ey', split_axis=0, concat_axis=0, tiled=True)  9.34 us
  transfers between devices with their start and end apart: 14, of which 12 were waited for; matrix products, arithmetic and copies ran while one was open for 10% of the time, Pallas kernels for 0%

profile of v13, /device:TPU:1, one launch (start us, length us, event | category | flops | bytes accessed | tf_op | source)
XLA Modules:
  0.0 310.6 jit_solution(18014166007486798350)
XLA Ops:
  12.5 11.4 %all_to_all.30 = bf16[4,476,128]{2,1,0:T(8,128)(2,1)S(1)} all-to-all(bf16[4,476,128]{2,1,0:T(8,128)(2,1)S(1)} %reshape.221), channel_id=1, replica_groups=mesh['pipe'=16,'ex'=4,'ey'=8] {'ex'}, dimensions={0} | all-to-all | bytes 974848 | tf_op jit(solution)/shard_map/all_to_all | solution.py:56
  25.3 4.7 %collective-permute-start.3 = (bf16[128,3584]{1,0:T(8,128)(2,1)}, bf16[128,3584]{1,0:T(8,128)(2,1)S(1)}, u32[]{:S(2)}, u32[]{:S(2)}) collective-permute-start(bf16[128,3584]{1,0:T(8,128)(2,1)} %bitcast.107), channel_id=1, source_target_pairs={{0,1},{1,2},{2,3},{3,4},{4,5},{5,6},{6,7},{7,0},{8,9},{9,10},{10,1... | collective-permute-start | bytes 2752520 | tf_op jit(solution)/shard_map/ppermute | solution.py:20
  30.0 3.8 %collective-permute-start = (bf16[128,3584]{1,0:T(8,128)(2,1)}, bf16[128,3584]{1,0:T(8,128)(2,1)}, u32[]{:S(2)}, u32[]{:S(2)}) collective-permute-start(bf16[128,3584]{1,0:T(8,128)(2,1)} %bitcast.108), channel_id=1, source_target_pairs={{0,7},{1,0},{2,1},{3,2},{4,3},{5,4},{6,5},{7,6},{8,15},{9,8},{10,9... | collective-permute-start | bytes 2752520 | tf_op jit(solution)/shard_map/ppermute | solution.py:20
  33.8 15.0 %collective-permute-done.3 = bf16[128,3584]{1,0:T(8,128)(2,1)S(1)} collective-permute-done((bf16[128,3584]{1,0:T(8,128)(2,1)}, bf16[128,3584]{1,0:T(8,128)(2,1)S(1)}, u32[]{:S(2)}, u32[]{:S(2)}) %collective-permute-start.3) | collective-permute-done | bytes 917536 | tf_op jit(solution)/shard_map/ppermute | solution.py:20
  48.8 5.3 %collective-permute-start.4 = (bf16[128,3584]{1,0:T(8,128)(2,1)S(1)}, bf16[128,3584]{1,0:T(8,128)(2,1)}, u32[]{:S(2)}, u32[]{:S(2)}) collective-permute-start(bf16[128,3584]{1,0:T(8,128)(2,1)S(1)} %collective-permute-done.3), channel_id=1, source_target_pairs={{0,1},{1,2},{2,3},{3,4},{4,5},{5,6},{6,7},{7,0},{8,9},{9,10},{10,1... | collective-permute-start | bytes 2752520 | tf_op jit(solution)/shard_map/ppermute | solution.py:20
  54.8 4.9 %collective-permute-start.1 = (bf16[128,3584]{1,0:T(8,128)(2,1)}, bf16[128,3584]{1,0:T(8,128)(2,1)}, u32[]{:S(2)}, u32[]{:S(2)}) collective-permute-start(bf16[128,3584]{1,0:T(8,128)(2,1)} %collective-permute-done), channel_id=1, source_target_pairs={{0,7},{1,0},{2,1},{3,2},{4,3},{5,4},{6,5},{7,6},{8,15},{9,8},{10,9... | collective-permute-start | bytes 2752520 | tf_op jit(solution)/shard_map/ppermute | solution.py:20
  59.7 35.1 %collective-permute-done.4 = bf16[128,3584]{1,0:T(8,128)(2,1)} collective-permute-done((bf16[128,3584]{1,0:T(8,128)(2,1)S(1)}, bf16[128,3584]{1,0:T(8,128)(2,1)}, u32[]{:S(2)}, u32[]{:S(2)}) %collective-permute-start.4) | collective-permute-done | bytes 917536 | tf_op jit(solution)/shard_map/ppermute | solution.py:20
  96.7 20.3 %all-gather.5.cloned.1.call-done = bf16[576,3584]{1,0:T(8,128)(2,1)} async-done(((bf16[72,3584]{1,0:T(8,128)(2,1)}), bf16[576,3584]{1,0:T(8,128)(2,1)}) %all-gather.5.cloned.1.call-update) | async-done | bytes 4128784 | tf_op jit(solution)/shard_map/all_gather | solution.py:60
  120.4 4.3 %fusion.7 = bf16[576,128]{1,0:T(8,128)(2,1)} fusion(bf16[576,3584]{1,0:T(8,128)(2,1)} %all-gather.5.cloned.1.call-done, bf16[1,1,3584,128]{3,2,1,0:T(8,128)(2,1)} %param.12, f32[576,128]{1,0:T(8,128)S(1)} %fusion.21), kind=kOutput, calls=%fused_computation.30 | convolution fusion | flops 528924672 | bytes 5488640 | tf_op jit(solution)/shard_map/dot_general | solution.py:64
  124.7 5.1 %all-to-all-start.1 = ((bf16[8,68,128]{2,1,0:T(8,128)(2,1)}), bf16[8,68,128]{2,1,0:T(8,128)(2,1)S(1)}, u32[]{:S(2)}, u32[]{:S(2)}) async-start(bf16[8,68,128]{2,1,0:T(8,128)(2,1)} %bitcast.105), calls=%async_computation.1 | async-start | bytes 294912 | tf_op jit(solution)/shard_map/all_to_all | solution.py:67
  129.9 4.6 %collective-permute-start.2 = (bf16[128,3584]{1,0:T(8,128)(2,1)}, bf16[128,3584]{1,0:T(8,128)(2,1)}, u32[]{:S(2)}, u32[]{:S(2)}) collective-permute-start(bf16[128,3584]{1,0:T(8,128)(2,1)} %collective-permute-done.1), channel_id=1, source_target_pairs={{0,7},{1,0},{2,1},{3,2},{4,3},{5,4},{6,5},{7,6},{8,15},{9,8},{10,9... | collective-permute-start | bytes 2752520 | tf_op jit(solution)/shard_map/ppermute | solution.py:20
  145.2 10.5 %collective-permute-done.2 = bf16[128,3584]{1,0:T(8,128)(2,1)} collective-permute-done((bf16[128,3584]{1,0:T(8,128)(2,1)}, bf16[128,3584]{1,0:T(8,128)(2,1)}, u32[]{:S(2)}, u32[]{:S(2)}) %collective-permute-start.2) | collective-permute-done | bytes 917536 | tf_op jit(solution)/shard_map/ppermute | solution.py:20
  161.1 4.0 %all-to-all-start.2 = ((f32[4,476,128]{2,1,0:T(8,128)}), f32[4,476,128]{2,1,0:T(8,128)S(1)}, u32[]{:S(2)}, u32[]{:S(2)}) async-start(f32[4,476,128]{2,1,0:T(8,128)} %reshape.225), calls=%async_computation.2 | async-start | bytes 1966080 | tf_op jit(solution)/shard_map/all_to_all | solution.py:81
  165.1 11.6 %all-to-all-done.2 = f32[4,476,128]{2,1,0:T(8,128)S(1)} async-done(((f32[4,476,128]{2,1,0:T(8,128)}), f32[4,476,128]{2,1,0:T(8,128)S(1)}, u32[]{:S(2)}, u32[]{:S(2)}) %all-to-all-start.2) | async-done | bytes 974880 | tf_op jit(solution)/shard_map/all_to_all | solution.py:81
  178.0 5.0 %collective-permute-start.7 = (bf16[64,3584]{1,0:T(8,128)(2,1)S(1)}, bf16[64,3584]{1,0:T(8,128)(2,1)S(1)}, u32[]{:S(2)}, u32[]{:S(2)}) collective-permute-start(bf16[64,3584]{1,0:T(8,128)(2,1)S(1)} %fusion.16), channel_id=1, source_target_pairs={{0,32},{32,64},{64,96},{96,128},{128,160},{160,192},{192,224},{224... | collective-permute-start | bytes 1376264 | tf_op jit(solution)/shard_map/ppermute | solution.py:20
  182.9 5.4 %collective-permute-done.7 = bf16[64,3584]{1,0:T(8,128)(2,1)S(1)} collective-permute-done((bf16[64,3584]{1,0:T(8,128)(2,1)S(1)}, bf16[64,3584]{1,0:T(8,128)(2,1)S(1)}, u32[]{:S(2)}, u32[]{:S(2)}) %collective-permute-start.7) | collective-permute-done | bytes 458784 | tf_op jit(solution)/shard_map/ppermute | solution.py:20
  190.3 10.9 %all_to_all.31 = bf16[4,476,128]{2,1,0:T(8,128)(2,1)} all-to-all(bf16[4,476,128]{2,1,0:T(8,128)(2,1)} %reshape.227), channel_id=1, replica_groups=mesh['pipe'=16,'ex'=4,'ey'=8] {'ex'}, dimensions={0} | all-to-all | bytes 974848 | tf_op jit(solution)/shard_map/all_to_all | solution.py:56
  218.0 42.7 %all-gather.7.cloned.1.call-done = bf16[576,3584]{1,0:T(8,128)(2,1)} async-done(((bf16[72,3584]{1,0:T(8,128)(2,1)}), bf16[576,3584]{1,0:T(8,128)(2,1)}) %all-gather.7.cloned.1.call-update) | async-done | bytes 4128784 | tf_op jit(solution)/shard_map/all_gather | solution.py:60
  264.1 4.1 %fusion.8 = bf16[576,128]{1,0:T(8,128)(2,1)} fusion(bf16[576,3584]{1,0:T(8,128)(2,1)} %all-gather.7.cloned.1.call-done, bf16[1,1,3584,128]{3,2,1,0:T(8,128)(2,1)S(1)} %copy-done.8, f32[576,128]{1,0:T(8,128)S(1)} %fusion.19), kind=kOutput, calls=%fused_computation.31 | convolution fusion | flops 528924672 | bytes 5488640 | tf_op jit(solution)/shard_map/dot_general | solution.py:64
  268.1 4.2 %all-to-all-start.4 = ((bf16[8,68,128]{2,1,0:T(8,128)(2,1)}), bf16[8,68,128]{2,1,0:T(8,128)(2,1)S(1)}, u32[]{:S(2)}, u32[]{:S(2)}) async-start(bf16[8,68,128]{2,1,0:T(8,128)(2,1)} %bitcast.106), calls=%async_computation.4 | async-start | bytes 294912 | tf_op jit(solution)/shard_map/all_to_all | solution.py:67
  273.3 6.9 %all-to-all-done.4 = bf16[8,68,128]{2,1,0:T(8,128)(2,1)S(1)} async-done(((bf16[8,68,128]{2,1,0:T(8,128)(2,1)}), bf16[8,68,128]{2,1,0:T(8,128)(2,1)S(1)}, u32[]{:S(2)}, u32[]{:S(2)}) %all-to-all-start.4) | async-done | bytes 139296 | tf_op jit(solution)/shard_map/all_to_all | solution.py:67
  280.8 4.5 %reduce-precision_reduce_fusion = f32[68,3584]{1,0:T(8,128)S(1)} fusion(bf16[8,128,3584]{2,1,0:T(8,128)(2,1)} %bitcast_dynamic-update-slice_fusion, bf16[8,68,128]{2,1,0:T(8,128)(2,1)S(1)} %gather_fusion.3, pred[8]{0:T(512)(128)(4,1)S(1)} %compare_and_fusion), kind=kOutput, calls=%fused_computation.4 | convolution fusion | flops 502847488 | bytes 8454152 | tf_op jit(solution)/shard_map/jrh,jhd->jrd/dot_general | solution.py:77
  286.3 4.0 %all-to-all-start.5 = ((f32[4,476,128]{2,1,0:T(8,128)}), f32[4,476,128]{2,1,0:T(8,128)S(1)}, u32[]{:S(2)}, u32[]{:S(2)}) async-start(f32[4,476,128]{2,1,0:T(8,128)} %reshape.231), calls=%async_computation.5 | async-start | bytes 1966080 | tf_op jit(solution)/shard_map/all_to_all | solution.py:81
  290.3 11.4 %all-to-all-done.5 = f32[4,476,128]{2,1,0:T(8,128)S(1)} async-done(((f32[4,476,128]{2,1,0:T(8,128)}), f32[4,476,128]{2,1,0:T(8,128)S(1)}, u32[]{:S(2)}, u32[]{:S(2)}) %all-to-all-start.5) | async-done | bytes 974880 | tf_op jit(solution)/shard_map/all_to_all | solution.py:81
  (85 shorter events, 57.2 us)
Async XLA Ops:
  6.5 110.5 %copy-start = (bf16[1,1,3584,128]{3,2,1,0:T(8,128)(2,1)S(1)}, bf16[1,1,3584,128]{3,2,1,0:T(8,128)(2,1)}, u32[]{:S(2)}) copy-start(bf16[1,1,3584,128]{3,2,1,0:T(8,128)(2,1)} %param.11) | copy-start | bytes 2752516
  6.5 110.5 %all-gather.5.cloned.1.call-start = ((), (), s32[]{:S(2)}) async-start(), calls=%async_computation.6 | async-start | bytes 4644864 | tf_op jit(solution)/shard_map/all_gather | solution.py:60
  25.3 23.5 %collective-permute-start.3 = (bf16[128,3584]{1,0:T(8,128)(2,1)}, bf16[128,3584]{1,0:T(8,128)(2,1)S(1)}, u32[]{:S(2)}, u32[]{:S(2)}) collective-permute-start(bf16[128,3584]{1,0:T(8,128)(2,1)} %bitcast.107), channel_id=1, source_target_pairs={{0,1},{1,2},{2,3},{3,4},{4,5},{5,6},{6,7},{7,0},{8,9},{9,10},{10,1... | collective-permute-start | bytes 2752520 | tf_op jit(solution)/shard_map/ppermute | solution.py:20
  30.0 24.8 %collective-permute-start = (bf16[128,3584]{1,0:T(8,128)(2,1)}, bf16[128,3584]{1,0:T(8,128)(2,1)}, u32[]{:S(2)}, u32[]{:S(2)}) collective-permute-start(bf16[128,3584]{1,0:T(8,128)(2,1)} %bitcast.108), channel_id=1, source_target_pairs={{0,7},{1,0},{2,1},{3,2},{4,3},{5,4},{6,5},{7,6},{8,15},{9,8},{10,9... | collective-permute-start | bytes 2752520 | tf_op jit(solution)/shard_map/ppermute | solution.py:20
  48.8 90.2 %copy-start.4 = (bf16[128,3584]{1,0:T(8,128)(2,1)}, bf16[128,3584]{1,0:T(8,128)(2,1)S(1)}, u32[]{:S(2)}) copy-start(bf16[128,3584]{1,0:T(8,128)(2,1)S(1)} %collective-permute-done.3) | copy-start | bytes 2752516
  48.8 46.0 %collective-permute-start.4 = (bf16[128,3584]{1,0:T(8,128)(2,1)S(1)}, bf16[128,3584]{1,0:T(8,128)(2,1)}, u32[]{:S(2)}, u32[]{:S(2)}) collective-permute-start(bf16[128,3584]{1,0:T(8,128)(2,1)S(1)} %collective-permute-done.3), channel_id=1, source_target_pairs={{0,1},{1,2},{2,3},{3,4},{4,5},{5,6},{6,7},{7,0},{8,9},{9,10},{10,1... | collective-permute-start | bytes 2752520 | tf_op jit(solution)/shard_map/ppermute | solution.py:20
  54.1 84.6 %copy-start.2 = (bf16[1,1,128,3584]{3,2,1,0:T(8,128)(2,1)S(1)}, bf16[1,1,128,3584]{3,2,1,0:T(8,128)(2,1)}, u32[]{:S(2)}) copy-start(bf16[1,1,128,3584]{3,2,1,0:T(8,128)(2,1)} %param.13) | copy-start | bytes 2752516
  54.8 75.2 %collective-permute-start.1 = (bf16[128,3584]{1,0:T(8,128)(2,1)}, bf16[128,3584]{1,0:T(8,128)(2,1)}, u32[]{:S(2)}, u32[]{:S(2)}) collective-permute-start(bf16[128,3584]{1,0:T(8,128)(2,1)} %collective-permute-done), channel_id=1, source_target_pairs={{0,7},{1,0},{2,1},{3,2},{4,3},{5,4},{6,5},{7,6},{8,15},{9,8},{10,9... | collective-permute-start | bytes 2752520 | tf_op jit(solution)/shard_map/ppermute | solution.py:20
  94.8 39.7 %collective-permute-start.5 = (bf16[128,3584]{1,0:T(8,128)(2,1)}, bf16[128,3584]{1,0:T(8,128)(2,1)}, u32[]{:S(2)}, u32[]{:S(2)}) collective-permute-start(bf16[128,3584]{1,0:T(8,128)(2,1)} %collective-permute-done.4), channel_id=1, source_target_pairs={{0,1},{1,2},{2,3},{3,4},{4,5},{5,6},{6,7},{7,0},{8,9},{9,10},{10,1... | collective-permute-start | bytes 2752520 | tf_op jit(solution)/shard_map/ppermute | solution.py:20
  124.7 13.3 %all-to-all-start.1 = ((bf16[8,68,128]{2,1,0:T(8,128)(2,1)}), bf16[8,68,128]{2,1,0:T(8,128)(2,1)S(1)}, u32[]{:S(2)}, u32[]{:S(2)}) async-start(bf16[8,68,128]{2,1,0:T(8,128)(2,1)} %bitcast.105), calls=%async_computation.1 | async-start | bytes 294912 | tf_op jit(solution)/shard_map/all_to_all | solution.py:67
  129.9 25.7 %collective-permute-start.2 = (bf16[128,3584]{1,0:T(8,128)(2,1)}, bf16[128,3584]{1,0:T(8,128)(2,1)}, u32[]{:S(2)}, u32[]{:S(2)}) collective-permute-start(bf16[128,3584]{1,0:T(8,128)(2,1)} %collective-permute-done.1), channel_id=1, source_target_pairs={{0,7},{1,0},{2,1},{3,2},{4,3},{5,4},{6,5},{7,6},{8,15},{9,8},{10,9... | collective-permute-start | bytes 2752520 | tf_op jit(solution)/shard_map/ppermute | solution.py:20
  134.5 24.0 %collective-permute-start.6 = (bf16[128,3584]{1,0:T(8,128)(2,1)}, bf16[128,3584]{1,0:T(8,128)(2,1)}, u32[]{:S(2)}, u32[]{:S(2)}) collective-permute-start(bf16[128,3584]{1,0:T(8,128)(2,1)} %collective-permute-done.5), channel_id=1, source_target_pairs={{0,1},{1,2},{2,3},{3,4},{4,5},{5,6},{6,7},{7,0},{8,9},{9,10},{10,1... | collective-permute-start | bytes 2752520 | tf_op jit(solution)/shard_map/ppermute | solution.py:20
  143.7 21.4 %copy-start.6 = (s32[1,2,64,1]{2,3,1,0:T(1,128)S(1)}, s32[1,2,64,1]{2,3,1,0:T(1,128)}, u32[]{:S(2)}) copy-start(s32[1,2,64,1]{2,3,1,0:T(1,128)} %param.14) | copy-start | bytes 1540
  143.7 21.4 %copy-start.7 = (s32[1,2,64,1]{2,3,1,0:T(1,128)S(1)}, s32[1,2,64,1]{2,3,1,0:T(1,128)}, u32[]{:S(2)}) copy-start(s32[1,2,64,1]{2,3,1,0:T(1,128)} %param.15) | copy-start | bytes 1540
  160.0 17.7 %copy-start.1 = (bf16[1,64,3584]{2,1,0:T(8,128)(2,1)S(1)}, bf16[1,64,3584]{2,1,0:T(8,128)(2,1)}, u32[]{:S(2)}) copy-start(bf16[1,64,3584]{2,1,0:T(8,128)(2,1)} %param.9) | copy-start | bytes 1376260
  161.1 15.6 %all-to-all-start.2 = ((f32[4,476,128]{2,1,0:T(8,128)}), f32[4,476,128]{2,1,0:T(8,128)S(1)}, u32[]{:S(2)}, u32[]{:S(2)}) async-start(f32[4,476,128]{2,1,0:T(8,128)} %reshape.225), calls=%async_computation.2 | async-start | bytes 1966080 | tf_op jit(solution)/shard_map/all_to_all | solution.py:81
  165.1 95.6 %all-gather.7.cloned.1.call-start = ((), (), s32[]{:S(2)}) async-start(), calls=%async_computation.7 | async-start | bytes 4644864 | tf_op jit(solution)/shard_map/all_gather | solution.py:60
  177.8 26.0 %copy-start.3 = (bf16[1,1,128,3584]{3,2,1,0:T(8,128)(2,1)S(1)}, bf16[1,1,128,3584]{3,2,1,0:T(8,128)(2,1)}, u32[]{:S(2)}) copy-start(bf16[1,1,128,3584]{3,2,1,0:T(8,128)(2,1)} %param.13) | copy-start | bytes 2752516
  178.0 10.4 %collective-permute-start.7 = (bf16[64,3584]{1,0:T(8,128)(2,1)S(1)}, bf16[64,3584]{1,0:T(8,128)(2,1)S(1)}, u32[]{:S(2)}, u32[]{:S(2)}) collective-permute-start(bf16[64,3584]{1,0:T(8,128)(2,1)S(1)} %fusion.16), channel_id=1, source_target_pairs={{0,32},{32,64},{64,96},{96,128},{128,160},{160,192},{192,224},{224... | collective-permute-start | bytes 1376264 | tf_op jit(solution)/shard_map/ppermute | solution.py:20
  209.1 54.9 %copy-start.8 = (bf16[1,1,3584,128]{3,2,1,0:T(8,128)(2,1)S(1)}, bf16[1,1,3584,128]{3,2,1,0:T(8,128)(2,1)}, u32[]{:S(2)}) copy-start(bf16[1,1,3584,128]{3,2,1,0:T(8,128)(2,1)} %param.12) | copy-start | bytes 2752516
  217.9 54.4 %copy-start.5 = (bf16[128,3584]{1,0:T(8,128)(2,1)S(1)}, bf16[128,3584]{1,0:T(8,128)(2,1)}, u32[]{:S(2)}) copy-start(bf16[128,3584]{1,0:T(8,128)(2,1)} %copy-done.4) | copy-start | bytes 2752516
  268.1 12.1 %all-to-all-start.4 = ((bf16[8,68,128]{2,1,0:T(8,128)(2,1)}), bf16[8,68,128]{2,1,0:T(8,128)(2,1)S(1)}, u32[]{:S(2)}, u32[]{:S(2)}) async-start(bf16[8,68,128]{2,1,0:T(8,128)(2,1)} %bitcast.106), calls=%async_computation.4 | async-start | bytes 294912 | tf_op jit(solution)/shard_map/all_to_all | solution.py:67
  286.3 15.4 %all-to-all-start.5 = ((f32[4,476,128]{2,1,0:T(8,128)}), f32[4,476,128]{2,1,0:T(8,128)S(1)}, u32[]{:S(2)}, u32[]{:S(2)}) async-start(f32[4,476,128]{2,1,0:T(8,128)} %reshape.231), calls=%async_computation.5 | async-start | bytes 1966080 | tf_op jit(solution)/shard_map/all_to_all | solution.py:81
Sparse Core Ops, SparseCore 0:
  25.4 91.5 all-gather.4
  203.9 56.7 all-gather.6

commit v14 on v13

--- a/solution.py
+++ b/solution.py
@@ -58,6 +58,8 @@
     padded = -(-held // SUBLANE) * SUBLANE
     own_rows = jnp.pad(from_x.reshape(held, model_width), ((0, padded - held), (0, 0)))
     slot_rows = lax.all_gather(own_rows, "ey", axis=0, tiled=False)
+    if callable(down_all):
+        slot_rows, down_all = down_all(slot_rows)
     n_y = slot_rows.shape[0]
     flat_rows = slot_rows.reshape(-1, model_width)
     gate_act = jnp.dot(flat_rows, w_gate, preferred_element_type=jnp.float32)
@@ -98,10 +100,25 @@
     gain_row = norm_gain[0]
     w_gate = gate_w[0, 0]
     w_up = up_w[0, 0]
-    down_all = ring_gather(down_w[0, 0], "ey")
+    own_down = down_w[0, 0]
+    forward_1 = shifted(own_down, "ey", 1)
+    backward_1 = shifted(own_down, "ey", -1)
+    forward_2 = shifted(forward_1, "ey", 1)
+    backward_2 = shifted(backward_1, "ey", -1)
+    gathered = []
+
+    def ring_rest(slot_rows):
+        slot_rows, forward, backward = lax.optimization_barrier((slot_rows, forward_2, backward_2))
+        forward_3 = shifted(forward, "ey", 1)
+        backward_3 = shifted(backward, "ey", -1)
+        forward_4 = shifted(forward_3, "ey", 1)
+        gathered.append([own_down, backward_1, backward, backward_3, forward_4, forward_3, forward, forward_1])
+        return slot_rows, gathered[0]
+
     values, branch = layer_terms(
-        rows_in, gain_row, w_gate, w_up, down_all, route_ids[0, 0], route_wts[0, 0]
+        rows_in, gain_row, w_gate, w_up, ring_rest, route_ids[0, 0], route_wts[0, 0]
     )
+    down_all = gathered[0]
     first_out = (values + branch).astype(jnp.bfloat16)
     arrived = shifted(first_out, "pipe", 1)
     first_out, down_all = lax.optimization_barrier((first_out, down_all))

time: 314 us -> 329 us (1.048)
  waiting for transfers between devices: 163 us -> 176 us
    ppermute x8, waiting for transfers between devices: 68.1 us -> 75.8 us  [shifted(): return lax.ppermute(value, axis, pairs)]
    all_to_all x2, waiting for transfers between devices: 8.45 us -> 13.8 us  [routed_branch(): lax.all_to_all(hidden, 'ey', split_axis=0, concat_axis=0, tiled=True)]
    unnamed x25 -> x33, local copies, waits for them, and re-layouts: 14.2 us -> 13 us
  transfers between devices with their start and end apart: 14 -> 14, of which waited for: 12 -> 13; matrix products, arithmetic and copies ran while one was open for 10% -> 8% of each run, Pallas kernels for 0% -> 0%
where the time goes in v14:
time: 329 us; the launch traced here: 326 us
  waiting for transfers between devices  176 us (53%)
  starting transfers between devices  51.3 us (16%)
  matrix products  29.6 us (9%)
  local copies, waits for them, and re-layouts  28.8 us (9%)
  blocking collectives  22.4 us (7%)
  between operations  13.8 us (4%)
  other arithmetic  4.77 us (1%)
    ppermute x8, waiting for transfers between devices, shifted(): return lax.ppermute(value, axis, pairs)  75.8 us
    all_gather x2, waiting for transfers between devices, routed_branch(): slot_rows = lax.all_gather(own_rows, 'ey', axis=0, tiled=False)  63.1 us
    ppermute x8, starting transfers between devices, shifted(): return lax.ppermute(value, axis, pairs)  33.6 us
    all_to_all x2, waiting for transfers between devices, routed_branch(): lax.all_to_all(expert_out, 'ex', split_axis=0, concat_axis=0, tiled=True)  23 us
    all_to_all x2, blocking collectives, routed_branch(): lax.all_to_all(per_expert, 'ex', split_axis=0, concat_axis=0, tiled=True)  22.4 us
    all_to_all x2, waiting for transfers between devices, routed_branch(): lax.all_to_all(hidden, 'ey', split_axis=0, concat_axis=0, tiled=True)  13.8 us
    unnamed x33, local copies, waits for them, and re-layouts  13 us
    all_to_all x2, starting transfers between devices, routed_branch(): lax.all_to_all(hidden, 'ey', split_axis=0, concat_axis=0, tiled=True)  10.2 us
  transfers between devices with their start and end apart: 14, of which 13 were waited for; matrix products, arithmetic and copies ran while one was open for 8% of the time, Pallas kernels for 0%

profile of v14, /device:TPU:1, one launch (start us, length us, event | category | flops | bytes accessed | tf_op | source)
XLA Modules:
  0.0 326.2 jit_solution(4230069496608883360)
XLA Ops:
  12.5 11.4 %all_to_all.30 = bf16[4,476,128]{2,1,0:T(8,128)(2,1)S(1)} all-to-all(bf16[4,476,128]{2,1,0:T(8,128)(2,1)S(1)} %reshape.221), channel_id=1, replica_groups=mesh['pipe'=16,'ex'=4,'ey'=8] {'ex'}, dimensions={0} | all-to-all | bytes 974848 | tf_op jit(solution)/shard_map/all_to_all | solution.py:56
  25.3 4.7 %collective-permute-start = (bf16[128,3584]{1,0:T(8,128)(2,1)}, bf16[128,3584]{1,0:T(8,128)(2,1)S(1)}, u32[]{:S(2)}, u32[]{:S(2)}) collective-permute-start(bf16[128,3584]{1,0:T(8,128)(2,1)} %bitcast.109), channel_id=1, source_target_pairs={{0,1},{1,2},{2,3},{3,4},{4,5},{5,6},{6,7},{7,0},{8,9},{9,10},{10,1... | collective-permute-start | bytes 2752520 | tf_op jit(solution)/shard_map/ppermute | solution.py:20
  33.8 15.0 %collective-permute-done = bf16[128,3584]{1,0:T(8,128)(2,1)S(1)} collective-permute-done((bf16[128,3584]{1,0:T(8,128)(2,1)}, bf16[128,3584]{1,0:T(8,128)(2,1)S(1)}, u32[]{:S(2)}, u32[]{:S(2)}) %collective-permute-start) | collective-permute-done | bytes 917536 | tf_op jit(solution)/shard_map/ppermute | solution.py:20
  48.8 5.3 %collective-permute-start.1 = (bf16[128,3584]{1,0:T(8,128)(2,1)S(1)}, bf16[128,3584]{1,0:T(8,128)(2,1)}, u32[]{:S(2)}, u32[]{:S(2)}) collective-permute-start(bf16[128,3584]{1,0:T(8,128)(2,1)S(1)} %collective-permute-done), channel_id=1, source_target_pairs={{0,1},{1,2},{2,3},{3,4},{4,5},{5,6},{6,7},{7,0},{8,9},{9,10},{10,1... | collective-permute-start | bytes 2752520 | tf_op jit(solution)/shard_map/ppermute | solution.py:20
  54.8 4.9 %collective-permute-start.3 = (bf16[128,3584]{1,0:T(8,128)(2,1)}, bf16[128,3584]{1,0:T(8,128)(2,1)S(1)}, u32[]{:S(2)}, u32[]{:S(2)}) collective-permute-start(bf16[128,3584]{1,0:T(8,128)(2,1)} %collective-permute-done.2), channel_id=1, source_target_pairs={{0,7},{1,0},{2,1},{3,2},{4,3},{5,4},{6,5},{7,6},{8,15},{9,8},{10,9... | collective-permute-start | bytes 2752520 | tf_op jit(solution)/shard_map/ppermute | solution.py:20
  59.7 35.1 %collective-permute-done.1 = bf16[128,3584]{1,0:T(8,128)(2,1)} collective-permute-done((bf16[128,3584]{1,0:T(8,128)(2,1)S(1)}, bf16[128,3584]{1,0:T(8,128)(2,1)}, u32[]{:S(2)}, u32[]{:S(2)}) %collective-permute-start.1) | collective-permute-done | bytes 917536 | tf_op jit(solution)/shard_map/ppermute | solution.py:20
  97.7 15.7 %all-gather.5.cloned.1.call-done = bf16[576,3584]{1,0:T(8,128)(2,1)} async-done(((bf16[72,3584]{1,0:T(8,128)(2,1)}), bf16[576,3584]{1,0:T(8,128)(2,1)}) %all-gather.5.cloned.1.call-update) | async-done | bytes 4128784 | tf_op jit(solution)/shard_map/all_gather | solution.py:60
  120.1 4.3 %fusion.7 = bf16[576,128]{1,0:T(8,128)(2,1)} fusion(bf16[576,3584]{1,0:T(8,128)(2,1)} %all-gather.5.cloned.1.call-done, bf16[1,1,3584,128]{3,2,1,0:T(8,128)(2,1)} %param.12, f32[576,128]{1,0:T(8,128)S(1)} %fusion.21), kind=kOutput, calls=%fused_computation.30 | convolution fusion | flops 528924672 | bytes 5488640 | tf_op jit(solution)/shard_map/dot_general | solution.py:66
  124.4 6.0 %all-to-all-start.1 = ((bf16[8,68,128]{2,1,0:T(8,128)(2,1)}), bf16[8,68,128]{2,1,0:T(8,128)(2,1)S(1)}, u32[]{:S(2)}, u32[]{:S(2)}) async-start(bf16[8,68,128]{2,1,0:T(8,128)(2,1)} %bitcast.107), calls=%async_computation.1 | async-start | bytes 294912 | tf_op jit(solution)/shard_map/all_to_all | solution.py:69
  130.5 4.6 %collective-permute-start.4 = (bf16[128,3584]{1,0:T(8,128)(2,1)}, bf16[128,3584]{1,0:T(8,128)(2,1)}, u32[]{:S(2)}, u32[]{:S(2)}) collective-permute-start(bf16[128,3584]{1,0:T(8,128)(2,1)} %copy-done.10), channel_id=1, source_target_pairs={{0,7},{1,0},{2,1},{3,2},{4,3},{5,4},{6,5},{7,6},{8,15},{9,8},{10,9... | collective-permute-start | bytes 2752520 | tf_op jit(solution)/shard_map/ppermute | solution.py:20
  135.1 6.9 %all-to-all-done.1 = bf16[8,68,128]{2,1,0:T(8,128)(2,1)S(1)} async-done(((bf16[8,68,128]{2,1,0:T(8,128)(2,1)}), bf16[8,68,128]{2,1,0:T(8,128)(2,1)S(1)}, u32[]{:S(2)}, u32[]{:S(2)}) %all-to-all-start.1) | async-done | bytes 139296 | tf_op jit(solution)/shard_map/all_to_all | solution.py:69
  148.2 8.0 %collective-permute-done.4 = bf16[128,3584]{1,0:T(8,128)(2,1)} collective-permute-done((bf16[128,3584]{1,0:T(8,128)(2,1)}, bf16[128,3584]{1,0:T(8,128)(2,1)}, u32[]{:S(2)}, u32[]{:S(2)}) %collective-permute-start.4) | collective-permute-done | bytes 917536 | tf_op jit(solution)/shard_map/ppermute | solution.py:20
  157.6 8.7 %collective-permute-done.6 = bf16[128,3584]{1,0:T(8,128)(2,1)S(1)} collective-permute-done((bf16[128,3584]{1,0:T(8,128)(2,1)S(1)}, bf16[128,3584]{1,0:T(8,128)(2,1)S(1)}, u32[]{:S(2)}, u32[]{:S(2)}) %collective-permute-start.6) | collective-permute-done | bytes 917536 | tf_op jit(solution)/shard_map/ppermute | solution.py:20
  173.2 11.6 %all-to-all-done.2 = f32[4,476,128]{2,1,0:T(8,128)S(1)} async-done(((f32[4,476,128]{2,1,0:T(8,128)}), f32[4,476,128]{2,1,0:T(8,128)S(1)}, u32[]{:S(2)}, u32[]{:S(2)}) %all-to-all-start.2) | async-done | bytes 974880 | tf_op jit(solution)/shard_map/all_to_all | solution.py:83
  186.0 5.2 %collective-permute-start.7 = (bf16[64,3584]{1,0:T(8,128)(2,1)S(1)}, bf16[64,3584]{1,0:T(8,128)(2,1)S(1)}, u32[]{:S(2)}, u32[]{:S(2)}) collective-permute-start(bf16[64,3584]{1,0:T(8,128)(2,1)S(1)} %fusion.16), channel_id=1, source_target_pairs={{0,32},{32,64},{64,96},{96,128},{128,160},{160,192},{192,224},{224... | collective-permute-start | bytes 1376264 | tf_op jit(solution)/shard_map/ppermute | solution.py:20
  191.2 5.4 %collective-permute-done.7 = bf16[64,3584]{1,0:T(8,128)(2,1)S(1)} collective-permute-done((bf16[64,3584]{1,0:T(8,128)(2,1)S(1)}, bf16[64,3584]{1,0:T(8,128)(2,1)S(1)}, u32[]{:S(2)}, u32[]{:S(2)}) %collective-permute-start.7) | collective-permute-done | bytes 458784 | tf_op jit(solution)/shard_map/ppermute | solution.py:20
  200.4 11.0 %all_to_all.31 = bf16[4,476,128]{2,1,0:T(8,128)(2,1)} all-to-all(bf16[4,476,128]{2,1,0:T(8,128)(2,1)} %reshape.227), channel_id=1, replica_groups=mesh['pipe'=16,'ex'=4,'ey'=8] {'ex'}, dimensions={0} | all-to-all | bytes 974848 | tf_op jit(solution)/shard_map/all_to_all | solution.py:56
  228.6 47.4 %all-gather.7.cloned.1.call-done = bf16[576,3584]{1,0:T(8,128)(2,1)} async-done(((bf16[72,3584]{1,0:T(8,128)(2,1)}), bf16[576,3584]{1,0:T(8,128)(2,1)}) %all-gather.7.cloned.1.call-update) | async-done | bytes 4128784 | tf_op jit(solution)/shard_map/all_gather | solution.py:60
  279.4 4.3 %fusion.8 = bf16[576,128]{1,0:T(8,128)(2,1)} fusion(bf16[576,3584]{1,0:T(8,128)(2,1)} %all-gather.7.cloned.1.call-done, bf16[1,1,3584,128]{3,2,1,0:T(8,128)(2,1)} %param.12, f32[576,128]{1,0:T(8,128)S(1)} %fusion.19), kind=kOutput, calls=%fused_computation.31 | convolution fusion | flops 528924672 | bytes 5488640 | tf_op jit(solution)/shard_map/dot_general | solution.py:66
  283.7 4.2 %all-to-all-start.4 = ((bf16[8,68,128]{2,1,0:T(8,128)(2,1)}), bf16[8,68,128]{2,1,0:T(8,128)(2,1)S(1)}, u32[]{:S(2)}, u32[]{:S(2)}) async-start(bf16[8,68,128]{2,1,0:T(8,128)(2,1)} %bitcast.108), calls=%async_computation.4 | async-start | bytes 294912 | tf_op jit(solution)/shard_map/all_to_all | solution.py:69
  288.9 6.9 %all-to-all-done.4 = bf16[8,68,128]{2,1,0:T(8,128)(2,1)S(1)} async-done(((bf16[8,68,128]{2,1,0:T(8,128)(2,1)}), bf16[8,68,128]{2,1,0:T(8,128)(2,1)S(1)}, u32[]{:S(2)}, u32[]{:S(2)}) %all-to-all-start.4) | async-done | bytes 139296 | tf_op jit(solution)/shard_map/all_to_all | solution.py:69
  296.4 4.5 %reduce-precision_reduce_fusion = f32[68,3584]{1,0:T(8,128)S(1)} fusion(bf16[8,128,3584]{2,1,0:T(8,128)(2,1)} %bitcast_dynamic-update-slice_fusion, bf16[8,68,128]{2,1,0:T(8,128)(2,1)S(1)} %gather_fusion.3, pred[8]{0:T(512)(128)(4,1)S(1)} %compare_and_fusion), kind=kOutput, calls=%fused_computation.4 | convolution fusion | flops 502847488 | bytes 8454152 | tf_op jit(solution)/shard_map/jrh,jhd->jrd/dot_general | solution.py:79
  301.9 4.0 %all-to-all-start.5 = ((f32[4,476,128]{2,1,0:T(8,128)}), f32[4,476,128]{2,1,0:T(8,128)S(1)}, u32[]{:S(2)}, u32[]{:S(2)}) async-start(f32[4,476,128]{2,1,0:T(8,128)} %reshape.231), calls=%async_computation.5 | async-start | bytes 1966080 | tf_op jit(solution)/shard_map/all_to_all | solution.py:83
  305.9 11.4 %all-to-all-done.5 = f32[4,476,128]{2,1,0:T(8,128)S(1)} async-done(((f32[4,476,128]{2,1,0:T(8,128)}), f32[4,476,128]{2,1,0:T(8,128)S(1)}, u32[]{:S(2)}, u32[]{:S(2)}) %all-to-all-start.5) | async-done | bytes 974880 | tf_op jit(solution)/shard_map/all_to_all | solution.py:83
  (93 shorter events, 66.0 us)
Async XLA Ops:
  6.5 110.1 %copy-start = (bf16[1,1,3584,128]{3,2,1,0:T(8,128)(2,1)S(1)}, bf16[1,1,3584,128]{3,2,1,0:T(8,128)(2,1)}, u32[]{:S(2)}) copy-start(bf16[1,1,3584,128]{3,2,1,0:T(8,128)(2,1)} %param.11) | copy-start | bytes 2752516
  6.5 106.8 %all-gather.5.cloned.1.call-start = ((), (), s32[]{:S(2)}) async-start(), calls=%async_computation.6 | async-start | bytes 4644864 | tf_op jit(solution)/shard_map/all_gather | solution.py:60
  25.3 23.5 %collective-permute-start = (bf16[128,3584]{1,0:T(8,128)(2,1)}, bf16[128,3584]{1,0:T(8,128)(2,1)S(1)}, u32[]{:S(2)}, u32[]{:S(2)}) collective-permute-start(bf16[128,3584]{1,0:T(8,128)(2,1)} %bitcast.109), channel_id=1, source_target_pairs={{0,1},{1,2},{2,3},{3,4},{4,5},{5,6},{6,7},{7,0},{8,9},{9,10},{10,1... | collective-permute-start | bytes 2752520 | tf_op jit(solution)/shard_map/ppermute | solution.py:20
  30.0 24.8 %collective-permute-start.2 = (bf16[128,3584]{1,0:T(8,128)(2,1)}, bf16[128,3584]{1,0:T(8,128)(2,1)}, u32[]{:S(2)}, u32[]{:S(2)}) collective-permute-start(bf16[128,3584]{1,0:T(8,128)(2,1)} %bitcast.110), channel_id=1, source_target_pairs={{0,7},{1,0},{2,1},{3,2},{4,3},{5,4},{6,5},{7,6},{8,15},{9,8},{10,9... | collective-permute-start | bytes 2752520 | tf_op jit(solution)/shard_map/ppermute | solution.py:20
  48.8 67.8 %copy-start.7 = (bf16[128,3584]{1,0:T(8,128)(2,1)}, bf16[128,3584]{1,0:T(8,128)(2,1)S(1)}, u32[]{:S(2)}) copy-start(bf16[128,3584]{1,0:T(8,128)(2,1)S(1)} %collective-permute-done) | copy-start | bytes 2752516
  48.8 46.0 %collective-permute-start.1 = (bf16[128,3584]{1,0:T(8,128)(2,1)S(1)}, bf16[128,3584]{1,0:T(8,128)(2,1)}, u32[]{:S(2)}, u32[]{:S(2)}) collective-permute-start(bf16[128,3584]{1,0:T(8,128)(2,1)S(1)} %collective-permute-done), channel_id=1, source_target_pairs={{0,1},{1,2},{2,3},{3,4},{4,5},{5,6},{6,7},{7,0},{8,9},{9,10},{10,1... | collective-permute-start | bytes 2752520 | tf_op jit(solution)/shard_map/ppermute | solution.py:20
  54.8 42.9 %collective-permute-start.3 = (bf16[128,3584]{1,0:T(8,128)(2,1)}, bf16[128,3584]{1,0:T(8,128)(2,1)S(1)}, u32[]{:S(2)}, u32[]{:S(2)}) collective-permute-start(bf16[128,3584]{1,0:T(8,128)(2,1)} %collective-permute-done.2), channel_id=1, source_target_pairs={{0,7},{1,0},{2,1},{3,2},{4,3},{5,4},{6,5},{7,6},{8,15},{9,8},{10,9... | collective-permute-start | bytes 2752520 | tf_op jit(solution)/shard_map/ppermute | solution.py:20
  97.7 15.7 %copy-start.10 = (bf16[128,3584]{1,0:T(8,128)(2,1)}, bf16[128,3584]{1,0:T(8,128)(2,1)S(1)}, u32[]{:S(2)}) copy-start(bf16[128,3584]{1,0:T(8,128)(2,1)S(1)} %collective-permute-done.3) | copy-start | bytes 2752516
  113.4 29.5 %collective-permute-start.5 = (bf16[128,3584]{1,0:T(8,128)(2,1)}, bf16[128,3584]{1,0:T(8,128)(2,1)S(1)}, u32[]{:S(2)}, u32[]{:S(2)}) collective-permute-start(bf16[128,3584]{1,0:T(8,128)(2,1)} %collective-permute-done.1), channel_id=1, source_target_pairs={{0,1},{1,2},{2,3},{3,4},{4,5},{5,6},{6,7},{7,0},{8,9},{9,10},{10,1... | collective-permute-start | bytes 2752520 | tf_op jit(solution)/shard_map/ppermute | solution.py:20
  116.6 26.0 %copy-start.4 = (bf16[1,1,128,3584]{3,2,1,0:T(8,128)(2,1)S(1)}, bf16[1,1,128,3584]{3,2,1,0:T(8,128)(2,1)}, u32[]{:S(2)}) copy-start(bf16[1,1,128,3584]{3,2,1,0:T(8,128)(2,1)} %param.13) | copy-start | bytes 2752516
  124.4 17.5 %all-to-all-start.1 = ((bf16[8,68,128]{2,1,0:T(8,128)(2,1)}), bf16[8,68,128]{2,1,0:T(8,128)(2,1)S(1)}, u32[]{:S(2)}, u32[]{:S(2)}) async-start(bf16[8,68,128]{2,1,0:T(8,128)(2,1)} %bitcast.107), calls=%async_computation.1 | async-start | bytes 294912 | tf_op jit(solution)/shard_map/all_to_all | solution.py:69
  130.5 25.7 %collective-permute-start.4 = (bf16[128,3584]{1,0:T(8,128)(2,1)}, bf16[128,3584]{1,0:T(8,128)(2,1)}, u32[]{:S(2)}, u32[]{:S(2)}) collective-permute-start(bf16[128,3584]{1,0:T(8,128)(2,1)} %copy-done.10), channel_id=1, source_target_pairs={{0,7},{1,0},{2,1},{3,2},{4,3},{5,4},{6,5},{7,6},{8,15},{9,8},{10,9... | collective-permute-start | bytes 2752520 | tf_op jit(solution)/shard_map/ppermute | solution.py:20
  142.9 23.8 %copy-start.5 = (bf16[128,3584]{1,0:T(8,128)(2,1)}, bf16[128,3584]{1,0:T(8,128)(2,1)S(1)}, u32[]{:S(2)}) copy-start(bf16[128,3584]{1,0:T(8,128)(2,1)S(1)} %collective-permute-done.5) | copy-start | bytes 2752516
  142.9 23.4 %collective-permute-start.6 = (bf16[128,3584]{1,0:T(8,128)(2,1)S(1)}, bf16[128,3584]{1,0:T(8,128)(2,1)S(1)}, u32[]{:S(2)}, u32[]{:S(2)}) collective-permute-start(bf16[128,3584]{1,0:T(8,128)(2,1)S(1)} %collective-permute-done.5), channel_id=1, source_target_pairs={{0,1},{1,2},{2,3},{3,4},{4,5},{5,6},{6,7},{7,0},{8,9},{9,10},{10,1... | collective-permute-start | bytes 2752520 | tf_op jit(solution)/shard_map/ppermute | solution.py:20
  146.3 21.8 %copy-start.8 = (bf16[128,3584]{1,0:T(8,128)(2,1)S(1)}, bf16[128,3584]{1,0:T(8,128)(2,1)}, u32[]{:S(2)}) copy-start(bf16[128,3584]{1,0:T(8,128)(2,1)} %copy-done.7) | copy-start | bytes 2752516
  168.5 17.3 %copy-start.1 = (bf16[1,64,3584]{2,1,0:T(8,128)(2,1)S(1)}, bf16[1,64,3584]{2,1,0:T(8,128)(2,1)}, u32[]{:S(2)}) copy-start(bf16[1,64,3584]{2,1,0:T(8,128)(2,1)} %param.9) | copy-start | bytes 1376260
  169.5 15.2 %all-to-all-start.2 = ((f32[4,476,128]{2,1,0:T(8,128)}), f32[4,476,128]{2,1,0:T(8,128)S(1)}, u32[]{:S(2)}, u32[]{:S(2)}) async-start(f32[4,476,128]{2,1,0:T(8,128)} %reshape.225), calls=%async_computation.2 | async-start | bytes 1966080 | tf_op jit(solution)/shard_map/all_to_all | solution.py:83
  173.0 103.0 %all-gather.7.cloned.1.call-start = ((), (), s32[]{:S(2)}) async-start(), calls=%async_computation.7 | async-start | bytes 4644864 | tf_op jit(solution)/shard_map/all_gather | solution.py:60
  185.8 38.6 %copy-start.3 = (bf16[128,3584]{1,0:T(8,128)(2,1)S(1)}, bf16[128,3584]{1,0:T(8,128)(2,1)}, u32[]{:S(2)}) copy-start(bf16[128,3584]{1,0:T(8,128)(2,1)} %copy-done.2) | copy-start | bytes 2752516
  186.0 10.6 %collective-permute-start.7 = (bf16[64,3584]{1,0:T(8,128)(2,1)S(1)}, bf16[64,3584]{1,0:T(8,128)(2,1)S(1)}, u32[]{:S(2)}, u32[]{:S(2)}) collective-permute-start(bf16[64,3584]{1,0:T(8,128)(2,1)S(1)} %fusion.16), channel_id=1, source_target_pairs={{0,32},{32,64},{64,96},{96,128},{128,160},{160,192},{192,224},{224... | collective-permute-start | bytes 1376264 | tf_op jit(solution)/shard_map/ppermute | solution.py:20
  196.8 28.6 %copy-start.6 = (bf16[128,3584]{1,0:T(8,128)(2,1)S(1)}, bf16[128,3584]{1,0:T(8,128)(2,1)}, u32[]{:S(2)}) copy-start(bf16[128,3584]{1,0:T(8,128)(2,1)} %copy-done.5) | copy-start | bytes 2752516
  228.6 59.3 %copy-start.9 = (bf16[128,3584]{1,0:T(8,128)(2,1)S(1)}, bf16[128,3584]{1,0:T(8,128)(2,1)}, u32[]{:S(2)}) copy-start(bf16[128,3584]{1,0:T(8,128)(2,1)} %copy-done.7) | copy-start | bytes 2752516
  283.7 12.1 %all-to-all-start.4 = ((bf16[8,68,128]{2,1,0:T(8,128)(2,1)}), bf16[8,68,128]{2,1,0:T(8,128)(2,1)S(1)}, u32[]{:S(2)}, u32[]{:S(2)}) async-start(bf16[8,68,128]{2,1,0:T(8,128)(2,1)} %bitcast.108), calls=%async_computation.4 | async-start | bytes 294912 | tf_op jit(solution)/shard_map/all_to_all | solution.py:69
  301.9 15.4 %all-to-all-start.5 = ((f32[4,476,128]{2,1,0:T(8,128)}), f32[4,476,128]{2,1,0:T(8,128)S(1)}, u32[]{:S(2)}, u32[]{:S(2)}) async-start(f32[4,476,128]{2,1,0:T(8,128)} %reshape.231), calls=%async_computation.5 | async-start | bytes 1966080 | tf_op jit(solution)/shard_map/all_to_all | solution.py:83
  (3 other events, 32.8 us)
Sparse Core Ops, SparseCore 0:
  25.4 87.8 all-gather.4
  215.8 60.2 all-gather.6

commit v15 on v13

--- a/solution.py
+++ b/solution.py
@@ -60,8 +60,8 @@
     slot_rows = lax.all_gather(own_rows, "ey", axis=0, tiled=False)
     n_y = slot_rows.shape[0]
     flat_rows = slot_rows.reshape(-1, model_width)
-    gate_act = jnp.dot(flat_rows, w_gate, preferred_element_type=jnp.float32)
-    up_act = jnp.dot(flat_rows, w_up, preferred_element_type=jnp.float32)
+    both = jnp.dot(flat_rows, w_up, preferred_element_type=jnp.float32)
+    gate_act, up_act = both[:, : w_gate.shape[1]], both[:, w_gate.shape[1]:]
     hidden = (jax.nn.silu(gate_act) * up_act).astype(jnp.bfloat16)
     hidden = hidden.reshape(n_y, -1, hidden.shape[-1])[:, : n_x * MOST]
     hidden_here = lax.all_to_all(hidden, "ey", split_axis=0, concat_axis=0, tiled=True)
@@ -97,7 +97,7 @@
     rows_in = acts[0]
     gain_row = norm_gain[0]
     w_gate = gate_w[0, 0]
-    w_up = up_w[0, 0]
+    w_up = jnp.concatenate([gate_w[0, 0], up_w[0, 0]], axis=1)
     down_all = ring_gather(down_w[0, 0], "ey")
     values, branch = layer_terms(
         rows_in, gain_row, w_gate, w_up, down_all, route_ids[0, 0], route_wts[0, 0]

time: 314 us -> 304 us (0.968)
  matrix products: 30.7 us -> 22 us
    dot_general x4 -> x2, matrix products: 15.2 us -> 7.57 us  [routed_branch(): both = jnp.dot(flat_rows, w_up, preferred_element_type=jnp.float32)]
  transfers between devices with their start and end apart: 14 -> 14, of which waited for: 12 -> 12; matrix products, arithmetic and copies ran while one was open for 10% -> 9% of each run, Pallas kernels for 0% -> 0%
where the time goes in v15:
time: 304 us; the launch traced here: 301 us
  waiting for transfers between devices  165 us (54%)
  starting transfers between devices  49.4 us (16%)
  local copies, waits for them, and re-layouts  24.1 us (8%)
  matrix products  22 us (7%)
  blocking collectives  20.7 us (7%)
  between operations  13.8 us (5%)
  other arithmetic  6.21 us (2%)
    ppermute x8, waiting for transfers between devices, shifted(): return lax.ppermute(value, axis, pairs)  69.4 us
    all_gather x2, waiting for transfers between devices, routed_branch(): slot_rows = lax.all_gather(own_rows, 'ey', axis=0, tiled=False)  64.1 us
    ppermute x8, starting transfers between devices, shifted(): return lax.ppermute(value, axis, pairs)  32.1 us
    all_to_all x2, waiting for transfers between devices, routed_branch(): lax.all_to_all(expert_out, 'ex', split_axis=0, concat_axis=0, tiled=True)  23 us
    all_to_all x2, blocking collectives, routed_branch(): lax.all_to_all(per_expert, 'ex', split_axis=0, concat_axis=0, tiled=True)  20.7 us
    unnamed x25, local copies, waits for them, and re-layouts  13 us
    all_to_all x2, starting transfers between devices, routed_branch(): lax.all_to_all(hidden, 'ey', split_axis=0, concat_axis=0, tiled=True)  9.33 us
    all_to_all x2, waiting for transfers between devices, routed_branch(): lax.all_to_all(hidden, 'ey', split_axis=0, concat_axis=0, tiled=True)  8.26 us
  transfers between devices with their start and end apart: 14, of which 12 were waited for; matrix products, arithmetic and copies ran while one was open for 9% of the time, Pallas kernels for 0%

profile of v15, /device:TPU:1, one launch (start us, length us, event | category | flops | bytes accessed | tf_op | source)
XLA Modules:
  0.0 300.9 jit_solution(15218897098158924331)
XLA Ops:
  12.4 11.4 %all_to_all.30 = bf16[4,476,128]{2,1,0:T(8,128)(2,1)S(1)} all-to-all(bf16[4,476,128]{2,1,0:T(8,128)(2,1)S(1)} %reshape.221), channel_id=1, replica_groups=mesh['pipe'=16,'ex'=4,'ey'=8] {'ex'}, dimensions={0} | all-to-all | bytes 974848 | tf_op jit(solution)/shard_map/all_to_all | solution.py:56
  25.3 4.7 %collective-permute-start.3 = (bf16[128,3584]{1,0:T(8,128)(2,1)}, bf16[128,3584]{1,0:T(8,128)(2,1)S(1)}, u32[]{:S(2)}, u32[]{:S(2)}) collective-permute-start(bf16[128,3584]{1,0:T(8,128)(2,1)} %bitcast.97), channel_id=1, source_target_pairs={{0,1},{1,2},{2,3},{3,4},{4,5},{5,6},{6,7},{7,0},{8,9},{9,10},{10,1... | collective-permute-start | bytes 2752520 | tf_op jit(solution)/shard_map/ppermute | solution.py:20
  29.9 3.8 %collective-permute-start = (bf16[128,3584]{1,0:T(8,128)(2,1)}, bf16[128,3584]{1,0:T(8,128)(2,1)}, u32[]{:S(2)}, u32[]{:S(2)}) collective-permute-start(bf16[128,3584]{1,0:T(8,128)(2,1)} %bitcast.98), channel_id=1, source_target_pairs={{0,7},{1,0},{2,1},{3,2},{4,3},{5,4},{6,5},{7,6},{8,15},{9,8},{10,9... | collective-permute-start | bytes 2752520 | tf_op jit(solution)/shard_map/ppermute | solution.py:20
  33.7 14.9 %collective-permute-done.3 = bf16[128,3584]{1,0:T(8,128)(2,1)S(1)} collective-permute-done((bf16[128,3584]{1,0:T(8,128)(2,1)}, bf16[128,3584]{1,0:T(8,128)(2,1)S(1)}, u32[]{:S(2)}, u32[]{:S(2)}) %collective-permute-start.3) | collective-permute-done | bytes 917536 | tf_op jit(solution)/shard_map/ppermute | solution.py:20
  48.7 5.3 %collective-permute-start.4 = (bf16[128,3584]{1,0:T(8,128)(2,1)S(1)}, bf16[128,3584]{1,0:T(8,128)(2,1)S(1)}, u32[]{:S(2)}, u32[]{:S(2)}) collective-permute-start(bf16[128,3584]{1,0:T(8,128)(2,1)S(1)} %collective-permute-done.3), channel_id=1, source_target_pairs={{0,1},{1,2},{2,3},{3,4},{4,5},{5,6},{6,7},{7,0},{8,9},{9,10},{10,1... | collective-permute-start | bytes 2752520 | tf_op jit(solution)/shard_map/ppermute | solution.py:20
  54.7 5.0 %collective-permute-start.1 = (bf16[128,3584]{1,0:T(8,128)(2,1)}, bf16[128,3584]{1,0:T(8,128)(2,1)}, u32[]{:S(2)}, u32[]{:S(2)}) collective-permute-start(bf16[128,3584]{1,0:T(8,128)(2,1)} %collective-permute-done), channel_id=1, source_target_pairs={{0,7},{1,0},{2,1},{3,2},{4,3},{5,4},{6,5},{7,6},{8,15},{9,8},{10,9... | collective-permute-start | bytes 2752520 | tf_op jit(solution)/shard_map/ppermute | solution.py:20
  59.6 35.1 %collective-permute-done.4 = bf16[128,3584]{1,0:T(8,128)(2,1)S(1)} collective-permute-done((bf16[128,3584]{1,0:T(8,128)(2,1)S(1)}, bf16[128,3584]{1,0:T(8,128)(2,1)S(1)}, u32[]{:S(2)}, u32[]{:S(2)}) %collective-permute-start.4) | collective-permute-done | bytes 917536 | tf_op jit(solution)/shard_map/ppermute | solution.py:20
  96.7 20.5 %all-gather.5.cloned.1.call-done = bf16[576,3584]{1,0:T(8,128)(2,1)} async-done(((bf16[72,3584]{1,0:T(8,128)(2,1)}), bf16[576,3584]{1,0:T(8,128)(2,1)}) %all-gather.5.cloned.1.call-update) | async-done | bytes 4128784 | tf_op jit(solution)/shard_map/all_gather | solution.py:60
  117.1 3.9 %fusion.8 = f32[576,256]{1,0:T(8,128)S(1)} fusion(bf16[576,3584]{1,0:T(8,128)(2,1)} %all-gather.5.cloned.1.call-done, bf16[3584,128]{1,0:T(8,128)(2,1)} %bitcast.100, bf16[3584,128]{1,0:T(8,128)(2,1)} %bitcast.102), kind=kOutput, calls=%fused_computation.30 | convolution fusion | flops 1060634624 | bytes 6553600 | tf_op jit(solution)/shard_map/dot_general | solution.py:63
  121.8 5.1 %all-to-all-start.1 = ((bf16[8,68,128]{2,1,0:T(8,128)(2,1)}), bf16[8,68,128]{2,1,0:T(8,128)(2,1)S(1)}, u32[]{:S(2)}, u32[]{:S(2)}) async-start(bf16[8,68,128]{2,1,0:T(8,128)(2,1)} %bitcast.95), calls=%async_computation.1 | async-start | bytes 294912 | tf_op jit(solution)/shard_map/all_to_all | solution.py:67
  127.0 4.6 %collective-permute-start.2 = (bf16[128,3584]{1,0:T(8,128)(2,1)}, bf16[128,3584]{1,0:T(8,128)(2,1)}, u32[]{:S(2)}, u32[]{:S(2)}) collective-permute-start(bf16[128,3584]{1,0:T(8,128)(2,1)} %collective-permute-done.1), channel_id=1, source_target_pairs={{0,7},{1,0},{2,1},{3,2},{4,3},{5,4},{6,5},{7,6},{8,15},{9,8},{10,9... | collective-permute-start | bytes 2752520 | tf_op jit(solution)/shard_map/ppermute | solution.py:20
  140.9 11.8 %collective-permute-done.2 = bf16[128,3584]{1,0:T(8,128)(2,1)} collective-permute-done((bf16[128,3584]{1,0:T(8,128)(2,1)}, bf16[128,3584]{1,0:T(8,128)(2,1)}, u32[]{:S(2)}, u32[]{:S(2)}) %collective-permute-start.2) | collective-permute-done | bytes 917536 | tf_op jit(solution)/shard_map/ppermute | solution.py:20
  158.2 4.0 %all-to-all-start.2 = ((f32[4,476,128]{2,1,0:T(8,128)}), f32[4,476,128]{2,1,0:T(8,128)S(1)}, u32[]{:S(2)}, u32[]{:S(2)}) async-start(f32[4,476,128]{2,1,0:T(8,128)} %reshape.225), calls=%async_computation.2 | async-start | bytes 1966080 | tf_op jit(solution)/shard_map/all_to_all | solution.py:81
  162.2 11.6 %all-to-all-done.2 = f32[4,476,128]{2,1,0:T(8,128)S(1)} async-done(((f32[4,476,128]{2,1,0:T(8,128)}), f32[4,476,128]{2,1,0:T(8,128)S(1)}, u32[]{:S(2)}, u32[]{:S(2)}) %all-to-all-start.2) | async-done | bytes 974880 | tf_op jit(solution)/shard_map/all_to_all | solution.py:81
  175.0 5.0 %collective-permute-start.7 = (bf16[64,3584]{1,0:T(8,128)(2,1)S(1)}, bf16[64,3584]{1,0:T(8,128)(2,1)S(1)}, u32[]{:S(2)}, u32[]{:S(2)}) collective-permute-start(bf16[64,3584]{1,0:T(8,128)(2,1)S(1)} %fusion.16), channel_id=1, source_target_pairs={{0,32},{32,64},{64,96},{96,128},{128,160},{160,192},{192,224},{224... | collective-permute-start | bytes 1376264 | tf_op jit(solution)/shard_map/ppermute | solution.py:20
  180.0 5.4 %collective-permute-done.7 = bf16[64,3584]{1,0:T(8,128)(2,1)S(1)} collective-permute-done((bf16[64,3584]{1,0:T(8,128)(2,1)S(1)}, bf16[64,3584]{1,0:T(8,128)(2,1)S(1)}, u32[]{:S(2)}, u32[]{:S(2)}) %collective-permute-start.7) | collective-permute-done | bytes 458784 | tf_op jit(solution)/shard_map/ppermute | solution.py:20
  186.6 9.3 %all_to_all.31 = bf16[4,476,128]{2,1,0:T(8,128)(2,1)S(1)} all-to-all(bf16[4,476,128]{2,1,0:T(8,128)(2,1)S(1)} %reshape.227), channel_id=1, replica_groups=mesh['pipe'=16,'ex'=4,'ey'=8] {'ex'}, dimensions={0} | all-to-all | bytes 974848 | tf_op jit(solution)/shard_map/all_to_all | solution.py:56
  210.4 43.6 %all-gather.7.cloned.1.call-done = bf16[576,3584]{1,0:T(8,128)(2,1)} async-done(((bf16[72,3584]{1,0:T(8,128)(2,1)}), bf16[576,3584]{1,0:T(8,128)(2,1)}) %all-gather.7.cloned.1.call-update) | async-done | bytes 4128784 | tf_op jit(solution)/shard_map/all_gather | solution.py:60
  254.0 3.7 %fusion.7 = f32[576,256]{1,0:T(8,128)S(1)} fusion(bf16[576,3584]{1,0:T(8,128)(2,1)} %all-gather.7.cloned.1.call-done, bf16[3584,128]{1,0:T(8,128)(2,1)S(1)} %bitcast.101, bf16[3584,128]{1,0:T(8,128)(2,1)} %bitcast.103), kind=kOutput, calls=%fused_computation.29 | convolution fusion | flops 1060634624 | bytes 6553600 | tf_op jit(solution)/shard_map/dot_general | solution.py:63
  258.4 4.2 %all-to-all-start.4 = ((bf16[8,68,128]{2,1,0:T(8,128)(2,1)}), bf16[8,68,128]{2,1,0:T(8,128)(2,1)S(1)}, u32[]{:S(2)}, u32[]{:S(2)}) async-start(bf16[8,68,128]{2,1,0:T(8,128)(2,1)} %bitcast.96), calls=%async_computation.4 | async-start | bytes 294912 | tf_op jit(solution)/shard_map/all_to_all | solution.py:67
  263.6 6.9 %all-to-all-done.4 = bf16[8,68,128]{2,1,0:T(8,128)(2,1)S(1)} async-done(((bf16[8,68,128]{2,1,0:T(8,128)(2,1)}), bf16[8,68,128]{2,1,0:T(8,128)(2,1)S(1)}, u32[]{:S(2)}, u32[]{:S(2)}) %all-to-all-start.4) | async-done | bytes 139296 | tf_op jit(solution)/shard_map/all_to_all | solution.py:67
  271.1 4.5 %reduce-precision_reduce_fusion = f32[68,3584]{1,0:T(8,128)S(1)} fusion(bf16[8,128,3584]{2,1,0:T(8,128)(2,1)} %bitcast_dynamic-update-slice_fusion, bf16[8,68,128]{2,1,0:T(8,128)(2,1)S(1)} %gather_fusion.3, pred[8]{0:T(512)(128)(4,1)S(1)} %compare_and_fusion), kind=kOutput, calls=%fused_computation.4 | convolution fusion | flops 502847488 | bytes 8454152 | tf_op jit(solution)/shard_map/jrh,jhd->jrd/dot_general | solution.py:77
  276.7 4.0 %all-to-all-start.5 = ((f32[4,476,128]{2,1,0:T(8,128)}), f32[4,476,128]{2,1,0:T(8,128)S(1)}, u32[]{:S(2)}, u32[]{:S(2)}) async-start(f32[4,476,128]{2,1,0:T(8,128)} %reshape.231), calls=%async_computation.5 | async-start | bytes 1966080 | tf_op jit(solution)/shard_map/all_to_all | solution.py:81
  280.6 11.4 %all-to-all-done.5 = f32[4,476,128]{2,1,0:T(8,128)S(1)} async-done(((f32[4,476,128]{2,1,0:T(8,128)}), f32[4,476,128]{2,1,0:T(8,128)S(1)}, u32[]{:S(2)}, u32[]{:S(2)}) %all-to-all-start.5) | async-done | bytes 974880 | tf_op jit(solution)/shard_map/all_to_all | solution.py:81
  (85 shorter events, 47.5 us)
Async XLA Ops:
  6.5 110.6 %all-gather.5.cloned.1.call-start = ((), (), s32[]{:S(2)}) async-start(), calls=%async_computation.6 | async-start | bytes 4644864 | tf_op jit(solution)/shard_map/all_gather | solution.py:60
  23.8 111.7 %copy-start.1 = (bf16[1,1,128,3584]{3,2,1,0:T(8,128)(2,1)S(1)}, bf16[1,1,128,3584]{3,2,1,0:T(8,128)(2,1)}, u32[]{:S(2)}) copy-start(bf16[1,1,128,3584]{3,2,1,0:T(8,128)(2,1)} %param.13) | copy-start | bytes 2752516
  25.3 23.4 %collective-permute-start.3 = (bf16[128,3584]{1,0:T(8,128)(2,1)}, bf16[128,3584]{1,0:T(8,128)(2,1)S(1)}, u32[]{:S(2)}, u32[]{:S(2)}) collective-permute-start(bf16[128,3584]{1,0:T(8,128)(2,1)} %bitcast.97), channel_id=1, source_target_pairs={{0,1},{1,2},{2,3},{3,4},{4,5},{5,6},{6,7},{7,0},{8,9},{9,10},{10,1... | collective-permute-start | bytes 2752520 | tf_op jit(solution)/shard_map/ppermute | solution.py:20
  29.9 24.7 %collective-permute-start = (bf16[128,3584]{1,0:T(8,128)(2,1)}, bf16[128,3584]{1,0:T(8,128)(2,1)}, u32[]{:S(2)}, u32[]{:S(2)}) collective-permute-start(bf16[128,3584]{1,0:T(8,128)(2,1)} %bitcast.98), channel_id=1, source_target_pairs={{0,7},{1,0},{2,1},{3,2},{4,3},{5,4},{6,5},{7,6},{8,15},{9,8},{10,9... | collective-permute-start | bytes 2752520 | tf_op jit(solution)/shard_map/ppermute | solution.py:20
  48.7 89.0 %copy-start.2 = (bf16[128,3584]{1,0:T(8,128)(2,1)}, bf16[128,3584]{1,0:T(8,128)(2,1)S(1)}, u32[]{:S(2)}) copy-start(bf16[128,3584]{1,0:T(8,128)(2,1)S(1)} %collective-permute-done.3) | copy-start | bytes 2752516
  48.7 46.1 %collective-permute-start.4 = (bf16[128,3584]{1,0:T(8,128)(2,1)S(1)}, bf16[128,3584]{1,0:T(8,128)(2,1)S(1)}, u32[]{:S(2)}, u32[]{:S(2)}) collective-permute-start(bf16[128,3584]{1,0:T(8,128)(2,1)S(1)} %collective-permute-done.3), channel_id=1, source_target_pairs={{0,1},{1,2},{2,3},{3,4},{4,5},{5,6},{6,7},{7,0},{8,9},{9,10},{10,1... | collective-permute-start | bytes 2752520 | tf_op jit(solution)/shard_map/ppermute | solution.py:20
  54.7 72.3 %collective-permute-start.1 = (bf16[128,3584]{1,0:T(8,128)(2,1)}, bf16[128,3584]{1,0:T(8,128)(2,1)}, u32[]{:S(2)}, u32[]{:S(2)}) collective-permute-start(bf16[128,3584]{1,0:T(8,128)(2,1)} %collective-permute-done), channel_id=1, source_target_pairs={{0,7},{1,0},{2,1},{3,2},{4,3},{5,4},{6,5},{7,6},{8,15},{9,8},{10,9... | collective-permute-start | bytes 2752520 | tf_op jit(solution)/shard_map/ppermute | solution.py:20
  94.8 42.6 %copy-start.4 = (bf16[128,3584]{1,0:T(8,128)(2,1)}, bf16[128,3584]{1,0:T(8,128)(2,1)S(1)}, u32[]{:S(2)}) copy-start(bf16[128,3584]{1,0:T(8,128)(2,1)S(1)} %collective-permute-done.4) | copy-start | bytes 2752516
  94.8 36.8 %collective-permute-start.5 = (bf16[128,3584]{1,0:T(8,128)(2,1)S(1)}, bf16[128,3584]{1,0:T(8,128)(2,1)}, u32[]{:S(2)}, u32[]{:S(2)}) collective-permute-start(bf16[128,3584]{1,0:T(8,128)(2,1)S(1)} %collective-permute-done.4), channel_id=1, source_target_pairs={{0,1},{1,2},{2,3},{3,4},{4,5},{5,6},{6,7},{7,0},{8,9},{9,10},{10,1... | collective-permute-start | bytes 2752520 | tf_op jit(solution)/shard_map/ppermute | solution.py:20
  121.8 13.1 %all-to-all-start.1 = ((bf16[8,68,128]{2,1,0:T(8,128)(2,1)}), bf16[8,68,128]{2,1,0:T(8,128)(2,1)S(1)}, u32[]{:S(2)}, u32[]{:S(2)}) async-start(bf16[8,68,128]{2,1,0:T(8,128)(2,1)} %bitcast.95), calls=%async_computation.1 | async-start | bytes 294912 | tf_op jit(solution)/shard_map/all_to_all | solution.py:67
  127.0 25.7 %collective-permute-start.2 = (bf16[128,3584]{1,0:T(8,128)(2,1)}, bf16[128,3584]{1,0:T(8,128)(2,1)}, u32[]{:S(2)}, u32[]{:S(2)}) collective-permute-start(bf16[128,3584]{1,0:T(8,128)(2,1)} %collective-permute-done.1), channel_id=1, source_target_pairs={{0,7},{1,0},{2,1},{3,2},{4,3},{5,4},{6,5},{7,6},{8,15},{9,8},{10,9... | collective-permute-start | bytes 2752520 | tf_op jit(solution)/shard_map/ppermute | solution.py:20
  131.6 24.0 %collective-permute-start.6 = (bf16[128,3584]{1,0:T(8,128)(2,1)}, bf16[128,3584]{1,0:T(8,128)(2,1)}, u32[]{:S(2)}, u32[]{:S(2)}) collective-permute-start(bf16[128,3584]{1,0:T(8,128)(2,1)} %collective-permute-done.5), channel_id=1, source_target_pairs={{0,1},{1,2},{2,3},{3,4},{4,5},{5,6},{6,7},{7,0},{8,9},{9,10},{10,1... | collective-permute-start | bytes 2752520 | tf_op jit(solution)/shard_map/ppermute | solution.py:20
  139.4 22.8 %copy-start.6 = (s32[1,2,64,1]{2,3,1,0:T(1,128)S(1)}, s32[1,2,64,1]{2,3,1,0:T(1,128)}, u32[]{:S(2)}) copy-start(s32[1,2,64,1]{2,3,1,0:T(1,128)} %param.14) | copy-start | bytes 1540
  139.4 22.8 %copy-start.7 = (s32[1,2,64,1]{2,3,1,0:T(1,128)S(1)}, s32[1,2,64,1]{2,3,1,0:T(1,128)}, u32[]{:S(2)}) copy-start(s32[1,2,64,1]{2,3,1,0:T(1,128)} %param.15) | copy-start | bytes 1540
  157.1 17.7 %copy-start = (bf16[1,64,3584]{2,1,0:T(8,128)(2,1)S(1)}, bf16[1,64,3584]{2,1,0:T(8,128)(2,1)}, u32[]{:S(2)}) copy-start(bf16[1,64,3584]{2,1,0:T(8,128)(2,1)} %param.9) | copy-start | bytes 1376260
  158.2 15.6 %all-to-all-start.2 = ((f32[4,476,128]{2,1,0:T(8,128)}), f32[4,476,128]{2,1,0:T(8,128)S(1)}, u32[]{:S(2)}, u32[]{:S(2)}) async-start(f32[4,476,128]{2,1,0:T(8,128)} %reshape.225), calls=%async_computation.2 | async-start | bytes 1966080 | tf_op jit(solution)/shard_map/all_to_all | solution.py:81
  162.2 91.8 %all-gather.7.cloned.1.call-start = ((), (), s32[]{:S(2)}) async-start(), calls=%async_computation.7 | async-start | bytes 4644864 | tf_op jit(solution)/shard_map/all_gather | solution.py:60
  175.0 10.4 %collective-permute-start.7 = (bf16[64,3584]{1,0:T(8,128)(2,1)S(1)}, bf16[64,3584]{1,0:T(8,128)(2,1)S(1)}, u32[]{:S(2)}, u32[]{:S(2)}) collective-permute-start(bf16[64,3584]{1,0:T(8,128)(2,1)S(1)} %fusion.16), channel_id=1, source_target_pairs={{0,32},{32,64},{64,96},{96,128},{128,160},{160,192},{192,224},{224... | collective-permute-start | bytes 1376264 | tf_op jit(solution)/shard_map/ppermute | solution.py:20
  186.6 22.8 %copy-start.5 = (bf16[128,3584]{1,0:T(8,128)(2,1)S(1)}, bf16[128,3584]{1,0:T(8,128)(2,1)}, u32[]{:S(2)}) copy-start(bf16[128,3584]{1,0:T(8,128)(2,1)} %copy-done.4) | copy-start | bytes 2752516
  197.3 56.7 %copy-start.8 = (bf16[1,1,3584,128]{3,2,1,0:T(8,128)(2,1)S(1)}, bf16[1,1,3584,128]{3,2,1,0:T(8,128)(2,1)}, u32[]{:S(2)}) copy-start(bf16[1,1,3584,128]{3,2,1,0:T(8,128)(2,1)} %param.12) | copy-start | bytes 2752516
  207.1 55.5 %copy-start.3 = (bf16[128,3584]{1,0:T(8,128)(2,1)S(1)}, bf16[128,3584]{1,0:T(8,128)(2,1)}, u32[]{:S(2)}) copy-start(bf16[128,3584]{1,0:T(8,128)(2,1)} %copy-done.2) | copy-start | bytes 2752516
  258.4 12.1 %all-to-all-start.4 = ((bf16[8,68,128]{2,1,0:T(8,128)(2,1)}), bf16[8,68,128]{2,1,0:T(8,128)(2,1)S(1)}, u32[]{:S(2)}, u32[]{:S(2)}) async-start(bf16[8,68,128]{2,1,0:T(8,128)(2,1)} %bitcast.96), calls=%async_computation.4 | async-start | bytes 294912 | tf_op jit(solution)/shard_map/all_to_all | solution.py:67
  276.7 15.4 %all-to-all-start.5 = ((f32[4,476,128]{2,1,0:T(8,128)}), f32[4,476,128]{2,1,0:T(8,128)S(1)}, u32[]{:S(2)}, u32[]{:S(2)}) async-start(f32[4,476,128]{2,1,0:T(8,128)} %reshape.231), calls=%async_computation.5 | async-start | bytes 1966080 | tf_op jit(solution)/shard_map/all_to_all | solution.py:81
Sparse Core Ops, SparseCore 0:
  25.4 91.7 all-gather.4
  197.5 56.4 all-gather.6
